TPU v7x, 256 devices: a whole 4x4x8 slice. The times are simulated.
256 devices in a mesh: walker: 32 (over z, x_lo, core), vec: 8 (over x_hi, y).
Axes of the slice: x: 4 (x_hi: 2, x_lo: 2; x = x_hi * 2 + x_lo), y: 4, z: 8, core: 2. Of those that a mesh axis runs over, the one named last changes fastest.
Arguments:
- copy_counts: int32 [32], P('walker'), may hold values from 0 to 2, as said below
- panels: bfloat16 [32, 200, 2048], P('walker', 'vec'), may hold values from -6 to 6
- inverse_intersection: bfloat16 [32, 200, 200], P('walker', 'vec'), may hold values from -0.4375 to 0.4375
- trial_orbitals: bfloat16 [200, 2048], replicated, may hold values from -0.0625 to 0.0625
- chol_tiles: bfloat16 [256, 128, 128], P(('walker', 'vec')), may hold values from -1.25 to 1.25
- tile_blocks: int32 [256, 2], replicated, may hold values from 0 to 15
- aux_fields: float32 [32, 64], P('walker'), may hold values from -6 to 6
Outputs:
- new_panels: bfloat16 [32, 200, 2048], P('walker', 'vec')
Inputs may be any that keep to these rules, and one draw needn't show every extreme that they name: `copy_counts`: for k = 0 .. 32 let e_k be the sum of the counts of walkers 0 .. k - 1 minus k. Every e_k lies in 0 .. 1, the first and the last are 0 (the counts sum to 32), and e_k = 1 for at least one k. Some walker has exactly 2 copies.
All inputs are finite; a program needn't handle non-finite values.
Results may differ from a plain program's by a relative error of at most 0.007.
Values may be sent and summed in bfloat16 or wider, within the bound.
No kernel may reach another device: no remote copies, remote signals or barrier semaphores. Data moves between devices by JAX's collectives and lax.ppermute only.
A program may use at most 64 MiB of HBM per device.

v0:
```python
import math

import jax
import jax.numpy as jnp
from jax import lax
from jax.sharding import PartitionSpec as P

KT = 4
TERMS = 3


TIME_STEP_ROOT = 0.1


def from_behind(value, axis, steps):
    count = lax.axis_size(axis)
    leading, last = (max(0, -steps), min(count, count - steps))
    return lax.ppermute(value, axis, [(source, source + steps) for source in range(leading, last)])


def tile_bias(tile_piece, row_blocks, col_blocks, panel_blocks, green_blocks):
    chosen = jnp.take(green_blocks, col_blocks, axis=2)
    product = jnp.einsum("wirl,rkl->wirk", chosen, tile_piece, preferred_element_type=jnp.float32)
    facing = jnp.take(panel_blocks, row_blocks, axis=2)
    return jnp.sum(product * facing, axis=(1, 3))


def force_bias(walker_panels, walker_inverse, trial_orbitals, chol_tiles, tile_blocks):
    walkers, cols_local, orbitals = walker_panels.shape
    tile_size = chol_tiles.shape[1]
    block_count = orbitals // tile_size
    tiles_total = tile_blocks.shape[0]
    green_rows = jnp.einsum(
        "wij,jm->wim", walker_inverse, trial_orbitals, preferred_element_type=jnp.float32
    ).astype(jnp.bfloat16)
    panel_blocks = walker_panels.reshape(walkers, cols_local, block_count, tile_size)
    green_blocks = green_rows.reshape(walkers, cols_local, block_count, tile_size)
    tile_piece = lax.all_gather(chol_tiles, ("walker", "vec"), axis=0, tiled=True)
    contrib = tile_bias(
        tile_piece, tile_blocks[:, 0], tile_blocks[:, 1], panel_blocks, green_blocks
    )
    partial_bias = contrib
    stored = tile_piece
    partial_bias, stored = (partial_bias, stored)
    per_vector = partial_bias.reshape(walkers, tiles_total // KT, KT).sum(axis=2)
    summed_bias = lax.psum(per_vector, "vec")
    return (jnp.clip(TIME_STEP_ROOT * summed_bias, -1.0, 1.0), stored)


def propagate(start_panels, scales, stored, tile_blocks):
    slot_count, cols_local, orbitals = start_panels.shape
    tile_size = stored.shape[1]
    block_count = orbitals // tile_size
    tiles_total = stored.shape[0]
    step_tiles = math.gcd(tiles_total, 256)
    rows_hot = (
        tile_blocks[:, 0][None, :] == jnp.arange(block_count, dtype=jnp.int32)[:, None]
    ).astype(jnp.float32)
    weights = jnp.repeat(scales, KT, axis=1)[:, None, :] * rows_hot[None, :, :]
    col_blocks = tile_blocks[:, 1]
    running = start_panels.astype(jnp.float32)
    series = start_panels
    for degree in range(1, TERMS + 1):
        series_blocks = series.reshape(slot_count, cols_local, block_count, tile_size)

        def add_block(block_index, summed):
            chosen = jnp.take(series_blocks, col_blocks, axis=2)
            product = jnp.einsum(
                "qitl,tkl->qitk", chosen, stored, preferred_element_type=jnp.float32
            )
            return summed + jnp.einsum(
                "qitk,qat->qiak", product, weights, precision=lax.Precision.HIGHEST
            )

        result = lax.fori_loop(
            0,
            tiles_total // step_tiles,
            add_block,
            jnp.zeros((slot_count, cols_local, block_count, tile_size), jnp.float32),
        )
        series = (result / degree).reshape(slot_count, cols_local, orbitals).astype(jnp.bfloat16)
        running = running + series.astype(jnp.float32)
    return running.astype(jnp.bfloat16)


def shards(
    copy_counts, panels, inverse_intersection, trial_orbitals, chol_tiles, tile_blocks, aux_fields
):
    walkers = panels.shape[0]
    every_count = lax.all_gather(copy_counts, "walker", axis=0, tiled=True)
    running_sum = jnp.cumsum(every_count)
    first_slot = lax.axis_index("walker") * walkers
    bias, stored = force_bias(panels, inverse_intersection, trial_orbitals, chol_tiles, tile_blocks)
    own_sums = lax.dynamic_slice_in_dim(running_sum, first_slot, walkers, 0)
    surplus = own_sums[0] - copy_counts[0] - first_slot
    new_index = first_slot + jnp.arange(2 * walkers, dtype=jnp.int32)
    parent = jnp.minimum(
        jnp.sum((own_sums[None, :] <= new_index[:, None]).astype(jnp.int32), axis=1), walkers - 1
    )
    right_fields = from_behind(aux_fields, "walker", -1)
    field_pool = jnp.concatenate([aux_fields, right_fields], axis=0)
    scales = TIME_STEP_ROOT * (field_pool - jnp.take(bias, parent, axis=0))
    copies = propagate(jnp.take(panels, parent, axis=0), scales, stored, tile_blocks)
    arrived = from_behind(copies[walkers:], "walker", 1)
    keep_own = (jnp.arange(walkers, dtype=jnp.int32) >= surplus)[:, None, None]
    return jnp.where(keep_own, copies[:walkers], arrived)


def solution(mesh):
    return jax.shard_map(
        shards,
        mesh=mesh,
        in_specs=(
            P("walker"),
            P("walker", "vec", None),
            P("walker", "vec", None),
            P(),
            P(("walker", "vec"), None, None),
            P(),
            P("walker", None),
        ),
        out_specs=P("walker", "vec", None),
        check_vma=False,
    )
```

profile of v0, /device:TPU:2, one launch (start us, length us, event | category | flops | bytes accessed | tf_op | source)
XLA Modules:
  0.0 865.9 jit_solution(1294676800339931212)
XLA Ops:
  7.3 1.9 collective-permute-start
  9.2 1.0 convolution_convert_fusion
  10.3 0.9 copy.50
  11.9 1.2 dynamic-slice.1
  13.9 19.8 %all-reduce = s32[32]{0:T(128)S(1)} all-reduce(s32[32]{0:T(128)S(1)} %dynamic-update-slice), channel_id=1, replica_groups=mesh['walker'=32,'vec'=8] {'walker'}, use_global_device_ids=true, to_apply=%add | all-reduce | flops 32 | bytes 256
  34.6 1.0 gather_fusion
  37.0 15.0 %gather_fusion.2 = bf16[256,2,25,128]{3,1,2,0:T(2,128)(2,1)} fusion(bf16[2,25,16,128]{3,0,2,1:T(2,128)(2,1)S(1)} %broadcast_select_fusion.3, s32[1024]{0:T(1024)S(1)} %pad_clamp_fusion.1), kind=kCustom, calls=%fused_computation.1.clone | custom fusion | bytes 6554624 | tf_op jit(solution)/shard_map/while/body/eval_jaxpr/jit(_take)/gather | solution.py:67
  52.0 2.3 gather_fusion.1
  54.3 6.8 fusion.16
  61.1 670.6 %all-gather.2.cloned.1.call-done = bf16[256,128,128]{2,1,0:T(8,128)(2,1)} async-done(((bf16[1,128,128]{2,1,0:T(8,128)(2,1)}), bf16[256,128,128]{2,1,0:T(8,128)(2,1)}) %all-gather.2.cloned.1.call-update) | async-done | bytes 8388624 | tf_op jit(solution)/shard_map/all_gather | solution.py:38
  731.7 8.1 fusion.12
  740.1 19.0 %psum.7 = f32[1,64]{1,0:T(1,128)S(1)} all-reduce(f32[1,64]{1,0:T(1,128)S(1)} %bitcast.126), channel_id=1, replica_groups=mesh['walker'=32,'vec'=8] {'vec'}, use_global_device_ids=true, to_apply=%region_3.5 | all-reduce | flops 64 | bytes 512 | tf_op jit(solution)/shard_map/psum | solution.py:46
  759.3 10.2 %fusion.19 = f32[2,25,256,128]{3,1,0,2:T(8,128)S(1)} fusion(bf16[256,128,128]{2,1,0:T(8,128)(2,1)} %all-gather.2.cloned.1.call-done, bf16[2,25,256,128]{3,0,1,2:T(2,128)(2,1)} %fusion.16), kind=kOutput, calls=%fused_computation.28 | convolution fusion | flops 419430400 | bytes 18219008 | tf_op jit(solution)/shard_map/while/body/eval_jaxpr/qitl,tkl->qitk/dot_general | solution.py:68
  769.6 6.8 fusion.58
  776.5 15.4 %gather_fusion.3 = bf16[256,2,25,128]{3,1,2,0:T(2,128)(2,1)} fusion(bf16[2,25,16,128]{3,0,2,1:T(2,128)(2,1)S(1)} %copy.38, s32[1024]{0:T(1024)S(1)} %pad_clamp_fusion.1), kind=kCustom, calls=%fused_computation.3.clone | custom fusion | bytes 6554624 | tf_op jit(solution)/shard_map/while/body/eval_jaxpr/jit(_take)/gather | solution.py:67
  791.8 5.0 fusion.17
  796.9 8.3 fusion.24
  805.2 6.8 fusion.61
  813.7 15.2 %gather_fusion.4 = bf16[256,2,25,128]{3,1,2,0:T(2,128)(2,1)} fusion(bf16[2,25,16,128]{3,0,2,1:T(2,128)(2,1)S(1)} %copy.42, s32[1024]{0:T(1024)S(1)} %pad_clamp_fusion.1), kind=kCustom, calls=%fused_computation.4.clone | custom fusion | bytes 6554624 | tf_op jit(solution)/shard_map/while/body/eval_jaxpr/jit(_take)/gather | solution.py:67
  828.9 5.0 fusion.18
  833.9 8.4 fusion.29
  842.3 6.8 fusion.49
  850.6 1.9 collective-permute-start.1
  853.1 4.5 collective-permute-done.1
  (50 shorter events, 8.8 us)
Async XLA Ops:
  6.5 2.7 copy-start
  6.5 30.2 %copy-start.3 = (bf16[1,25,2048]{2,1,0:T(8,128)(2,1)S(1)}, bf16[1,25,2048]{2,1,0:T(8,128)(2,1)}, u32[]{:S(2)}) copy-start(bf16[1,25,2048]{2,1,0:T(8,128)(2,1)} %param.12) | copy-start | bytes 307204
  6.5 725.2 %all-gather.2.cloned.1.call-start = ((), (), s32[]{:S(2)}) async-start(), calls=%async_computation | async-start | bytes 8421376 | tf_op jit(solution)/shard_map/all_gather | solution.py:38
  7.3 751.8 %collective-permute-start = (f32[1,64]{1,0:T(1,128)}, f32[1,64]{1,0:T(1,128)S(1)}, u32[]{:S(2)}, u32[]{:S(2)}) collective-permute-start(f32[1,64]{1,0:T(1,128)} %param.17), channel_id=1, source_target_pairs={{8,0},{16,8},{24,16},{32,24},{40,32},{48,40},{56,48},{64,56},{72,6... | collective-permute-start | bytes 776 | tf_op jit(solution)/shard_map/ppermute | solution.py:18
  731.7 27.3 %copy-start.4 = (f32[1,64]{1,0:T(1,128)S(1)}, f32[1,64]{1,0:T(1,128)}, u32[]{:S(2)}) copy-start(f32[1,64]{1,0:T(1,128)} %param.17) | copy-start | bytes 772
  842.3 7.0 copy-start.1
  842.3 7.3 copy-start.2
  850.6 7.1 collective-permute-start.1
Sparse Core Ops, SparseCore 0:
  9.2 722.4 all-gather.1
where the time goes:
time: 882 us; the launch traced here: 866 us
  waiting for transfers between devices  676 us (77%)
  local copies, waits for them, and re-layouts  57 us (6%)
  matrix products  56.3 us (6%)
  blocking collectives  38.8 us (4%)
  other arithmetic  18.9 us (2%)
  between operations  15.4 us (2%)
    all_gather x1, waiting for transfers between devices, force_bias(): lax.all_gather(chol_tiles, ('walker', 'vec'), axis=0, tiled=True)  671 us
    gather x3, local copies, waits for them, and re-layouts, add_block(): chosen = jnp.take(series_blocks, col_blocks, axis=2)  45.5 us
    dot_general x3, matrix products, add_block(): jnp.einsum('qitl,tkl->qitk', chosen, stored, preferred_element_type=jnp.f...  26.9 us
    dot_general x3, matrix products, add_block(): jnp.einsum('qitk,qat->qiak', product, weights, precision=lax.Precision.HI...  20.3 us
    unnamed x1, blocking collectives  19.8 us
    psum x1, blocking collectives, force_bias(): summed_bias = lax.psum(per_vector, 'vec')  19 us
  transfers between devices with their start and end apart: 3, of which 2 were waited for; matrix products, arithmetic and copies ran while one was open for 5% of the time, Pallas kernels for 0%

commit v1 on v0

v1 whole, which is shorter than its diff:
```python
import functools

import jax
import jax.numpy as jnp
from jax import lax
from jax.experimental import pallas as pl
from jax.experimental.pallas import tpu as pltpu
from jax.sharding import PartitionSpec as P

KT = 4
TERMS = 3
TIME_STEP_ROOT = 0.1
ROWS = 32
INTERPRET = False


def shift_from(value, axis, steps):
    count = lax.axis_size(axis)
    return lax.ppermute(value, axis, [(i, i + steps) for i in range(count - steps)])


def butterfly_sum(value, axis):
    count = lax.axis_size(axis)
    step = 1
    while step < count:
        value = value + lax.ppermute(value, axis, [(i, i ^ step) for i in range(count)])
        step *= 2
    return value


def bias_kernel(rb_ref, cb_ref, pt_ref, g_ref, tiles_ref, out_ref, m_ref):
    blocks, size, _ = m_ref.shape
    for a in range(blocks):
        m_ref[a] = jnp.dot(
            pt_ref[a * size:(a + 1) * size, :], g_ref[...], preferred_element_type=jnp.float32
        )

    def one(t, carry):
        col = pl.multiple_of(cb_ref[t] * size, size)
        blk = m_ref[rb_ref[t], :, pl.ds(col, size)]
        prod = blk * tiles_ref[t].astype(jnp.float32)
        out_ref[pl.ds(t, 1), :] = jnp.sum(prod, axis=0, keepdims=True)
        return carry

    lax.fori_loop(0, tiles_ref.shape[0], one, 0)


def tile_bias(panel_t, green, tiles, rb, cb):
    tiles_total, size, _ = tiles.shape
    orbitals = green.shape[1]
    blocks = orbitals // size
    return pl.pallas_call(
        bias_kernel,
        out_shape=jax.ShapeDtypeStruct((tiles_total, size), jnp.float32),
        in_specs=[
            pl.BlockSpec(memory_space=pltpu.SMEM),
            pl.BlockSpec(memory_space=pltpu.SMEM),
            pl.BlockSpec(memory_space=pltpu.VMEM),
            pl.BlockSpec(memory_space=pltpu.VMEM),
            pl.BlockSpec(memory_space=pltpu.VMEM),
        ],
        out_specs=pl.BlockSpec(memory_space=pltpu.VMEM),
        scratch_shapes=[pltpu.VMEM((blocks, size, orbitals), jnp.float32)],
        compiler_params=pltpu.CompilerParams(vmem_limit_bytes=48 * 1024 * 1024),
        interpret=INTERPRET,
    )(rb, cb, panel_t, green, tiles)


def prop_kernel(rb_ref, cb_ref, s_ref, x_ref, tiles_ref, out_ref, a_ref, hi_ref, lo_ref, y_ref):
    blocks, size, orbitals = a_ref.shape
    a_ref[...] = jnp.zeros(a_ref.shape, jnp.float32)

    def build(t, carry):
        col = pl.multiple_of(cb_ref[t] * size, size)
        row = rb_ref[t]
        a_ref[row, :, pl.ds(col, size)] += s_ref[t] * tiles_ref[t].astype(jnp.float32)
        return carry

    lax.fori_loop(0, tiles_ref.shape[0], build, 0)

    def split(a, carry):
        whole = a_ref[a]
        high = whole.astype(jnp.bfloat16)
        hi_ref[a] = high
        lo_ref[a] = (whole - high.astype(jnp.float32)).astype(jnp.bfloat16)
        return carry

    lax.fori_loop(0, blocks, split, 0)

    dims = (((1,), (1,)), ((), ()))
    series = x_ref[...]
    running = series.astype(jnp.float32)
    for degree in range(1, TERMS + 1):
        for a in range(blocks):
            y_ref[:, a * size:(a + 1) * size] = lax.dot_general(
                series, hi_ref[a], dims, preferred_element_type=jnp.float32
            ) + lax.dot_general(series, lo_ref[a], dims, preferred_element_type=jnp.float32)
        series = (y_ref[...] / degree).astype(jnp.bfloat16)
        running = running + series.astype(jnp.float32)
    out_ref[...] = running.astype(out_ref.dtype)


def propagate(x0, tiles, rb, cb, scales):
    tiles_total, size, _ = tiles.shape
    rows, orbitals = x0.shape
    blocks = orbitals // size
    return pl.pallas_call(
        prop_kernel,
        out_shape=jax.ShapeDtypeStruct((rows, orbitals), jnp.bfloat16),
        in_specs=[
            pl.BlockSpec(memory_space=pltpu.SMEM),
            pl.BlockSpec(memory_space=pltpu.SMEM),
            pl.BlockSpec(memory_space=pltpu.SMEM),
            pl.BlockSpec(memory_space=pltpu.VMEM),
            pl.BlockSpec(memory_space=pltpu.VMEM),
        ],
        out_specs=pl.BlockSpec(memory_space=pltpu.VMEM),
        scratch_shapes=[
            pltpu.VMEM((blocks, size, orbitals), jnp.float32),
            pltpu.VMEM((blocks, size, orbitals), jnp.bfloat16),
            pltpu.VMEM((blocks, size, orbitals), jnp.bfloat16),
            pltpu.VMEM((rows, orbitals), jnp.float32),
        ],
        compiler_params=pltpu.CompilerParams(vmem_limit_bytes=56 * 1024 * 1024),
        interpret=INTERPRET,
    )(rb, cb, scales, x0, tiles)


def pad_rows(x):
    return jnp.pad(x, ((0, ROWS - x.shape[0]), (0, 0)))


def shards(
    copy_counts, panels, inverse_intersection, trial_orbitals, chol_tiles, tile_blocks, aux_fields
):
    cols_local = panels.shape[1]
    walker_id = lax.axis_index("walker")
    running = copy_counts
    step = 1
    while step < lax.axis_size("walker"):
        running = running + shift_from(running, "walker", step)
        step *= 2
    surplus = running[0] - copy_counts[0] - walker_id
    from_prev = surplus > 0

    prev_panel = shift_from(panels, "walker", 1)
    tiles = lax.all_gather(
        lax.all_gather(chol_tiles, "vec", axis=0, tiled=True), "walker", axis=0, tiled=True
    )
    rb = tile_blocks[:, 0]
    cb = tile_blocks[:, 1]
    tiles_total = tiles.shape[0]

    own = panels[0]
    green = jnp.dot(
        inverse_intersection[0], trial_orbitals, preferred_element_type=jnp.float32
    ).astype(jnp.bfloat16)
    partial = tile_bias(pad_rows(own).T, pad_rows(green), tiles, rb, cb)
    per_vector = partial.reshape(tiles_total // KT, KT * partial.shape[1]).sum(axis=1)
    raw = butterfly_sum(per_vector, "vec")
    bias_own = jnp.clip(TIME_STEP_ROOT * raw, -1.0, 1.0)
    bias_prev = shift_from(bias_own, "walker", 1)
    bias = jnp.where(from_prev, bias_prev, bias_own)
    scales = TIME_STEP_ROOT * (aux_fields[0] - bias)
    tile_scales = jnp.repeat(scales, KT)
    start = jnp.where(from_prev, prev_panel[0], own)
    out = propagate(pad_rows(start), tiles, rb, cb, tile_scales)
    return out[:cols_local][None]


def solution(mesh):
    return jax.shard_map(
        shards,
        mesh=mesh,
        in_specs=(
            P("walker"),
            P("walker", "vec", None),
            P("walker", "vec", None),
            P(),
            P(("walker", "vec"), None, None),
            P(),
            P("walker", None),
        ),
        out_specs=P("walker", "vec", None),
        check_vma=False,
    )
```

time: 882 us -> 205 us (0.23); the launches traced: 866 us -> 203 us
  waiting for transfers between devices: 676 us -> 64.7 us
  matrix products: 56.3 us -> 0.98 us
  local copies, waits for them, and re-layouts: 57 us -> 5.12 us
  Pallas kernels: 0 us -> 40.9 us
  starting transfers between devices: 3.85 us -> 37 us
  other arithmetic: 18.9 us -> 0.26 us
    all_gather x1, waiting for transfers between devices: 671 us -> 59.6 us  [shards(): lax.all_gather(lax.all_gather(chol_tiles, 'vec', axis=0, tiled=True), 'wa...]
    dot_general x8 -> x1, matrix products: 56.3 us -> 0.98 us  [shards(): jnp.dot(inverse_intersection[0], trial_orbitals, preferred_element_type=j...]
    gather x5 -> x0, local copies, waits for them, and re-layouts: 48.8 us -> none  [the longest x3 45.5 us: add_block(): chosen = jnp.take(series_blocks, col_blocks, axis=2)]
    pallas_call x0 -> x2, Pallas kernels: none -> 40.9 us  [the longest x1 28.2 us: propagate(): pl.pallas_call(prop_kernel, out_shape=jax.ShapeDtypeStruct((rows, orbital...]
    all_gather x0 -> x1, blocking collectives: none -> 36.8 us  [shards(): lax.all_gather(chol_tiles, 'vec', axis=0, tiled=True)]
    ppermute x2 -> x10, starting transfers between devices: 3.84 us -> 37 us  [the longest x7 30.7 us: shift_from(): lax.ppermute(value, axis, [(i, i + steps) for i in range(count - steps)])]
    unnamed x1 -> x0, blocking collectives: 19.8 us -> none
    psum x1 -> x0, blocking collectives: 19 us -> none  [force_bias(): summed_bias = lax.psum(per_vector, 'vec')]
  transfers between devices with their start and end apart: 3 -> 11, of which waited for: 2 -> 3; matrix products, arithmetic and copies ran while one was open for 5% -> 2% of each run, Pallas kernels for 0% -> 6%
where the time goes in v1:
time: 205 us; the launch traced here: 203 us
  waiting for transfers between devices  64.7 us (32%)
  Pallas kernels  40.9 us (20%)
  starting transfers between devices  37 us (18%)
  blocking collectives  36.8 us (18%)
  between operations  17.3 us (8%)
  local copies, waits for them, and re-layouts  5.12 us (2%)
    all_gather x1, waiting for transfers between devices, shards(): lax.all_gather(lax.all_gather(chol_tiles, 'vec', axis=0, tiled=True), 'wa...  59.6 us
    all_gather x1, blocking collectives, shards(): lax.all_gather(chol_tiles, 'vec', axis=0, tiled=True)  36.8 us
    ppermute x7, starting transfers between devices, shift_from(): lax.ppermute(value, axis, [(i, i + steps) for i in range(count - steps)])  30.7 us
    pallas_call x1, Pallas kernels, propagate(): pl.pallas_call(prop_kernel, out_shape=jax.ShapeDtypeStruct((rows, orbital...  28.2 us
    pallas_call x1, Pallas kernels, tile_bias(): pl.pallas_call(bias_kernel, out_shape=jax.ShapeDtypeStruct((tiles_total,...  12.7 us
    ppermute x3, starting transfers between devices, butterfly_sum(): lax.ppermute(value, axis, [(i, i ^ step) for i in range(count)])  6.31 us
  transfers between devices with their start and end apart: 11, of which 3 were waited for; matrix products, arithmetic and copies ran while one was open for 2% of the time, Pallas kernels for 6%

profile of v1, /device:TPU:2, one launch (start us, length us, event | category | flops | bytes accessed | tf_op | source)
XLA Modules:
  0.0 203.1 jit_solution(16420506200610088832)
XLA Ops:
  6.5 36.8 %all_gather.6 = bf16[8,128,128]{2,1,0:T(8,128)(2,1)} all-gather(bf16[1,128,128]{2,1,0:T(8,128)(2,1)} %param.11), channel_id=1, replica_groups=mesh['walker'=32,'vec'=8] {'vec'}, dimensions={0}, use_global_device_ids=true | all-gather | bytes 294912 | tf_op jit(solution)/shard_map/all_gather | solution.py:148
  43.4 1.9 collective-permute-start
  45.3 4.4 %collective-permute-start.9 = (bf16[1,25,2048]{2,1,0:T(8,128)(2,1)}, bf16[1,25,2048]{2,1,0:T(8,128)(2,1)S(1)}, u32[]{:S(2)}, u32[]{:S(2)}) collective-permute-start(bf16[1,25,2048]{2,1,0:T(8,128)(2,1)} %param.8), channel_id=1, source_target_pairs={{0,8},{8,16},{16,24},{24,32},{32,40},{40,48},{48,56},{56,64},{64,7... | collective-permute-start | bytes 307208 | tf_op jit(solution)/shard_map/ppermute | solution.py:19
  50.4 0.9 pad_bitcast_fusion
  51.3 0.3 copy.10.pt_ref
  51.6 1.0 convolution_convert_fusion
  52.6 0.8 fusion.3
  54.0 4.2 %collective-permute-start.1 = (s32[1]{0:T(128)}, s32[1]{0:T(128)}, u32[]{:S(2)}, u32[]{:S(2)}) collective-permute-start(s32[1]{0:T(128)} %add.30), channel_id=1, source_target_pairs={{0,16},{8,24},{16,32},{24,40},{32,48},{40,56},{48,64},{56,72},{64,... | collective-permute-start | bytes 20 | tf_op jit(solution)/shard_map/ppermute | solution.py:19
  58.2 59.6 %all-gather.2.cloned.1.call-done.tiles_ref = bf16[256,128,128]{2,1,0:T(8,128)(2,1)} async-done(((bf16[8,128,128]{2,1,0:T(8,128)(2,1)}), bf16[256,128,128]{2,1,0:T(8,128)(2,1)}) %all-gather.2.cloned.1.call-update) | async-done | bytes 8388624 | tf_op jit(solution)/shard_map/all_gather | solution.py:147
  117.8 12.7 %shard_map.73 = f32[256,128]{1,0:T(8,128)S(1)} custom-call(s32[256]{0:T(256)S(1)} %bitcast.19, s32[256]{0:T(256)S(1)} %bitcast.17, bf16[2048,32]{1,0:T(8,128)(2,1)S(1)} %copy.10.pt_ref, bf16[32,2048]{1,0:T(8,128)(2,1)S(1)} %pad.11.g_ref, bf16[256,128,128]{2,1,0:T(8,128)(2,1)} %all-gather.2.cloned.1.call-done.tiles_ref), custom_call_target="tpu_custom_call" | custom-call | tf_op jit(solution)/shard_map/pallas_call | solution.py:52
  130.5 0.1 reduce_sum.10
  130.9 1.5 collective-permute-start.5
  133.1 3.8 %collective-permute-start.2 = (s32[1]{0:T(128)}, s32[1]{0:T(128)}, u32[]{:S(2)}, u32[]{:S(2)}) collective-permute-start(s32[1]{0:T(128)} %add.31), channel_id=1, source_target_pairs={{0,32},{8,40},{16,48},{24,56},{32,64},{40,72},{48,80},{56,88},{64,... | collective-permute-start | bytes 20 | tf_op jit(solution)/shard_map/ppermute | solution.py:19
  137.5 6.4 %collective-permute-start.3 = (s32[1]{0:T(128)}, s32[1]{0:T(128)}, u32[]{:S(2)}, u32[]{:S(2)}) collective-permute-start(s32[1]{0:T(128)} %add.32), channel_id=1, source_target_pairs={{0,64},{8,72},{16,80},{24,88},{32,96},{40,104},{48,112},{56,120},{... | collective-permute-start | bytes 20 | tf_op jit(solution)/shard_map/ppermute | solution.py:19
  143.9 2.6 %collective-permute-start.6 = (f32[64]{0:T(128)S(1)}, f32[64]{0:T(128)S(1)}, u32[]{:S(2)}, u32[]{:S(2)}) collective-permute-start(f32[64]{0:T(128)S(1)} %add.35), channel_id=1, source_target_pairs={{0,2},{1,3},{2,0},{3,1},{4,6},{5,7},{6,4},{7,5},{8,10},{9,11},{10,... | collective-permute-start | bytes 776 | tf_op jit(solution)/shard_map/ppermute | solution.py:26
  147.1 7.9 %collective-permute-start.4 = (s32[1]{0:T(128)}, s32[1]{0:T(128)}, u32[]{:S(2)}, u32[]{:S(2)}) collective-permute-start(s32[1]{0:T(128)} %add.33), channel_id=1, source_target_pairs={{0,128},{8,136},{16,144},{24,152},{32,160},{40,168},{48,176},{56,1... | collective-permute-start | bytes 20 | tf_op jit(solution)/shard_map/ppermute | solution.py:19
  155.7 2.2 %collective-permute-start.7 = (f32[64]{0:T(128)S(1)}, f32[64]{0:T(128)S(1)}, u32[]{:S(2)}, u32[]{:S(2)}) collective-permute-start(f32[64]{0:T(128)S(1)} %add.36), channel_id=1, source_target_pairs={{0,4},{1,5},{2,6},{3,7},{4,0},{5,1},{6,2},{7,3},{8,12},{9,13},{10,... | collective-permute-start | bytes 776 | tf_op jit(solution)/shard_map/ppermute | solution.py:26
  157.8 3.0 %collective-permute-done.7 = f32[64]{0:T(128)S(1)} collective-permute-done((f32[64]{0:T(128)S(1)}, f32[64]{0:T(128)S(1)}, u32[]{:S(2)}, u32[]{:S(2)}) %collective-permute-start.7) | collective-permute-done | bytes 288 | tf_op jit(solution)/shard_map/ppermute | solution.py:26
  160.8 2.1 %collective-permute-start.8 = (f32[64]{0:T(128)S(1)}, f32[64]{0:T(128)S(1)}, u32[]{:S(2)}, u32[]{:S(2)}) collective-permute-start(f32[64]{0:T(128)S(1)} %multiply_clamp_fusion), channel_id=1, source_target_pairs={{0,8},{8,16},{16,24},{24,32},{32,40},{40,48},{48,56},{56,64},{64,7... | collective-permute-start | bytes 776 | tf_op jit(solution)/shard_map/ppermute | solution.py:19
  163.0 0.7 pad.12.x_ref
  163.6 2.1 %collective-permute-done.8 = f32[64]{0:T(128)S(1)} collective-permute-done((f32[64]{0:T(128)S(1)}, f32[64]{0:T(128)S(1)}, u32[]{:S(2)}, u32[]{:S(2)}) %collective-permute-start.8) | collective-permute-done | bytes 288 | tf_op jit(solution)/shard_map/ppermute | solution.py:19
  165.8 0.7 reshape.6.s_ref
  166.5 28.2 %shard_map.74 = bf16[32,2048]{1,0:T(8,128)(2,1)} custom-call(s32[256]{0:T(256)} %bitcast.20, s32[256]{0:T(256)} %bitcast.18, f32[256]{0:T(256)} %reshape.6.s_ref, bf16[32,2048]{1,0:T(8,128)(2,1)} %pad.12.x_ref, bf16[256,128,128]{2,1,0:T(8,128)(2,1)} %all-gather.2.cloned.1.call-done.tiles_ref), custom_call_target="tpu_custom_call" | custom-call | tf_op jit(solution)/shard_map/pallas_call | solution.py:107
  194.7 1.6 slice_bitcast_fusion
  (29 shorter events, 0.4 us)
Async XLA Ops:
  6.5 45.1 %copy-start = (bf16[200,2048]{1,0:T(8,128)(2,1)S(1)}, bf16[200,2048]{1,0:T(8,128)(2,1)}, u32[]{:S(2)}) copy-start(bf16[200,2048]{1,0:T(8,128)(2,1)} %param.10) | copy-start | bytes 2457604
  6.5 156.4 %copy-start.3 = (bf16[1,25,2048]{2,1,0:T(8,128)(2,1)S(1)}, bf16[1,25,2048]{2,1,0:T(8,128)(2,1)}, u32[]{:S(2)}) copy-start(bf16[1,25,2048]{2,1,0:T(8,128)(2,1)} %param.8) | copy-start | bytes 307204
  6.5 159.2 %copy-start.4 = (f32[1,64]{1,0:T(1,128)S(1)}, f32[1,64]{1,0:T(1,128)}, u32[]{:S(2)}) copy-start(f32[1,64]{1,0:T(1,128)} %param.13) | copy-start | bytes 772
  6.5 111.3 %all-gather.2.cloned.1.call-start = ((), (), s32[]{:S(2)}) async-start(), calls=%async_computation | async-start | bytes 8650752 | tf_op jit(solution)/shard_map/all_gather | solution.py:147
  43.4 10.0 %collective-permute-start = (s32[1]{0:T(128)}, s32[1]{0:T(128)}, u32[]{:S(2)}, u32[]{:S(2)}) collective-permute-start(s32[1]{0:T(128)} %param.7), channel_id=1, source_target_pairs={{0,8},{8,16},{16,24},{24,32},{32,40},{40,48},{48,56},{56,64},{64,7... | collective-permute-start | bytes 20 | tf_op jit(solution)/shard_map/ppermute | solution.py:19
  45.3 117.6 %collective-permute-start.9 = (bf16[1,25,2048]{2,1,0:T(8,128)(2,1)}, bf16[1,25,2048]{2,1,0:T(8,128)(2,1)S(1)}, u32[]{:S(2)}, u32[]{:S(2)}) collective-permute-start(bf16[1,25,2048]{2,1,0:T(8,128)(2,1)} %param.8), channel_id=1, source_target_pairs={{0,8},{8,16},{16,24},{24,32},{32,40},{40,48},{48,56},{56,64},{64,7... | collective-permute-start | bytes 307208 | tf_op jit(solution)/shard_map/ppermute | solution.py:19
  53.4 113.1 %copy-start.1 = (s32[256,1]{0,1:T(1,128)}, s32[256,1]{0,1:T(1,128)S(1)}, u32[]{:S(2)}) copy-start(s32[256,1]{0,1:T(1,128)S(1)} %get-tuple-element.5) | copy-start | bytes 3076
  53.4 113.1 %copy-start.2 = (s32[256,1]{0,1:T(1,128)}, s32[256,1]{0,1:T(1,128)S(1)}, u32[]{:S(2)}) copy-start(s32[256,1]{0,1:T(1,128)S(1)} %get-tuple-element.6) | copy-start | bytes 3076
  54.0 78.4 %collective-permute-start.1 = (s32[1]{0:T(128)}, s32[1]{0:T(128)}, u32[]{:S(2)}, u32[]{:S(2)}) collective-permute-start(s32[1]{0:T(128)} %add.30), channel_id=1, source_target_pairs={{0,16},{8,24},{16,32},{24,40},{32,48},{40,56},{48,64},{56,72},{64,... | collective-permute-start | bytes 20 | tf_op jit(solution)/shard_map/ppermute | solution.py:19
  130.9 13.0 %collective-permute-start.5 = (f32[64]{0:T(128)S(1)}, f32[64]{0:T(128)S(1)}, u32[]{:S(2)}, u32[]{:S(2)}) collective-permute-start(f32[64]{0:T(128)S(1)} %reduce_sum.18), channel_id=1, source_target_pairs={{0,1},{1,0},{2,3},{3,2},{4,5},{5,4},{6,7},{7,6},{8,9},{9,8},{10,11... | collective-permute-start | bytes 776 | tf_op jit(solution)/shard_map/ppermute | solution.py:26
  133.1 3.8 %collective-permute-start.2 = (s32[1]{0:T(128)}, s32[1]{0:T(128)}, u32[]{:S(2)}, u32[]{:S(2)}) collective-permute-start(s32[1]{0:T(128)} %add.31), channel_id=1, source_target_pairs={{0,32},{8,40},{16,48},{24,56},{32,64},{40,72},{48,80},{56,88},{64,... | collective-permute-start | bytes 20 | tf_op jit(solution)/shard_map/ppermute | solution.py:19
  137.5 9.0 %collective-permute-start.3 = (s32[1]{0:T(128)}, s32[1]{0:T(128)}, u32[]{:S(2)}, u32[]{:S(2)}) collective-permute-start(s32[1]{0:T(128)} %add.32), channel_id=1, source_target_pairs={{0,64},{8,72},{16,80},{24,88},{32,96},{40,104},{48,112},{56,120},{... | collective-permute-start | bytes 20 | tf_op jit(solution)/shard_map/ppermute | solution.py:19
  143.9 11.7 %collective-permute-start.6 = (f32[64]{0:T(128)S(1)}, f32[64]{0:T(128)S(1)}, u32[]{:S(2)}, u32[]{:S(2)}) collective-permute-start(f32[64]{0:T(128)S(1)} %add.35), channel_id=1, source_target_pairs={{0,2},{1,3},{2,0},{3,1},{4,6},{5,7},{6,4},{7,5},{8,10},{9,11},{10,... | collective-permute-start | bytes 776 | tf_op jit(solution)/shard_map/ppermute | solution.py:26
  147.1 7.9 %collective-permute-start.4 = (s32[1]{0:T(128)}, s32[1]{0:T(128)}, u32[]{:S(2)}, u32[]{:S(2)}) collective-permute-start(s32[1]{0:T(128)} %add.33), channel_id=1, source_target_pairs={{0,128},{8,136},{16,144},{24,152},{32,160},{40,168},{48,176},{56,1... | collective-permute-start | bytes 20 | tf_op jit(solution)/shard_map/ppermute | solution.py:19
  155.7 5.2 %collective-permute-start.7 = (f32[64]{0:T(128)S(1)}, f32[64]{0:T(128)S(1)}, u32[]{:S(2)}, u32[]{:S(2)}) collective-permute-start(f32[64]{0:T(128)S(1)} %add.36), channel_id=1, source_target_pairs={{0,4},{1,5},{2,6},{3,7},{4,0},{5,1},{6,2},{7,3},{8,12},{9,13},{10,... | collective-permute-start | bytes 776 | tf_op jit(solution)/shard_map/ppermute | solution.py:26
  160.8 4.9 %collective-permute-start.8 = (f32[64]{0:T(128)S(1)}, f32[64]{0:T(128)S(1)}, u32[]{:S(2)}, u32[]{:S(2)}) collective-permute-start(f32[64]{0:T(128)S(1)} %multiply_clamp_fusion), channel_id=1, source_target_pairs={{0,8},{8,16},{16,24},{24,32},{32,40},{40,48},{48,56},{56,64},{64,7... | collective-permute-start | bytes 776 | tf_op jit(solution)/shard_map/ppermute | solution.py:19
Sparse Core Ops, SparseCore 0:
  43.5 74.2 all-gather.1

commit v2 on v1

v2 whole, which is shorter than its diff:
```python
import functools

import jax
import jax.numpy as jnp
from jax import lax
from jax.experimental import pallas as pl
from jax.experimental.pallas import tpu as pltpu
from jax.sharding import PartitionSpec as P

KT = 4
TERMS = 3
TIME_STEP_ROOT = 0.1
ROWS = 32
INTERPRET = False


def shift_from(value, axis, steps):
    count = lax.axis_size(axis)
    return lax.ppermute(value, axis, [(i, i + steps) for i in range(count - steps)])


def butterfly_sum(value, axis):
    count = lax.axis_size(axis)
    step = 1
    while step < count:
        value = value + lax.ppermute(value, axis, [(i, i ^ step) for i in range(count)])
        step *= 2
    return value


def bias_kernel(*refs):
    count = len(STREAMS)
    rbs, cbs = refs[:count], refs[count:2 * count]
    pt_ref, g_ref = refs[2 * count], refs[2 * count + 1]
    parts = refs[2 * count + 2:3 * count + 2]
    outs = refs[3 * count + 2:4 * count + 2]
    m_ref = refs[-1]
    blocks, size, _ = m_ref.shape
    for a in range(blocks):
        m_ref[a] = jnp.dot(
            pt_ref[a * size:(a + 1) * size, :], g_ref[...], preferred_element_type=jnp.float32
        )
    for (_, low, high), rb_ref, cb_ref, part_ref, out_ref in zip(STREAMS, rbs, cbs, parts, outs):

        def one(t, carry, rb_ref=rb_ref, cb_ref=cb_ref, part_ref=part_ref, out_ref=out_ref, low=low, high=high):
            col = pl.multiple_of(cb_ref[t] * size, size)
            blk = m_ref[rb_ref[t], low:high, pl.ds(col, size)]
            prod = blk * part_ref[t].astype(jnp.float32)
            out_ref[pl.ds(t, 1), :] = jnp.sum(prod, axis=0, keepdims=True)
            return carry

        lax.fori_loop(0, part_ref.shape[0], one, 0)


def tile_bias(panel_t, green, parts, rbs, cbs):
    tiles_total, _, size = parts[0].shape
    orbitals = green.shape[1]
    blocks = orbitals // size
    count = len(parts)
    smem = pl.BlockSpec(memory_space=pltpu.SMEM)
    vmem = pl.BlockSpec(memory_space=pltpu.VMEM)
    return pl.pallas_call(
        bias_kernel,
        out_shape=[jax.ShapeDtypeStruct((tiles_total, size), jnp.float32)] * count,
        in_specs=[smem] * (2 * count) + [vmem] * (2 + count),
        out_specs=[vmem] * count,
        scratch_shapes=[pltpu.VMEM((blocks, size, orbitals), jnp.float32)],
        compiler_params=pltpu.CompilerParams(vmem_limit_bytes=48 * 1024 * 1024),
        interpret=INTERPRET,
    )(*rbs, *cbs, panel_t, green, *parts)


def prop_kernel(*refs):
    count = len(STREAMS)
    rbs, cbs, ss = refs[:count], refs[count:2 * count], refs[2 * count:3 * count]
    x_ref = refs[3 * count]
    parts = refs[3 * count + 1:4 * count + 1]
    out_ref, a_ref, hi_ref, lo_ref, y_ref = refs[4 * count + 1:]
    blocks, size, orbitals = a_ref.shape
    a_ref[...] = jnp.zeros(a_ref.shape, jnp.float32)
    for (_, low, high), rb_ref, cb_ref, s_ref, part_ref in zip(STREAMS, rbs, cbs, ss, parts):

        def build(t, carry, rb_ref=rb_ref, cb_ref=cb_ref, s_ref=s_ref, part_ref=part_ref, low=low, high=high):
            col = pl.multiple_of(cb_ref[t] * size, size)
            row = rb_ref[t]
            a_ref[row, low:high, pl.ds(col, size)] += s_ref[t] * part_ref[t].astype(jnp.float32)
            return carry

        lax.fori_loop(0, part_ref.shape[0], build, 0)

    def split(a, carry):
        whole = a_ref[a]
        high = whole.astype(jnp.bfloat16)
        hi_ref[a] = high
        lo_ref[a] = (whole - high.astype(jnp.float32)).astype(jnp.bfloat16)
        return carry

    lax.fori_loop(0, blocks, split, 0)

    dims = (((1,), (1,)), ((), ()))
    series = x_ref[...]
    running = series.astype(jnp.float32)
    for degree in range(1, TERMS + 1):
        for a in range(blocks):
            y_ref[:, a * size:(a + 1) * size] = lax.dot_general(
                series, hi_ref[a], dims, preferred_element_type=jnp.float32
            ) + lax.dot_general(series, lo_ref[a], dims, preferred_element_type=jnp.float32)
        series = (y_ref[...] / degree).astype(jnp.bfloat16)
        running = running + series.astype(jnp.float32)
    out_ref[...] = running.astype(out_ref.dtype)


def propagate(x0, parts, rbs, cbs, ss):
    size = parts[0].shape[2]
    rows, orbitals = x0.shape
    blocks = orbitals // size
    count = len(parts)
    smem = pl.BlockSpec(memory_space=pltpu.SMEM)
    vmem = pl.BlockSpec(memory_space=pltpu.VMEM)
    return pl.pallas_call(
        prop_kernel,
        out_shape=jax.ShapeDtypeStruct((rows, orbitals), jnp.bfloat16),
        in_specs=[smem] * (3 * count) + [vmem] * (1 + count),
        out_specs=vmem,
        scratch_shapes=[
            pltpu.VMEM((blocks, size, orbitals), jnp.float32),
            pltpu.VMEM((blocks, size, orbitals), jnp.bfloat16),
            pltpu.VMEM((blocks, size, orbitals), jnp.bfloat16),
            pltpu.VMEM((rows, orbitals), jnp.float32),
        ],
        compiler_params=pltpu.CompilerParams(vmem_limit_bytes=56 * 1024 * 1024),
        interpret=INTERPRET,
    )(*rbs, *cbs, *ss, x0, *parts)


STREAMS = (
    ((("walker", 16), ("walker", 8), ("walker", 4), ("vec", 4), ("walker", 2), ("vec", 2), ("vec", 1), ("walker", 1)), 0, 48),
    ((("vec", 2), ("vec", 1), ("walker", 16), ("walker", 8), ("walker", 4), ("vec", 4), ("walker", 2), ("walker", 1)), 48, 96),
    ((("vec", 4), ("walker", 2), ("vec", 2), ("vec", 1), ("walker", 16), ("walker", 8), ("walker", 4), ("walker", 1)), 96, 128),
)


def xor_gather(x, order):
    for axis, step in order:
        count = lax.axis_size(axis)
        other = lax.ppermute(x, axis, [(i, i ^ step) for i in range(count)])
        x = jnp.concatenate([x, other], axis=0)
    return x


def source_tiles(order):
    position = jnp.arange(2 ** len(order), dtype=jnp.int32)
    masks = {"walker": jnp.zeros_like(position), "vec": jnp.zeros_like(position)}
    for bit, (axis, step) in enumerate(order):
        masks[axis] = masks[axis] + ((position >> bit) & 1) * step
    walker = jnp.bitwise_xor(lax.axis_index("walker"), masks["walker"])
    vec = jnp.bitwise_xor(lax.axis_index("vec"), masks["vec"])
    return walker * lax.axis_size("vec") + vec


def pad_rows(x):
    return jnp.pad(x, ((0, ROWS - x.shape[0]), (0, 0)))


def shards(
    copy_counts, panels, inverse_intersection, trial_orbitals, chol_tiles, tile_blocks, aux_fields
):
    cols_local = panels.shape[1]
    walker_id = lax.axis_index("walker")
    running = copy_counts
    step = 1
    while step < lax.axis_size("walker"):
        running = running + shift_from(running, "walker", step)
        step *= 2
    from_prev = running[0] - copy_counts[0] - walker_id > 0

    prev_panel = shift_from(panels, "walker", 1)
    prev_inverse = shift_from(inverse_intersection, "walker", 1)
    parts, rbs, cbs, sources = [], [], [], []
    for order, low, high in STREAMS:
        parts.append(xor_gather(chol_tiles[:, low:high], order))
        source = source_tiles(order)
        sources.append(source)
        rbs.append(jnp.take(tile_blocks[:, 0], source))
        cbs.append(jnp.take(tile_blocks[:, 1], source))

    start = jnp.where(from_prev, prev_panel[0], panels[0])
    inverse = jnp.where(from_prev, prev_inverse[0], inverse_intersection[0])
    green = jnp.dot(inverse, trial_orbitals, preferred_element_type=jnp.float32).astype(jnp.bfloat16)
    partials = tile_bias(pad_rows(start).T, pad_rows(green), parts, rbs, cbs)
    vectors = tile_blocks.shape[0] // KT
    ids = jnp.concatenate([source // KT for source in sources])
    values = jnp.concatenate([partial.sum(axis=1) for partial in partials])
    hot = ids[:, None] == jnp.arange(vectors, dtype=ids.dtype)[None, :]
    per_vector = jnp.sum(jnp.where(hot, values[:, None], 0.0), axis=0)
    raw = butterfly_sum(per_vector, "vec")
    bias = jnp.clip(TIME_STEP_ROOT * raw, -1.0, 1.0)
    scales = TIME_STEP_ROOT * (aux_fields[0] - bias)
    ss = [jnp.take(scales, source // KT) for source in sources]
    out = propagate(pad_rows(start), parts, rbs, cbs, ss)
    return out[:cols_local][None]


def solution(mesh):
    return jax.shard_map(
        shards,
        mesh=mesh,
        in_specs=(
            P("walker"),
            P("walker", "vec", None),
            P("walker", "vec", None),
            P(),
            P(("walker", "vec"), None, None),
            P(),
            P("walker", None),
        ),
        out_specs=P("walker", "vec", None),
        check_vma=False,
    )
```

time: 205 us -> 230 us (1.12); the launches traced: 203 us -> 225 us
  local copies, waits for them, and re-layouts: 5.12 us -> 55.5 us
  blocking collectives: 36.8 us -> 0 us
  starting transfers between devices: 37 us -> 67.1 us
  waiting for transfers between devices: 64.7 us -> 43 us
  between operations: 17.3 us -> 4.28 us
  Pallas kernels: 40.9 us -> 49.9 us
  other arithmetic: 0.26 us -> 5.27 us
    all_gather x1 -> x0, waiting for transfers between devices: 59.6 us -> none  [shards(): lax.all_gather(lax.all_gather(chol_tiles, 'vec', axis=0, tiled=True), 'wa...]
    all_gather x1 -> x0, blocking collectives: 36.8 us -> none  [shards(): lax.all_gather(chol_tiles, 'vec', axis=0, tiled=True)]
    ppermute x0 -> x24, starting transfers between devices: none -> 31 us  [xor_gather(): other = lax.ppermute(x, axis, [(i, i ^ step) for i in range(count)])]
    ppermute x0 -> x24, waiting for transfers between devices: none -> 29.6 us  [xor_gather(): other = lax.ppermute(x, axis, [(i, i ^ step) for i in range(count)])]
    unnamed x10 -> x54, local copies, waits for them, and re-layouts: 0.02 us -> 20.9 us
    gather x0 -> x9, local copies, waits for them, and re-layouts: none -> 17.3 us  [the longest x3 5.83 us: shards(): rbs.append(jnp.take(tile_blocks[:, 0], source))]
    concatenate x0 -> x6, local copies, waits for them, and re-layouts: none -> 12.5 us  [xor_gather(): x = jnp.concatenate([x, other], axis=0)]
    ppermute x3, waiting for transfers between devices: 3 us -> 8.6 us  [butterfly_sum(): lax.ppermute(value, axis, [(i, i ^ step) for i in range(count)])]
  transfers between devices with their start and end apart: 11 -> 34, of which waited for: 3 -> 13; matrix products, arithmetic and copies ran while one was open for 2% -> 19% of each run, Pallas kernels for 6% -> 0%
where the time goes in v2:
time: 230 us; the launch traced here: 225 us
  starting transfers between devices  67.1 us (29%)
  local copies, waits for them, and re-layouts  55.5 us (24%)
  Pallas kernels  49.9 us (22%)
  waiting for transfers between devices  43 us (19%)
  other arithmetic  5.27 us (2%)
  between operations  4.28 us (2%)
    pallas_call x1, Pallas kernels, propagate(): pl.pallas_call(prop_kernel, out_shape=jax.ShapeDtypeStruct((rows, orbital...  32.4 us
    ppermute x24, starting transfers between devices, xor_gather(): other = lax.ppermute(x, axis, [(i, i ^ step) for i in range(count)])  31 us
    ppermute x7, starting transfers between devices, shift_from(): lax.ppermute(value, axis, [(i, i + steps) for i in range(count - steps)])  30.9 us
    ppermute x24, waiting for transfers between devices, xor_gather(): other = lax.ppermute(x, axis, [(i, i ^ step) for i in range(count)])  29.6 us
    unnamed x54, local copies, waits for them, and re-layouts  20.9 us
    pallas_call x1, Pallas kernels, tile_bias(): pl.pallas_call(bias_kernel, out_shape=[jax.ShapeDtypeStruct((tiles_total,...  17.6 us
    concatenate x6, local copies, waits for them, and re-layouts, xor_gather(): x = jnp.concatenate([x, other], axis=0)  12.5 us
    ppermute x3, waiting for transfers between devices, butterfly_sum(): lax.ppermute(value, axis, [(i, i ^ step) for i in range(count)])  8.6 us
  transfers between devices with their start and end apart: 34, of which 13 were waited for; matrix products, arithmetic and copies ran while one was open for 19% of the time, Pallas kernels for 0%

profile of v2, /device:TPU:2, one launch (start us, length us, event | category | flops | bytes accessed | tf_op | source)
XLA Modules:
  0.0 225.4 jit_solution(9902741180108378404)
XLA Ops:
  2.1 3.9 %collective-permute-start.6 = (bf16[1,25,200]{2,1,0:T(8,128)(2,1)}, bf16[1,25,200]{2,1,0:T(8,128)(2,1)S(1)}, u32[]{:S(2)}, u32[]{:S(2)}) collective-permute-start(bf16[1,25,200]{2,1,0:T(8,128)(2,1)} %param.13), channel_id=1, source_target_pairs={{0,8},{8,16},{16,24},{24,32},{32,40},{40,48},{48,56},{56,64},{64,7... | collective-permute-start | bytes 30008 | tf_op jit(solution)/shard_map/ppermute | solution.py:19
  7.4 6.3 %collective-permute-start.7 = (bf16[1,48,128]{2,1,0:T(8,128)(2,1)S(1)}, bf16[1,48,128]{2,1,0:T(8,128)(2,1)S(1)}, u32[]{:S(2)}, u32[]{:S(2)}) collective-permute-start(bf16[1,48,128]{2,1,0:T(8,128)(2,1)S(1)} %get-tuple-element.88), channel_id=1, source_target_pairs={{0,128},{8,136},{16,144},{24,152},{32,160},{40,168},{48,176},{56,1... | collective-permute-start | bytes 36872 | tf_op jit(solution)/shard_map/ppermute | solution.py:146
  13.7 3.2 %collective-permute-start.15 = (bf16[1,48,128]{2,1,0:T(8,128)(2,1)S(1)}, bf16[1,48,128]{2,1,0:T(8,128)(2,1)S(1)}, u32[]{:S(2)}, u32[]{:S(2)}) collective-permute-start(bf16[1,48,128]{2,1,0:T(8,128)(2,1)S(1)} %get-tuple-element.89), channel_id=1, source_target_pairs={{0,2},{1,3},{2,0},{3,1},{4,6},{5,7},{6,4},{7,5},{8,10},{9,11},{10,... | collective-permute-start | bytes 36872 | tf_op jit(solution)/shard_map/ppermute | solution.py:146
  18.2 2.4 %collective-permute-start.23 = (bf16[1,32,128]{2,1,0:T(8,128)(2,1)S(1)}, bf16[1,32,128]{2,1,0:T(8,128)(2,1)S(1)}, u32[]{:S(2)}, u32[]{:S(2)}) collective-permute-start(bf16[1,32,128]{2,1,0:T(8,128)(2,1)S(1)} %get-tuple-element.77), channel_id=1, source_target_pairs={{0,4},{1,5},{2,6},{3,7},{4,0},{5,1},{6,2},{7,3},{8,12},{9,13},{10,... | collective-permute-start | bytes 24584 | tf_op jit(solution)/shard_map/ppermute | solution.py:146
  40.0 2.3 %collective-permute-start.17 = (bf16[4,48,128]{2,1,0:T(8,128)(2,1)S(1)}, bf16[4,48,128]{2,1,0:T(8,128)(2,1)S(1)}, u32[]{:S(2)}, u32[]{:S(2)}) collective-permute-start(bf16[4,48,128]{2,1,0:T(8,128)(2,1)S(1)} %pad_maximum_fusion.4), channel_id=1, source_target_pairs={{0,128},{8,136},{16,144},{24,152},{32,160},{40,168},{48,176},{56,1... | collective-permute-start | bytes 147464 | tf_op jit(solution)/shard_map/ppermute | solution.py:146
  44.9 3.9 %collective-permute-done.17 = bf16[4,48,128]{2,1,0:T(8,128)(2,1)S(1)} collective-permute-done((bf16[4,48,128]{2,1,0:T(8,128)(2,1)S(1)}, bf16[4,48,128]{2,1,0:T(8,128)(2,1)S(1)}, u32[]{:S(2)}, u32[]{:S(2)}) %collective-permute-start.17) | collective-permute-done | bytes 49184 | tf_op jit(solution)/shard_map/ppermute | solution.py:146
  64.0 4.6 %collective-permute-done.26 = bf16[8,32,128]{2,1,0:T(8,128)(2,1)S(1)} collective-permute-done((bf16[8,32,128]{2,1,0:T(8,128)(2,1)S(1)}, bf16[8,32,128]{2,1,0:T(8,128)(2,1)S(1)}, u32[]{:S(2)}, u32[]{:S(2)}) %collective-permute-start.26) | collective-permute-done | bytes 65568 | tf_op jit(solution)/shard_map/ppermute | solution.py:146
  69.3 2.6 %collective-permute-start.27 = (bf16[16,32,128]{2,1,0:T(8,128)(2,1)S(1)}, bf16[16,32,128]{2,1,0:T(8,128)(2,1)S(1)}, u32[]{:S(2)}, u32[]{:S(2)}) collective-permute-start(bf16[16,32,128]{2,1,0:T(8,128)(2,1)S(1)} %get-tuple-element.56), channel_id=1, source_target_pairs={{0,128},{8,136},{16,144},{24,152},{32,160},{40,168},{48,176},{56,1... | collective-permute-start | bytes 393224 | tf_op jit(solution)/shard_map/ppermute | solution.py:146
  75.8 5.1 %collective-permute-done.27 = bf16[16,32,128]{2,1,0:T(8,128)(2,1)S(1)} collective-permute-done((bf16[16,32,128]{2,1,0:T(8,128)(2,1)S(1)}, bf16[16,32,128]{2,1,0:T(8,128)(2,1)S(1)}, u32[]{:S(2)}, u32[]{:S(2)}) %collective-permute-start.27) | collective-permute-done | bytes 131104 | tf_op jit(solution)/shard_map/ppermute | solution.py:146
  83.7 7.6 %collective-permute-done.28 = bf16[32,32,128]{2,1,0:T(8,128)(2,1)S(1)} collective-permute-done((bf16[32,32,128]{2,1,0:T(8,128)(2,1)}, bf16[32,32,128]{2,1,0:T(8,128)(2,1)S(1)}, u32[]{:S(2)}, u32[]{:S(2)}) %collective-permute-start.28) | collective-permute-done | bytes 262176 | tf_op jit(solution)/shard_map/ppermute | solution.py:146
  92.3 2.5 %constant_dynamic-update-slice_fusion.18 = (bf16[128,48,128]{2,1,0:T(8,128)(2,1)}, bf16[256,48,128]{2,1,0:T(8,128)(2,1)}) fusion(bf16[128,48,128]{2,1,0:T(8,128)(2,1)} %get-tuple-element.22, bf16[64,48,128]{2,1,0:T(8,128)(2,1)} %collective-permute-done.13, bf16[256,48,128]{2,1,0:T(8,128)(2,1)} %get-tuple-element.23), kind=kLoop, calls=%fused_computation.28 | loop fusion | bytes 2359296 | tf_op jit(solution)/shard_map/concatenate | solution.py:147
  94.8 2.5 %constant_dynamic-update-slice_fusion.53 = (bf16[128,48,128]{2,1,0:T(8,128)(2,1)}, bf16[256,48,128]{2,1,0:T(8,128)(2,1)}) fusion(bf16[128,48,128]{2,1,0:T(8,128)(2,1)} %get-tuple-element.19, bf16[64,48,128]{2,1,0:T(8,128)(2,1)} %collective-permute-done.21, bf16[256,48,128]{2,1,0:T(8,128)(2,1)} %get-tuple-element.20), kind=kLoop, calls=%fused_computation.63 | loop fusion | bytes 2359296 | tf_op jit(solution)/shard_map/concatenate | solution.py:147
  97.8 4.0 %collective-permute-done.29 = bf16[64,32,128]{2,1,0:T(8,128)(2,1)S(1)} collective-permute-done((bf16[64,32,128]{2,1,0:T(8,128)(2,1)}, bf16[64,32,128]{2,1,0:T(8,128)(2,1)S(1)}, u32[]{:S(2)}, u32[]{:S(2)}) %collective-permute-start.29) | collective-permute-done | bytes 524320 | tf_op jit(solution)/shard_map/ppermute | solution.py:146
  104.0 3.4 %collective-permute-start.1 = (s32[1]{0:T(128)}, s32[1]{0:T(128)}, u32[]{:S(2)}, u32[]{:S(2)}) collective-permute-start(s32[1]{0:T(128)} %add.127), channel_id=1, source_target_pairs={{0,16},{8,24},{16,32},{24,40},{32,48},{40,56},{48,64},{56,72},{64,... | collective-permute-start | bytes 20 | tf_op jit(solution)/shard_map/ppermute | solution.py:19
  110.1 3.4 %collective-permute-start.2 = (s32[1]{0:T(128)}, s32[1]{0:T(128)}, u32[]{:S(2)}, u32[]{:S(2)}) collective-permute-start(s32[1]{0:T(128)} %add.128), channel_id=1, source_target_pairs={{0,32},{8,40},{16,48},{24,56},{32,64},{40,72},{48,80},{56,88},{64,... | collective-permute-start | bytes 20 | tf_op jit(solution)/shard_map/ppermute | solution.py:19
  114.1 6.6 %collective-permute-start.3 = (s32[1]{0:T(128)}, s32[1]{0:T(128)}, u32[]{:S(2)}, u32[]{:S(2)}) collective-permute-start(s32[1]{0:T(128)} %add.129), channel_id=1, source_target_pairs={{0,64},{8,72},{16,80},{24,88},{32,96},{40,104},{48,112},{56,120},{... | collective-permute-start | bytes 20 | tf_op jit(solution)/shard_map/ppermute | solution.py:19
  121.4 9.5 %collective-permute-start.4 = (s32[1]{0:T(128)}, s32[1]{0:T(128)}, u32[]{:S(2)}, u32[]{:S(2)}) collective-permute-start(s32[1]{0:T(128)} %add.130), channel_id=1, source_target_pairs={{0,128},{8,136},{16,144},{24,152},{32,160},{40,168},{48,176},{56,1... | collective-permute-start | bytes 20 | tf_op jit(solution)/shard_map/ppermute | solution.py:19
  134.4 2.8 %collective-permute-done.5 = bf16[1,25,2048]{2,1,0:T(8,128)(2,1)S(1)} collective-permute-done((bf16[1,25,2048]{2,1,0:T(8,128)(2,1)S(1)}, bf16[1,25,2048]{2,1,0:T(8,128)(2,1)S(1)}, u32[]{:S(2)}, u32[]{:S(2)}) %collective-permute-start.5) | collective-permute-done | bytes 102432 | tf_op jit(solution)/shard_map/ppermute | solution.py:19
  140.5 3.5 %constant_dynamic-update-slice_fusion.26.refs_8_.refs_10_ = bf16[256,48,128]{2,1,0:T(8,128)(2,1)} fusion(bf16[256,48,128]{2,1,0:T(8,128)(2,1)} %get-tuple-element.16, bf16[128,48,128]{2,1,0:T(8,128)(2,1)} %collective-permute-done.14), kind=kLoop, calls=%fused_computation.36 | loop fusion | bytes 3145728 | tf_op jit(solution)/shard_map/concatenate | solution.py:147
  147.3 17.6 %shard_map.73 = (f32[256,128]{1,0:T(8,128)S(1)}, f32[256,128]{1,0:T(8,128)S(1)}, f32[256,128]{1,0:T(8,128)S(1)}) custom-call(s32[256]{0:T(256)S(1)} %broadcast_select_fusion.5.refs_0_, s32[256]{0:T(256)S(1)} %broadcast_select_fusion.4.refs_1_, s32[256]{0:T(256)S(1)} %broadcast_select_fusion.3.refs_2_, s32[256]{0:T(256)S(1)} %broadcast_select_fusion.2.refs_3_, ...), custom_call_target="tpu_custom_call" | custom-call | tf_op jit(solution)/shard_map/pallas_call | solution.py:62
  170.6 3.1 %collective-permute-done.31 = f32[64]{0:T(128)S(1)} collective-permute-done((f32[64]{0:T(128)S(1)}, f32[64]{0:T(128)S(1)}, u32[]{:S(2)}, u32[]{:S(2)}) %collective-permute-start.31) | collective-permute-done | bytes 288 | tf_op jit(solution)/shard_map/ppermute | solution.py:26
  174.8 4.0 %collective-permute-done.32 = f32[64]{0:T(128)S(1)} collective-permute-done((f32[64]{0:T(128)S(1)}, f32[64]{0:T(128)S(1)}, u32[]{:S(2)}, u32[]{:S(2)}) %collective-permute-start.32) | collective-permute-done | bytes 288 | tf_op jit(solution)/shard_map/ppermute | solution.py:26
  178.8 3.7 %collective-permute-start.33 = (f32[64]{0:T(128)S(1)}, f32[64]{0:T(128)S(1)}, u32[]{:S(2)}, u32[]{:S(2)}) collective-permute-start(f32[64]{0:T(128)S(1)} %add.133), channel_id=1, source_target_pairs={{0,4},{1,5},{2,6},{3,7},{4,0},{5,1},{6,2},{7,3},{8,12},{9,13},{10,... | collective-permute-start | bytes 776 | tf_op jit(solution)/shard_map/ppermute | solution.py:26
  191.4 32.4 %shard_map.74 = bf16[32,2048]{1,0:T(8,128)(2,1)} custom-call(s32[256]{0:T(256)} %copy-done.6, s32[256]{0:T(256)} %copy-done.7, s32[256]{0:T(256)} %copy-done.8, s32[256]{0:T(256)} %copy-done.9, s32[256]{0:T(256)} %copy-done.10, s32[256]{0:T(256)} %copy-done.11, f32[256]{0:T(256)} %and_select_fusion.2.refs_6_, f32[256]{0:T(256)} %and_select_fusion.1.refs_7_, ...), custom_call_target="tpu_custom_call" | custom-call | tf_op jit(solution)/shard_map/pallas_call | solution.py:120
  (160 shorter events, 80.2 us)
Async XLA Ops:
  0.0 103.4 %collective-permute-start = (s32[1]{0:T(128)}, s32[1]{0:T(128)}, u32[]{:S(2)}, u32[]{:S(2)}) collective-permute-start(s32[1]{0:T(128)} %param.11), channel_id=1, source_target_pairs={{0,8},{8,16},{16,24},{24,32},{32,40},{40,48},{48,56},{56,64},{64,7... | collective-permute-start | bytes 20 | tf_op jit(solution)/shard_map/ppermute | solution.py:19
  2.1 131.4 %collective-permute-start.6 = (bf16[1,25,200]{2,1,0:T(8,128)(2,1)}, bf16[1,25,200]{2,1,0:T(8,128)(2,1)S(1)}, u32[]{:S(2)}, u32[]{:S(2)}) collective-permute-start(bf16[1,25,200]{2,1,0:T(8,128)(2,1)} %param.13), channel_id=1, source_target_pairs={{0,8},{8,16},{16,24},{24,32},{32,40},{40,48},{48,56},{56,64},{64,7... | collective-permute-start | bytes 30008 | tf_op jit(solution)/shard_map/ppermute | solution.py:19
  7.4 26.0 %collective-permute-start.7 = (bf16[1,48,128]{2,1,0:T(8,128)(2,1)S(1)}, bf16[1,48,128]{2,1,0:T(8,128)(2,1)S(1)}, u32[]{:S(2)}, u32[]{:S(2)}) collective-permute-start(bf16[1,48,128]{2,1,0:T(8,128)(2,1)S(1)} %get-tuple-element.88), channel_id=1, source_target_pairs={{0,128},{8,136},{16,144},{24,152},{32,160},{40,168},{48,176},{56,1... | collective-permute-start | bytes 36872 | tf_op jit(solution)/shard_map/ppermute | solution.py:146
  13.7 21.3 %collective-permute-start.15 = (bf16[1,48,128]{2,1,0:T(8,128)(2,1)S(1)}, bf16[1,48,128]{2,1,0:T(8,128)(2,1)S(1)}, u32[]{:S(2)}, u32[]{:S(2)}) collective-permute-start(bf16[1,48,128]{2,1,0:T(8,128)(2,1)S(1)} %get-tuple-element.89), channel_id=1, source_target_pairs={{0,2},{1,3},{2,0},{3,1},{4,6},{5,7},{6,4},{7,5},{8,10},{9,11},{10,... | collective-permute-start | bytes 36872 | tf_op jit(solution)/shard_map/ppermute | solution.py:146
  18.2 13.2 %collective-permute-start.23 = (bf16[1,32,128]{2,1,0:T(8,128)(2,1)S(1)}, bf16[1,32,128]{2,1,0:T(8,128)(2,1)S(1)}, u32[]{:S(2)}, u32[]{:S(2)}) collective-permute-start(bf16[1,32,128]{2,1,0:T(8,128)(2,1)S(1)} %get-tuple-element.77), channel_id=1, source_target_pairs={{0,4},{1,5},{2,6},{3,7},{4,0},{5,1},{6,2},{7,3},{8,12},{9,13},{10,... | collective-permute-start | bytes 24584 | tf_op jit(solution)/shard_map/ppermute | solution.py:146
  36.9 25.8 %collective-permute-start.25 = (bf16[4,32,128]{2,1,0:T(8,128)(2,1)S(1)}, bf16[4,32,128]{2,1,0:T(8,128)(2,1)S(1)}, u32[]{:S(2)}, u32[]{:S(2)}) collective-permute-start(bf16[4,32,128]{2,1,0:T(8,128)(2,1)S(1)} %pad_maximum_fusion.5), channel_id=1, source_target_pairs={{0,2},{1,3},{2,0},{3,1},{4,6},{5,7},{6,4},{7,5},{8,10},{9,11},{10,... | collective-permute-start | bytes 98312 | tf_op jit(solution)/shard_map/ppermute | solution.py:146
  40.0 8.8 %collective-permute-start.17 = (bf16[4,48,128]{2,1,0:T(8,128)(2,1)S(1)}, bf16[4,48,128]{2,1,0:T(8,128)(2,1)S(1)}, u32[]{:S(2)}, u32[]{:S(2)}) collective-permute-start(bf16[4,48,128]{2,1,0:T(8,128)(2,1)S(1)} %pad_maximum_fusion.4), channel_id=1, source_target_pairs={{0,128},{8,136},{16,144},{24,152},{32,160},{40,168},{48,176},{56,1... | collective-permute-start | bytes 147464 | tf_op jit(solution)/shard_map/ppermute | solution.py:146
  43.7 7.4 %collective-permute-start.10 = (bf16[8,48,128]{2,1,0:T(8,128)(2,1)S(1)}, bf16[8,48,128]{2,1,0:T(8,128)(2,1)S(1)}, u32[]{:S(2)}, u32[]{:S(2)}) collective-permute-start(bf16[8,48,128]{2,1,0:T(8,128)(2,1)S(1)} %pad_maximum_fusion), channel_id=1, source_target_pairs={{0,4},{1,5},{2,6},{3,7},{4,0},{5,1},{6,2},{7,3},{8,12},{9,13},{10,... | collective-permute-start | bytes 294920 | tf_op jit(solution)/shard_map/ppermute | solution.py:146
  48.9 6.5 %collective-permute-start.18 = (bf16[8,48,128]{2,1,0:T(8,128)(2,1)S(1)}, bf16[8,48,128]{2,1,0:T(8,128)(2,1)S(1)}, u32[]{:S(2)}, u32[]{:S(2)}) collective-permute-start(bf16[8,48,128]{2,1,0:T(8,128)(2,1)S(1)} %pad_maximum_fusion.1), channel_id=1, source_target_pairs={{0,64},{8,72},{16,80},{24,88},{32,96},{40,104},{48,112},{56,120},{... | collective-permute-start | bytes 294920 | tf_op jit(solution)/shard_map/ppermute | solution.py:146
  52.0 5.9 %collective-permute-start.11 = (bf16[16,48,128]{2,1,0:T(8,128)(2,1)}, bf16[16,48,128]{2,1,0:T(8,128)(2,1)S(1)}, u32[]{:S(2)}, u32[]{:S(2)}) collective-permute-start(bf16[16,48,128]{2,1,0:T(8,128)(2,1)} %get-tuple-element.51), channel_id=1, source_target_pairs={{0,16},{8,24},{16,0},{24,8},{32,48},{40,56},{48,32},{56,40},{64,80... | collective-permute-start | bytes 589832 | tf_op jit(solution)/shard_map/ppermute | solution.py:146
  58.9 13.1 %collective-permute-start.12 = (bf16[32,48,128]{2,1,0:T(8,128)(2,1)}, bf16[32,48,128]{2,1,0:T(8,128)(2,1)S(1)}, u32[]{:S(2)}, u32[]{:S(2)}) collective-permute-start(bf16[32,48,128]{2,1,0:T(8,128)(2,1)} %get-tuple-element.35), channel_id=1, source_target_pairs={{0,2},{1,3},{2,0},{3,1},{4,6},{5,7},{6,4},{7,5},{8,10},{9,11},{10,... | collective-permute-start | bytes 1179656 | tf_op jit(solution)/shard_map/ppermute | solution.py:146
  62.8 11.1 %collective-permute-start.20 = (bf16[32,48,128]{2,1,0:T(8,128)(2,1)}, bf16[32,48,128]{2,1,0:T(8,128)(2,1)S(1)}, u32[]{:S(2)}, u32[]{:S(2)}) collective-permute-start(bf16[32,48,128]{2,1,0:T(8,128)(2,1)} %get-tuple-element.31), channel_id=1, source_target_pairs={{0,4},{1,5},{2,6},{3,7},{4,0},{5,1},{6,2},{7,3},{8,12},{9,13},{10,... | collective-permute-start | bytes 1179656 | tf_op jit(solution)/shard_map/ppermute | solution.py:146
  62.8 5.8 %collective-permute-start.26 = (bf16[8,32,128]{2,1,0:T(8,128)(2,1)S(1)}, bf16[8,32,128]{2,1,0:T(8,128)(2,1)S(1)}, u32[]{:S(2)}, u32[]{:S(2)}) collective-permute-start(bf16[8,32,128]{2,1,0:T(8,128)(2,1)S(1)} %pad_maximum_fusion.2), channel_id=1, source_target_pairs={{0,1},{1,0},{2,3},{3,2},{4,5},{5,4},{6,7},{7,6},{8,9},{9,8},{10,11... | collective-permute-start | bytes 196616 | tf_op jit(solution)/shard_map/ppermute | solution.py:146
  69.3 11.5 %collective-permute-start.27 = (bf16[16,32,128]{2,1,0:T(8,128)(2,1)S(1)}, bf16[16,32,128]{2,1,0:T(8,128)(2,1)S(1)}, u32[]{:S(2)}, u32[]{:S(2)}) collective-permute-start(bf16[16,32,128]{2,1,0:T(8,128)(2,1)S(1)} %get-tuple-element.56), channel_id=1, source_target_pairs={{0,128},{8,136},{16,144},{24,152},{32,160},{40,168},{48,176},{56,1... | collective-permute-start | bytes 393224 | tf_op jit(solution)/shard_map/ppermute | solution.py:146
  73.2 19.1 %collective-permute-start.13 = (bf16[64,48,128]{2,1,0:T(8,128)(2,1)}, bf16[64,48,128]{2,1,0:T(8,128)(2,1)}, u32[]{:S(2)}, u32[]{:S(2)}) collective-permute-start(bf16[64,48,128]{2,1,0:T(8,128)(2,1)} %get-tuple-element.24), channel_id=1, source_target_pairs={{0,1},{1,0},{2,3},{3,2},{4,5},{5,4},{6,7},{7,6},{8,9},{9,8},{10,11... | collective-permute-start | bytes 2359304 | tf_op jit(solution)/shard_map/ppermute | solution.py:146
  75.0 19.7 %collective-permute-start.21 = (bf16[64,48,128]{2,1,0:T(8,128)(2,1)}, bf16[64,48,128]{2,1,0:T(8,128)(2,1)}, u32[]{:S(2)}, u32[]{:S(2)}) collective-permute-start(bf16[64,48,128]{2,1,0:T(8,128)(2,1)} %get-tuple-element.21), channel_id=1, source_target_pairs={{0,16},{8,24},{16,0},{24,8},{32,48},{40,56},{48,32},{56,40},{64,80... | collective-permute-start | bytes 2359304 | tf_op jit(solution)/shard_map/ppermute | solution.py:146
  81.7 9.6 %collective-permute-start.28 = (bf16[32,32,128]{2,1,0:T(8,128)(2,1)}, bf16[32,32,128]{2,1,0:T(8,128)(2,1)S(1)}, u32[]{:S(2)}, u32[]{:S(2)}) collective-permute-start(bf16[32,32,128]{2,1,0:T(8,128)(2,1)} %get-tuple-element.41), channel_id=1, source_target_pairs={{0,64},{8,72},{16,80},{24,88},{32,96},{40,104},{48,112},{56,120},{... | collective-permute-start | bytes 786440 | tf_op jit(solution)/shard_map/ppermute | solution.py:146
  92.2 9.5 %collective-permute-start.29 = (bf16[64,32,128]{2,1,0:T(8,128)(2,1)}, bf16[64,32,128]{2,1,0:T(8,128)(2,1)S(1)}, u32[]{:S(2)}, u32[]{:S(2)}) collective-permute-start(bf16[64,32,128]{2,1,0:T(8,128)(2,1)} %get-tuple-element.27), channel_id=1, source_target_pairs={{0,32},{8,40},{16,48},{24,56},{32,0},{40,8},{48,16},{56,24},{64,96... | collective-permute-start | bytes 1572872 | tf_op jit(solution)/shard_map/ppermute | solution.py:146
  94.7 45.8 %collective-permute-start.14 = (bf16[128,48,128]{2,1,0:T(8,128)(2,1)}, bf16[128,48,128]{2,1,0:T(8,128)(2,1)}, u32[]{:S(2)}, u32[]{:S(2)}) collective-permute-start(bf16[128,48,128]{2,1,0:T(8,128)(2,1)} %get-tuple-element.15), channel_id=1, source_target_pairs={{0,8},{8,0},{16,24},{24,16},{32,40},{40,32},{48,56},{56,48},{64,72... | collective-permute-start | bytes 4718600 | tf_op jit(solution)/shard_map/ppermute | solution.py:146
  97.3 46.7 %collective-permute-start.22 = (bf16[128,48,128]{2,1,0:T(8,128)(2,1)}, bf16[128,48,128]{2,1,0:T(8,128)(2,1)}, u32[]{:S(2)}, u32[]{:S(2)}) collective-permute-start(bf16[128,48,128]{2,1,0:T(8,128)(2,1)} %get-tuple-element.13), channel_id=1, source_target_pairs={{0,8},{8,0},{16,24},{24,16},{32,40},{40,32},{48,56},{56,48},{64,72... | collective-permute-start | bytes 4718600 | tf_op jit(solution)/shard_map/ppermute | solution.py:146
  102.7 36.4 %collective-permute-start.30 = (bf16[128,32,128]{2,1,0:T(8,128)(2,1)}, bf16[128,32,128]{2,1,0:T(8,128)(2,1)}, u32[]{:S(2)}, u32[]{:S(2)}) collective-permute-start(bf16[128,32,128]{2,1,0:T(8,128)(2,1)} %get-tuple-element.17), channel_id=1, source_target_pairs={{0,8},{8,0},{16,24},{24,16},{32,40},{40,32},{48,56},{56,48},{64,72... | collective-permute-start | bytes 3145736 | tf_op jit(solution)/shard_map/ppermute | solution.py:146
  114.1 6.6 %collective-permute-start.3 = (s32[1]{0:T(128)}, s32[1]{0:T(128)}, u32[]{:S(2)}, u32[]{:S(2)}) collective-permute-start(s32[1]{0:T(128)} %add.129), channel_id=1, source_target_pairs={{0,64},{8,72},{16,80},{24,88},{32,96},{40,104},{48,112},{56,120},{... | collective-permute-start | bytes 20 | tf_op jit(solution)/shard_map/ppermute | solution.py:19
  121.4 9.5 %collective-permute-start.4 = (s32[1]{0:T(128)}, s32[1]{0:T(128)}, u32[]{:S(2)}, u32[]{:S(2)}) collective-permute-start(s32[1]{0:T(128)} %add.130), channel_id=1, source_target_pairs={{0,128},{8,136},{16,144},{24,152},{32,160},{40,168},{48,176},{56,1... | collective-permute-start | bytes 20 | tf_op jit(solution)/shard_map/ppermute | solution.py:19
  130.9 6.3 %collective-permute-start.5 = (bf16[1,25,2048]{2,1,0:T(8,128)(2,1)S(1)}, bf16[1,25,2048]{2,1,0:T(8,128)(2,1)S(1)}, u32[]{:S(2)}, u32[]{:S(2)}) collective-permute-start(bf16[1,25,2048]{2,1,0:T(8,128)(2,1)S(1)} %copy-done.14), channel_id=1, source_target_pairs={{0,8},{8,16},{16,24},{24,32},{32,40},{40,48},{48,56},{56,64},{64,7... | collective-permute-start | bytes 307208 | tf_op jit(solution)/shard_map/ppermute | solution.py:19
  (27 other events, 948.2 us)

commit v3 on v2

--- a/solution.py
+++ b/solution.py
@@ -45,7 +45,7 @@
         def one(t, carry, rb_ref=rb_ref, cb_ref=cb_ref, part_ref=part_ref, out_ref=out_ref, low=low, high=high):
             col = pl.multiple_of(cb_ref[t] * size, size)
             blk = m_ref[rb_ref[t], low:high, pl.ds(col, size)]
-            prod = blk * part_ref[t].astype(jnp.float32)
+            prod = blk * part_ref[t, 0:high - low, :].astype(jnp.float32)
             out_ref[pl.ds(t, 1), :] = jnp.sum(prod, axis=0, keepdims=True)
             return carry
 
@@ -83,7 +83,7 @@
         def build(t, carry, rb_ref=rb_ref, cb_ref=cb_ref, s_ref=s_ref, part_ref=part_ref, low=low, high=high):
             col = pl.multiple_of(cb_ref[t] * size, size)
             row = rb_ref[t]
-            a_ref[row, low:high, pl.ds(col, size)] += s_ref[t] * part_ref[t].astype(jnp.float32)
+            a_ref[row, low:high, pl.ds(col, size)] += s_ref[t] * part_ref[t, 0:high - low, :].astype(jnp.float32)
             return carry
 
         lax.fori_loop(0, part_ref.shape[0], build, 0)
@@ -158,6 +158,11 @@
     return walker * lax.axis_size("vec") + vec
 
 
+def pick(table, index):
+    hot = index[:, None] == jnp.arange(table.shape[0], dtype=index.dtype)[None, :]
+    return jnp.sum(jnp.where(hot, table[None, :], jnp.zeros((), table.dtype)), axis=1)
+
+
 def pad_rows(x):
     return jnp.pad(x, ((0, ROWS - x.shape[0]), (0, 0)))
 
@@ -167,26 +172,33 @@
 ):
     cols_local = panels.shape[1]
     walker_id = lax.axis_index("walker")
-    running = copy_counts
-    step = 1
-    while step < lax.axis_size("walker"):
-        running = running + shift_from(running, "walker", step)
-        step *= 2
-    from_prev = running[0] - copy_counts[0] - walker_id > 0
-
+    vec_id = lax.axis_index("vec")
+    vecs = lax.axis_size("vec")
     prev_panel = shift_from(panels, "walker", 1)
     prev_inverse = shift_from(inverse_intersection, "walker", 1)
+    size = chol_tiles.shape[2]
+    meta = jnp.zeros((1, 16, size), chol_tiles.dtype).at[0, 0, 0].set(copy_counts[0].astype(chol_tiles.dtype))
     parts, rbs, cbs, sources = [], [], [], []
-    for order, low, high in STREAMS:
-        parts.append(xor_gather(chol_tiles[:, low:high], order))
+    for index, (order, low, high) in enumerate(STREAMS):
+        piece = chol_tiles[:, low:high]
+        if index == len(STREAMS) - 1:
+            piece = jnp.concatenate([piece, meta], axis=1)
+        parts.append(xor_gather(piece, order))
         source = source_tiles(order)
         sources.append(source)
-        rbs.append(jnp.take(tile_blocks[:, 0], source))
-        cbs.append(jnp.take(tile_blocks[:, 1], source))
-
+        rbs.append(pick(tile_blocks[:, 0], source))
+        cbs.append(pick(tile_blocks[:, 1], source))
+    last = STREAMS[-1]
+    counts = parts[-1][:, last[2] - last[1], 0].astype(jnp.float32)
+    source = sources[-1]
+    before = (source % vecs == vec_id) & (source // vecs < walker_id)
+    surplus = jnp.sum(jnp.where(before, counts, 0.0)) - walker_id.astype(jnp.float32)
+    from_prev = surplus > 0.5
+
+    green_own = jnp.dot(inverse_intersection[0], trial_orbitals, preferred_element_type=jnp.float32).astype(jnp.bfloat16)
+    green_prev = jnp.dot(prev_inverse[0], trial_orbitals, preferred_element_type=jnp.float32).astype(jnp.bfloat16)
     start = jnp.where(from_prev, prev_panel[0], panels[0])
-    inverse = jnp.where(from_prev, prev_inverse[0], inverse_intersection[0])
-    green = jnp.dot(inverse, trial_orbitals, preferred_element_type=jnp.float32).astype(jnp.bfloat16)
+    green = jnp.where(from_prev, green_prev, green_own)
     partials = tile_bias(pad_rows(start).T, pad_rows(green), parts, rbs, cbs)
     vectors = tile_blocks.shape[0] // KT
     ids = jnp.concatenate([source // KT for source in sources])
@@ -196,7 +208,7 @@
     raw = butterfly_sum(per_vector, "vec")
     bias = jnp.clip(TIME_STEP_ROOT * raw, -1.0, 1.0)
     scales = TIME_STEP_ROOT * (aux_fields[0] - bias)
-    ss = [jnp.take(scales, source // KT) for source in sources]
+    ss = [pick(scales, source // KT) for source in sources]
     out = propagate(pad_rows(start), parts, rbs, cbs, ss)
     return out[:cols_local][None]
 

time: 230 us -> 204 us (0.89); the launches traced: 225 us -> 203 us
  local copies, waits for them, and re-layouts: 55.5 us -> 31.3 us
  waiting for transfers between devices: 43 us -> 66.9 us
  starting transfers between devices: 67.1 us -> 45.9 us
  between operations: 4.28 us -> 1.62 us
    ppermute x24, waiting for transfers between devices: 29.6 us -> 57.1 us  [xor_gather(): other = lax.ppermute(x, axis, [(i, i ^ step) for i in range(count)])]
    ppermute x7 -> x2, starting transfers between devices: 30.9 us -> 5.1 us  [shift_from(): lax.ppermute(value, axis, [(i, i + steps) for i in range(count - steps)])]
    gather x9 -> x0, local copies, waits for them, and re-layouts: 17.3 us -> none  [the longest x3 5.83 us: shards(): rbs.append(jnp.take(tile_blocks[:, 0], source))]
    ppermute x24, starting transfers between devices: 31 us -> 36.8 us  [xor_gather(): other = lax.ppermute(x, axis, [(i, i ^ step) for i in range(count)])]
    unnamed x54 -> x43, local copies, waits for them, and re-layouts: 20.9 us -> 16.1 us
    ppermute x7 -> x2, waiting for transfers between devices: 4.77 us -> 0.01 us  [shift_from(): lax.ppermute(value, axis, [(i, i + steps) for i in range(count - steps)])]
    reduce_sum x3, other arithmetic: 3.04 us -> 0.33 us  [shards(): values = jnp.concatenate([partial.sum(axis=1) for partial in partials])]
  transfers between devices with their start and end apart: 34 -> 29, of which waited for: 13 -> 14; matrix products, arithmetic and copies ran while one was open for 19% -> 15% of each run, Pallas kernels for 0% -> 0%
where the time goes in v3:
time: 204 us; the launch traced here: 203 us
  waiting for transfers between devices  66.9 us (33%)
  Pallas kernels  51.1 us (25%)
  starting transfers between devices  45.9 us (22%)
  local copies, waits for them, and re-layouts  31.3 us (15%)
  other arithmetic  6.04 us (3%)
    ppermute x24, waiting for transfers between devices, xor_gather(): other = lax.ppermute(x, axis, [(i, i ^ step) for i in range(count)])  57.1 us
    ppermute x24, starting transfers between devices, xor_gather(): other = lax.ppermute(x, axis, [(i, i ^ step) for i in range(count)])  36.8 us
    pallas_call x1, Pallas kernels, propagate(): pl.pallas_call(prop_kernel, out_shape=jax.ShapeDtypeStruct((rows, orbital...  32.6 us
    pallas_call x1, Pallas kernels, tile_bias(): pl.pallas_call(bias_kernel, out_shape=[jax.ShapeDtypeStruct((tiles_total,...  18.5 us
    unnamed x43, local copies, waits for them, and re-layouts  16.1 us
    concatenate x6, local copies, waits for them, and re-layouts, xor_gather(): x = jnp.concatenate([x, other], axis=0)  12 us
    ppermute x3, waiting for transfers between devices, butterfly_sum(): lax.ppermute(value, axis, [(i, i ^ step) for i in range(count)])  9.76 us
    ppermute x2, starting transfers between devices, shift_from(): lax.ppermute(value, axis, [(i, i + steps) for i in range(count - steps)])  5.1 us
  transfers between devices with their start and end apart: 29, of which 14 were waited for; matrix products, arithmetic and copies ran while one was open for 15% of the time, Pallas kernels for 0%

profile of v3, /device:TPU:2, one launch (start us, length us, event | category | flops | bytes accessed | tf_op | source)
XLA Modules:
  0.0 203.4 jit_solution(5049701884181052084)
XLA Ops:
  1.5 3.2 %collective-permute-start.18 = (bf16[1,48,128]{2,1,0:T(8,128)(2,1)S(1)}, bf16[1,48,128]{2,1,0:T(8,128)(2,1)S(1)}, u32[]{:S(2)}, u32[]{:S(2)}) collective-permute-start(bf16[1,48,128]{2,1,0:T(8,128)(2,1)S(1)} %get-tuple-element.101), channel_id=1, source_target_pairs={{0,2},{1,3},{2,0},{3,1},{4,6},{5,7},{6,4},{7,5},{8,10},{9,11},{10,... | collective-permute-start | bytes 36872 | tf_op jit(solution)/shard_map/ppermute | solution.py:146
  4.6 7.2 %collective-permute-start.10 = (bf16[1,48,128]{2,1,0:T(8,128)(2,1)S(1)}, bf16[1,48,128]{2,1,0:T(8,128)(2,1)S(1)}, u32[]{:S(2)}, u32[]{:S(2)}) collective-permute-start(bf16[1,48,128]{2,1,0:T(8,128)(2,1)S(1)} %get-tuple-element.102), channel_id=1, source_target_pairs={{0,128},{8,136},{16,144},{24,152},{32,160},{40,168},{48,176},{56,1... | collective-permute-start | bytes 36872 | tf_op jit(solution)/shard_map/ppermute | solution.py:146
  13.8 2.1 %collective-permute-start = (bf16[1,48,128]{2,1,0:T(8,128)(2,1)S(1)}, bf16[1,48,128]{2,1,0:T(8,128)(2,1)S(1)}, u32[]{:S(2)}, u32[]{:S(2)}) collective-permute-start(bf16[1,48,128]{2,1,0:T(8,128)(2,1)S(1)} %get-tuple-element.138), channel_id=1, source_target_pairs={{0,4},{1,5},{2,6},{3,7},{4,0},{5,1},{6,2},{7,3},{8,12},{9,13},{10,... | collective-permute-start | bytes 36872 | tf_op jit(solution)/shard_map/ppermute | solution.py:146
  24.4 4.5 %collective-permute-done.2 = bf16[4,48,128]{2,1,0:T(8,128)(2,1)S(1)} collective-permute-done((bf16[4,48,128]{2,1,0:T(8,128)(2,1)S(1)}, bf16[4,48,128]{2,1,0:T(8,128)(2,1)S(1)}, u32[]{:S(2)}, u32[]{:S(2)}) %collective-permute-start.2) | collective-permute-done | bytes 49184 | tf_op jit(solution)/shard_map/ppermute | solution.py:146
  30.5 3.3 %collective-permute-done.3 = bf16[8,48,128]{2,1,0:T(8,128)(2,1)S(1)} collective-permute-done((bf16[8,48,128]{2,1,0:T(8,128)(2,1)S(1)}, bf16[8,48,128]{2,1,0:T(8,128)(2,1)S(1)}, u32[]{:S(2)}, u32[]{:S(2)}) %collective-permute-start.3) | collective-permute-done | bytes 98336 | tf_op jit(solution)/shard_map/ppermute | solution.py:146
  36.4 4.1 %collective-permute-start.20 = (bf16[4,48,128]{2,1,0:T(8,128)(2,1)S(1)}, bf16[4,48,128]{2,1,0:T(8,128)(2,1)S(1)}, u32[]{:S(2)}, u32[]{:S(2)}) collective-permute-start(bf16[4,48,128]{2,1,0:T(8,128)(2,1)S(1)} %pad_maximum_fusion.5), channel_id=1, source_target_pairs={{0,128},{8,136},{16,144},{24,152},{32,160},{40,168},{48,176},{56,1... | collective-permute-start | bytes 147464 | tf_op jit(solution)/shard_map/ppermute | solution.py:146
  41.6 5.9 %collective-permute-done.4 = bf16[16,48,128]{2,1,0:T(8,128)(2,1)S(1)} collective-permute-done((bf16[16,48,128]{2,1,0:T(8,128)(2,1)S(1)}, bf16[16,48,128]{2,1,0:T(8,128)(2,1)S(1)}, u32[]{:S(2)}, u32[]{:S(2)}) %collective-permute-start.4) | collective-permute-done | bytes 196640 | tf_op jit(solution)/shard_map/ppermute | solution.py:146
  49.8 3.0 %collective-permute-start.21 = (bf16[8,48,128]{2,1,0:T(8,128)(2,1)S(1)}, bf16[8,48,128]{2,1,0:T(8,128)(2,1)S(1)}, u32[]{:S(2)}, u32[]{:S(2)}) collective-permute-start(bf16[8,48,128]{2,1,0:T(8,128)(2,1)S(1)} %pad_maximum_fusion.2), channel_id=1, source_target_pairs={{0,64},{8,72},{16,80},{24,88},{32,96},{40,104},{48,112},{56,120},{... | collective-permute-start | bytes 294920 | tf_op jit(solution)/shard_map/ppermute | solution.py:146
  52.8 2.2 %collective-permute-start.13 = (bf16[8,48,128]{2,1,0:T(8,128)(2,1)S(1)}, bf16[8,48,128]{2,1,0:T(8,128)(2,1)S(1)}, u32[]{:S(2)}, u32[]{:S(2)}) collective-permute-start(bf16[8,48,128]{2,1,0:T(8,128)(2,1)S(1)} %pad_maximum_fusion.1), channel_id=1, source_target_pairs={{0,4},{1,5},{2,6},{3,7},{4,0},{5,1},{6,2},{7,3},{8,12},{9,13},{10,... | collective-permute-start | bytes 294920 | tf_op jit(solution)/shard_map/ppermute | solution.py:146
  55.1 10.6 %collective-permute-done.5 = bf16[32,48,128]{2,1,0:T(8,128)(2,1)S(1)} collective-permute-done((bf16[32,48,128]{2,1,0:T(8,128)(2,1)S(1)}, bf16[32,48,128]{2,1,0:T(8,128)(2,1)S(1)}, u32[]{:S(2)}, u32[]{:S(2)}) %collective-permute-start.5) | collective-permute-done | bytes 393248 | tf_op jit(solution)/shard_map/ppermute | solution.py:146
  74.1 3.2 %collective-permute-start.9 = (bf16[1,25,200]{2,1,0:T(8,128)(2,1)S(1)}, bf16[1,25,200]{2,1,0:T(8,128)(2,1)S(1)}, u32[]{:S(2)}, u32[]{:S(2)}) collective-permute-start(bf16[1,25,200]{2,1,0:T(8,128)(2,1)S(1)} %copy-done.8), channel_id=1, source_target_pairs={{0,8},{8,16},{16,24},{24,32},{32,40},{40,48},{48,56},{56,64},{64,7... | collective-permute-start | bytes 30008 | tf_op jit(solution)/shard_map/ppermute | solution.py:19
  77.3 11.8 %collective-permute-done.22 = bf16[16,48,128]{2,1,0:T(8,128)(2,1)S(1)} collective-permute-done((bf16[16,48,128]{2,1,0:T(8,128)(2,1)S(1)}, bf16[16,48,128]{2,1,0:T(8,128)(2,1)S(1)}, u32[]{:S(2)}, u32[]{:S(2)}) %collective-permute-start.22) | collective-permute-done | bytes 196640 | tf_op jit(solution)/shard_map/ppermute | solution.py:146
  90.0 2.0 %collective-permute-start.23 = (bf16[32,48,128]{2,1,0:T(8,128)(2,1)S(1)}, bf16[32,48,128]{2,1,0:T(8,128)(2,1)S(1)}, u32[]{:S(2)}, u32[]{:S(2)}) collective-permute-start(bf16[32,48,128]{2,1,0:T(8,128)(2,1)S(1)} %get-tuple-element.50), channel_id=1, source_target_pairs={{0,4},{1,5},{2,6},{3,7},{4,0},{5,1},{6,2},{7,3},{8,12},{9,13},{10,... | collective-permute-start | bytes 1179656 | tf_op jit(solution)/shard_map/ppermute | solution.py:146
  95.0 5.2 %collective-permute-done.23 = bf16[32,48,128]{2,1,0:T(8,128)(2,1)S(1)} collective-permute-done((bf16[32,48,128]{2,1,0:T(8,128)(2,1)S(1)}, bf16[32,48,128]{2,1,0:T(8,128)(2,1)S(1)}, u32[]{:S(2)}, u32[]{:S(2)}) %collective-permute-start.23) | collective-permute-done | bytes 393248 | tf_op jit(solution)/shard_map/ppermute | solution.py:146
  106.2 11.9 %collective-permute-done.24 = bf16[64,48,128]{2,1,0:T(8,128)(2,1)S(1)} collective-permute-done((bf16[64,48,128]{2,1,0:T(8,128)(2,1)}, bf16[64,48,128]{2,1,0:T(8,128)(2,1)S(1)}, u32[]{:S(2)}, u32[]{:S(2)}) %collective-permute-start.24) | collective-permute-done | bytes 786464 | tf_op jit(solution)/shard_map/ppermute | solution.py:146
  120.9 2.5 %constant_dynamic-update-slice_fusion.53 = (bf16[128,48,128]{2,1,0:T(8,128)(2,1)}, bf16[256,48,128]{2,1,0:T(8,128)(2,1)}) fusion(bf16[128,48,128]{2,1,0:T(8,128)(2,1)} %get-tuple-element.41, bf16[64,48,128]{2,1,0:T(8,128)(2,1)} %collective-permute-done.16, bf16[256,48,128]{2,1,0:T(8,128)(2,1)} %get-tuple-element.42), kind=kLoop, calls=%fused_computation.65 | loop fusion | bytes 2359296 | tf_op jit(solution)/shard_map/concatenate | solution.py:147
  124.7 2.1 %fusion.1 = f32[256]{0:T(256)S(1)} fusion(bf16[256,48,128]{2,1,0:T(8,128)(2,1)} %constant_dynamic-update-slice_fusion.26.refs_10_.refs_12_), kind=kLoop, calls=%fused_computation.121 | loop fusion | flops 256 | bytes 1536 | tf_op jit(solution)/shard_map/convert_element_type | solution.py:192
  130.2 2.8 %constant_dynamic-update-slice_fusion.96.refs_9_.refs_11_ = bf16[256,48,128]{2,1,0:T(8,128)(2,1)} fusion(bf16[256,48,128]{2,1,0:T(8,128)(2,1)} %get-tuple-element.33, bf16[128,48,128]{2,1,0:T(8,128)(2,1)} %collective-permute-done.25), kind=kLoop, calls=%fused_computation.108 | loop fusion | bytes 3145728 | tf_op jit(solution)/shard_map/concatenate | solution.py:147
  133.0 2.7 %constant_dynamic-update-slice_fusion.61.refs_8_.refs_10_ = bf16[256,48,128]{2,1,0:T(8,128)(2,1)} fusion(bf16[256,48,128]{2,1,0:T(8,128)(2,1)} %get-tuple-element.35, bf16[128,48,128]{2,1,0:T(8,128)(2,1)} %collective-permute-done.17), kind=kLoop, calls=%fused_computation.73 | loop fusion | bytes 3145728 | tf_op jit(solution)/shard_map/concatenate | solution.py:147
  135.8 18.5 %shard_map.73 = (f32[256,128]{1,0:T(8,128)S(1)}, f32[256,128]{1,0:T(8,128)S(1)}, f32[256,128]{1,0:T(8,128)S(1)}) custom-call(s32[256]{0:T(256)S(1)} %get-tuple-element.27.refs_0_, s32[256]{0:T(256)S(1)} %get-tuple-element.25.refs_1_, s32[256]{0:T(256)S(1)} %get-tuple-element.24.refs_2_, s32[256]{0:T(256)S(1)} %get-tuple-element.28.refs_3_, ...), custom_call_target="tpu_custom_call" | custom-call | tf_op jit(solution)/shard_map/pallas_call | solution.py:62
  155.9 2.5 %collective-permute-done.26 = f32[64]{0:T(128)S(1)} collective-permute-done((f32[64]{0:T(128)S(1)}, f32[64]{0:T(128)S(1)}, u32[]{:S(2)}, u32[]{:S(2)}) %collective-permute-start.26) | collective-permute-done | bytes 288 | tf_op jit(solution)/shard_map/ppermute | solution.py:26
  160.1 3.4 %collective-permute-done.27 = f32[64]{0:T(128)S(1)} collective-permute-done((f32[64]{0:T(128)S(1)}, f32[64]{0:T(128)S(1)}, u32[]{:S(2)}, u32[]{:S(2)}) %collective-permute-start.27) | collective-permute-done | bytes 288 | tf_op jit(solution)/shard_map/ppermute | solution.py:26
  164.6 3.9 %collective-permute-done.28 = f32[64]{0:T(128)S(1)} collective-permute-done((f32[64]{0:T(128)S(1)}, f32[64]{0:T(128)S(1)}, u32[]{:S(2)}, u32[]{:S(2)}) %collective-permute-start.28) | collective-permute-done | bytes 288 | tf_op jit(solution)/shard_map/ppermute | solution.py:26
  169.2 32.6 %shard_map.74 = bf16[32,2048]{1,0:T(8,128)(2,1)} custom-call(s32[256]{0:T(256)} %copy-done.5, s32[256]{0:T(256)} %copy-done.3, s32[256]{0:T(256)} %copy-done.2, s32[256]{0:T(256)} %copy-done.6, s32[256]{0:T(256)} %copy-done.4, s32[256]{0:T(256)} %copy-done.1, f32[256]{0:T(256)} %get-tuple-element.31.refs_6_, f32[256]{0:T(256)} %get-tuple-element.30.refs_7_, ...), custom_call_target="tpu_custom_call" | custom-call | tf_op jit(solution)/shard_map/pallas_call | solution.py:120
  (121 shorter events, 50.6 us)
Async XLA Ops:
  1.5 14.5 %collective-permute-start.18 = (bf16[1,48,128]{2,1,0:T(8,128)(2,1)S(1)}, bf16[1,48,128]{2,1,0:T(8,128)(2,1)S(1)}, u32[]{:S(2)}, u32[]{:S(2)}) collective-permute-start(bf16[1,48,128]{2,1,0:T(8,128)(2,1)S(1)} %get-tuple-element.101), channel_id=1, source_target_pairs={{0,2},{1,3},{2,0},{3,1},{4,6},{5,7},{6,4},{7,5},{8,10},{9,11},{10,... | collective-permute-start | bytes 36872 | tf_op jit(solution)/shard_map/ppermute | solution.py:146
  4.6 12.0 %collective-permute-start.10 = (bf16[1,48,128]{2,1,0:T(8,128)(2,1)S(1)}, bf16[1,48,128]{2,1,0:T(8,128)(2,1)S(1)}, u32[]{:S(2)}, u32[]{:S(2)}) collective-permute-start(bf16[1,48,128]{2,1,0:T(8,128)(2,1)S(1)} %get-tuple-element.102), channel_id=1, source_target_pairs={{0,128},{8,136},{16,144},{24,152},{32,160},{40,168},{48,176},{56,1... | collective-permute-start | bytes 36872 | tf_op jit(solution)/shard_map/ppermute | solution.py:146
  13.8 5.2 %collective-permute-start = (bf16[1,48,128]{2,1,0:T(8,128)(2,1)S(1)}, bf16[1,48,128]{2,1,0:T(8,128)(2,1)S(1)}, u32[]{:S(2)}, u32[]{:S(2)}) collective-permute-start(bf16[1,48,128]{2,1,0:T(8,128)(2,1)S(1)} %get-tuple-element.138), channel_id=1, source_target_pairs={{0,4},{1,5},{2,6},{3,7},{4,0},{5,1},{6,2},{7,3},{8,12},{9,13},{10,... | collective-permute-start | bytes 36872 | tf_op jit(solution)/shard_map/ppermute | solution.py:146
  16.0 20.4 %collective-permute-start.19 = (bf16[2,48,128]{2,1,0:T(8,128)(2,1)S(1)}, bf16[2,48,128]{2,1,0:T(8,128)(2,1)S(1)}, u32[]{:S(2)}, u32[]{:S(2)}) collective-permute-start(bf16[2,48,128]{2,1,0:T(8,128)(2,1)S(1)} %pad_maximum_fusion.8), channel_id=1, source_target_pairs={{0,1},{1,0},{2,3},{3,2},{4,5},{5,4},{6,7},{7,6},{8,9},{9,8},{10,11... | collective-permute-start | bytes 73736 | tf_op jit(solution)/shard_map/ppermute | solution.py:146
  16.6 23.9 %collective-permute-start.11 = (bf16[2,48,128]{2,1,0:T(8,128)(2,1)S(1)}, bf16[2,48,128]{2,1,0:T(8,128)(2,1)S(1)}, u32[]{:S(2)}, u32[]{:S(2)}) collective-permute-start(bf16[2,48,128]{2,1,0:T(8,128)(2,1)S(1)} %pad_maximum_fusion.7), channel_id=1, source_target_pairs={{0,64},{8,72},{16,80},{24,88},{32,96},{40,104},{48,112},{56,120},{... | collective-permute-start | bytes 73736 | tf_op jit(solution)/shard_map/ppermute | solution.py:146
  22.9 6.1 %collective-permute-start.2 = (bf16[4,48,128]{2,1,0:T(8,128)(2,1)S(1)}, bf16[4,48,128]{2,1,0:T(8,128)(2,1)S(1)}, u32[]{:S(2)}, u32[]{:S(2)}) collective-permute-start(bf16[4,48,128]{2,1,0:T(8,128)(2,1)S(1)} %pad_maximum_fusion.3), channel_id=1, source_target_pairs={{0,2},{1,3},{2,0},{3,1},{4,6},{5,7},{6,4},{7,5},{8,10},{9,11},{10,... | collective-permute-start | bytes 147464 | tf_op jit(solution)/shard_map/ppermute | solution.py:146
  34.5 13.1 %collective-permute-start.4 = (bf16[16,48,128]{2,1,0:T(8,128)(2,1)S(1)}, bf16[16,48,128]{2,1,0:T(8,128)(2,1)S(1)}, u32[]{:S(2)}, u32[]{:S(2)}) collective-permute-start(bf16[16,48,128]{2,1,0:T(8,128)(2,1)S(1)} %get-tuple-element.75), channel_id=1, source_target_pairs={{0,128},{8,136},{16,144},{24,152},{32,160},{40,168},{48,176},{56,1... | collective-permute-start | bytes 589832 | tf_op jit(solution)/shard_map/ppermute | solution.py:146
  36.4 13.4 %collective-permute-start.20 = (bf16[4,48,128]{2,1,0:T(8,128)(2,1)S(1)}, bf16[4,48,128]{2,1,0:T(8,128)(2,1)S(1)}, u32[]{:S(2)}, u32[]{:S(2)}) collective-permute-start(bf16[4,48,128]{2,1,0:T(8,128)(2,1)S(1)} %pad_maximum_fusion.5), channel_id=1, source_target_pairs={{0,128},{8,136},{16,144},{24,152},{32,160},{40,168},{48,176},{56,1... | collective-permute-start | bytes 147464 | tf_op jit(solution)/shard_map/ppermute | solution.py:146
  40.5 12.3 %collective-permute-start.12 = (bf16[4,48,128]{2,1,0:T(8,128)(2,1)S(1)}, bf16[4,48,128]{2,1,0:T(8,128)(2,1)S(1)}, u32[]{:S(2)}, u32[]{:S(2)}) collective-permute-start(bf16[4,48,128]{2,1,0:T(8,128)(2,1)S(1)} %pad_maximum_fusion.4), channel_id=1, source_target_pairs={{0,32},{8,40},{16,48},{24,56},{32,0},{40,8},{48,16},{56,24},{64,96... | collective-permute-start | bytes 147464 | tf_op jit(solution)/shard_map/ppermute | solution.py:146
  48.5 17.2 %collective-permute-start.5 = (bf16[32,48,128]{2,1,0:T(8,128)(2,1)S(1)}, bf16[32,48,128]{2,1,0:T(8,128)(2,1)S(1)}, u32[]{:S(2)}, u32[]{:S(2)}) collective-permute-start(bf16[32,48,128]{2,1,0:T(8,128)(2,1)S(1)} %get-tuple-element.58), channel_id=1, source_target_pairs={{0,64},{8,72},{16,80},{24,88},{32,96},{40,104},{48,112},{56,120},{... | collective-permute-start | bytes 1179656 | tf_op jit(solution)/shard_map/ppermute | solution.py:146
  49.8 17.7 %collective-permute-start.21 = (bf16[8,48,128]{2,1,0:T(8,128)(2,1)S(1)}, bf16[8,48,128]{2,1,0:T(8,128)(2,1)S(1)}, u32[]{:S(2)}, u32[]{:S(2)}) collective-permute-start(bf16[8,48,128]{2,1,0:T(8,128)(2,1)S(1)} %pad_maximum_fusion.2), channel_id=1, source_target_pairs={{0,64},{8,72},{16,80},{24,88},{32,96},{40,104},{48,112},{56,120},{... | collective-permute-start | bytes 294920 | tf_op jit(solution)/shard_map/ppermute | solution.py:146
  52.8 18.1 %collective-permute-start.13 = (bf16[8,48,128]{2,1,0:T(8,128)(2,1)S(1)}, bf16[8,48,128]{2,1,0:T(8,128)(2,1)S(1)}, u32[]{:S(2)}, u32[]{:S(2)}) collective-permute-start(bf16[8,48,128]{2,1,0:T(8,128)(2,1)S(1)} %pad_maximum_fusion.1), channel_id=1, source_target_pairs={{0,4},{1,5},{2,6},{3,7},{4,0},{5,1},{6,2},{7,3},{8,12},{9,13},{10,... | collective-permute-start | bytes 294920 | tf_op jit(solution)/shard_map/ppermute | solution.py:146
  66.7 26.9 %collective-permute-start.6 = (bf16[64,48,128]{2,1,0:T(8,128)(2,1)}, bf16[64,48,128]{2,1,0:T(8,128)(2,1)S(1)}, u32[]{:S(2)}, u32[]{:S(2)}) collective-permute-start(bf16[64,48,128]{2,1,0:T(8,128)(2,1)} %get-tuple-element.46), channel_id=1, source_target_pairs={{0,32},{8,40},{16,48},{24,56},{32,0},{40,8},{48,16},{56,24},{64,96... | collective-permute-start | bytes 2359304 | tf_op jit(solution)/shard_map/ppermute | solution.py:146
  68.3 20.8 %collective-permute-start.22 = (bf16[16,48,128]{2,1,0:T(8,128)(2,1)S(1)}, bf16[16,48,128]{2,1,0:T(8,128)(2,1)S(1)}, u32[]{:S(2)}, u32[]{:S(2)}) collective-permute-start(bf16[16,48,128]{2,1,0:T(8,128)(2,1)S(1)} %get-tuple-element.65), channel_id=1, source_target_pairs={{0,32},{8,40},{16,48},{24,56},{32,0},{40,8},{48,16},{56,24},{64,96... | collective-permute-start | bytes 589832 | tf_op jit(solution)/shard_map/ppermute | solution.py:146
  71.8 20.3 %collective-permute-start.14 = (bf16[16,48,128]{2,1,0:T(8,128)(2,1)S(1)}, bf16[16,48,128]{2,1,0:T(8,128)(2,1)S(1)}, u32[]{:S(2)}, u32[]{:S(2)}) collective-permute-start(bf16[16,48,128]{2,1,0:T(8,128)(2,1)S(1)} %get-tuple-element.70), channel_id=1, source_target_pairs={{0,16},{8,24},{16,0},{24,8},{32,48},{40,56},{48,32},{56,40},{64,80... | collective-permute-start | bytes 589832 | tf_op jit(solution)/shard_map/ppermute | solution.py:146
  72.1 55.9 %collective-permute-start.8 = (bf16[1,25,2048]{2,1,0:T(8,128)(2,1)S(1)}, bf16[1,25,2048]{2,1,0:T(8,128)(2,1)}, u32[]{:S(2)}, u32[]{:S(2)}) collective-permute-start(bf16[1,25,2048]{2,1,0:T(8,128)(2,1)S(1)} %copy-done.7), channel_id=1, source_target_pairs={{0,8},{8,16},{16,24},{24,32},{32,40},{40,48},{48,56},{56,64},{64,7... | collective-permute-start | bytes 307208 | tf_op jit(solution)/shard_map/ppermute | solution.py:19
  74.1 55.9 %collective-permute-start.9 = (bf16[1,25,200]{2,1,0:T(8,128)(2,1)S(1)}, bf16[1,25,200]{2,1,0:T(8,128)(2,1)S(1)}, u32[]{:S(2)}, u32[]{:S(2)}) collective-permute-start(bf16[1,25,200]{2,1,0:T(8,128)(2,1)S(1)} %copy-done.8), channel_id=1, source_target_pairs={{0,8},{8,16},{16,24},{24,32},{32,40},{40,48},{48,56},{56,64},{64,7... | collective-permute-start | bytes 30008 | tf_op jit(solution)/shard_map/ppermute | solution.py:19
  90.0 10.2 %collective-permute-start.23 = (bf16[32,48,128]{2,1,0:T(8,128)(2,1)S(1)}, bf16[32,48,128]{2,1,0:T(8,128)(2,1)S(1)}, u32[]{:S(2)}, u32[]{:S(2)}) collective-permute-start(bf16[32,48,128]{2,1,0:T(8,128)(2,1)S(1)} %get-tuple-element.50), channel_id=1, source_target_pairs={{0,4},{1,5},{2,6},{3,7},{4,0},{5,1},{6,2},{7,3},{8,12},{9,13},{10,... | collective-permute-start | bytes 1179656 | tf_op jit(solution)/shard_map/ppermute | solution.py:146
  93.0 9.9 %collective-permute-start.15 = (bf16[32,48,128]{2,1,0:T(8,128)(2,1)}, bf16[32,48,128]{2,1,0:T(8,128)(2,1)S(1)}, u32[]{:S(2)}, u32[]{:S(2)}) collective-permute-start(bf16[32,48,128]{2,1,0:T(8,128)(2,1)} %get-tuple-element.54), channel_id=1, source_target_pairs={{0,2},{1,3},{2,0},{3,1},{4,6},{5,7},{6,4},{7,5},{8,10},{9,11},{10,... | collective-permute-start | bytes 1179656 | tf_op jit(solution)/shard_map/ppermute | solution.py:146
  95.0 28.4 %collective-permute-start.7 = (bf16[128,48,128]{2,1,0:T(8,128)(2,1)}, bf16[128,48,128]{2,1,0:T(8,128)(2,1)S(1)}, u32[]{:S(2)}, u32[]{:S(2)}) collective-permute-start(bf16[128,48,128]{2,1,0:T(8,128)(2,1)} %get-tuple-element.36), channel_id=1, source_target_pairs={{0,8},{8,0},{16,24},{24,16},{32,40},{40,32},{48,56},{56,48},{64,72... | collective-permute-start | bytes 4718600 | tf_op jit(solution)/shard_map/ppermute | solution.py:146
  101.4 16.8 %collective-permute-start.24 = (bf16[64,48,128]{2,1,0:T(8,128)(2,1)}, bf16[64,48,128]{2,1,0:T(8,128)(2,1)S(1)}, u32[]{:S(2)}, u32[]{:S(2)}) collective-permute-start(bf16[64,48,128]{2,1,0:T(8,128)(2,1)} %get-tuple-element.40), channel_id=1, source_target_pairs={{0,16},{8,24},{16,0},{24,8},{32,48},{40,56},{48,32},{56,40},{64,80... | collective-permute-start | bytes 2359304 | tf_op jit(solution)/shard_map/ppermute | solution.py:146
  104.2 16.7 %collective-permute-start.16 = (bf16[64,48,128]{2,1,0:T(8,128)(2,1)}, bf16[64,48,128]{2,1,0:T(8,128)(2,1)}, u32[]{:S(2)}, u32[]{:S(2)}) collective-permute-start(bf16[64,48,128]{2,1,0:T(8,128)(2,1)} %get-tuple-element.43), channel_id=1, source_target_pairs={{0,1},{1,0},{2,3},{3,2},{4,5},{5,4},{6,7},{7,6},{8,9},{9,8},{10,11... | collective-permute-start | bytes 2359304 | tf_op jit(solution)/shard_map/ppermute | solution.py:146
  119.5 10.7 %collective-permute-start.25 = (bf16[128,48,128]{2,1,0:T(8,128)(2,1)}, bf16[128,48,128]{2,1,0:T(8,128)(2,1)}, u32[]{:S(2)}, u32[]{:S(2)}) collective-permute-start(bf16[128,48,128]{2,1,0:T(8,128)(2,1)} %get-tuple-element.32), channel_id=1, source_target_pairs={{0,8},{8,0},{16,24},{24,16},{32,40},{40,32},{48,56},{56,48},{64,72... | collective-permute-start | bytes 4718600 | tf_op jit(solution)/shard_map/ppermute | solution.py:146
  123.4 9.6 %collective-permute-start.17 = (bf16[128,48,128]{2,1,0:T(8,128)(2,1)}, bf16[128,48,128]{2,1,0:T(8,128)(2,1)}, u32[]{:S(2)}, u32[]{:S(2)}) collective-permute-start(bf16[128,48,128]{2,1,0:T(8,128)(2,1)} %get-tuple-element.34), channel_id=1, source_target_pairs={{0,8},{8,0},{16,24},{24,16},{32,40},{40,32},{48,56},{56,48},{64,72... | collective-permute-start | bytes 4718600 | tf_op jit(solution)/shard_map/ppermute | solution.py:146
  (17 other events, 446.9 us)

commit v4 on v3

--- a/solution.py
+++ b/solution.py
@@ -40,16 +40,16 @@
         m_ref[a] = jnp.dot(
             pt_ref[a * size:(a + 1) * size, :], g_ref[...], preferred_element_type=jnp.float32
         )
-    for (_, low, high), rb_ref, cb_ref, part_ref, out_ref in zip(STREAMS, rbs, cbs, parts, outs):
-
-        def one(t, carry, rb_ref=rb_ref, cb_ref=cb_ref, part_ref=part_ref, out_ref=out_ref, low=low, high=high):
+
+    def one(t, carry):
+        for (_, low, high), rb_ref, cb_ref, part_ref, out_ref in zip(STREAMS, rbs, cbs, parts, outs):
             col = pl.multiple_of(cb_ref[t] * size, size)
             blk = m_ref[rb_ref[t], low:high, pl.ds(col, size)]
             prod = blk * part_ref[t, 0:high - low, :].astype(jnp.float32)
             out_ref[pl.ds(t, 1), :] = jnp.sum(prod, axis=0, keepdims=True)
-            return carry
-
-        lax.fori_loop(0, part_ref.shape[0], one, 0)
+        return carry
+
+    lax.fori_loop(0, parts[0].shape[0], one, 0, unroll=2)
 
 
 def tile_bias(panel_t, green, parts, rbs, cbs):
@@ -75,36 +75,38 @@
     rbs, cbs, ss = refs[:count], refs[count:2 * count], refs[2 * count:3 * count]
     x_ref = refs[3 * count]
     parts = refs[3 * count + 1:4 * count + 1]
-    out_ref, a_ref, hi_ref, lo_ref, y_ref = refs[4 * count + 1:]
-    blocks, size, orbitals = a_ref.shape
-    a_ref[...] = jnp.zeros(a_ref.shape, jnp.float32)
-    for (_, low, high), rb_ref, cb_ref, s_ref, part_ref in zip(STREAMS, rbs, cbs, ss, parts):
-
-        def build(t, carry, rb_ref=rb_ref, cb_ref=cb_ref, s_ref=s_ref, part_ref=part_ref, low=low, high=high):
-            col = pl.multiple_of(cb_ref[t] * size, size)
-            row = rb_ref[t]
-            a_ref[row, low:high, pl.ds(col, size)] += s_ref[t] * part_ref[t, 0:high - low, :].astype(jnp.float32)
-            return carry
-
-        lax.fori_loop(0, part_ref.shape[0], build, 0)
-
-    def split(a, carry):
-        whole = a_ref[a]
-        high = whole.astype(jnp.bfloat16)
-        hi_ref[a] = high
-        lo_ref[a] = (whole - high.astype(jnp.float32)).astype(jnp.bfloat16)
+    out_ref, hi_ref, lo_ref, y_ref = refs[4 * count + 1:]
+    orbitals = hi_ref.shape[0]
+    size = parts[0].shape[2]
+    hi_ref[...] = jnp.zeros(hi_ref.shape, hi_ref.dtype)
+    lo_ref[...] = jnp.zeros(lo_ref.shape, lo_ref.dtype)
+
+    def build(t, carry):
+        for (_, low, high), rb_ref, cb_ref, s_ref, part_ref in zip(STREAMS, rbs, cbs, ss, parts):
+            rows = pl.ds(pl.multiple_of(rb_ref[t] * size + low, 16), high - low)
+            cols = pl.ds(pl.multiple_of(cb_ref[t] * size, size), size)
+            whole = (
+                hi_ref[rows, cols].astype(jnp.float32)
+                + lo_ref[rows, cols].astype(jnp.float32)
+                + s_ref[t] * part_ref[t, 0:high - low, :].astype(jnp.float32)
+            )
+            upper = whole.astype(jnp.bfloat16)
+            hi_ref[rows, cols] = upper
+            lo_ref[rows, cols] = (whole - upper.astype(jnp.float32)).astype(jnp.bfloat16)
         return carry
 
-    lax.fori_loop(0, blocks, split, 0)
+    lax.fori_loop(0, parts[0].shape[0], build, 0)
 
     dims = (((1,), (1,)), ((), ()))
+    chunk = 512
     series = x_ref[...]
     running = series.astype(jnp.float32)
     for degree in range(1, TERMS + 1):
-        for a in range(blocks):
-            y_ref[:, a * size:(a + 1) * size] = lax.dot_general(
-                series, hi_ref[a], dims, preferred_element_type=jnp.float32
-            ) + lax.dot_general(series, lo_ref[a], dims, preferred_element_type=jnp.float32)
+        for c in range(orbitals // chunk):
+            span = slice(c * chunk, (c + 1) * chunk)
+            y_ref[:, span] = lax.dot_general(
+                series, hi_ref[span, :], dims, preferred_element_type=jnp.float32
+            ) + lax.dot_general(series, lo_ref[span, :], dims, preferred_element_type=jnp.float32)
         series = (y_ref[...] / degree).astype(jnp.bfloat16)
         running = running + series.astype(jnp.float32)
     out_ref[...] = running.astype(out_ref.dtype)
@@ -123,12 +125,11 @@
         in_specs=[smem] * (3 * count) + [vmem] * (1 + count),
         out_specs=vmem,
         scratch_shapes=[
-            pltpu.VMEM((blocks, size, orbitals), jnp.float32),
-            pltpu.VMEM((blocks, size, orbitals), jnp.bfloat16),
-            pltpu.VMEM((blocks, size, orbitals), jnp.bfloat16),
+            pltpu.VMEM((orbitals, orbitals), jnp.bfloat16),
+            pltpu.VMEM((orbitals, orbitals), jnp.bfloat16),
             pltpu.VMEM((rows, orbitals), jnp.float32),
         ],
-        compiler_params=pltpu.CompilerParams(vmem_limit_bytes=56 * 1024 * 1024),
+        compiler_params=pltpu.CompilerParams(vmem_limit_bytes=48 * 1024 * 1024),
         interpret=INTERPRET,
     )(*rbs, *cbs, *ss, x0, *parts)
 

time: 204 us -> 193 us (0.946)
  Pallas kernels: 51.1 us -> 41.7 us
    pallas_call x1, Pallas kernels: 18.5 us -> 10.3 us  [tile_bias(): pl.pallas_call(bias_kernel, out_shape=[jax.ShapeDtypeStruct((tiles_total,...]
    unnamed x43 -> x29, local copies, waits for them, and re-layouts: 16.1 us -> 16.3 us
  transfers between devices with their start and end apart: 29 -> 29, of which waited for: 14 -> 13; matrix products, arithmetic and copies ran while one was open for 15% -> 16% of each run, Pallas kernels for 0% -> 0%
where the time goes in v4:
time: 193 us; the launch traced here: 192 us
  waiting for transfers between devices  67.5 us (35%)
  starting transfers between devices  45.4 us (24%)
  Pallas kernels  41.7 us (22%)
  local copies, waits for them, and re-layouts  29.9 us (15%)
  other arithmetic  5.45 us (3%)
    ppermute x24, waiting for transfers between devices, xor_gather(): other = lax.ppermute(x, axis, [(i, i ^ step) for i in range(count)])  57.4 us
    ppermute x24, starting transfers between devices, xor_gather(): other = lax.ppermute(x, axis, [(i, i ^ step) for i in range(count)])  36.7 us
    pallas_call x1, Pallas kernels, propagate(): pl.pallas_call(prop_kernel, out_shape=jax.ShapeDtypeStruct((rows, orbital...  31.4 us
    unnamed x29, local copies, waits for them, and re-layouts  16.3 us
    concatenate x6, local copies, waits for them, and re-layouts, xor_gather(): x = jnp.concatenate([x, other], axis=0)  11.9 us
    pallas_call x1, Pallas kernels, tile_bias(): pl.pallas_call(bias_kernel, out_shape=[jax.ShapeDtypeStruct((tiles_total,...  10.3 us
    ppermute x3, waiting for transfers between devices, butterfly_sum(): lax.ppermute(value, axis, [(i, i ^ step) for i in range(count)])  10.1 us
    ppermute x2, starting transfers between devices, shift_from(): lax.ppermute(value, axis, [(i, i + steps) for i in range(count - steps)])  5.11 us
  transfers between devices with their start and end apart: 29, of which 13 were waited for; matrix products, arithmetic and copies ran while one was open for 16% of the time, Pallas kernels for 0%

profile of v4, /device:TPU:2, one launch (start us, length us, event | category | flops | bytes accessed | tf_op | source)
XLA Modules:
  0.0 192.1 jit_solution(17219346842012645129)
XLA Ops:
  1.5 3.2 %collective-permute-start.18 = (bf16[1,48,128]{2,1,0:T(8,128)(2,1)S(1)}, bf16[1,48,128]{2,1,0:T(8,128)(2,1)S(1)}, u32[]{:S(2)}, u32[]{:S(2)}) collective-permute-start(bf16[1,48,128]{2,1,0:T(8,128)(2,1)S(1)} %get-tuple-element.101), channel_id=1, source_target_pairs={{0,2},{1,3},{2,0},{3,1},{4,6},{5,7},{6,4},{7,5},{8,10},{9,11},{10,... | collective-permute-start | bytes 36872 | tf_op jit(solution)/shard_map/ppermute | solution.py:147
  4.7 7.2 %collective-permute-start.10 = (bf16[1,48,128]{2,1,0:T(8,128)(2,1)S(1)}, bf16[1,48,128]{2,1,0:T(8,128)(2,1)S(1)}, u32[]{:S(2)}, u32[]{:S(2)}) collective-permute-start(bf16[1,48,128]{2,1,0:T(8,128)(2,1)S(1)} %get-tuple-element.102), channel_id=1, source_target_pairs={{0,128},{8,136},{16,144},{24,152},{32,160},{40,168},{48,176},{56,1... | collective-permute-start | bytes 36872 | tf_op jit(solution)/shard_map/ppermute | solution.py:147
  13.8 2.1 %collective-permute-start = (bf16[1,48,128]{2,1,0:T(8,128)(2,1)S(1)}, bf16[1,48,128]{2,1,0:T(8,128)(2,1)S(1)}, u32[]{:S(2)}, u32[]{:S(2)}) collective-permute-start(bf16[1,48,128]{2,1,0:T(8,128)(2,1)S(1)} %get-tuple-element.138), channel_id=1, source_target_pairs={{0,4},{1,5},{2,6},{3,7},{4,0},{5,1},{6,2},{7,3},{8,12},{9,13},{10,... | collective-permute-start | bytes 36872 | tf_op jit(solution)/shard_map/ppermute | solution.py:147
  24.5 4.5 %collective-permute-done.2 = bf16[4,48,128]{2,1,0:T(8,128)(2,1)S(1)} collective-permute-done((bf16[4,48,128]{2,1,0:T(8,128)(2,1)S(1)}, bf16[4,48,128]{2,1,0:T(8,128)(2,1)S(1)}, u32[]{:S(2)}, u32[]{:S(2)}) %collective-permute-start.2) | collective-permute-done | bytes 49184 | tf_op jit(solution)/shard_map/ppermute | solution.py:147
  30.5 3.3 %collective-permute-done.3 = bf16[8,48,128]{2,1,0:T(8,128)(2,1)S(1)} collective-permute-done((bf16[8,48,128]{2,1,0:T(8,128)(2,1)S(1)}, bf16[8,48,128]{2,1,0:T(8,128)(2,1)S(1)}, u32[]{:S(2)}, u32[]{:S(2)}) %collective-permute-start.3) | collective-permute-done | bytes 98336 | tf_op jit(solution)/shard_map/ppermute | solution.py:147
  36.4 4.1 %collective-permute-start.20 = (bf16[4,48,128]{2,1,0:T(8,128)(2,1)S(1)}, bf16[4,48,128]{2,1,0:T(8,128)(2,1)S(1)}, u32[]{:S(2)}, u32[]{:S(2)}) collective-permute-start(bf16[4,48,128]{2,1,0:T(8,128)(2,1)S(1)} %pad_maximum_fusion.5), channel_id=1, source_target_pairs={{0,128},{8,136},{16,144},{24,152},{32,160},{40,168},{48,176},{56,1... | collective-permute-start | bytes 147464 | tf_op jit(solution)/shard_map/ppermute | solution.py:147
  41.6 5.9 %collective-permute-done.4 = bf16[16,48,128]{2,1,0:T(8,128)(2,1)S(1)} collective-permute-done((bf16[16,48,128]{2,1,0:T(8,128)(2,1)S(1)}, bf16[16,48,128]{2,1,0:T(8,128)(2,1)S(1)}, u32[]{:S(2)}, u32[]{:S(2)}) %collective-permute-start.4) | collective-permute-done | bytes 196640 | tf_op jit(solution)/shard_map/ppermute | solution.py:147
  49.8 3.0 %collective-permute-start.21 = (bf16[8,48,128]{2,1,0:T(8,128)(2,1)S(1)}, bf16[8,48,128]{2,1,0:T(8,128)(2,1)S(1)}, u32[]{:S(2)}, u32[]{:S(2)}) collective-permute-start(bf16[8,48,128]{2,1,0:T(8,128)(2,1)S(1)} %pad_maximum_fusion.2), channel_id=1, source_target_pairs={{0,64},{8,72},{16,80},{24,88},{32,96},{40,104},{48,112},{56,120},{... | collective-permute-start | bytes 294920 | tf_op jit(solution)/shard_map/ppermute | solution.py:147
  52.8 2.2 %collective-permute-start.13 = (bf16[8,48,128]{2,1,0:T(8,128)(2,1)S(1)}, bf16[8,48,128]{2,1,0:T(8,128)(2,1)S(1)}, u32[]{:S(2)}, u32[]{:S(2)}) collective-permute-start(bf16[8,48,128]{2,1,0:T(8,128)(2,1)S(1)} %pad_maximum_fusion.1), channel_id=1, source_target_pairs={{0,4},{1,5},{2,6},{3,7},{4,0},{5,1},{6,2},{7,3},{8,12},{9,13},{10,... | collective-permute-start | bytes 294920 | tf_op jit(solution)/shard_map/ppermute | solution.py:147
  55.1 10.6 %collective-permute-done.5 = bf16[32,48,128]{2,1,0:T(8,128)(2,1)S(1)} collective-permute-done((bf16[32,48,128]{2,1,0:T(8,128)(2,1)S(1)}, bf16[32,48,128]{2,1,0:T(8,128)(2,1)S(1)}, u32[]{:S(2)}, u32[]{:S(2)}) %collective-permute-start.5) | collective-permute-done | bytes 393248 | tf_op jit(solution)/shard_map/ppermute | solution.py:147
  74.1 3.2 %collective-permute-start.9 = (bf16[1,25,200]{2,1,0:T(8,128)(2,1)S(1)}, bf16[1,25,200]{2,1,0:T(8,128)(2,1)S(1)}, u32[]{:S(2)}, u32[]{:S(2)}) collective-permute-start(bf16[1,25,200]{2,1,0:T(8,128)(2,1)S(1)} %copy-done.1), channel_id=1, source_target_pairs={{0,8},{8,16},{16,24},{24,32},{32,40},{40,48},{48,56},{56,64},{64,7... | collective-permute-start | bytes 30008 | tf_op jit(solution)/shard_map/ppermute | solution.py:19
  77.3 11.7 %collective-permute-done.22 = bf16[16,48,128]{2,1,0:T(8,128)(2,1)S(1)} collective-permute-done((bf16[16,48,128]{2,1,0:T(8,128)(2,1)S(1)}, bf16[16,48,128]{2,1,0:T(8,128)(2,1)S(1)}, u32[]{:S(2)}, u32[]{:S(2)}) %collective-permute-start.22) | collective-permute-done | bytes 196640 | tf_op jit(solution)/shard_map/ppermute | solution.py:147
  90.1 2.1 %collective-permute-start.23 = (bf16[32,48,128]{2,1,0:T(8,128)(2,1)}, bf16[32,48,128]{2,1,0:T(8,128)(2,1)S(1)}, u32[]{:S(2)}, u32[]{:S(2)}) collective-permute-start(bf16[32,48,128]{2,1,0:T(8,128)(2,1)} %get-tuple-element.50), channel_id=1, source_target_pairs={{0,4},{1,5},{2,6},{3,7},{4,0},{5,1},{6,2},{7,3},{8,12},{9,13},{10,... | collective-permute-start | bytes 1179656 | tf_op jit(solution)/shard_map/ppermute | solution.py:147
  95.1 5.4 %collective-permute-done.23 = bf16[32,48,128]{2,1,0:T(8,128)(2,1)S(1)} collective-permute-done((bf16[32,48,128]{2,1,0:T(8,128)(2,1)}, bf16[32,48,128]{2,1,0:T(8,128)(2,1)S(1)}, u32[]{:S(2)}, u32[]{:S(2)}) %collective-permute-start.23) | collective-permute-done | bytes 393248 | tf_op jit(solution)/shard_map/ppermute | solution.py:147
  106.2 12.2 %collective-permute-done.24 = bf16[64,48,128]{2,1,0:T(8,128)(2,1)S(1)} collective-permute-done((bf16[64,48,128]{2,1,0:T(8,128)(2,1)}, bf16[64,48,128]{2,1,0:T(8,128)(2,1)S(1)}, u32[]{:S(2)}, u32[]{:S(2)}) %collective-permute-start.24) | collective-permute-done | bytes 786464 | tf_op jit(solution)/shard_map/ppermute | solution.py:147
  121.2 2.5 %constant_dynamic-update-slice_fusion.53 = (bf16[128,48,128]{2,1,0:T(8,128)(2,1)}, bf16[256,48,128]{2,1,0:T(8,128)(2,1)}) fusion(bf16[128,48,128]{2,1,0:T(8,128)(2,1)} %get-tuple-element.41, bf16[64,48,128]{2,1,0:T(8,128)(2,1)} %collective-permute-done.16, bf16[256,48,128]{2,1,0:T(8,128)(2,1)} %get-tuple-element.42), kind=kLoop, calls=%fused_computation.65 | loop fusion | bytes 2359296 | tf_op jit(solution)/shard_map/concatenate | solution.py:148
  124.9 2.1 %fusion.1 = f32[256]{0:T(256)S(1)} fusion(bf16[256,48,128]{2,1,0:T(8,128)(2,1)} %constant_dynamic-update-slice_fusion.26.refs_10_.refs_12_), kind=kLoop, calls=%fused_computation.121 | loop fusion | flops 256 | bytes 1536 | tf_op jit(solution)/shard_map/convert_element_type | solution.py:193
  129.9 2.8 %constant_dynamic-update-slice_fusion.96.refs_9_.refs_11_ = bf16[256,48,128]{2,1,0:T(8,128)(2,1)} fusion(bf16[256,48,128]{2,1,0:T(8,128)(2,1)} %get-tuple-element.33, bf16[128,48,128]{2,1,0:T(8,128)(2,1)} %collective-permute-done.25), kind=kLoop, calls=%fused_computation.108 | loop fusion | bytes 3145728 | tf_op jit(solution)/shard_map/concatenate | solution.py:148
  132.6 2.7 %constant_dynamic-update-slice_fusion.61.refs_8_.refs_10_ = bf16[256,48,128]{2,1,0:T(8,128)(2,1)} fusion(bf16[256,48,128]{2,1,0:T(8,128)(2,1)} %get-tuple-element.35, bf16[128,48,128]{2,1,0:T(8,128)(2,1)} %collective-permute-done.17), kind=kLoop, calls=%fused_computation.73 | loop fusion | bytes 3145728 | tf_op jit(solution)/shard_map/concatenate | solution.py:148
  135.3 10.3 %shard_map.73 = (f32[256,128]{1,0:T(8,128)S(1)}, f32[256,128]{1,0:T(8,128)S(1)}, f32[256,128]{1,0:T(8,128)S(1)}) custom-call(s32[256]{0:T(256)S(1)} %get-tuple-element.27.refs_0_, s32[256]{0:T(256)S(1)} %get-tuple-element.25.refs_1_, s32[256]{0:T(256)S(1)} %get-tuple-element.24.refs_2_, s32[256]{0:T(256)S(1)} %get-tuple-element.28.refs_3_, ...), custom_call_target="tpu_custom_call" | custom-call | tf_op jit(solution)/shard_map/pallas_call | solution.py:62
  147.1 2.7 %collective-permute-done.26 = f32[64]{0:T(128)S(1)} collective-permute-done((f32[64]{0:T(128)S(1)}, f32[64]{0:T(128)S(1)}, u32[]{:S(2)}, u32[]{:S(2)}) %collective-permute-start.26) | collective-permute-done | bytes 288 | tf_op jit(solution)/shard_map/ppermute | solution.py:26
  151.3 3.5 %collective-permute-done.27 = f32[64]{0:T(128)S(1)} collective-permute-done((f32[64]{0:T(128)S(1)}, f32[64]{0:T(128)S(1)}, u32[]{:S(2)}, u32[]{:S(2)}) %collective-permute-start.27) | collective-permute-done | bytes 288 | tf_op jit(solution)/shard_map/ppermute | solution.py:26
  155.9 4.0 %collective-permute-done.28 = f32[64]{0:T(128)S(1)} collective-permute-done((f32[64]{0:T(128)S(1)}, f32[64]{0:T(128)S(1)}, u32[]{:S(2)}, u32[]{:S(2)}) %collective-permute-start.28) | collective-permute-done | bytes 288 | tf_op jit(solution)/shard_map/ppermute | solution.py:26
  160.0 31.4 %shard_map.74 = bf16[32,2048]{1,0:T(8,128)(2,1)S(1)} custom-call(s32[256]{0:T(256)S(1)} %get-tuple-element.27.refs_0_, s32[256]{0:T(256)S(1)} %get-tuple-element.25.refs_1_, s32[256]{0:T(256)S(1)} %get-tuple-element.24.refs_2_, s32[256]{0:T(256)S(1)} %get-tuple-element.28.refs_3_, s32[256]{0:T(256)S(1)} %get-tuple-element.26.refs_4_, ...), custom_call_target="tpu_custom_call" | custom-call | tf_op jit(solution)/shard_map/pallas_call | solution.py:122
  (107 shorter events, 48.0 us)
Async XLA Ops:
  1.5 14.5 %collective-permute-start.18 = (bf16[1,48,128]{2,1,0:T(8,128)(2,1)S(1)}, bf16[1,48,128]{2,1,0:T(8,128)(2,1)S(1)}, u32[]{:S(2)}, u32[]{:S(2)}) collective-permute-start(bf16[1,48,128]{2,1,0:T(8,128)(2,1)S(1)} %get-tuple-element.101), channel_id=1, source_target_pairs={{0,2},{1,3},{2,0},{3,1},{4,6},{5,7},{6,4},{7,5},{8,10},{9,11},{10,... | collective-permute-start | bytes 36872 | tf_op jit(solution)/shard_map/ppermute | solution.py:147
  4.7 12.0 %collective-permute-start.10 = (bf16[1,48,128]{2,1,0:T(8,128)(2,1)S(1)}, bf16[1,48,128]{2,1,0:T(8,128)(2,1)S(1)}, u32[]{:S(2)}, u32[]{:S(2)}) collective-permute-start(bf16[1,48,128]{2,1,0:T(8,128)(2,1)S(1)} %get-tuple-element.102), channel_id=1, source_target_pairs={{0,128},{8,136},{16,144},{24,152},{32,160},{40,168},{48,176},{56,1... | collective-permute-start | bytes 36872 | tf_op jit(solution)/shard_map/ppermute | solution.py:147
  13.8 5.2 %collective-permute-start = (bf16[1,48,128]{2,1,0:T(8,128)(2,1)S(1)}, bf16[1,48,128]{2,1,0:T(8,128)(2,1)S(1)}, u32[]{:S(2)}, u32[]{:S(2)}) collective-permute-start(bf16[1,48,128]{2,1,0:T(8,128)(2,1)S(1)} %get-tuple-element.138), channel_id=1, source_target_pairs={{0,4},{1,5},{2,6},{3,7},{4,0},{5,1},{6,2},{7,3},{8,12},{9,13},{10,... | collective-permute-start | bytes 36872 | tf_op jit(solution)/shard_map/ppermute | solution.py:147
  16.0 20.4 %collective-permute-start.19 = (bf16[2,48,128]{2,1,0:T(8,128)(2,1)S(1)}, bf16[2,48,128]{2,1,0:T(8,128)(2,1)S(1)}, u32[]{:S(2)}, u32[]{:S(2)}) collective-permute-start(bf16[2,48,128]{2,1,0:T(8,128)(2,1)S(1)} %pad_maximum_fusion.8), channel_id=1, source_target_pairs={{0,1},{1,0},{2,3},{3,2},{4,5},{5,4},{6,7},{7,6},{8,9},{9,8},{10,11... | collective-permute-start | bytes 73736 | tf_op jit(solution)/shard_map/ppermute | solution.py:147
  16.7 23.9 %collective-permute-start.11 = (bf16[2,48,128]{2,1,0:T(8,128)(2,1)S(1)}, bf16[2,48,128]{2,1,0:T(8,128)(2,1)S(1)}, u32[]{:S(2)}, u32[]{:S(2)}) collective-permute-start(bf16[2,48,128]{2,1,0:T(8,128)(2,1)S(1)} %pad_maximum_fusion.7), channel_id=1, source_target_pairs={{0,64},{8,72},{16,80},{24,88},{32,96},{40,104},{48,112},{56,120},{... | collective-permute-start | bytes 73736 | tf_op jit(solution)/shard_map/ppermute | solution.py:147
  22.9 6.1 %collective-permute-start.2 = (bf16[4,48,128]{2,1,0:T(8,128)(2,1)S(1)}, bf16[4,48,128]{2,1,0:T(8,128)(2,1)S(1)}, u32[]{:S(2)}, u32[]{:S(2)}) collective-permute-start(bf16[4,48,128]{2,1,0:T(8,128)(2,1)S(1)} %pad_maximum_fusion.3), channel_id=1, source_target_pairs={{0,2},{1,3},{2,0},{3,1},{4,6},{5,7},{6,4},{7,5},{8,10},{9,11},{10,... | collective-permute-start | bytes 147464 | tf_op jit(solution)/shard_map/ppermute | solution.py:147
  34.5 13.1 %collective-permute-start.4 = (bf16[16,48,128]{2,1,0:T(8,128)(2,1)S(1)}, bf16[16,48,128]{2,1,0:T(8,128)(2,1)S(1)}, u32[]{:S(2)}, u32[]{:S(2)}) collective-permute-start(bf16[16,48,128]{2,1,0:T(8,128)(2,1)S(1)} %get-tuple-element.75), channel_id=1, source_target_pairs={{0,128},{8,136},{16,144},{24,152},{32,160},{40,168},{48,176},{56,1... | collective-permute-start | bytes 589832 | tf_op jit(solution)/shard_map/ppermute | solution.py:147
  36.4 13.4 %collective-permute-start.20 = (bf16[4,48,128]{2,1,0:T(8,128)(2,1)S(1)}, bf16[4,48,128]{2,1,0:T(8,128)(2,1)S(1)}, u32[]{:S(2)}, u32[]{:S(2)}) collective-permute-start(bf16[4,48,128]{2,1,0:T(8,128)(2,1)S(1)} %pad_maximum_fusion.5), channel_id=1, source_target_pairs={{0,128},{8,136},{16,144},{24,152},{32,160},{40,168},{48,176},{56,1... | collective-permute-start | bytes 147464 | tf_op jit(solution)/shard_map/ppermute | solution.py:147
  40.5 12.3 %collective-permute-start.12 = (bf16[4,48,128]{2,1,0:T(8,128)(2,1)S(1)}, bf16[4,48,128]{2,1,0:T(8,128)(2,1)S(1)}, u32[]{:S(2)}, u32[]{:S(2)}) collective-permute-start(bf16[4,48,128]{2,1,0:T(8,128)(2,1)S(1)} %pad_maximum_fusion.4), channel_id=1, source_target_pairs={{0,32},{8,40},{16,48},{24,56},{32,0},{40,8},{48,16},{56,24},{64,96... | collective-permute-start | bytes 147464 | tf_op jit(solution)/shard_map/ppermute | solution.py:147
  48.5 17.2 %collective-permute-start.5 = (bf16[32,48,128]{2,1,0:T(8,128)(2,1)S(1)}, bf16[32,48,128]{2,1,0:T(8,128)(2,1)S(1)}, u32[]{:S(2)}, u32[]{:S(2)}) collective-permute-start(bf16[32,48,128]{2,1,0:T(8,128)(2,1)S(1)} %get-tuple-element.58), channel_id=1, source_target_pairs={{0,64},{8,72},{16,80},{24,88},{32,96},{40,104},{48,112},{56,120},{... | collective-permute-start | bytes 1179656 | tf_op jit(solution)/shard_map/ppermute | solution.py:147
  49.8 17.7 %collective-permute-start.21 = (bf16[8,48,128]{2,1,0:T(8,128)(2,1)S(1)}, bf16[8,48,128]{2,1,0:T(8,128)(2,1)S(1)}, u32[]{:S(2)}, u32[]{:S(2)}) collective-permute-start(bf16[8,48,128]{2,1,0:T(8,128)(2,1)S(1)} %pad_maximum_fusion.2), channel_id=1, source_target_pairs={{0,64},{8,72},{16,80},{24,88},{32,96},{40,104},{48,112},{56,120},{... | collective-permute-start | bytes 294920 | tf_op jit(solution)/shard_map/ppermute | solution.py:147
  52.8 18.2 %collective-permute-start.13 = (bf16[8,48,128]{2,1,0:T(8,128)(2,1)S(1)}, bf16[8,48,128]{2,1,0:T(8,128)(2,1)S(1)}, u32[]{:S(2)}, u32[]{:S(2)}) collective-permute-start(bf16[8,48,128]{2,1,0:T(8,128)(2,1)S(1)} %pad_maximum_fusion.1), channel_id=1, source_target_pairs={{0,4},{1,5},{2,6},{3,7},{4,0},{5,1},{6,2},{7,3},{8,12},{9,13},{10,... | collective-permute-start | bytes 294920 | tf_op jit(solution)/shard_map/ppermute | solution.py:147
  66.7 26.9 %collective-permute-start.6 = (bf16[64,48,128]{2,1,0:T(8,128)(2,1)}, bf16[64,48,128]{2,1,0:T(8,128)(2,1)S(1)}, u32[]{:S(2)}, u32[]{:S(2)}) collective-permute-start(bf16[64,48,128]{2,1,0:T(8,128)(2,1)} %get-tuple-element.46), channel_id=1, source_target_pairs={{0,32},{8,40},{16,48},{24,56},{32,0},{40,8},{48,16},{56,24},{64,96... | collective-permute-start | bytes 2359304 | tf_op jit(solution)/shard_map/ppermute | solution.py:147
  68.3 20.7 %collective-permute-start.22 = (bf16[16,48,128]{2,1,0:T(8,128)(2,1)S(1)}, bf16[16,48,128]{2,1,0:T(8,128)(2,1)S(1)}, u32[]{:S(2)}, u32[]{:S(2)}) collective-permute-start(bf16[16,48,128]{2,1,0:T(8,128)(2,1)S(1)} %get-tuple-element.65), channel_id=1, source_target_pairs={{0,32},{8,40},{16,48},{24,56},{32,0},{40,8},{48,16},{56,24},{64,96... | collective-permute-start | bytes 589832 | tf_op jit(solution)/shard_map/ppermute | solution.py:147
  71.8 20.3 %collective-permute-start.14 = (bf16[16,48,128]{2,1,0:T(8,128)(2,1)S(1)}, bf16[16,48,128]{2,1,0:T(8,128)(2,1)S(1)}, u32[]{:S(2)}, u32[]{:S(2)}) collective-permute-start(bf16[16,48,128]{2,1,0:T(8,128)(2,1)S(1)} %get-tuple-element.70), channel_id=1, source_target_pairs={{0,16},{8,24},{16,0},{24,8},{32,48},{40,56},{48,32},{56,40},{64,80... | collective-permute-start | bytes 589832 | tf_op jit(solution)/shard_map/ppermute | solution.py:147
  72.2 56.1 %collective-permute-start.8 = (bf16[1,25,2048]{2,1,0:T(8,128)(2,1)}, bf16[1,25,2048]{2,1,0:T(8,128)(2,1)}, u32[]{:S(2)}, u32[]{:S(2)}) collective-permute-start(bf16[1,25,2048]{2,1,0:T(8,128)(2,1)} %param.10), channel_id=1, source_target_pairs={{0,8},{8,16},{16,24},{24,32},{32,40},{40,48},{48,56},{56,64},{64,7... | collective-permute-start | bytes 307208 | tf_op jit(solution)/shard_map/ppermute | solution.py:19
  74.1 55.4 %collective-permute-start.9 = (bf16[1,25,200]{2,1,0:T(8,128)(2,1)S(1)}, bf16[1,25,200]{2,1,0:T(8,128)(2,1)S(1)}, u32[]{:S(2)}, u32[]{:S(2)}) collective-permute-start(bf16[1,25,200]{2,1,0:T(8,128)(2,1)S(1)} %copy-done.1), channel_id=1, source_target_pairs={{0,8},{8,16},{16,24},{24,32},{32,40},{40,48},{48,56},{56,64},{64,7... | collective-permute-start | bytes 30008 | tf_op jit(solution)/shard_map/ppermute | solution.py:19
  90.1 10.4 %collective-permute-start.23 = (bf16[32,48,128]{2,1,0:T(8,128)(2,1)}, bf16[32,48,128]{2,1,0:T(8,128)(2,1)S(1)}, u32[]{:S(2)}, u32[]{:S(2)}) collective-permute-start(bf16[32,48,128]{2,1,0:T(8,128)(2,1)} %get-tuple-element.50), channel_id=1, source_target_pairs={{0,4},{1,5},{2,6},{3,7},{4,0},{5,1},{6,2},{7,3},{8,12},{9,13},{10,... | collective-permute-start | bytes 1179656 | tf_op jit(solution)/shard_map/ppermute | solution.py:147
  93.1 10.0 %collective-permute-start.15 = (bf16[32,48,128]{2,1,0:T(8,128)(2,1)}, bf16[32,48,128]{2,1,0:T(8,128)(2,1)S(1)}, u32[]{:S(2)}, u32[]{:S(2)}) collective-permute-start(bf16[32,48,128]{2,1,0:T(8,128)(2,1)} %get-tuple-element.54), channel_id=1, source_target_pairs={{0,2},{1,3},{2,0},{3,1},{4,6},{5,7},{6,4},{7,5},{8,10},{9,11},{10,... | collective-permute-start | bytes 1179656 | tf_op jit(solution)/shard_map/ppermute | solution.py:147
  95.0 28.7 %collective-permute-start.7 = (bf16[128,48,128]{2,1,0:T(8,128)(2,1)}, bf16[128,48,128]{2,1,0:T(8,128)(2,1)S(1)}, u32[]{:S(2)}, u32[]{:S(2)}) collective-permute-start(bf16[128,48,128]{2,1,0:T(8,128)(2,1)} %get-tuple-element.36), channel_id=1, source_target_pairs={{0,8},{8,0},{16,24},{24,16},{32,40},{40,32},{48,56},{56,48},{64,72... | collective-permute-start | bytes 4718600 | tf_op jit(solution)/shard_map/ppermute | solution.py:147
  101.6 16.8 %collective-permute-start.24 = (bf16[64,48,128]{2,1,0:T(8,128)(2,1)}, bf16[64,48,128]{2,1,0:T(8,128)(2,1)S(1)}, u32[]{:S(2)}, u32[]{:S(2)}) collective-permute-start(bf16[64,48,128]{2,1,0:T(8,128)(2,1)} %get-tuple-element.40), channel_id=1, source_target_pairs={{0,16},{8,24},{16,0},{24,8},{32,48},{40,56},{48,32},{56,40},{64,80... | collective-permute-start | bytes 2359304 | tf_op jit(solution)/shard_map/ppermute | solution.py:147
  104.4 16.8 %collective-permute-start.16 = (bf16[64,48,128]{2,1,0:T(8,128)(2,1)}, bf16[64,48,128]{2,1,0:T(8,128)(2,1)}, u32[]{:S(2)}, u32[]{:S(2)}) collective-permute-start(bf16[64,48,128]{2,1,0:T(8,128)(2,1)} %get-tuple-element.43), channel_id=1, source_target_pairs={{0,1},{1,0},{2,3},{3,2},{4,5},{5,4},{6,7},{7,6},{8,9},{9,8},{10,11... | collective-permute-start | bytes 2359304 | tf_op jit(solution)/shard_map/ppermute | solution.py:147
  119.8 10.1 %collective-permute-start.25 = (bf16[128,48,128]{2,1,0:T(8,128)(2,1)}, bf16[128,48,128]{2,1,0:T(8,128)(2,1)}, u32[]{:S(2)}, u32[]{:S(2)}) collective-permute-start(bf16[128,48,128]{2,1,0:T(8,128)(2,1)} %get-tuple-element.32), channel_id=1, source_target_pairs={{0,8},{8,0},{16,24},{24,16},{32,40},{40,32},{48,56},{56,48},{64,72... | collective-permute-start | bytes 4718600 | tf_op jit(solution)/shard_map/ppermute | solution.py:147
  123.7 8.9 %collective-permute-start.17 = (bf16[128,48,128]{2,1,0:T(8,128)(2,1)}, bf16[128,48,128]{2,1,0:T(8,128)(2,1)}, u32[]{:S(2)}, u32[]{:S(2)}) collective-permute-start(bf16[128,48,128]{2,1,0:T(8,128)(2,1)} %get-tuple-element.34), channel_id=1, source_target_pairs={{0,8},{8,0},{16,24},{24,16},{32,40},{40,32},{48,56},{56,48},{64,72... | collective-permute-start | bytes 4718600 | tf_op jit(solution)/shard_map/ppermute | solution.py:147
  (10 other events, 216.8 us)

commit v5 on v4

--- a/solution.py
+++ b/solution.py
@@ -97,16 +97,15 @@
 
     lax.fori_loop(0, parts[0].shape[0], build, 0)
 
-    dims = (((1,), (1,)), ((), ()))
     chunk = 512
     series = x_ref[...]
     running = series.astype(jnp.float32)
     for degree in range(1, TERMS + 1):
         for c in range(orbitals // chunk):
             span = slice(c * chunk, (c + 1) * chunk)
-            y_ref[:, span] = lax.dot_general(
-                series, hi_ref[span, :], dims, preferred_element_type=jnp.float32
-            ) + lax.dot_general(series, lo_ref[span, :], dims, preferred_element_type=jnp.float32)
+            y_ref[span, :] = jnp.dot(
+                hi_ref[span, :], series, preferred_element_type=jnp.float32
+            ) + jnp.dot(lo_ref[span, :], series, preferred_element_type=jnp.float32)
         series = (y_ref[...] / degree).astype(jnp.bfloat16)
         running = running + series.astype(jnp.float32)
     out_ref[...] = running.astype(out_ref.dtype)
@@ -114,20 +113,20 @@
 
 def propagate(x0, parts, rbs, cbs, ss):
     size = parts[0].shape[2]
-    rows, orbitals = x0.shape
+    orbitals, rows = x0.shape
     blocks = orbitals // size
     count = len(parts)
     smem = pl.BlockSpec(memory_space=pltpu.SMEM)
     vmem = pl.BlockSpec(memory_space=pltpu.VMEM)
     return pl.pallas_call(
         prop_kernel,
-        out_shape=jax.ShapeDtypeStruct((rows, orbitals), jnp.bfloat16),
+        out_shape=jax.ShapeDtypeStruct((orbitals, rows), jnp.bfloat16),
         in_specs=[smem] * (3 * count) + [vmem] * (1 + count),
         out_specs=vmem,
         scratch_shapes=[
             pltpu.VMEM((orbitals, orbitals), jnp.bfloat16),
             pltpu.VMEM((orbitals, orbitals), jnp.bfloat16),
-            pltpu.VMEM((rows, orbitals), jnp.float32),
+            pltpu.VMEM((orbitals, rows), jnp.float32),
         ],
         compiler_params=pltpu.CompilerParams(vmem_limit_bytes=48 * 1024 * 1024),
         interpret=INTERPRET,
@@ -210,8 +209,8 @@
     bias = jnp.clip(TIME_STEP_ROOT * raw, -1.0, 1.0)
     scales = TIME_STEP_ROOT * (aux_fields[0] - bias)
     ss = [pick(scales, source // KT) for source in sources]
-    out = propagate(pad_rows(start), parts, rbs, cbs, ss)
-    return out[:cols_local][None]
+    out = propagate(pad_rows(start).T, parts, rbs, cbs, ss)
+    return out.T[:cols_local][None]
 
 
 def solution(mesh):

time: 193 us -> 193 us (level)
    ppermute x24, starting transfers between devices: 36.7 us -> 39.9 us  [xor_gather(): other = lax.ppermute(x, axis, [(i, i ^ step) for i in range(count)])]
    unnamed x29 -> x34, local copies, waits for them, and re-layouts: 16.3 us -> 15.9 us
  transfers between devices with their start and end apart: 29 -> 29, of which waited for: 13 -> 15; matrix products, arithmetic and copies ran while one was open for 16% -> 15% of each run, Pallas kernels for 0% -> 0%
where the time goes in v5:
time: 193 us; the launch traced here: 192 us
  waiting for transfers between devices  68.4 us (35%)
  starting transfers between devices  46.9 us (24%)
  Pallas kernels  40.5 us (21%)
  local copies, waits for them, and re-layouts  29.5 us (15%)
  other arithmetic  4.58 us (2%)
    ppermute x24, waiting for transfers between devices, xor_gather(): other = lax.ppermute(x, axis, [(i, i ^ step) for i in range(count)])  57.3 us
    ppermute x24, starting transfers between devices, xor_gather(): other = lax.ppermute(x, axis, [(i, i ^ step) for i in range(count)])  39.9 us
    pallas_call x1, Pallas kernels, propagate(): pl.pallas_call(prop_kernel, out_shape=jax.ShapeDtypeStruct((orbitals, row...  30.2 us
    unnamed x34, local copies, waits for them, and re-layouts  15.9 us
    concatenate x6, local copies, waits for them, and re-layouts, xor_gather(): x = jnp.concatenate([x, other], axis=0)  11.9 us
    ppermute x3, waiting for transfers between devices, butterfly_sum(): lax.ppermute(value, axis, [(i, i ^ step) for i in range(count)])  11.1 us
    pallas_call x1, Pallas kernels, tile_bias(): pl.pallas_call(bias_kernel, out_shape=[jax.ShapeDtypeStruct((tiles_total,...  10.3 us
    ppermute x2, starting transfers between devices, shift_from(): lax.ppermute(value, axis, [(i, i + steps) for i in range(count - steps)])  4.32 us
  transfers between devices with their start and end apart: 29, of which 15 were waited for; matrix products, arithmetic and copies ran while one was open for 15% of the time, Pallas kernels for 0%

profile of v5, /device:TPU:2, one launch (start us, length us, event | category | flops | bytes accessed | tf_op | source)
XLA Modules:
  0.0 192.0 jit_solution(7074506889888682705)
XLA Ops:
  1.4 3.2 %collective-permute-start.18 = (bf16[1,48,128]{2,1,0:T(8,128)(2,1)S(1)}, bf16[1,48,128]{2,1,0:T(8,128)(2,1)S(1)}, u32[]{:S(2)}, u32[]{:S(2)}) collective-permute-start(bf16[1,48,128]{2,1,0:T(8,128)(2,1)S(1)} %get-tuple-element.99), channel_id=1, source_target_pairs={{0,2},{1,3},{2,0},{3,1},{4,6},{5,7},{6,4},{7,5},{8,10},{9,11},{10,... | collective-permute-start | bytes 36872 | tf_op jit(solution)/shard_map/ppermute | solution.py:146
  4.6 7.2 %collective-permute-start.10 = (bf16[1,48,128]{2,1,0:T(8,128)(2,1)S(1)}, bf16[1,48,128]{2,1,0:T(8,128)(2,1)S(1)}, u32[]{:S(2)}, u32[]{:S(2)}) collective-permute-start(bf16[1,48,128]{2,1,0:T(8,128)(2,1)S(1)} %get-tuple-element.100), channel_id=1, source_target_pairs={{0,128},{8,136},{16,144},{24,152},{32,160},{40,168},{48,176},{56,1... | collective-permute-start | bytes 36872 | tf_op jit(solution)/shard_map/ppermute | solution.py:146
  25.1 3.8 %collective-permute-done.2 = bf16[4,48,128]{2,1,0:T(8,128)(2,1)S(1)} collective-permute-done((bf16[4,48,128]{2,1,0:T(8,128)(2,1)S(1)}, bf16[4,48,128]{2,1,0:T(8,128)(2,1)S(1)}, u32[]{:S(2)}, u32[]{:S(2)}) %collective-permute-start.2) | collective-permute-done | bytes 49184 | tf_op jit(solution)/shard_map/ppermute | solution.py:146
  30.1 3.5 %collective-permute-done.3 = bf16[8,48,128]{2,1,0:T(8,128)(2,1)S(1)} collective-permute-done((bf16[8,48,128]{2,1,0:T(8,128)(2,1)S(1)}, bf16[8,48,128]{2,1,0:T(8,128)(2,1)S(1)}, u32[]{:S(2)}, u32[]{:S(2)}) %collective-permute-start.3) | collective-permute-done | bytes 98336 | tf_op jit(solution)/shard_map/ppermute | solution.py:146
  34.3 3.8 %collective-permute-start.4 = (bf16[16,48,128]{2,1,0:T(8,128)(2,1)S(1)}, bf16[16,48,128]{2,1,0:T(8,128)(2,1)S(1)}, u32[]{:S(2)}, u32[]{:S(2)}) collective-permute-start(bf16[16,48,128]{2,1,0:T(8,128)(2,1)S(1)} %get-tuple-element.73), channel_id=1, source_target_pairs={{0,128},{8,136},{16,144},{24,152},{32,160},{40,168},{48,176},{56,1... | collective-permute-start | bytes 589832 | tf_op jit(solution)/shard_map/ppermute | solution.py:146
  40.6 3.7 %collective-permute-done.4 = bf16[16,48,128]{2,1,0:T(8,128)(2,1)S(1)} collective-permute-done((bf16[16,48,128]{2,1,0:T(8,128)(2,1)S(1)}, bf16[16,48,128]{2,1,0:T(8,128)(2,1)S(1)}, u32[]{:S(2)}, u32[]{:S(2)}) %collective-permute-start.4) | collective-permute-done | bytes 196640 | tf_op jit(solution)/shard_map/ppermute | solution.py:146
  45.2 4.1 %collective-permute-start.5 = (bf16[32,48,128]{2,1,0:T(8,128)(2,1)S(1)}, bf16[32,48,128]{2,1,0:T(8,128)(2,1)S(1)}, u32[]{:S(2)}, u32[]{:S(2)}) collective-permute-start(bf16[32,48,128]{2,1,0:T(8,128)(2,1)S(1)} %get-tuple-element.58), channel_id=1, source_target_pairs={{0,64},{8,72},{16,80},{24,88},{32,96},{40,104},{48,112},{56,120},{... | collective-permute-start | bytes 1179656 | tf_op jit(solution)/shard_map/ppermute | solution.py:146
  49.2 8.3 %collective-permute-done.21 = bf16[8,48,128]{2,1,0:T(8,128)(2,1)S(1)} collective-permute-done((bf16[8,48,128]{2,1,0:T(8,128)(2,1)S(1)}, bf16[8,48,128]{2,1,0:T(8,128)(2,1)S(1)}, u32[]{:S(2)}, u32[]{:S(2)}) %collective-permute-start.21) | collective-permute-done | bytes 98336 | tf_op jit(solution)/shard_map/ppermute | solution.py:146
  61.1 8.9 %collective-permute-done.22 = bf16[16,48,128]{2,1,0:T(8,128)(2,1)S(1)} collective-permute-done((bf16[16,48,128]{2,1,0:T(8,128)(2,1)S(1)}, bf16[16,48,128]{2,1,0:T(8,128)(2,1)S(1)}, u32[]{:S(2)}, u32[]{:S(2)}) %collective-permute-start.22) | collective-permute-done | bytes 196640 | tf_op jit(solution)/shard_map/ppermute | solution.py:146
  73.9 2.3 %collective-permute-start.13 = (bf16[8,48,128]{2,1,0:T(8,128)(2,1)S(1)}, bf16[8,48,128]{2,1,0:T(8,128)(2,1)S(1)}, u32[]{:S(2)}, u32[]{:S(2)}) collective-permute-start(bf16[8,48,128]{2,1,0:T(8,128)(2,1)S(1)} %pad_maximum_fusion.1), channel_id=1, source_target_pairs={{0,4},{1,5},{2,6},{3,7},{4,0},{5,1},{6,2},{7,3},{8,12},{9,13},{10,... | collective-permute-start | bytes 294920 | tf_op jit(solution)/shard_map/ppermute | solution.py:146
  76.9 8.5 %collective-permute-done.13 = bf16[8,48,128]{2,1,0:T(8,128)(2,1)S(1)} collective-permute-done((bf16[8,48,128]{2,1,0:T(8,128)(2,1)S(1)}, bf16[8,48,128]{2,1,0:T(8,128)(2,1)S(1)}, u32[]{:S(2)}, u32[]{:S(2)}) %collective-permute-start.13) | collective-permute-done | bytes 98336 | tf_op jit(solution)/shard_map/ppermute | solution.py:146
  89.3 4.7 %collective-permute-done.14 = bf16[16,48,128]{2,1,0:T(8,128)(2,1)S(1)} collective-permute-done((bf16[16,48,128]{2,1,0:T(8,128)(2,1)S(1)}, bf16[16,48,128]{2,1,0:T(8,128)(2,1)S(1)}, u32[]{:S(2)}, u32[]{:S(2)}) %collective-permute-start.14) | collective-permute-done | bytes 196640 | tf_op jit(solution)/shard_map/ppermute | solution.py:146
  94.9 2.4 %collective-permute-start.15 = (bf16[32,48,128]{2,1,0:T(8,128)(2,1)}, bf16[32,48,128]{2,1,0:T(8,128)(2,1)S(1)}, u32[]{:S(2)}, u32[]{:S(2)}) collective-permute-start(bf16[32,48,128]{2,1,0:T(8,128)(2,1)} %get-tuple-element.54), channel_id=1, source_target_pairs={{0,2},{1,3},{2,0},{3,1},{4,6},{5,7},{6,4},{7,5},{8,10},{9,11},{10,... | collective-permute-start | bytes 1179656 | tf_op jit(solution)/shard_map/ppermute | solution.py:146
  98.9 2.4 %collective-permute-start.8 = (bf16[1,25,2048]{1,2,0:T(8,128)(2,1)S(1)}, bf16[1,25,2048]{1,2,0:T(8,128)(2,1)}, u32[]{:S(2)}, u32[]{:S(2)}) collective-permute-start(bf16[1,25,2048]{1,2,0:T(8,128)(2,1)S(1)} %copy.14), channel_id=1, source_target_pairs={{0,8},{8,16},{16,24},{24,32},{32,40},{40,48},{48,56},{56,64},{64,7... | collective-permute-start | bytes 307208 | tf_op jit(solution)/shard_map/ppermute | solution.py:19
  107.0 3.9 %collective-permute-done.24 = bf16[64,48,128]{2,1,0:T(8,128)(2,1)} collective-permute-done((bf16[64,48,128]{2,1,0:T(8,128)(2,1)}, bf16[64,48,128]{2,1,0:T(8,128)(2,1)}, u32[]{:S(2)}, u32[]{:S(2)}) %collective-permute-start.24) | collective-permute-done | bytes 786464 | tf_op jit(solution)/shard_map/ppermute | solution.py:146
  110.9 2.5 %constant_dynamic-update-slice_fusion.88 = (bf16[128,48,128]{2,1,0:T(8,128)(2,1)}, bf16[256,48,128]{2,1,0:T(8,128)(2,1)}) fusion(bf16[128,48,128]{2,1,0:T(8,128)(2,1)} %copy-done.6, bf16[64,48,128]{2,1,0:T(8,128)(2,1)} %collective-permute-done.24, bf16[256,48,128]{2,1,0:T(8,128)(2,1)} %get-tuple-element.39), kind=kLoop, calls=%fused_computation.103 | loop fusion | bytes 2359296 | tf_op jit(solution)/shard_map/concatenate | solution.py:147
  114.2 10.0 %collective-permute-done.16 = bf16[64,48,128]{2,1,0:T(8,128)(2,1)S(1)} collective-permute-done((bf16[64,48,128]{2,1,0:T(8,128)(2,1)}, bf16[64,48,128]{2,1,0:T(8,128)(2,1)S(1)}, u32[]{:S(2)}, u32[]{:S(2)}) %collective-permute-start.16) | collective-permute-done | bytes 786464 | tf_op jit(solution)/shard_map/ppermute | solution.py:146
  130.6 2.7 %constant_dynamic-update-slice_fusion.96.refs_9_.refs_11_ = bf16[256,48,128]{2,1,0:T(8,128)(2,1)} fusion(bf16[256,48,128]{2,1,0:T(8,128)(2,1)} %get-tuple-element.33, bf16[128,48,128]{2,1,0:T(8,128)(2,1)} %collective-permute-done.25), kind=kLoop, calls=%fused_computation.111 | loop fusion | bytes 3145728 | tf_op jit(solution)/shard_map/concatenate | solution.py:147
  133.5 2.6 %constant_dynamic-update-slice_fusion.61.refs_8_.refs_10_ = bf16[256,48,128]{2,1,0:T(8,128)(2,1)} fusion(bf16[256,48,128]{2,1,0:T(8,128)(2,1)} %get-tuple-element.35, bf16[128,48,128]{2,1,0:T(8,128)(2,1)} %collective-permute-done.17), kind=kLoop, calls=%fused_computation.76 | loop fusion | bytes 3145728 | tf_op jit(solution)/shard_map/concatenate | solution.py:147
  136.1 10.3 %shard_map.73 = (f32[256,128]{1,0:T(8,128)S(1)}, f32[256,128]{1,0:T(8,128)S(1)}, f32[256,128]{1,0:T(8,128)S(1)}) custom-call(s32[256]{0:T(256)S(1)} %get-tuple-element.27.refs_0_, s32[256]{0:T(256)S(1)} %get-tuple-element.25.refs_1_, s32[256]{0:T(256)S(1)} %get-tuple-element.24.refs_2_, s32[256]{0:T(256)S(1)} %get-tuple-element.28.refs_3_, ...), custom_call_target="tpu_custom_call" | custom-call | tf_op jit(solution)/shard_map/pallas_call | solution.py:62
  147.3 3.3 %collective-permute-done.26 = f32[64]{0:T(128)S(1)} collective-permute-done((f32[64]{0:T(128)S(1)}, f32[64]{0:T(128)S(1)}, u32[]{:S(2)}, u32[]{:S(2)}) %collective-permute-start.26) | collective-permute-done | bytes 288 | tf_op jit(solution)/shard_map/ppermute | solution.py:26
  152.0 3.6 %collective-permute-done.27 = f32[64]{0:T(128)S(1)} collective-permute-done((f32[64]{0:T(128)S(1)}, f32[64]{0:T(128)S(1)}, u32[]{:S(2)}, u32[]{:S(2)}) %collective-permute-start.27) | collective-permute-done | bytes 288 | tf_op jit(solution)/shard_map/ppermute | solution.py:26
  156.5 4.2 %collective-permute-done.28 = f32[64]{0:T(128)S(1)} collective-permute-done((f32[64]{0:T(128)S(1)}, f32[64]{0:T(128)S(1)}, u32[]{:S(2)}, u32[]{:S(2)}) %collective-permute-start.28) | collective-permute-done | bytes 288 | tf_op jit(solution)/shard_map/ppermute | solution.py:26
  160.8 30.2 %shard_map.74 = bf16[2048,32]{1,0:T(8,128)(2,1)S(1)} custom-call(s32[256]{0:T(256)S(1)} %get-tuple-element.27.refs_0_, s32[256]{0:T(256)S(1)} %get-tuple-element.25.refs_1_, s32[256]{0:T(256)S(1)} %get-tuple-element.24.refs_2_, s32[256]{0:T(256)S(1)} %get-tuple-element.28.refs_3_, s32[256]{0:T(256)S(1)} %get-tuple-element.26.refs_4_, ...), custom_call_target="tpu_custom_call" | custom-call | tf_op jit(solution)/shard_map/pallas_call | solution.py:121
  (112 shorter events, 50.4 us)
Async XLA Ops:
  1.4 14.5 %collective-permute-start.18 = (bf16[1,48,128]{2,1,0:T(8,128)(2,1)S(1)}, bf16[1,48,128]{2,1,0:T(8,128)(2,1)S(1)}, u32[]{:S(2)}, u32[]{:S(2)}) collective-permute-start(bf16[1,48,128]{2,1,0:T(8,128)(2,1)S(1)} %get-tuple-element.99), channel_id=1, source_target_pairs={{0,2},{1,3},{2,0},{3,1},{4,6},{5,7},{6,4},{7,5},{8,10},{9,11},{10,... | collective-permute-start | bytes 36872 | tf_op jit(solution)/shard_map/ppermute | solution.py:146
  4.6 12.0 %collective-permute-start.10 = (bf16[1,48,128]{2,1,0:T(8,128)(2,1)S(1)}, bf16[1,48,128]{2,1,0:T(8,128)(2,1)S(1)}, u32[]{:S(2)}, u32[]{:S(2)}) collective-permute-start(bf16[1,48,128]{2,1,0:T(8,128)(2,1)S(1)} %get-tuple-element.100), channel_id=1, source_target_pairs={{0,128},{8,136},{16,144},{24,152},{32,160},{40,168},{48,176},{56,1... | collective-permute-start | bytes 36872 | tf_op jit(solution)/shard_map/ppermute | solution.py:146
  13.8 5.2 %collective-permute-start = (bf16[1,48,128]{2,1,0:T(8,128)(2,1)S(1)}, bf16[1,48,128]{2,1,0:T(8,128)(2,1)S(1)}, u32[]{:S(2)}, u32[]{:S(2)}) collective-permute-start(bf16[1,48,128]{2,1,0:T(8,128)(2,1)S(1)} %get-tuple-element.136), channel_id=1, source_target_pairs={{0,4},{1,5},{2,6},{3,7},{4,0},{5,1},{6,2},{7,3},{8,12},{9,13},{10,... | collective-permute-start | bytes 36872 | tf_op jit(solution)/shard_map/ppermute | solution.py:146
  16.6 42.3 %collective-permute-start.11 = (bf16[2,48,128]{2,1,0:T(8,128)(2,1)S(1)}, bf16[2,48,128]{2,1,0:T(8,128)(2,1)S(1)}, u32[]{:S(2)}, u32[]{:S(2)}) collective-permute-start(bf16[2,48,128]{2,1,0:T(8,128)(2,1)S(1)} %pad_maximum_fusion.7), channel_id=1, source_target_pairs={{0,64},{8,72},{16,80},{24,88},{32,96},{40,104},{48,112},{56,120},{... | collective-permute-start | bytes 73736 | tf_op jit(solution)/shard_map/ppermute | solution.py:146
  20.8 17.4 %collective-permute-start.20 = (bf16[4,48,128]{2,1,0:T(8,128)(2,1)S(1)}, bf16[4,48,128]{2,1,0:T(8,128)(2,1)S(1)}, u32[]{:S(2)}, u32[]{:S(2)}) collective-permute-start(bf16[4,48,128]{2,1,0:T(8,128)(2,1)S(1)} %pad_maximum_fusion.5), channel_id=1, source_target_pairs={{0,128},{8,136},{16,144},{24,152},{32,160},{40,168},{48,176},{56,1... | collective-permute-start | bytes 147464 | tf_op jit(solution)/shard_map/ppermute | solution.py:146
  22.8 6.0 %collective-permute-start.2 = (bf16[4,48,128]{2,1,0:T(8,128)(2,1)S(1)}, bf16[4,48,128]{2,1,0:T(8,128)(2,1)S(1)}, u32[]{:S(2)}, u32[]{:S(2)}) collective-permute-start(bf16[4,48,128]{2,1,0:T(8,128)(2,1)S(1)} %pad_maximum_fusion.3), channel_id=1, source_target_pairs={{0,2},{1,3},{2,0},{3,1},{4,6},{5,7},{6,4},{7,5},{8,10},{9,11},{10,... | collective-permute-start | bytes 147464 | tf_op jit(solution)/shard_map/ppermute | solution.py:146
  34.3 9.9 %collective-permute-start.4 = (bf16[16,48,128]{2,1,0:T(8,128)(2,1)S(1)}, bf16[16,48,128]{2,1,0:T(8,128)(2,1)S(1)}, u32[]{:S(2)}, u32[]{:S(2)}) collective-permute-start(bf16[16,48,128]{2,1,0:T(8,128)(2,1)S(1)} %get-tuple-element.73), channel_id=1, source_target_pairs={{0,128},{8,136},{16,144},{24,152},{32,160},{40,168},{48,176},{56,1... | collective-permute-start | bytes 589832 | tf_op jit(solution)/shard_map/ppermute | solution.py:146
  38.2 19.4 %collective-permute-start.21 = (bf16[8,48,128]{2,1,0:T(8,128)(2,1)S(1)}, bf16[8,48,128]{2,1,0:T(8,128)(2,1)S(1)}, u32[]{:S(2)}, u32[]{:S(2)}) collective-permute-start(bf16[8,48,128]{2,1,0:T(8,128)(2,1)S(1)} %pad_maximum_fusion.2), channel_id=1, source_target_pairs={{0,64},{8,72},{16,80},{24,88},{32,96},{40,104},{48,112},{56,120},{... | collective-permute-start | bytes 294920 | tf_op jit(solution)/shard_map/ppermute | solution.py:146
  45.2 27.0 %collective-permute-start.5 = (bf16[32,48,128]{2,1,0:T(8,128)(2,1)S(1)}, bf16[32,48,128]{2,1,0:T(8,128)(2,1)S(1)}, u32[]{:S(2)}, u32[]{:S(2)}) collective-permute-start(bf16[32,48,128]{2,1,0:T(8,128)(2,1)S(1)} %get-tuple-element.58), channel_id=1, source_target_pairs={{0,64},{8,72},{16,80},{24,88},{32,96},{40,104},{48,112},{56,120},{... | collective-permute-start | bytes 1179656 | tf_op jit(solution)/shard_map/ppermute | solution.py:146
  58.3 11.7 %collective-permute-start.22 = (bf16[16,48,128]{2,1,0:T(8,128)(2,1)S(1)}, bf16[16,48,128]{2,1,0:T(8,128)(2,1)S(1)}, u32[]{:S(2)}, u32[]{:S(2)}) collective-permute-start(bf16[16,48,128]{2,1,0:T(8,128)(2,1)S(1)} %get-tuple-element.63), channel_id=1, source_target_pairs={{0,32},{8,40},{16,48},{24,56},{32,0},{40,8},{48,16},{56,24},{64,96... | collective-permute-start | bytes 589832 | tf_op jit(solution)/shard_map/ppermute | solution.py:146
  58.9 15.0 %collective-permute-start.12 = (bf16[4,48,128]{2,1,0:T(8,128)(2,1)S(1)}, bf16[4,48,128]{2,1,0:T(8,128)(2,1)S(1)}, u32[]{:S(2)}, u32[]{:S(2)}) collective-permute-start(bf16[4,48,128]{2,1,0:T(8,128)(2,1)S(1)} %pad_maximum_fusion.4), channel_id=1, source_target_pairs={{0,32},{8,40},{16,48},{24,56},{32,0},{40,8},{48,16},{56,24},{64,96... | collective-permute-start | bytes 147464 | tf_op jit(solution)/shard_map/ppermute | solution.py:146
  70.8 15.3 %collective-permute-start.23 = (bf16[32,48,128]{2,1,0:T(8,128)(2,1)S(1)}, bf16[32,48,128]{2,1,0:T(8,128)(2,1)S(1)}, u32[]{:S(2)}, u32[]{:S(2)}) collective-permute-start(bf16[32,48,128]{2,1,0:T(8,128)(2,1)S(1)} %get-tuple-element.50), channel_id=1, source_target_pairs={{0,4},{1,5},{2,6},{3,7},{4,0},{5,1},{6,2},{7,3},{8,12},{9,13},{10,... | collective-permute-start | bytes 1179656 | tf_op jit(solution)/shard_map/ppermute | solution.py:146
  73.3 24.0 %collective-permute-start.6 = (bf16[64,48,128]{2,1,0:T(8,128)(2,1)S(1)}, bf16[64,48,128]{2,1,0:T(8,128)(2,1)S(1)}, u32[]{:S(2)}, u32[]{:S(2)}) collective-permute-start(bf16[64,48,128]{2,1,0:T(8,128)(2,1)S(1)} %get-tuple-element.46), channel_id=1, source_target_pairs={{0,32},{8,40},{16,48},{24,56},{32,0},{40,8},{48,16},{56,24},{64,96... | collective-permute-start | bytes 2359304 | tf_op jit(solution)/shard_map/ppermute | solution.py:146
  73.9 11.5 %collective-permute-start.13 = (bf16[8,48,128]{2,1,0:T(8,128)(2,1)S(1)}, bf16[8,48,128]{2,1,0:T(8,128)(2,1)S(1)}, u32[]{:S(2)}, u32[]{:S(2)}) collective-permute-start(bf16[8,48,128]{2,1,0:T(8,128)(2,1)S(1)} %pad_maximum_fusion.1), channel_id=1, source_target_pairs={{0,4},{1,5},{2,6},{3,7},{4,0},{5,1},{6,2},{7,3},{8,12},{9,13},{10,... | collective-permute-start | bytes 294920 | tf_op jit(solution)/shard_map/ppermute | solution.py:146
  86.2 7.8 %collective-permute-start.14 = (bf16[16,48,128]{2,1,0:T(8,128)(2,1)S(1)}, bf16[16,48,128]{2,1,0:T(8,128)(2,1)S(1)}, u32[]{:S(2)}, u32[]{:S(2)}) collective-permute-start(bf16[16,48,128]{2,1,0:T(8,128)(2,1)S(1)} %get-tuple-element.68), channel_id=1, source_target_pairs={{0,16},{8,24},{16,0},{24,8},{32,48},{40,56},{48,32},{56,40},{64,80... | collective-permute-start | bytes 589832 | tf_op jit(solution)/shard_map/ppermute | solution.py:146
  87.3 23.7 %collective-permute-start.24 = (bf16[64,48,128]{2,1,0:T(8,128)(2,1)}, bf16[64,48,128]{2,1,0:T(8,128)(2,1)}, u32[]{:S(2)}, u32[]{:S(2)}) collective-permute-start(bf16[64,48,128]{2,1,0:T(8,128)(2,1)} %get-tuple-element.40), channel_id=1, source_target_pairs={{0,16},{8,24},{16,0},{24,8},{32,48},{40,56},{48,32},{56,40},{64,80... | collective-permute-start | bytes 2359304 | tf_op jit(solution)/shard_map/ppermute | solution.py:146
  94.9 9.5 %collective-permute-start.15 = (bf16[32,48,128]{2,1,0:T(8,128)(2,1)}, bf16[32,48,128]{2,1,0:T(8,128)(2,1)S(1)}, u32[]{:S(2)}, u32[]{:S(2)}) collective-permute-start(bf16[32,48,128]{2,1,0:T(8,128)(2,1)} %get-tuple-element.54), channel_id=1, source_target_pairs={{0,2},{1,3},{2,0},{3,1},{4,6},{5,7},{6,4},{7,5},{8,10},{9,11},{10,... | collective-permute-start | bytes 1179656 | tf_op jit(solution)/shard_map/ppermute | solution.py:146
  98.6 27.0 %collective-permute-start.7 = (bf16[128,48,128]{2,1,0:T(8,128)(2,1)}, bf16[128,48,128]{2,1,0:T(8,128)(2,1)S(1)}, u32[]{:S(2)}, u32[]{:S(2)}) collective-permute-start(bf16[128,48,128]{2,1,0:T(8,128)(2,1)} %get-tuple-element.36), channel_id=1, source_target_pairs={{0,8},{8,0},{16,24},{24,16},{32,40},{40,32},{48,56},{56,48},{64,72... | collective-permute-start | bytes 4718600 | tf_op jit(solution)/shard_map/ppermute | solution.py:146
  98.9 34.4 %collective-permute-start.8 = (bf16[1,25,2048]{1,2,0:T(8,128)(2,1)S(1)}, bf16[1,25,2048]{1,2,0:T(8,128)(2,1)}, u32[]{:S(2)}, u32[]{:S(2)}) collective-permute-start(bf16[1,25,2048]{1,2,0:T(8,128)(2,1)S(1)} %copy.14), channel_id=1, source_target_pairs={{0,8},{8,16},{16,24},{24,32},{32,40},{40,48},{48,56},{56,64},{64,7... | collective-permute-start | bytes 307208 | tf_op jit(solution)/shard_map/ppermute | solution.py:19
  101.4 28.9 %collective-permute-start.9 = (bf16[1,25,200]{2,1,0:T(8,128)(2,1)S(1)}, bf16[1,25,200]{2,1,0:T(8,128)(2,1)S(1)}, u32[]{:S(2)}, u32[]{:S(2)}) collective-permute-start(bf16[1,25,200]{2,1,0:T(8,128)(2,1)S(1)} %copy-done.2), channel_id=1, source_target_pairs={{0,8},{8,16},{16,24},{24,32},{32,40},{40,48},{48,56},{56,64},{64,7... | collective-permute-start | bytes 30008 | tf_op jit(solution)/shard_map/ppermute | solution.py:19
  105.5 18.6 %collective-permute-start.16 = (bf16[64,48,128]{2,1,0:T(8,128)(2,1)}, bf16[64,48,128]{2,1,0:T(8,128)(2,1)S(1)}, u32[]{:S(2)}, u32[]{:S(2)}) collective-permute-start(bf16[64,48,128]{2,1,0:T(8,128)(2,1)} %get-tuple-element.43), channel_id=1, source_target_pairs={{0,1},{1,0},{2,3},{3,2},{4,5},{5,4},{6,7},{7,6},{8,9},{9,8},{10,11... | collective-permute-start | bytes 2359304 | tf_op jit(solution)/shard_map/ppermute | solution.py:146
  113.4 17.2 %collective-permute-start.25 = (bf16[128,48,128]{2,1,0:T(8,128)(2,1)}, bf16[128,48,128]{2,1,0:T(8,128)(2,1)}, u32[]{:S(2)}, u32[]{:S(2)}) collective-permute-start(bf16[128,48,128]{2,1,0:T(8,128)(2,1)} %get-tuple-element.32), channel_id=1, source_target_pairs={{0,8},{8,0},{16,24},{24,16},{32,40},{40,32},{48,56},{56,48},{64,72... | collective-permute-start | bytes 4718600 | tf_op jit(solution)/shard_map/ppermute | solution.py:146
  125.6 7.9 %collective-permute-start.17 = (bf16[128,48,128]{2,1,0:T(8,128)(2,1)}, bf16[128,48,128]{2,1,0:T(8,128)(2,1)}, u32[]{:S(2)}, u32[]{:S(2)}) collective-permute-start(bf16[128,48,128]{2,1,0:T(8,128)(2,1)} %get-tuple-element.34), channel_id=1, source_target_pairs={{0,8},{8,0},{16,24},{24,16},{32,40},{40,32},{48,56},{56,48},{64,72... | collective-permute-start | bytes 4718600 | tf_op jit(solution)/shard_map/ppermute | solution.py:146
  155.6 5.1 %collective-permute-start.28 = (f32[64]{0:T(128)S(1)}, f32[64]{0:T(128)S(1)}, u32[]{:S(2)}, u32[]{:S(2)}) collective-permute-start(f32[64]{0:T(128)S(1)} %add.272), channel_id=1, source_target_pairs={{0,4},{1,5},{2,6},{3,7},{4,0},{5,1},{6,2},{7,3},{8,12},{9,13},{10,... | collective-permute-start | bytes 776 | tf_op jit(solution)/shard_map/ppermute | solution.py:26
  (12 other events, 241.6 us)

commit v6 on v5

--- a/solution.py
+++ b/solution.py
@@ -133,11 +133,7 @@
     )(*rbs, *cbs, *ss, x0, *parts)
 
 
-STREAMS = (
-    ((("walker", 16), ("walker", 8), ("walker", 4), ("vec", 4), ("walker", 2), ("vec", 2), ("vec", 1), ("walker", 1)), 0, 48),
-    ((("vec", 2), ("vec", 1), ("walker", 16), ("walker", 8), ("walker", 4), ("vec", 4), ("walker", 2), ("walker", 1)), 48, 96),
-    ((("vec", 4), ("walker", 2), ("vec", 2), ("vec", 1), ("walker", 16), ("walker", 8), ("walker", 4), ("walker", 1)), 96, 128),
-)
+STREAMS = ((None, 0, 128),)
 
 
 def xor_gather(x, order):
@@ -172,28 +168,23 @@
 ):
     cols_local = panels.shape[1]
     walker_id = lax.axis_index("walker")
-    vec_id = lax.axis_index("vec")
     vecs = lax.axis_size("vec")
     prev_panel = shift_from(panels, "walker", 1)
     prev_inverse = shift_from(inverse_intersection, "walker", 1)
     size = chol_tiles.shape[2]
     meta = jnp.zeros((1, 16, size), chol_tiles.dtype).at[0, 0, 0].set(copy_counts[0].astype(chol_tiles.dtype))
-    parts, rbs, cbs, sources = [], [], [], []
-    for index, (order, low, high) in enumerate(STREAMS):
-        piece = chol_tiles[:, low:high]
-        if index == len(STREAMS) - 1:
-            piece = jnp.concatenate([piece, meta], axis=1)
-        parts.append(xor_gather(piece, order))
-        source = source_tiles(order)
-        sources.append(source)
-        rbs.append(pick(tile_blocks[:, 0], source))
-        cbs.append(pick(tile_blocks[:, 1], source))
-    last = STREAMS[-1]
-    counts = parts[-1][:, last[2] - last[1], 0].astype(jnp.float32)
-    source = sources[-1]
-    before = (source % vecs == vec_id) & (source // vecs < walker_id)
-    surplus = jnp.sum(jnp.where(before, counts, 0.0)) - walker_id.astype(jnp.float32)
+    payload = jnp.concatenate([chol_tiles, meta], axis=1)
+    gathered = lax.all_gather(
+        lax.all_gather(payload, "vec", axis=0, tiled=True), "walker", axis=0, tiled=True
+    )
+    tiles_rows = chol_tiles.shape[1]
+    counts = gathered[::vecs, tiles_rows, 0].astype(jnp.float32)
+    walkers = jnp.arange(counts.shape[0])
+    surplus = jnp.sum(jnp.where(walkers < walker_id, counts, 0.0)) - walker_id.astype(jnp.float32)
     from_prev = surplus > 0.5
+    rbs = [tile_blocks[:, 0]]
+    cbs = [tile_blocks[:, 1]]
+    parts = [gathered]
 
     green_own = jnp.dot(inverse_intersection[0], trial_orbitals, preferred_element_type=jnp.float32).astype(jnp.bfloat16)
     green_prev = jnp.dot(prev_inverse[0], trial_orbitals, preferred_element_type=jnp.float32).astype(jnp.bfloat16)
@@ -201,14 +192,11 @@
     green = jnp.where(from_prev, green_prev, green_own)
     partials = tile_bias(pad_rows(start).T, pad_rows(green), parts, rbs, cbs)
     vectors = tile_blocks.shape[0] // KT
-    ids = jnp.concatenate([source // KT for source in sources])
-    values = jnp.concatenate([partial.sum(axis=1) for partial in partials])
-    hot = ids[:, None] == jnp.arange(vectors, dtype=ids.dtype)[None, :]
-    per_vector = jnp.sum(jnp.where(hot, values[:, None], 0.0), axis=0)
+    per_vector = partials[0].reshape(vectors, KT * size).sum(axis=1)
     raw = butterfly_sum(per_vector, "vec")
     bias = jnp.clip(TIME_STEP_ROOT * raw, -1.0, 1.0)
     scales = TIME_STEP_ROOT * (aux_fields[0] - bias)
-    ss = [pick(scales, source // KT) for source in sources]
+    ss = [jnp.repeat(scales, KT)]
     out = propagate(pad_rows(start).T, parts, rbs, cbs, ss)
     return out.T[:cols_local][None]
 

time: 193 us -> 182 us (0.943)
  blocking collectives: 0 us -> 36.5 us
  starting transfers between devices: 46.9 us -> 13.1 us
  local copies, waits for them, and re-layouts: 29.5 us -> 3.32 us
  between operations: 1.56 us -> 14.9 us
  waiting for transfers between devices: 68.4 us -> 72.9 us
  Pallas kernels: 40.5 us -> 37.1 us
    all_gather x0 -> x1, waiting for transfers between devices: none -> 65.8 us  [shards(): lax.all_gather(lax.all_gather(payload, 'vec', axis=0, tiled=True), 'walke...]
    ppermute x24 -> x0, waiting for transfers between devices: 57.3 us -> none  [xor_gather(): other = lax.ppermute(x, axis, [(i, i ^ step) for i in range(count)])]
    ppermute x24 -> x0, starting transfers between devices: 39.9 us -> none  [xor_gather(): other = lax.ppermute(x, axis, [(i, i ^ step) for i in range(count)])]
    all_gather x0 -> x1, blocking collectives: none -> 36.5 us  [shards(): lax.all_gather(payload, 'vec', axis=0, tiled=True)]
    unnamed x34 -> x5, local copies, waits for them, and re-layouts: 15.9 us -> 1.21 us
    concatenate x6 -> x0, local copies, waits for them, and re-layouts: 11.9 us -> none  [xor_gather(): x = jnp.concatenate([x, other], axis=0)]
    ppermute x3, starting transfers between devices: 2.67 us -> 6.79 us  [butterfly_sum(): lax.ppermute(value, axis, [(i, i ^ step) for i in range(count)])]
    ppermute x3, waiting for transfers between devices: 11.1 us -> 7.01 us  [butterfly_sum(): lax.ppermute(value, axis, [(i, i ^ step) for i in range(count)])]
  transfers between devices with their start and end apart: 29 -> 6, of which waited for: 15 -> 4; matrix products, arithmetic and copies ran while one was open for 15% -> 3% of each run, Pallas kernels for 0% -> 0%
where the time goes in v6:
time: 182 us
  waiting for transfers between devices  72.9 us (40%)
  Pallas kernels  37.1 us (20%)
  blocking collectives  36.5 us (20%)
  between operations  14.9 us (8%)
  starting transfers between devices  13.1 us (7%)
  local copies, waits for them, and re-layouts  3.32 us (2%)
  other arithmetic  2.82 us (2%)
    all_gather x1, waiting for transfers between devices, shards(): lax.all_gather(lax.all_gather(payload, 'vec', axis=0, tiled=True), 'walke...  65.8 us
    all_gather x1, blocking collectives, shards(): lax.all_gather(payload, 'vec', axis=0, tiled=True)  36.5 us
    pallas_call x1, Pallas kernels, propagate(): pl.pallas_call(prop_kernel, out_shape=jax.ShapeDtypeStruct((orbitals, row...  27.1 us
    pallas_call x1, Pallas kernels, tile_bias(): pl.pallas_call(bias_kernel, out_shape=[jax.ShapeDtypeStruct((tiles_total,...  10 us
    ppermute x3, waiting for transfers between devices, butterfly_sum(): lax.ppermute(value, axis, [(i, i ^ step) for i in range(count)])  7.01 us
    ppermute x3, starting transfers between devices, butterfly_sum(): lax.ppermute(value, axis, [(i, i ^ step) for i in range(count)])  6.79 us
    ppermute x2, starting transfers between devices, shift_from(): lax.ppermute(value, axis, [(i, i + steps) for i in range(count - steps)])  6.32 us
  transfers between devices with their start and end apart: 6, of which 4 were waited for; matrix products, arithmetic and copies ran while one was open for 3% of the time, Pallas kernels for 0%

profile of v6, /device:TPU:2, one launch (start us, length us, event | category | flops | bytes accessed | tf_op | source)
XLA Modules:
  0.0 181.9 jit_solution(14216335679961022711)
XLA Ops:
  7.3 0.8 fusion.2
  8.0 36.5 %all_gather.6 = bf16[8,144,128]{2,1,0:T(8,128)(2,1)} all-gather(bf16[1,144,128]{2,1,0:T(8,128)(2,1)S(1)} %fusion.2), channel_id=1, replica_groups=mesh['walker'=32,'vec'=8] {'vec'}, dimensions={0}, use_global_device_ids=true | all-gather | bytes 331776 | tf_op jit(solution)/shard_map/all_gather | solution.py:178
  44.6 1.2 copy.14
  45.8 1.9 %collective-permute-start = (bf16[1,25,2048]{1,2,0:T(8,128)(2,1)S(1)}, bf16[1,25,2048]{1,2,0:T(8,128)(2,1)S(1)}, u32[]{:S(2)}, u32[]{:S(2)}) collective-permute-start(bf16[1,25,2048]{1,2,0:T(8,128)(2,1)S(1)} %copy.14), channel_id=1, source_target_pairs={{0,8},{8,16},{16,24},{24,32},{32,40},{40,48},{48,56},{56,64},{64,7... | collective-permute-start | bytes 307208 | tf_op jit(solution)/shard_map/ppermute | solution.py:19
  47.7 4.4 %collective-permute-start.1 = (bf16[1,25,200]{2,1,0:T(8,128)(2,1)}, bf16[1,25,200]{2,1,0:T(8,128)(2,1)S(1)}, u32[]{:S(2)}, u32[]{:S(2)}) collective-permute-start(bf16[1,25,200]{2,1,0:T(8,128)(2,1)} %param.11), channel_id=1, source_target_pairs={{0,8},{8,16},{16,24},{24,32},{32,40},{40,48},{48,56},{56,64},{64,7... | collective-permute-start | bytes 30008 | tf_op jit(solution)/shard_map/ppermute | solution.py:19
  52.1 0.8 fusion.7
  52.9 1.0 convolution_convert_fusion
  53.9 65.8 %all-gather.2.cloned.1.call-done.refs_4_ = bf16[256,144,128]{2,1,0:T(8,128)(2,1)} async-done(((bf16[8,144,128]{2,1,0:T(8,128)(2,1)}), bf16[256,144,128]{2,1,0:T(8,128)(2,1)}) %all-gather.2.cloned.1.call-update) | async-done | bytes 9437200 | tf_op jit(solution)/shard_map/all_gather | solution.py:177
  119.7 1.2 convert_reduce_fusion
  120.9 0.6 fusion.5
  122.2 0.1 pad_bitcast_fusion.refs_2_.refs_3_
  122.3 0.3 fusion
  122.6 10.0 %shard_map.73 = f32[256,128]{1,0:T(8,128)S(1)} custom-call(s32[256]{0:T(256)S(1)} %bitcast.25, s32[256]{0:T(256)S(1)} %bitcast.23, bf16[2048,32]{1,0:T(8,128)(2,1)S(1)} %pad_bitcast_fusion.refs_2_.refs_3_, bf16[32,2048]{1,0:T(8,128)(2,1)S(1)} %pad.14.refs_3_, bf16[256,144,128]{2,1,0:T(8,128)(2,1)} %all-gather.2.cloned.1.call-done.refs_4_), custom_call_target="tpu_custom_call" | custom-call | tf_op jit(solution)/shard_map/pallas_call | solution.py:62
  132.7 0.1 reduce_sum.26
  132.9 0.1 reduce_sum.28
  133.0 1.6 collective-permute-start.2
  134.6 2.0 %collective-permute-done.2 = f32[64]{0:T(128)S(1)} collective-permute-done((f32[64]{0:T(128)S(1)}, f32[64]{0:T(128)S(1)}, u32[]{:S(2)}, u32[]{:S(2)}) %collective-permute-start.2) | collective-permute-done | bytes 288 | tf_op jit(solution)/shard_map/ppermute | solution.py:26
  136.7 3.0 %collective-permute-start.3 = (f32[64]{0:T(128)S(1)}, f32[64]{0:T(128)S(1)}, u32[]{:S(2)}, u32[]{:S(2)}) collective-permute-start(f32[64]{0:T(128)S(1)} %add.17), channel_id=1, source_target_pairs={{0,2},{1,3},{2,0},{3,1},{4,6},{5,7},{6,4},{7,5},{8,10},{9,11},{10,... | collective-permute-start | bytes 776 | tf_op jit(solution)/shard_map/ppermute | solution.py:26
  139.7 2.0 %collective-permute-done.3 = f32[64]{0:T(128)S(1)} collective-permute-done((f32[64]{0:T(128)S(1)}, f32[64]{0:T(128)S(1)}, u32[]{:S(2)}, u32[]{:S(2)}) %collective-permute-start.3) | collective-permute-done | bytes 288 | tf_op jit(solution)/shard_map/ppermute | solution.py:26
  141.8 2.1 %collective-permute-start.4 = (f32[64]{0:T(128)S(1)}, f32[64]{0:T(128)S(1)}, u32[]{:S(2)}, u32[]{:S(2)}) collective-permute-start(f32[64]{0:T(128)S(1)} %add.18), channel_id=1, source_target_pairs={{0,4},{1,5},{2,6},{3,7},{4,0},{5,1},{6,2},{7,3},{8,12},{9,13},{10,... | collective-permute-start | bytes 776 | tf_op jit(solution)/shard_map/ppermute | solution.py:26
  143.9 2.9 %collective-permute-done.4 = f32[64]{0:T(128)S(1)} collective-permute-done((f32[64]{0:T(128)S(1)}, f32[64]{0:T(128)S(1)}, u32[]{:S(2)}, u32[]{:S(2)}) %collective-permute-start.4) | collective-permute-done | bytes 288 | tf_op jit(solution)/shard_map/ppermute | solution.py:26
  146.9 0.1 reshape.48.refs_2_
  147.0 27.1 %shard_map.74 = bf16[2048,32]{1,0:T(8,128)(2,1)S(1)} custom-call(s32[256]{0:T(256)S(1)} %bitcast.26, s32[256]{0:T(256)S(1)} %bitcast.24, f32[256]{0:T(256)S(1)} %reshape.48.refs_2_, bf16[2048,32]{1,0:T(8,128)(2,1)S(1)} %pad_bitcast_fusion.refs_2_.refs_3_, bf16[256,144,128]{2,1,0:T(8,128)(2,1)} %all-gather.2.cloned.1.call-done.refs_4_), custom_call_target="tpu_custom_call" | custom-call | tf_op jit(solution)/shard_map/pallas_call | solution.py:121
  174.1 0.9 copy.16
  (16 shorter events, 0.3 us)
Async XLA Ops:
  6.5 46.4 %copy-start = (bf16[200,2048]{1,0:T(8,128)(2,1)S(1)}, bf16[200,2048]{1,0:T(8,128)(2,1)}, u32[]{:S(2)}) copy-start(bf16[200,2048]{1,0:T(8,128)(2,1)} %param.12) | copy-start | bytes 2457604
  6.5 140.3 %copy-start.1 = (f32[1,64]{1,0:T(1,128)S(1)}, f32[1,64]{1,0:T(1,128)}, u32[]{:S(2)}) copy-start(f32[1,64]{1,0:T(1,128)} %param.15) | copy-start | bytes 772
  6.5 113.2 %all-gather.2.cloned.1.call-start = ((), (), s32[]{:S(2)}) async-start(), calls=%async_computation | async-start | bytes 9732096 | tf_op jit(solution)/shard_map/all_gather | solution.py:177
  45.8 76.3 %collective-permute-start = (bf16[1,25,2048]{1,2,0:T(8,128)(2,1)S(1)}, bf16[1,25,2048]{1,2,0:T(8,128)(2,1)S(1)}, u32[]{:S(2)}, u32[]{:S(2)}) collective-permute-start(bf16[1,25,2048]{1,2,0:T(8,128)(2,1)S(1)} %copy.14), channel_id=1, source_target_pairs={{0,8},{8,16},{16,24},{24,32},{32,40},{40,48},{48,56},{56,64},{64,7... | collective-permute-start | bytes 307208 | tf_op jit(solution)/shard_map/ppermute | solution.py:19
  47.7 74.6 %collective-permute-start.1 = (bf16[1,25,200]{2,1,0:T(8,128)(2,1)}, bf16[1,25,200]{2,1,0:T(8,128)(2,1)S(1)}, u32[]{:S(2)}, u32[]{:S(2)}) collective-permute-start(bf16[1,25,200]{2,1,0:T(8,128)(2,1)} %param.11), channel_id=1, source_target_pairs={{0,8},{8,16},{16,24},{24,32},{32,40},{40,48},{48,56},{56,64},{64,7... | collective-permute-start | bytes 30008 | tf_op jit(solution)/shard_map/ppermute | solution.py:19
  133.0 3.7 %collective-permute-start.2 = (f32[64]{0:T(128)S(1)}, f32[64]{0:T(128)S(1)}, u32[]{:S(2)}, u32[]{:S(2)}) collective-permute-start(f32[64]{0:T(128)S(1)} %reduce_sum.28), channel_id=1, source_target_pairs={{0,1},{1,0},{2,3},{3,2},{4,5},{5,4},{6,7},{7,6},{8,9},{9,8},{10,11... | collective-permute-start | bytes 776 | tf_op jit(solution)/shard_map/ppermute | solution.py:26
  136.7 5.1 %collective-permute-start.3 = (f32[64]{0:T(128)S(1)}, f32[64]{0:T(128)S(1)}, u32[]{:S(2)}, u32[]{:S(2)}) collective-permute-start(f32[64]{0:T(128)S(1)} %add.17), channel_id=1, source_target_pairs={{0,2},{1,3},{2,0},{3,1},{4,6},{5,7},{6,4},{7,5},{8,10},{9,11},{10,... | collective-permute-start | bytes 776 | tf_op jit(solution)/shard_map/ppermute | solution.py:26
  141.8 5.1 %collective-permute-start.4 = (f32[64]{0:T(128)S(1)}, f32[64]{0:T(128)S(1)}, u32[]{:S(2)}, u32[]{:S(2)}) collective-permute-start(f32[64]{0:T(128)S(1)} %add.18), channel_id=1, source_target_pairs={{0,4},{1,5},{2,6},{3,7},{4,0},{5,1},{6,2},{7,3},{8,12},{9,13},{10,... | collective-permute-start | bytes 776 | tf_op jit(solution)/shard_map/ppermute | solution.py:26
Sparse Core Ops, SparseCore 0:
  44.7 74.9 all-gather.1

commit v7 on v6

--- a/solution.py
+++ b/solution.py
@@ -174,16 +174,17 @@
     size = chol_tiles.shape[2]
     meta = jnp.zeros((1, 16, size), chol_tiles.dtype).at[0, 0, 0].set(copy_counts[0].astype(chol_tiles.dtype))
     payload = jnp.concatenate([chol_tiles, meta], axis=1)
-    gathered = lax.all_gather(
-        lax.all_gather(payload, "vec", axis=0, tiled=True), "walker", axis=0, tiled=True
-    )
+    order = (("vec", 4), ("vec", 2), ("vec", 1))
+    gathered = lax.all_gather(xor_gather(payload, order), "walker", axis=0, tiled=True)
     tiles_rows = chol_tiles.shape[1]
     counts = gathered[::vecs, tiles_rows, 0].astype(jnp.float32)
     walkers = jnp.arange(counts.shape[0])
     surplus = jnp.sum(jnp.where(walkers < walker_id, counts, 0.0)) - walker_id.astype(jnp.float32)
     from_prev = surplus > 0.5
-    rbs = [tile_blocks[:, 0]]
-    cbs = [tile_blocks[:, 1]]
+    local = source_tiles(order) % vecs
+    source = (walkers[:, None] * vecs + local[None, :]).reshape(-1)
+    rbs = [pick(tile_blocks[:, 0], source)]
+    cbs = [pick(tile_blocks[:, 1], source)]
     parts = [gathered]
 
     green_own = jnp.dot(inverse_intersection[0], trial_orbitals, preferred_element_type=jnp.float32).astype(jnp.bfloat16)
@@ -192,11 +193,13 @@
     green = jnp.where(from_prev, green_prev, green_own)
     partials = tile_bias(pad_rows(start).T, pad_rows(green), parts, rbs, cbs)
     vectors = tile_blocks.shape[0] // KT
-    per_vector = partials[0].reshape(vectors, KT * size).sum(axis=1)
+    values = partials[0].sum(axis=1)
+    hot = (source // KT)[:, None] == jnp.arange(vectors, dtype=source.dtype)[None, :]
+    per_vector = jnp.sum(jnp.where(hot, values[:, None], 0.0), axis=0)
     raw = butterfly_sum(per_vector, "vec")
     bias = jnp.clip(TIME_STEP_ROOT * raw, -1.0, 1.0)
     scales = TIME_STEP_ROOT * (aux_fields[0] - bias)
-    ss = [jnp.repeat(scales, KT)]
+    ss = [pick(scales, source // KT)]
     out = propagate(pad_rows(start).T, parts, rbs, cbs, ss)
     return out.T[:cols_local][None]
 

time: 182 us -> 166 us (0.912)
  blocking collectives: 36.5 us -> 0 us
  waiting for transfers between devices: 72.9 us -> 82.8 us
  starting transfers between devices: 13.1 us -> 19.6 us
  other arithmetic: 2.82 us -> 6.27 us
    all_gather x1 -> x0, blocking collectives: 36.5 us -> none  [shards(): lax.all_gather(payload, 'vec', axis=0, tiled=True)]
    ppermute x0 -> x3, waiting for transfers between devices: none -> 9.57 us  [xor_gather(): other = lax.ppermute(x, axis, [(i, i ^ step) for i in range(count)])]
    ppermute x0 -> x3, starting transfers between devices: none -> 6.98 us  [xor_gather(): other = lax.ppermute(x, axis, [(i, i ^ step) for i in range(count)])]
    concatenate x0 -> x3, other arithmetic: none -> 3.03 us  [xor_gather(): x = jnp.concatenate([x, other], axis=0)]
  transfers between devices with their start and end apart: 6 -> 9, of which waited for: 4 -> 7; matrix products, arithmetic and copies ran while one was open for 3% -> 3% of each run, Pallas kernels for 0% -> 0%
where the time goes in v7:
time: 166 us; the launch traced here: 165 us
  waiting for transfers between devices  82.8 us (50%)
  Pallas kernels  37.1 us (22%)
  starting transfers between devices  19.6 us (12%)
  between operations  14.9 us (9%)
  other arithmetic  6.27 us (4%)
  local copies, waits for them, and re-layouts  3.12 us (2%)
    all_gather x1, waiting for transfers between devices, shards(): lax.all_gather(xor_gather(payload, order), 'walker', axis=0, tiled=True)  66.1 us
    pallas_call x1, Pallas kernels, propagate(): pl.pallas_call(prop_kernel, out_shape=jax.ShapeDtypeStruct((orbitals, row...  27.1 us
    pallas_call x1, Pallas kernels, tile_bias(): pl.pallas_call(bias_kernel, out_shape=[jax.ShapeDtypeStruct((tiles_total,...  10 us
    ppermute x3, waiting for transfers between devices, xor_gather(): other = lax.ppermute(x, axis, [(i, i ^ step) for i in range(count)])  9.57 us
    ppermute x3, waiting for transfers between devices, butterfly_sum(): lax.ppermute(value, axis, [(i, i ^ step) for i in range(count)])  7.05 us
    ppermute x3, starting transfers between devices, xor_gather(): other = lax.ppermute(x, axis, [(i, i ^ step) for i in range(count)])  6.98 us
    ppermute x3, starting transfers between devices, butterfly_sum(): lax.ppermute(value, axis, [(i, i ^ step) for i in range(count)])  6.75 us
    ppermute x2, starting transfers between devices, shift_from(): lax.ppermute(value, axis, [(i, i + steps) for i in range(count - steps)])  5.82 us
  transfers between devices with their start and end apart: 9, of which 7 were waited for; matrix products, arithmetic and copies ran while one was open for 3% of the time, Pallas kernels for 0%

profile of v7, /device:TPU:2, one launch (start us, length us, event | category | flops | bytes accessed | tf_op | source)
XLA Modules:
  0.0 165.0 jit_solution(8438862372075086160)
XLA Ops:
  8.1 2.1 %collective-permute-start = (bf16[1,144,128]{2,1,0:T(8,128)(2,1)S(1)}, bf16[1,144,128]{2,1,0:T(8,128)(2,1)S(1)}, u32[]{:S(2)}, u32[]{:S(2)}) collective-permute-start(bf16[1,144,128]{2,1,0:T(8,128)(2,1)S(1)} %pad_maximum_fusion.3), channel_id=1, source_target_pairs={{0,4},{1,5},{2,6},{3,7},{4,0},{5,1},{6,2},{7,3},{8,12},{9,13},{10,... | collective-permute-start | bytes 110600 | tf_op jit(solution)/shard_map/ppermute | solution.py:142
  10.2 3.3 %collective-permute-done = bf16[1,144,128]{2,1,0:T(8,128)(2,1)S(1)} collective-permute-done((bf16[1,144,128]{2,1,0:T(8,128)(2,1)S(1)}, bf16[1,144,128]{2,1,0:T(8,128)(2,1)S(1)}, u32[]{:S(2)}, u32[]{:S(2)}) %collective-permute-start) | collective-permute-done | bytes 36896 | tf_op jit(solution)/shard_map/ppermute | solution.py:142
  14.3 3.2 %collective-permute-start.1 = (bf16[2,144,128]{2,1,0:T(8,128)(2,1)S(1)}, bf16[2,144,128]{2,1,0:T(8,128)(2,1)S(1)}, u32[]{:S(2)}, u32[]{:S(2)}) collective-permute-start(bf16[2,144,128]{2,1,0:T(8,128)(2,1)S(1)} %pad_maximum_fusion.2), channel_id=1, source_target_pairs={{0,2},{1,3},{2,0},{3,1},{4,6},{5,7},{6,4},{7,5},{8,10},{9,11},{10,... | collective-permute-start | bytes 221192 | tf_op jit(solution)/shard_map/ppermute | solution.py:142
  17.5 2.7 %collective-permute-done.1 = bf16[2,144,128]{2,1,0:T(8,128)(2,1)S(1)} collective-permute-done((bf16[2,144,128]{2,1,0:T(8,128)(2,1)S(1)}, bf16[2,144,128]{2,1,0:T(8,128)(2,1)S(1)}, u32[]{:S(2)}, u32[]{:S(2)}) %collective-permute-start.1) | collective-permute-done | bytes 73760 | tf_op jit(solution)/shard_map/ppermute | solution.py:142
  20.1 0.8 pad_maximum_fusion.1
  20.9 1.7 %collective-permute-start.2 = (bf16[4,144,128]{2,1,0:T(8,128)(2,1)S(1)}, bf16[4,144,128]{2,1,0:T(8,128)(2,1)S(1)}, u32[]{:S(2)}, u32[]{:S(2)}) collective-permute-start(bf16[4,144,128]{2,1,0:T(8,128)(2,1)S(1)} %pad_maximum_fusion.1), channel_id=1, source_target_pairs={{0,1},{1,0},{2,3},{3,2},{4,5},{5,4},{6,7},{7,6},{8,9},{9,8},{10,11... | collective-permute-start | bytes 442376 | tf_op jit(solution)/shard_map/ppermute | solution.py:142
  22.6 3.6 %collective-permute-done.2 = bf16[4,144,128]{2,1,0:T(8,128)(2,1)S(1)} collective-permute-done((bf16[4,144,128]{2,1,0:T(8,128)(2,1)S(1)}, bf16[4,144,128]{2,1,0:T(8,128)(2,1)S(1)}, u32[]{:S(2)}, u32[]{:S(2)}) %collective-permute-start.2) | collective-permute-done | bytes 147488 | tf_op jit(solution)/shard_map/ppermute | solution.py:142
  26.1 1.5 pad_maximum_fusion
  27.7 1.2 copy.17
  28.9 1.9 %collective-permute-start.3 = (bf16[1,25,2048]{1,2,0:T(8,128)(2,1)S(1)}, bf16[1,25,2048]{1,2,0:T(8,128)(2,1)S(1)}, u32[]{:S(2)}, u32[]{:S(2)}) collective-permute-start(bf16[1,25,2048]{1,2,0:T(8,128)(2,1)S(1)} %copy.17), channel_id=1, source_target_pairs={{0,8},{8,16},{16,24},{24,32},{32,40},{40,48},{48,56},{56,64},{64,7... | collective-permute-start | bytes 307208 | tf_op jit(solution)/shard_map/ppermute | solution.py:19
  30.8 3.9 %collective-permute-start.4 = (bf16[1,25,200]{2,1,0:T(8,128)(2,1)}, bf16[1,25,200]{2,1,0:T(8,128)(2,1)S(1)}, u32[]{:S(2)}, u32[]{:S(2)}) collective-permute-start(bf16[1,25,200]{2,1,0:T(8,128)(2,1)} %param.11), channel_id=1, source_target_pairs={{0,8},{8,16},{16,24},{24,32},{32,40},{40,48},{48,56},{56,64},{64,7... | collective-permute-start | bytes 30008 | tf_op jit(solution)/shard_map/ppermute | solution.py:19
  34.9 0.8 fusion.15
  35.9 1.0 convolution_convert_fusion
  36.9 66.1 %all-gather.2.cloned.1.call-done.refs_4_ = bf16[256,144,128]{2,1,0:T(8,128)(2,1)} async-done(((bf16[8,144,128]{2,1,0:T(8,128)(2,1)}), bf16[256,144,128]{2,1,0:T(8,128)(2,1)}) %all-gather.2.cloned.1.call-update) | async-done | bytes 9437200 | tf_op jit(solution)/shard_map/all_gather | solution.py:178
  103.0 1.2 convert_reduce_fusion
  106.0 10.0 %shard_map.73 = f32[256,128]{1,0:T(8,128)S(1)} custom-call(s32[256]{0:T(256)S(1)} %get-tuple-element.18.refs_0_, s32[256]{0:T(256)S(1)} %get-tuple-element.17.refs_1_, bf16[2048,32]{1,0:T(8,128)(2,1)S(1)} %pad_bitcast_fusion.refs_2_.refs_3_, bf16[32,2048]{1,0:T(8,128)(2,1)S(1)} %pad.14.refs_3_, bf16[256,144,128]{2,1,0:T(8,128)(2,1)} %all-gather.2.cloned.1.call-done.refs_4_), custom_call_target="tpu_custom_call" | custom-call | tf_op jit(solution)/shard_map/pallas_call | solution.py:62
  116.2 1.6 collective-permute-start.5
  117.8 2.1 %collective-permute-done.5 = f32[64]{0:T(128)S(1)} collective-permute-done((f32[64]{0:T(128)S(1)}, f32[64]{0:T(128)S(1)}, u32[]{:S(2)}, u32[]{:S(2)}) %collective-permute-start.5) | collective-permute-done | bytes 288 | tf_op jit(solution)/shard_map/ppermute | solution.py:26
  119.9 3.0 %collective-permute-start.6 = (f32[64]{0:T(128)S(1)}, f32[64]{0:T(128)S(1)}, u32[]{:S(2)}, u32[]{:S(2)}) collective-permute-start(f32[64]{0:T(128)S(1)} %add.85), channel_id=1, source_target_pairs={{0,2},{1,3},{2,0},{3,1},{4,6},{5,7},{6,4},{7,5},{8,10},{9,11},{10,... | collective-permute-start | bytes 776 | tf_op jit(solution)/shard_map/ppermute | solution.py:26
  122.9 2.0 %collective-permute-done.6 = f32[64]{0:T(128)S(1)} collective-permute-done((f32[64]{0:T(128)S(1)}, f32[64]{0:T(128)S(1)}, u32[]{:S(2)}, u32[]{:S(2)}) %collective-permute-start.6) | collective-permute-done | bytes 288 | tf_op jit(solution)/shard_map/ppermute | solution.py:26
  125.0 2.1 %collective-permute-start.7 = (f32[64]{0:T(128)S(1)}, f32[64]{0:T(128)S(1)}, u32[]{:S(2)}, u32[]{:S(2)}) collective-permute-start(f32[64]{0:T(128)S(1)} %add.86), channel_id=1, source_target_pairs={{0,4},{1,5},{2,6},{3,7},{4,0},{5,1},{6,2},{7,3},{8,12},{9,13},{10,... | collective-permute-start | bytes 776 | tf_op jit(solution)/shard_map/ppermute | solution.py:26
  127.1 3.0 %collective-permute-done.7 = f32[64]{0:T(128)S(1)} collective-permute-done((f32[64]{0:T(128)S(1)}, f32[64]{0:T(128)S(1)}, u32[]{:S(2)}, u32[]{:S(2)}) %collective-permute-start.7) | collective-permute-done | bytes 288 | tf_op jit(solution)/shard_map/ppermute | solution.py:26
  130.2 27.1 %shard_map.74 = bf16[2048,32]{1,0:T(8,128)(2,1)S(1)} custom-call(s32[256]{0:T(256)S(1)} %get-tuple-element.18.refs_0_, s32[256]{0:T(256)S(1)} %get-tuple-element.17.refs_1_, f32[256]{0:T(256)S(1)} %select_reduce_fusion.2.refs_2_, bf16[2048,32]{1,0:T(8,128)(2,1)S(1)} %pad_bitcast_fusion.refs_2_.refs_3_, ...), custom_call_target="tpu_custom_call" | custom-call | tf_op jit(solution)/shard_map/pallas_call | solution.py:121
  157.3 0.9 copy.19
  (29 shorter events, 3.4 us)
Async XLA Ops:
  6.5 29.4 %copy-start = (bf16[200,2048]{1,0:T(8,128)(2,1)S(1)}, bf16[200,2048]{1,0:T(8,128)(2,1)}, u32[]{:S(2)}) copy-start(bf16[200,2048]{1,0:T(8,128)(2,1)} %param.12) | copy-start | bytes 2457604
  6.5 123.5 %copy-start.1 = (f32[1,64]{1,0:T(1,128)S(1)}, f32[1,64]{1,0:T(1,128)}, u32[]{:S(2)}) copy-start(f32[1,64]{1,0:T(1,128)} %param.15) | copy-start | bytes 772
  6.5 96.5 %all-gather.2.cloned.1.call-start = ((), (), s32[]{:S(2)}) async-start(), calls=%async_computation | async-start | bytes 9732096 | tf_op jit(solution)/shard_map/all_gather | solution.py:178
  8.1 5.5 %collective-permute-start = (bf16[1,144,128]{2,1,0:T(8,128)(2,1)S(1)}, bf16[1,144,128]{2,1,0:T(8,128)(2,1)S(1)}, u32[]{:S(2)}, u32[]{:S(2)}) collective-permute-start(bf16[1,144,128]{2,1,0:T(8,128)(2,1)S(1)} %pad_maximum_fusion.3), channel_id=1, source_target_pairs={{0,4},{1,5},{2,6},{3,7},{4,0},{5,1},{6,2},{7,3},{8,12},{9,13},{10,... | collective-permute-start | bytes 110600 | tf_op jit(solution)/shard_map/ppermute | solution.py:142
  14.3 5.9 %collective-permute-start.1 = (bf16[2,144,128]{2,1,0:T(8,128)(2,1)S(1)}, bf16[2,144,128]{2,1,0:T(8,128)(2,1)S(1)}, u32[]{:S(2)}, u32[]{:S(2)}) collective-permute-start(bf16[2,144,128]{2,1,0:T(8,128)(2,1)S(1)} %pad_maximum_fusion.2), channel_id=1, source_target_pairs={{0,2},{1,3},{2,0},{3,1},{4,6},{5,7},{6,4},{7,5},{8,10},{9,11},{10,... | collective-permute-start | bytes 221192 | tf_op jit(solution)/shard_map/ppermute | solution.py:142
  20.9 5.2 %collective-permute-start.2 = (bf16[4,144,128]{2,1,0:T(8,128)(2,1)S(1)}, bf16[4,144,128]{2,1,0:T(8,128)(2,1)S(1)}, u32[]{:S(2)}, u32[]{:S(2)}) collective-permute-start(bf16[4,144,128]{2,1,0:T(8,128)(2,1)S(1)} %pad_maximum_fusion.1), channel_id=1, source_target_pairs={{0,1},{1,0},{2,3},{3,2},{4,5},{5,4},{6,7},{7,6},{8,9},{9,8},{10,11... | collective-permute-start | bytes 442376 | tf_op jit(solution)/shard_map/ppermute | solution.py:142
  28.9 76.6 %collective-permute-start.3 = (bf16[1,25,2048]{1,2,0:T(8,128)(2,1)S(1)}, bf16[1,25,2048]{1,2,0:T(8,128)(2,1)S(1)}, u32[]{:S(2)}, u32[]{:S(2)}) collective-permute-start(bf16[1,25,2048]{1,2,0:T(8,128)(2,1)S(1)} %copy.17), channel_id=1, source_target_pairs={{0,8},{8,16},{16,24},{24,32},{32,40},{40,48},{48,56},{56,64},{64,7... | collective-permute-start | bytes 307208 | tf_op jit(solution)/shard_map/ppermute | solution.py:19
  30.8 74.9 %collective-permute-start.4 = (bf16[1,25,200]{2,1,0:T(8,128)(2,1)}, bf16[1,25,200]{2,1,0:T(8,128)(2,1)S(1)}, u32[]{:S(2)}, u32[]{:S(2)}) collective-permute-start(bf16[1,25,200]{2,1,0:T(8,128)(2,1)} %param.11), channel_id=1, source_target_pairs={{0,8},{8,16},{16,24},{24,32},{32,40},{40,48},{48,56},{56,64},{64,7... | collective-permute-start | bytes 30008 | tf_op jit(solution)/shard_map/ppermute | solution.py:19
  116.2 3.7 %collective-permute-start.5 = (f32[64]{0:T(128)S(1)}, f32[64]{0:T(128)S(1)}, u32[]{:S(2)}, u32[]{:S(2)}) collective-permute-start(f32[64]{0:T(128)S(1)} %select_reduce_fusion.3), channel_id=1, source_target_pairs={{0,1},{1,0},{2,3},{3,2},{4,5},{5,4},{6,7},{7,6},{8,9},{9,8},{10,11... | collective-permute-start | bytes 776 | tf_op jit(solution)/shard_map/ppermute | solution.py:26
  119.9 5.1 %collective-permute-start.6 = (f32[64]{0:T(128)S(1)}, f32[64]{0:T(128)S(1)}, u32[]{:S(2)}, u32[]{:S(2)}) collective-permute-start(f32[64]{0:T(128)S(1)} %add.85), channel_id=1, source_target_pairs={{0,2},{1,3},{2,0},{3,1},{4,6},{5,7},{6,4},{7,5},{8,10},{9,11},{10,... | collective-permute-start | bytes 776 | tf_op jit(solution)/shard_map/ppermute | solution.py:26
  125.0 5.1 %collective-permute-start.7 = (f32[64]{0:T(128)S(1)}, f32[64]{0:T(128)S(1)}, u32[]{:S(2)}, u32[]{:S(2)}) collective-permute-start(f32[64]{0:T(128)S(1)} %add.86), channel_id=1, source_target_pairs={{0,4},{1,5},{2,6},{3,7},{4,0},{5,1},{6,2},{7,3},{8,12},{9,13},{10,... | collective-permute-start | bytes 776 | tf_op jit(solution)/shard_map/ppermute | solution.py:26
Sparse Core Ops, SparseCore 0:
  27.8 75.2 all-gather.1

commit v8 on v7

--- a/solution.py
+++ b/solution.py
@@ -157,6 +157,10 @@
 def pick(table, index):
     hot = index[:, None] == jnp.arange(table.shape[0], dtype=index.dtype)[None, :]
     return jnp.sum(jnp.where(hot, table[None, :], jnp.zeros((), table.dtype)), axis=1)
+
+
+def pad_to(x, rows):
+    return jnp.pad(x, ((0, rows - x.shape[0]), (0, 0)))
 
 
 def pad_rows(x):
@@ -187,16 +191,23 @@
     cbs = [pick(tile_blocks[:, 1], source)]
     parts = [gathered]
 
-    green_own = jnp.dot(inverse_intersection[0], trial_orbitals, preferred_element_type=jnp.float32).astype(jnp.bfloat16)
-    green_prev = jnp.dot(prev_inverse[0], trial_orbitals, preferred_element_type=jnp.float32).astype(jnp.bfloat16)
+    vec_order = (("vec", 1), ("vec", 2), ("vec", 4))
+    both_panels = xor_gather(jnp.concatenate([panels, prev_panel], axis=0)[None], vec_order)
+    both_inverse = xor_gather(jnp.concatenate([inverse_intersection, prev_inverse], axis=0)[None], vec_order)
+    choice = jnp.where(from_prev, 1, 0)
+    start_rows = lax.dynamic_index_in_dim(both_panels, choice, axis=1, keepdims=False)
+    inverse_rows = lax.dynamic_index_in_dim(both_inverse, choice, axis=1, keepdims=False)
+    full_rows = start_rows.shape[0] * start_rows.shape[1]
+    start_all = start_rows.reshape(full_rows, -1)
+    green_all = jnp.dot(
+        inverse_rows.reshape(full_rows, -1), trial_orbitals, preferred_element_type=jnp.float32
+    ).astype(jnp.bfloat16)
     start = jnp.where(from_prev, prev_panel[0], panels[0])
-    green = jnp.where(from_prev, green_prev, green_own)
-    partials = tile_bias(pad_rows(start).T, pad_rows(green), parts, rbs, cbs)
+    partials = tile_bias(pad_to(start_all, 256).T, pad_to(green_all, 256), parts, rbs, cbs)
     vectors = tile_blocks.shape[0] // KT
     values = partials[0].sum(axis=1)
     hot = (source // KT)[:, None] == jnp.arange(vectors, dtype=source.dtype)[None, :]
-    per_vector = jnp.sum(jnp.where(hot, values[:, None], 0.0), axis=0)
-    raw = butterfly_sum(per_vector, "vec")
+    raw = jnp.sum(jnp.where(hot, values[:, None], 0.0), axis=0)
     bias = jnp.clip(TIME_STEP_ROOT * raw, -1.0, 1.0)
     scales = TIME_STEP_ROOT * (aux_fields[0] - bias)
     ss = [pick(scales, source // KT)]

time: 166 us -> 175 us (1.054)
  waiting for transfers between devices: 82.8 us -> 72.4 us
  other arithmetic: 6.27 us -> 13.6 us
  starting transfers between devices: 19.6 us -> 26.1 us
  local copies, waits for them, and re-layouts: 3.12 us -> 7.35 us
    all_gather x1, waiting for transfers between devices: 66.1 us -> 40.8 us  [shards(): lax.all_gather(xor_gather(payload, order), 'walker', axis=0, tiled=True)]
    ppermute x3 -> x9, waiting for transfers between devices: 9.57 us -> 27.1 us  [xor_gather(): other = lax.ppermute(x, axis, [(i, i ^ step) for i in range(count)])]
    ppermute x3 -> x9, starting transfers between devices: 6.98 us -> 20.3 us  [xor_gather(): other = lax.ppermute(x, axis, [(i, i ^ step) for i in range(count)])]
    ppermute x3 -> x0, waiting for transfers between devices: 7.05 us -> none  [butterfly_sum(): lax.ppermute(value, axis, [(i, i ^ step) for i in range(count)])]
    concatenate x3 -> x9, other arithmetic: 3.03 us -> 9.9 us  [xor_gather(): x = jnp.concatenate([x, other], axis=0)]
    ppermute x3 -> x0, starting transfers between devices: 6.75 us -> none  [butterfly_sum(): lax.ppermute(value, axis, [(i, i ^ step) for i in range(count)])]
    ppermute x2, waiting for transfers between devices: 0.01 us -> 4.47 us  [shift_from(): lax.ppermute(value, axis, [(i, i + steps) for i in range(count - steps)])]
    reshape x0 -> x3, local copies, waits for them, and re-layouts: none -> 2.67 us  [the longest x2 2.61 us: shards(): start_all = start_rows.reshape(full_rows, -1)]
  transfers between devices with their start and end apart: 9 -> 12, of which waited for: 7 -> 9; matrix products, arithmetic and copies ran while one was open for 3% -> 8% of each run, Pallas kernels for 0% -> 0%
where the time goes in v8:
time: 175 us; the launch traced here: 172 us
  waiting for transfers between devices  72.4 us (41%)
  Pallas kernels  37.5 us (21%)
  starting transfers between devices  26.1 us (15%)
  between operations  15.1 us (9%)
  other arithmetic  13.6 us (8%)
  local copies, waits for them, and re-layouts  7.35 us (4%)
    all_gather x1, waiting for transfers between devices, shards(): lax.all_gather(xor_gather(payload, order), 'walker', axis=0, tiled=True)  40.8 us
    pallas_call x1, Pallas kernels, propagate(): pl.pallas_call(prop_kernel, out_shape=jax.ShapeDtypeStruct((orbitals, row...  27.3 us
    ppermute x9, waiting for transfers between devices, xor_gather(): other = lax.ppermute(x, axis, [(i, i ^ step) for i in range(count)])  27.1 us
    ppermute x9, starting transfers between devices, xor_gather(): other = lax.ppermute(x, axis, [(i, i ^ step) for i in range(count)])  20.3 us
    pallas_call x1, Pallas kernels, tile_bias(): pl.pallas_call(bias_kernel, out_shape=[jax.ShapeDtypeStruct((tiles_total,...  10.2 us
    concatenate x9, other arithmetic, xor_gather(): x = jnp.concatenate([x, other], axis=0)  9.9 us
    ppermute x2, starting transfers between devices, shift_from(): lax.ppermute(value, axis, [(i, i + steps) for i in range(count - steps)])  5.82 us
    ppermute x2, waiting for transfers between devices, shift_from(): lax.ppermute(value, axis, [(i, i + steps) for i in range(count - steps)])  4.47 us
  transfers between devices with their start and end apart: 12, of which 9 were waited for; matrix products, arithmetic and copies ran while one was open for 8% of the time, Pallas kernels for 0%

profile of v8, /device:TPU:2, one launch (start us, length us, event | category | flops | bytes accessed | tf_op | source)
XLA Modules:
  0.0 172.4 jit_solution(5580432532607790298)
XLA Ops:
  8.1 2.1 %collective-permute-start.4 = (bf16[1,144,128]{2,1,0:T(8,128)(2,1)S(1)}, bf16[1,144,128]{2,1,0:T(8,128)(2,1)S(1)}, u32[]{:S(2)}, u32[]{:S(2)}) collective-permute-start(bf16[1,144,128]{2,1,0:T(8,128)(2,1)S(1)} %pad_maximum_fusion.7), channel_id=1, source_target_pairs={{0,4},{1,5},{2,6},{3,7},{4,0},{5,1},{6,2},{7,3},{8,12},{9,13},{10,... | collective-permute-start | bytes 110600 | tf_op jit(solution)/shard_map/ppermute | solution.py:142
  10.2 3.3 %collective-permute-done.4 = bf16[1,144,128]{2,1,0:T(8,128)(2,1)S(1)} collective-permute-done((bf16[1,144,128]{2,1,0:T(8,128)(2,1)S(1)}, bf16[1,144,128]{2,1,0:T(8,128)(2,1)S(1)}, u32[]{:S(2)}, u32[]{:S(2)}) %collective-permute-start.4) | collective-permute-done | bytes 36896 | tf_op jit(solution)/shard_map/ppermute | solution.py:142
  14.3 3.2 %collective-permute-start.5 = (bf16[2,144,128]{2,1,0:T(8,128)(2,1)S(1)}, bf16[2,144,128]{2,1,0:T(8,128)(2,1)S(1)}, u32[]{:S(2)}, u32[]{:S(2)}) collective-permute-start(bf16[2,144,128]{2,1,0:T(8,128)(2,1)S(1)} %pad_maximum_fusion.5), channel_id=1, source_target_pairs={{0,2},{1,3},{2,0},{3,1},{4,6},{5,7},{6,4},{7,5},{8,10},{9,11},{10,... | collective-permute-start | bytes 221192 | tf_op jit(solution)/shard_map/ppermute | solution.py:142
  17.5 2.7 %collective-permute-done.5 = bf16[2,144,128]{2,1,0:T(8,128)(2,1)S(1)} collective-permute-done((bf16[2,144,128]{2,1,0:T(8,128)(2,1)S(1)}, bf16[2,144,128]{2,1,0:T(8,128)(2,1)S(1)}, u32[]{:S(2)}, u32[]{:S(2)}) %collective-permute-start.5) | collective-permute-done | bytes 73760 | tf_op jit(solution)/shard_map/ppermute | solution.py:142
  20.9 1.7 collective-permute-start.6
  22.6 3.6 %collective-permute-done.6 = bf16[4,144,128]{2,1,0:T(8,128)(2,1)S(1)} collective-permute-done((bf16[4,144,128]{2,1,0:T(8,128)(2,1)S(1)}, bf16[4,144,128]{2,1,0:T(8,128)(2,1)S(1)}, u32[]{:S(2)}, u32[]{:S(2)}) %collective-permute-start.6) | collective-permute-done | bytes 147488 | tf_op jit(solution)/shard_map/ppermute | solution.py:142
  26.2 1.5 pad_maximum_fusion.2
  28.9 1.9 %collective-permute-start = (bf16[1,25,2048]{1,2,0:T(8,128)(2,1)S(1)}, bf16[1,25,2048]{1,2,0:T(8,128)(2,1)S(1)}, u32[]{:S(2)}, u32[]{:S(2)}) collective-permute-start(bf16[1,25,2048]{1,2,0:T(8,128)(2,1)S(1)} %copy.31), channel_id=1, source_target_pairs={{0,8},{8,16},{16,24},{24,32},{32,40},{40,48},{48,56},{56,64},{64,7... | collective-permute-start | bytes 307208 | tf_op jit(solution)/shard_map/ppermute | solution.py:19
  30.9 3.9 %collective-permute-start.7 = (bf16[1,25,200]{2,1,0:T(8,128)(2,1)S(1)}, bf16[1,25,200]{2,1,0:T(8,128)(2,1)S(1)}, u32[]{:S(2)}, u32[]{:S(2)}) collective-permute-start(bf16[1,25,200]{2,1,0:T(8,128)(2,1)S(1)} %copy-done.4), channel_id=1, source_target_pairs={{0,8},{8,16},{16,24},{24,32},{32,40},{40,48},{48,56},{56,64},{64,7... | collective-permute-start | bytes 30008 | tf_op jit(solution)/shard_map/ppermute | solution.py:19
  35.0 4.5 %collective-permute-done = bf16[1,25,2048]{1,2,0:T(8,128)(2,1)S(1)} collective-permute-done((bf16[1,25,2048]{1,2,0:T(8,128)(2,1)S(1)}, bf16[1,25,2048]{1,2,0:T(8,128)(2,1)S(1)}, u32[]{:S(2)}, u32[]{:S(2)}) %collective-permute-start) | collective-permute-done | bytes 102432 | tf_op jit(solution)/shard_map/ppermute | solution.py:19
  40.4 1.7 collective-permute-start.1
  42.0 4.9 %collective-permute-done.1 = bf16[1,2,25,2048]{3,1,2,0:T(2,128)(2,1)S(1)} collective-permute-done((bf16[1,2,25,2048]{3,1,2,0:T(2,128)(2,1)S(1)}, bf16[1,2,25,2048]{3,1,2,0:T(2,128)(2,1)S(1)}, u32[]{:S(2)}, u32[]{:S(2)}) %collective-permute-start.1) | collective-permute-done | bytes 204832 | tf_op jit(solution)/shard_map/ppermute | solution.py:142
  47.5 3.3 %collective-permute-start.2 = (bf16[2,2,25,2048]{3,1,2,0:T(2,128)(2,1)S(1)}, bf16[2,2,25,2048]{3,1,2,0:T(2,128)(2,1)S(1)}, u32[]{:S(2)}, u32[]{:S(2)}) collective-permute-start(bf16[2,2,25,2048]{3,1,2,0:T(2,128)(2,1)S(1)} %pad_maximum_fusion.1), channel_id=1, source_target_pairs={{0,2},{1,3},{2,0},{3,1},{4,6},{5,7},{6,4},{7,5},{8,10},{9,11},{10,... | collective-permute-start | bytes 1228808 | tf_op jit(solution)/shard_map/ppermute | solution.py:142
  51.7 7.6 %collective-permute-done.2 = bf16[2,2,25,2048]{3,1,2,0:T(2,128)(2,1)S(1)} collective-permute-done((bf16[2,2,25,2048]{3,1,2,0:T(2,128)(2,1)S(1)}, bf16[2,2,25,2048]{3,1,2,0:T(2,128)(2,1)S(1)}, u32[]{:S(2)}, u32[]{:S(2)}) %collective-permute-start.2) | collective-permute-done | bytes 409632 | tf_op jit(solution)/shard_map/ppermute | solution.py:142
  59.6 2.3 %pad_maximum_fusion = bf16[4,2,25,2048]{3,0,2,1:T(4,128)(2,1)} fusion(bf16[2,2,25,2048]{3,0,2,1:T(2,128)(2,1)S(1)} %copy.39, bf16[1,2,25,2048]{3,0,2,1:T(2,128)(2,1)S(1)} %copy.38, bf16[1,2,25,2048]{3,0,2,1:T(2,128)(2,1)S(1)} %copy.37), kind=kLoop, calls=%fused_computation.9 | loop fusion | flops 2457600 | bytes 1638400 | tf_op jit(solution)/shard_map/concatenate | solution.py:143
  61.8 2.7 %collective-permute-start.3 = (bf16[4,2,25,2048]{3,0,2,1:T(4,128)(2,1)}, bf16[4,2,25,2048]{3,0,2,1:T(4,128)(2,1)S(1)}, u32[]{:S(2)}, u32[]{:S(2)}) collective-permute-start(bf16[4,2,25,2048]{3,0,2,1:T(4,128)(2,1)} %pad_maximum_fusion), channel_id=1, source_target_pairs={{0,4},{1,5},{2,6},{3,7},{4,0},{5,1},{6,2},{7,3},{8,12},{9,13},{10,... | collective-permute-start | bytes 2457608 | tf_op jit(solution)/shard_map/ppermute | solution.py:142
  64.6 1.7 collective-permute-start.8
  66.2 2.3 %collective-permute-done.8 = bf16[1,2,25,200]{3,2,1,0:T(8,128)(2,1)S(1)} collective-permute-done((bf16[1,2,25,200]{3,2,1,0:T(8,128)(2,1)S(1)}, bf16[1,2,25,200]{3,2,1,0:T(8,128)(2,1)S(1)}, u32[]{:S(2)}, u32[]{:S(2)}) %collective-permute-start.8) | collective-permute-done | bytes 20032 | tf_op jit(solution)/shard_map/ppermute | solution.py:142
  69.2 3.2 %collective-permute-start.9 = (bf16[2,2,25,200]{3,2,1,0:T(8,128)(2,1)}, bf16[2,2,25,200]{3,2,1,0:T(8,128)(2,1)}, u32[]{:S(2)}, u32[]{:S(2)}) collective-permute-start(bf16[2,2,25,200]{3,2,1,0:T(8,128)(2,1)} %pad_maximum_fusion.6), channel_id=1, source_target_pairs={{0,2},{1,3},{2,0},{3,1},{4,6},{5,7},{6,4},{7,5},{8,10},{9,11},{10,... | collective-permute-start | bytes 120008 | tf_op jit(solution)/shard_map/ppermute | solution.py:142
  72.6 2.7 %collective-permute-done.9 = bf16[2,2,25,200]{3,2,1,0:T(8,128)(2,1)} collective-permute-done((bf16[2,2,25,200]{3,2,1,0:T(8,128)(2,1)}, bf16[2,2,25,200]{3,2,1,0:T(8,128)(2,1)}, u32[]{:S(2)}, u32[]{:S(2)}) %collective-permute-start.9) | collective-permute-done | bytes 40032 | tf_op jit(solution)/shard_map/ppermute | solution.py:142
  75.3 1.5 pad_maximum_fusion.4
  77.7 40.8 %all-gather.2.cloned.1.call-done.refs_4_ = bf16[256,144,128]{2,1,0:T(8,128)(2,1)} async-done(((bf16[8,144,128]{2,1,0:T(8,128)(2,1)}), bf16[256,144,128]{2,1,0:T(8,128)(2,1)}) %all-gather.2.cloned.1.call-update) | async-done | bytes 9437200 | tf_op jit(solution)/shard_map/all_gather | solution.py:182
  126.6 10.2 %shard_map.73 = f32[256,128]{1,0:T(8,128)S(1)} custom-call(s32[256]{0:T(256)S(1)} %get-tuple-element.18.refs_0_, s32[256]{0:T(256)S(1)} %get-tuple-element.17.refs_1_, bf16[2048,256]{1,0:T(8,128)(2,1)S(1)} %pad_bitcast_fusion.refs_2_, bf16[256,2048]{1,0:T(8,128)(2,1)S(1)} %pad.17.refs_3_, bf16[256,144,128]{2,1,0:T(8,128)(2,1)} %all-gather.2.cloned.1.call-done.refs_4_), custom_call_target="tpu_custom_call" | custom-call | tf_op jit(solution)/shard_map/pallas_call | solution.py:62
  137.3 27.3 %shard_map.74 = bf16[2048,32]{1,0:T(8,128)(2,1)S(1)} custom-call(s32[256]{0:T(256)S(1)} %get-tuple-element.18.refs_0_, s32[256]{0:T(256)S(1)} %get-tuple-element.17.refs_1_, f32[256]{0:T(256)S(1)} %select_reduce_fusion.2.refs_2_, bf16[2048,32]{1,0:T(8,128)(2,1)S(1)} %pad_bitcast_fusion.1.refs_3_, bf16[256,144,128]{2,1,0:T(8,128)(2,1)} %all-gather.2.cloned.1.call-done.refs_4_), custom_call_target="tpu_custom_call" | custom-call | tf_op jit(solution)/shard_map/pallas_call | solution.py:121
  (60 shorter events, 16.9 us)
Async XLA Ops:
  6.5 119.5 %copy-start = (bf16[200,2048]{1,0:T(8,128)(2,1)S(1)}, bf16[200,2048]{1,0:T(8,128)(2,1)}, u32[]{:S(2)}) copy-start(bf16[200,2048]{1,0:T(8,128)(2,1)} %param.12) | copy-start | bytes 2457604
  6.5 28.2 %copy-start.3 = (bf16[1,25,2048]{2,1,0:T(8,128)(2,1)S(1)}, bf16[1,25,2048]{2,1,0:T(8,128)(2,1)}, u32[]{:S(2)}) copy-start(bf16[1,25,2048]{2,1,0:T(8,128)(2,1)} %param.10) | copy-start | bytes 307204
  6.5 24.3 %copy-start.4 = (bf16[1,25,200]{2,1,0:T(8,128)(2,1)S(1)}, bf16[1,25,200]{2,1,0:T(8,128)(2,1)}, u32[]{:S(2)}) copy-start(bf16[1,25,200]{2,1,0:T(8,128)(2,1)} %param.11) | copy-start | bytes 30004
  6.5 111.9 %all-gather.2.cloned.1.call-start = ((), (), s32[]{:S(2)}) async-start(), calls=%async_computation | async-start | bytes 9732096 | tf_op jit(solution)/shard_map/all_gather | solution.py:182
  8.1 5.5 %collective-permute-start.4 = (bf16[1,144,128]{2,1,0:T(8,128)(2,1)S(1)}, bf16[1,144,128]{2,1,0:T(8,128)(2,1)S(1)}, u32[]{:S(2)}, u32[]{:S(2)}) collective-permute-start(bf16[1,144,128]{2,1,0:T(8,128)(2,1)S(1)} %pad_maximum_fusion.7), channel_id=1, source_target_pairs={{0,4},{1,5},{2,6},{3,7},{4,0},{5,1},{6,2},{7,3},{8,12},{9,13},{10,... | collective-permute-start | bytes 110600 | tf_op jit(solution)/shard_map/ppermute | solution.py:142
  14.3 5.9 %collective-permute-start.5 = (bf16[2,144,128]{2,1,0:T(8,128)(2,1)S(1)}, bf16[2,144,128]{2,1,0:T(8,128)(2,1)S(1)}, u32[]{:S(2)}, u32[]{:S(2)}) collective-permute-start(bf16[2,144,128]{2,1,0:T(8,128)(2,1)S(1)} %pad_maximum_fusion.5), channel_id=1, source_target_pairs={{0,2},{1,3},{2,0},{3,1},{4,6},{5,7},{6,4},{7,5},{8,10},{9,11},{10,... | collective-permute-start | bytes 221192 | tf_op jit(solution)/shard_map/ppermute | solution.py:142
  20.9 5.2 %collective-permute-start.6 = (bf16[4,144,128]{2,1,0:T(8,128)(2,1)S(1)}, bf16[4,144,128]{2,1,0:T(8,128)(2,1)S(1)}, u32[]{:S(2)}, u32[]{:S(2)}) collective-permute-start(bf16[4,144,128]{2,1,0:T(8,128)(2,1)S(1)} %pad_maximum_fusion.3), channel_id=1, source_target_pairs={{0,1},{1,0},{2,3},{3,2},{4,5},{5,4},{6,7},{7,6},{8,9},{9,8},{10,11... | collective-permute-start | bytes 442376 | tf_op jit(solution)/shard_map/ppermute | solution.py:142
  27.7 23.3 %copy-start.5 = (s32[256,2]{0,1:T(2,128)S(1)}, s32[256,2]{0,1:T(2,128)}, u32[]{:S(2)}) copy-start(s32[256,2]{0,1:T(2,128)} %param.14) | copy-start | bytes 6148
  28.9 10.5 %collective-permute-start = (bf16[1,25,2048]{1,2,0:T(8,128)(2,1)S(1)}, bf16[1,25,2048]{1,2,0:T(8,128)(2,1)S(1)}, u32[]{:S(2)}, u32[]{:S(2)}) collective-permute-start(bf16[1,25,2048]{1,2,0:T(8,128)(2,1)S(1)} %copy.31), channel_id=1, source_target_pairs={{0,8},{8,16},{16,24},{24,32},{32,40},{40,48},{48,56},{56,64},{64,7... | collective-permute-start | bytes 307208 | tf_op jit(solution)/shard_map/ppermute | solution.py:19
  30.9 33.7 %collective-permute-start.7 = (bf16[1,25,200]{2,1,0:T(8,128)(2,1)S(1)}, bf16[1,25,200]{2,1,0:T(8,128)(2,1)S(1)}, u32[]{:S(2)}, u32[]{:S(2)}) collective-permute-start(bf16[1,25,200]{2,1,0:T(8,128)(2,1)S(1)} %copy-done.4), channel_id=1, source_target_pairs={{0,8},{8,16},{16,24},{24,32},{32,40},{40,48},{48,56},{56,64},{64,7... | collective-permute-start | bytes 30008 | tf_op jit(solution)/shard_map/ppermute | solution.py:19
  39.4 11.6 %copy-start.1 = (bf16[1,25,2048]{1,2,0:T(8,128)(2,1)}, bf16[1,25,2048]{1,2,0:T(8,128)(2,1)S(1)}, u32[]{:S(2)}) copy-start(bf16[1,25,2048]{1,2,0:T(8,128)(2,1)S(1)} %collective-permute-done) | copy-start | bytes 307204
  40.4 6.6 %collective-permute-start.1 = (bf16[1,2,25,2048]{3,1,2,0:T(2,128)(2,1)S(1)}, bf16[1,2,25,2048]{3,1,2,0:T(2,128)(2,1)S(1)}, u32[]{:S(2)}, u32[]{:S(2)}) collective-permute-start(bf16[1,2,25,2048]{3,1,2,0:T(2,128)(2,1)S(1)} %maximum_bitcast_fusion), channel_id=1, source_target_pairs={{0,1},{1,0},{2,3},{3,2},{4,5},{5,4},{6,7},{7,6},{8,9},{9,8},{10,11... | collective-permute-start | bytes 614408 | tf_op jit(solution)/shard_map/ppermute | solution.py:142
  47.5 11.7 %collective-permute-start.2 = (bf16[2,2,25,2048]{3,1,2,0:T(2,128)(2,1)S(1)}, bf16[2,2,25,2048]{3,1,2,0:T(2,128)(2,1)S(1)}, u32[]{:S(2)}, u32[]{:S(2)}) collective-permute-start(bf16[2,2,25,2048]{3,1,2,0:T(2,128)(2,1)S(1)} %pad_maximum_fusion.1), channel_id=1, source_target_pairs={{0,2},{1,3},{2,0},{3,1},{4,6},{5,7},{6,4},{7,5},{8,10},{9,11},{10,... | collective-permute-start | bytes 1228808 | tf_op jit(solution)/shard_map/ppermute | solution.py:142
  61.8 59.0 %collective-permute-start.3 = (bf16[4,2,25,2048]{3,0,2,1:T(4,128)(2,1)}, bf16[4,2,25,2048]{3,0,2,1:T(4,128)(2,1)S(1)}, u32[]{:S(2)}, u32[]{:S(2)}) collective-permute-start(bf16[4,2,25,2048]{3,0,2,1:T(4,128)(2,1)} %pad_maximum_fusion), channel_id=1, source_target_pairs={{0,4},{1,5},{2,6},{3,7},{4,0},{5,1},{6,2},{7,3},{8,12},{9,13},{10,... | collective-permute-start | bytes 2457608 | tf_op jit(solution)/shard_map/ppermute | solution.py:142
  64.6 4.0 %collective-permute-start.8 = (bf16[1,2,25,200]{3,2,1,0:T(8,128)(2,1)S(1)}, bf16[1,2,25,200]{3,2,1,0:T(8,128)(2,1)S(1)}, u32[]{:S(2)}, u32[]{:S(2)}) collective-permute-start(bf16[1,2,25,200]{3,2,1,0:T(8,128)(2,1)S(1)} %maximum_bitcast_fusion.1), channel_id=1, source_target_pairs={{0,1},{1,0},{2,3},{3,2},{4,5},{5,4},{6,7},{7,6},{8,9},{9,8},{10,11... | collective-permute-start | bytes 60008 | tf_op jit(solution)/shard_map/ppermute | solution.py:142
  69.2 6.1 %collective-permute-start.9 = (bf16[2,2,25,200]{3,2,1,0:T(8,128)(2,1)}, bf16[2,2,25,200]{3,2,1,0:T(8,128)(2,1)}, u32[]{:S(2)}, u32[]{:S(2)}) collective-permute-start(bf16[2,2,25,200]{3,2,1,0:T(8,128)(2,1)} %pad_maximum_fusion.6), channel_id=1, source_target_pairs={{0,2},{1,3},{2,0},{3,1},{4,6},{5,7},{6,4},{7,5},{8,10},{9,11},{10,... | collective-permute-start | bytes 120008 | tf_op jit(solution)/shard_map/ppermute | solution.py:142
  76.8 48.3 %collective-permute-start.10 = (bf16[4,2,25,200]{3,2,1,0:T(8,128)(2,1)}, bf16[4,2,25,200]{3,2,1,0:T(8,128)(2,1)}, u32[]{:S(2)}, u32[]{:S(2)}) collective-permute-start(bf16[4,2,25,200]{3,2,1,0:T(8,128)(2,1)} %pad_maximum_fusion.4), channel_id=1, source_target_pairs={{0,4},{1,5},{2,6},{3,7},{4,0},{5,1},{6,2},{7,3},{8,12},{9,13},{10,... | collective-permute-start | bytes 240008 | tf_op jit(solution)/shard_map/ppermute | solution.py:142
  126.6 10.5 %copy-start.6 = (f32[1,64]{1,0:T(1,128)S(1)}, f32[1,64]{1,0:T(1,128)}, u32[]{:S(2)}) copy-start(f32[1,64]{1,0:T(1,128)} %param.15) | copy-start | bytes 772
  126.6 10.6 %copy-start.2 = (bf16[1,25,2048]{1,2,0:T(8,128)(2,1)S(1)}, bf16[1,25,2048]{1,2,0:T(8,128)(2,1)}, u32[]{:S(2)}) copy-start(bf16[1,25,2048]{1,2,0:T(8,128)(2,1)} %copy-done.1) | copy-start | bytes 307204
Sparse Core Ops, SparseCore 0:
  27.8 90.5 all-gather.1

commit v9 on v8

--- a/solution.py
+++ b/solution.py
@@ -179,7 +179,11 @@
     meta = jnp.zeros((1, 16, size), chol_tiles.dtype).at[0, 0, 0].set(copy_counts[0].astype(chol_tiles.dtype))
     payload = jnp.concatenate([chol_tiles, meta], axis=1)
     order = (("vec", 4), ("vec", 2), ("vec", 1))
-    gathered = lax.all_gather(xor_gather(payload, order), "walker", axis=0, tiled=True)
+    vec_tiles = xor_gather(payload, order)
+    vec_tiles, panels_late, prev_late, inverse_late, prev_inverse_late = lax.optimization_barrier(
+        (vec_tiles, panels, prev_panel, inverse_intersection, prev_inverse)
+    )
+    gathered = lax.all_gather(vec_tiles, "walker", axis=0, tiled=True)
     tiles_rows = chol_tiles.shape[1]
     counts = gathered[::vecs, tiles_rows, 0].astype(jnp.float32)
     walkers = jnp.arange(counts.shape[0])
@@ -192,8 +196,8 @@
     parts = [gathered]
 
     vec_order = (("vec", 1), ("vec", 2), ("vec", 4))
-    both_panels = xor_gather(jnp.concatenate([panels, prev_panel], axis=0)[None], vec_order)
-    both_inverse = xor_gather(jnp.concatenate([inverse_intersection, prev_inverse], axis=0)[None], vec_order)
+    both_panels = xor_gather(jnp.concatenate([panels_late, prev_late], axis=0)[None], vec_order)
+    both_inverse = xor_gather(jnp.concatenate([inverse_late, prev_inverse_late], axis=0)[None], vec_order)
     choice = jnp.where(from_prev, 1, 0)
     start_rows = lax.dynamic_index_in_dim(both_panels, choice, axis=1, keepdims=False)
     inverse_rows = lax.dynamic_index_in_dim(both_inverse, choice, axis=1, keepdims=False)

time: 175 us -> 181 us (1.034)
  waiting for transfers between devices: 72.4 us -> 81.7 us
  starting transfers between devices: 26.1 us -> 23.3 us
    all_gather x1, waiting for transfers between devices: 40.8 us -> 52.1 us  [shards(): gathered = lax.all_gather(vec_tiles, 'walker', axis=0, tiled=True)]
    ppermute x9, starting transfers between devices: 20.3 us -> 17.5 us  [xor_gather(): other = lax.ppermute(x, axis, [(i, i ^ step) for i in range(count)])]
  transfers between devices with their start and end apart: 12 -> 12, of which waited for: 9 -> 8; matrix products, arithmetic and copies ran while one was open for 8% -> 9% of each run, Pallas kernels for 0% -> 0%
where the time goes in v9:
time: 181 us; the launch traced here: 179 us
  waiting for transfers between devices  81.7 us (45%)
  Pallas kernels  37.5 us (21%)
  starting transfers between devices  23.3 us (13%)
  between operations  15.1 us (8%)
  other arithmetic  13.6 us (8%)
  local copies, waits for them, and re-layouts  7.35 us (4%)
    all_gather x1, waiting for transfers between devices, shards(): gathered = lax.all_gather(vec_tiles, 'walker', axis=0, tiled=True)  52.1 us
    pallas_call x1, Pallas kernels, propagate(): pl.pallas_call(prop_kernel, out_shape=jax.ShapeDtypeStruct((orbitals, row...  27.3 us
    ppermute x9, waiting for transfers between devices, xor_gather(): other = lax.ppermute(x, axis, [(i, i ^ step) for i in range(count)])  26.2 us
    ppermute x9, starting transfers between devices, xor_gather(): other = lax.ppermute(x, axis, [(i, i ^ step) for i in range(count)])  17.5 us
    pallas_call x1, Pallas kernels, tile_bias(): pl.pallas_call(bias_kernel, out_shape=[jax.ShapeDtypeStruct((tiles_total,...  10.2 us
    concatenate x9, other arithmetic, xor_gather(): x = jnp.concatenate([x, other], axis=0)  9.92 us
    ppermute x2, starting transfers between devices, shift_from(): lax.ppermute(value, axis, [(i, i + steps) for i in range(count - steps)])  5.82 us
  transfers between devices with their start and end apart: 12, of which 8 were waited for; matrix products, arithmetic and copies ran while one was open for 9% of the time, Pallas kernels for 0%

profile of v9, /device:TPU:2, one launch (start us, length us, event | category | flops | bytes accessed | tf_op | source)
XLA Modules:
  0.0 178.9 jit_solution(5859705544691019568)
XLA Ops:
  8.1 2.1 %collective-permute-start = (bf16[1,144,128]{2,1,0:T(8,128)(2,1)S(1)}, bf16[1,144,128]{2,1,0:T(8,128)(2,1)S(1)}, u32[]{:S(2)}, u32[]{:S(2)}) collective-permute-start(bf16[1,144,128]{2,1,0:T(8,128)(2,1)S(1)} %pad_maximum_fusion.7), channel_id=1, source_target_pairs={{0,4},{1,5},{2,6},{3,7},{4,0},{5,1},{6,2},{7,3},{8,12},{9,13},{10,... | collective-permute-start | bytes 110600 | tf_op jit(solution)/shard_map/ppermute | solution.py:142
  10.2 3.3 %collective-permute-done = bf16[1,144,128]{2,1,0:T(8,128)(2,1)S(1)} collective-permute-done((bf16[1,144,128]{2,1,0:T(8,128)(2,1)S(1)}, bf16[1,144,128]{2,1,0:T(8,128)(2,1)S(1)}, u32[]{:S(2)}, u32[]{:S(2)}) %collective-permute-start) | collective-permute-done | bytes 36896 | tf_op jit(solution)/shard_map/ppermute | solution.py:142
  14.3 3.2 %collective-permute-start.1 = (bf16[2,144,128]{2,1,0:T(8,128)(2,1)S(1)}, bf16[2,144,128]{2,1,0:T(8,128)(2,1)S(1)}, u32[]{:S(2)}, u32[]{:S(2)}) collective-permute-start(bf16[2,144,128]{2,1,0:T(8,128)(2,1)S(1)} %pad_maximum_fusion.5), channel_id=1, source_target_pairs={{0,2},{1,3},{2,0},{3,1},{4,6},{5,7},{6,4},{7,5},{8,10},{9,11},{10,... | collective-permute-start | bytes 221192 | tf_op jit(solution)/shard_map/ppermute | solution.py:142
  17.5 2.7 %collective-permute-done.1 = bf16[2,144,128]{2,1,0:T(8,128)(2,1)S(1)} collective-permute-done((bf16[2,144,128]{2,1,0:T(8,128)(2,1)S(1)}, bf16[2,144,128]{2,1,0:T(8,128)(2,1)S(1)}, u32[]{:S(2)}, u32[]{:S(2)}) %collective-permute-start.1) | collective-permute-done | bytes 73760 | tf_op jit(solution)/shard_map/ppermute | solution.py:142
  20.9 1.7 collective-permute-start.2
  22.6 1.2 copy.31
  23.8 1.9 %collective-permute-start.3 = (bf16[1,25,2048]{1,2,0:T(8,128)(2,1)S(1)}, bf16[1,25,2048]{1,2,0:T(8,128)(2,1)S(1)}, u32[]{:S(2)}, u32[]{:S(2)}) collective-permute-start(bf16[1,25,2048]{1,2,0:T(8,128)(2,1)S(1)} %copy.31), channel_id=1, source_target_pairs={{0,8},{8,16},{16,24},{24,32},{32,40},{40,48},{48,56},{56,64},{64,7... | collective-permute-start | bytes 307208 | tf_op jit(solution)/shard_map/ppermute | solution.py:19
  25.7 3.9 %collective-permute-start.4 = (bf16[1,25,200]{2,1,0:T(8,128)(2,1)}, bf16[1,25,200]{2,1,0:T(8,128)(2,1)S(1)}, u32[]{:S(2)}, u32[]{:S(2)}) collective-permute-start(bf16[1,25,200]{2,1,0:T(8,128)(2,1)} %param.11), channel_id=1, source_target_pairs={{0,8},{8,16},{16,24},{24,32},{32,40},{40,48},{48,56},{56,64},{64,7... | collective-permute-start | bytes 30008 | tf_op jit(solution)/shard_map/ppermute | solution.py:19
  29.6 1.5 pad_maximum_fusion.2
  31.2 3.3 %collective-permute-done.4 = bf16[1,25,200]{2,1,0:T(8,128)(2,1)S(1)} collective-permute-done((bf16[1,25,200]{2,1,0:T(8,128)(2,1)}, bf16[1,25,200]{2,1,0:T(8,128)(2,1)S(1)}, u32[]{:S(2)}, u32[]{:S(2)}) %collective-permute-start.4) | collective-permute-done | bytes 10032 | tf_op jit(solution)/shard_map/ppermute | solution.py:19
  36.2 6.0 %collective-permute-done.5 = bf16[1,2,25,2048]{3,1,2,0:T(2,128)(2,1)S(1)} collective-permute-done((bf16[1,2,25,2048]{3,1,2,0:T(2,128)(2,1)S(1)}, bf16[1,2,25,2048]{3,1,2,0:T(2,128)(2,1)S(1)}, u32[]{:S(2)}, u32[]{:S(2)}) %collective-permute-start.5) | collective-permute-done | bytes 204832 | tf_op jit(solution)/shard_map/ppermute | solution.py:142
  42.8 3.0 %collective-permute-start.6 = (bf16[2,2,25,2048]{3,1,2,0:T(2,128)(2,1)S(1)}, bf16[2,2,25,2048]{3,1,2,0:T(2,128)(2,1)S(1)}, u32[]{:S(2)}, u32[]{:S(2)}) collective-permute-start(bf16[2,2,25,2048]{3,1,2,0:T(2,128)(2,1)S(1)} %pad_maximum_fusion.1), channel_id=1, source_target_pairs={{0,2},{1,3},{2,0},{3,1},{4,6},{5,7},{6,4},{7,5},{8,10},{9,11},{10,... | collective-permute-start | bytes 1228808 | tf_op jit(solution)/shard_map/ppermute | solution.py:142
  46.6 7.8 %collective-permute-done.6 = bf16[2,2,25,2048]{3,1,2,0:T(2,128)(2,1)S(1)} collective-permute-done((bf16[2,2,25,2048]{3,1,2,0:T(2,128)(2,1)S(1)}, bf16[2,2,25,2048]{3,1,2,0:T(2,128)(2,1)S(1)}, u32[]{:S(2)}, u32[]{:S(2)}) %collective-permute-start.6) | collective-permute-done | bytes 409632 | tf_op jit(solution)/shard_map/ppermute | solution.py:142
  54.7 2.3 %pad_maximum_fusion = bf16[4,2,25,2048]{3,0,2,1:T(4,128)(2,1)} fusion(bf16[2,2,25,2048]{3,0,2,1:T(2,128)(2,1)S(1)} %copy.39, bf16[1,2,25,2048]{3,0,2,1:T(2,128)(2,1)S(1)} %copy.38, bf16[1,2,25,2048]{3,0,2,1:T(2,128)(2,1)S(1)} %copy.37), kind=kLoop, calls=%fused_computation.9 | loop fusion | flops 2457600 | bytes 1638400 | tf_op jit(solution)/shard_map/concatenate | solution.py:143
  57.0 2.7 %collective-permute-start.7 = (bf16[4,2,25,2048]{3,0,2,1:T(4,128)(2,1)}, bf16[4,2,25,2048]{3,0,2,1:T(4,128)(2,1)S(1)}, u32[]{:S(2)}, u32[]{:S(2)}) collective-permute-start(bf16[4,2,25,2048]{3,0,2,1:T(4,128)(2,1)} %pad_maximum_fusion), channel_id=1, source_target_pairs={{0,4},{1,5},{2,6},{3,7},{4,0},{5,1},{6,2},{7,3},{8,12},{9,13},{10,... | collective-permute-start | bytes 2457608 | tf_op jit(solution)/shard_map/ppermute | solution.py:142
  60.3 3.5 %collective-permute-done.8 = bf16[1,2,25,200]{3,2,1,0:T(8,128)(2,1)S(1)} collective-permute-done((bf16[1,2,25,200]{3,2,1,0:T(8,128)(2,1)S(1)}, bf16[1,2,25,200]{3,2,1,0:T(8,128)(2,1)S(1)}, u32[]{:S(2)}, u32[]{:S(2)}) %collective-permute-start.8) | collective-permute-done | bytes 20032 | tf_op jit(solution)/shard_map/ppermute | solution.py:142
  64.4 2.9 %collective-permute-start.9 = (bf16[2,2,25,200]{3,2,1,0:T(8,128)(2,1)}, bf16[2,2,25,200]{3,2,1,0:T(8,128)(2,1)}, u32[]{:S(2)}, u32[]{:S(2)}) collective-permute-start(bf16[2,2,25,200]{3,2,1,0:T(8,128)(2,1)} %pad_maximum_fusion.6), channel_id=1, source_target_pairs={{0,2},{1,3},{2,0},{3,1},{4,6},{5,7},{6,4},{7,5},{8,10},{9,11},{10,... | collective-permute-start | bytes 120008 | tf_op jit(solution)/shard_map/ppermute | solution.py:142
  67.5 3.0 %collective-permute-done.9 = bf16[2,2,25,200]{3,2,1,0:T(8,128)(2,1)} collective-permute-done((bf16[2,2,25,200]{3,2,1,0:T(8,128)(2,1)}, bf16[2,2,25,200]{3,2,1,0:T(8,128)(2,1)}, u32[]{:S(2)}, u32[]{:S(2)}) %collective-permute-start.9) | collective-permute-done | bytes 40032 | tf_op jit(solution)/shard_map/ppermute | solution.py:142
  70.5 1.5 pad_maximum_fusion.4
  72.8 52.1 %all-gather.2.cloned.1.call-done.refs_4_ = bf16[256,144,128]{2,1,0:T(8,128)(2,1)} async-done(((bf16[8,144,128]{2,1,0:T(8,128)(2,1)}), bf16[256,144,128]{2,1,0:T(8,128)(2,1)}) %all-gather.2.cloned.1.call-update) | async-done | bytes 9437200 | tf_op jit(solution)/shard_map/all_gather | solution.py:186
  128.8 1.2 reshape.140
  130.0 1.4 copy.41
  133.1 10.2 %shard_map.73 = f32[256,128]{1,0:T(8,128)S(1)} custom-call(s32[256]{0:T(256)S(1)} %get-tuple-element.28.refs_0_, s32[256]{0:T(256)S(1)} %get-tuple-element.27.refs_1_, bf16[2048,256]{1,0:T(8,128)(2,1)S(1)} %pad_bitcast_fusion.refs_2_, bf16[256,2048]{1,0:T(8,128)(2,1)S(1)} %pad.17.refs_3_, bf16[256,144,128]{2,1,0:T(8,128)(2,1)} %all-gather.2.cloned.1.call-done.refs_4_), custom_call_target="tpu_custom_call" | custom-call | tf_op jit(solution)/shard_map/pallas_call | solution.py:62
  143.9 27.3 %shard_map.74 = bf16[2048,32]{1,0:T(8,128)(2,1)S(1)} custom-call(s32[256]{0:T(256)S(1)} %get-tuple-element.28.refs_0_, s32[256]{0:T(256)S(1)} %get-tuple-element.27.refs_1_, f32[256]{0:T(256)S(1)} %select_reduce_fusion.2.refs_2_, bf16[2048,32]{1,0:T(8,128)(2,1)S(1)} %pad_bitcast_fusion.1.refs_3_, bf16[256,144,128]{2,1,0:T(8,128)(2,1)} %all-gather.2.cloned.1.call-done.refs_4_), custom_call_target="tpu_custom_call" | custom-call | tf_op jit(solution)/shard_map/pallas_call | solution.py:121
  (60 shorter events, 14.2 us)
Async XLA Ops:
  6.5 126.1 %copy-start = (bf16[200,2048]{1,0:T(8,128)(2,1)S(1)}, bf16[200,2048]{1,0:T(8,128)(2,1)}, u32[]{:S(2)}) copy-start(bf16[200,2048]{1,0:T(8,128)(2,1)} %param.12) | copy-start | bytes 2457604
  6.5 28.4 %copy-start.3 = (bf16[1,25,2048]{2,1,0:T(8,128)(2,1)S(1)}, bf16[1,25,2048]{2,1,0:T(8,128)(2,1)}, u32[]{:S(2)}) copy-start(bf16[1,25,2048]{2,1,0:T(8,128)(2,1)} %param.10) | copy-start | bytes 307204
  6.5 118.4 %all-gather.2.cloned.1.call-start = ((), (), s32[]{:S(2)}) async-start(), calls=%async_computation | async-start | bytes 9732096 | tf_op jit(solution)/shard_map/all_gather | solution.py:186
  8.1 5.5 %collective-permute-start = (bf16[1,144,128]{2,1,0:T(8,128)(2,1)S(1)}, bf16[1,144,128]{2,1,0:T(8,128)(2,1)S(1)}, u32[]{:S(2)}, u32[]{:S(2)}) collective-permute-start(bf16[1,144,128]{2,1,0:T(8,128)(2,1)S(1)} %pad_maximum_fusion.7), channel_id=1, source_target_pairs={{0,4},{1,5},{2,6},{3,7},{4,0},{5,1},{6,2},{7,3},{8,12},{9,13},{10,... | collective-permute-start | bytes 110600 | tf_op jit(solution)/shard_map/ppermute | solution.py:142
  14.3 5.9 %collective-permute-start.1 = (bf16[2,144,128]{2,1,0:T(8,128)(2,1)S(1)}, bf16[2,144,128]{2,1,0:T(8,128)(2,1)S(1)}, u32[]{:S(2)}, u32[]{:S(2)}) collective-permute-start(bf16[2,144,128]{2,1,0:T(8,128)(2,1)S(1)} %pad_maximum_fusion.5), channel_id=1, source_target_pairs={{0,2},{1,3},{2,0},{3,1},{4,6},{5,7},{6,4},{7,5},{8,10},{9,11},{10,... | collective-permute-start | bytes 221192 | tf_op jit(solution)/shard_map/ppermute | solution.py:142
  20.9 8.7 %collective-permute-start.2 = (bf16[4,144,128]{2,1,0:T(8,128)(2,1)S(1)}, bf16[4,144,128]{2,1,0:T(8,128)(2,1)S(1)}, u32[]{:S(2)}, u32[]{:S(2)}) collective-permute-start(bf16[4,144,128]{2,1,0:T(8,128)(2,1)S(1)} %pad_maximum_fusion.3), channel_id=1, source_target_pairs={{0,1},{1,0},{2,3},{3,2},{4,5},{5,4},{6,7},{7,6},{8,9},{9,8},{10,11... | collective-permute-start | bytes 442376 | tf_op jit(solution)/shard_map/ppermute | solution.py:142
  23.8 22.2 %copy-start.5 = (s32[256,2]{0,1:T(2,128)S(1)}, s32[256,2]{0,1:T(2,128)}, u32[]{:S(2)}) copy-start(s32[256,2]{0,1:T(2,128)} %param.14) | copy-start | bytes 6148
  23.8 10.7 %collective-permute-start.3 = (bf16[1,25,2048]{1,2,0:T(8,128)(2,1)S(1)}, bf16[1,25,2048]{1,2,0:T(8,128)(2,1)S(1)}, u32[]{:S(2)}, u32[]{:S(2)}) collective-permute-start(bf16[1,25,2048]{1,2,0:T(8,128)(2,1)S(1)} %copy.31), channel_id=1, source_target_pairs={{0,8},{8,16},{16,24},{24,32},{32,40},{40,48},{48,56},{56,64},{64,7... | collective-permute-start | bytes 307208 | tf_op jit(solution)/shard_map/ppermute | solution.py:19
  25.7 8.7 %collective-permute-start.4 = (bf16[1,25,200]{2,1,0:T(8,128)(2,1)}, bf16[1,25,200]{2,1,0:T(8,128)(2,1)S(1)}, u32[]{:S(2)}, u32[]{:S(2)}) collective-permute-start(bf16[1,25,200]{2,1,0:T(8,128)(2,1)} %param.11), channel_id=1, source_target_pairs={{0,8},{8,16},{16,24},{24,32},{32,40},{40,48},{48,56},{56,64},{64,7... | collective-permute-start | bytes 30008 | tf_op jit(solution)/shard_map/ppermute | solution.py:19
  34.5 11.5 %copy-start.1 = (bf16[1,25,2048]{1,2,0:T(8,128)(2,1)}, bf16[1,25,2048]{1,2,0:T(8,128)(2,1)S(1)}, u32[]{:S(2)}) copy-start(bf16[1,25,2048]{1,2,0:T(8,128)(2,1)S(1)} %collective-permute-done.3) | copy-start | bytes 307204
  35.6 6.6 %collective-permute-start.5 = (bf16[1,2,25,2048]{3,1,2,0:T(2,128)(2,1)S(1)}, bf16[1,2,25,2048]{3,1,2,0:T(2,128)(2,1)S(1)}, u32[]{:S(2)}, u32[]{:S(2)}) collective-permute-start(bf16[1,2,25,2048]{3,1,2,0:T(2,128)(2,1)S(1)} %maximum_bitcast_fusion), channel_id=1, source_target_pairs={{0,1},{1,0},{2,3},{3,2},{4,5},{5,4},{6,7},{7,6},{8,9},{9,8},{10,11... | collective-permute-start | bytes 614408 | tf_op jit(solution)/shard_map/ppermute | solution.py:142
  42.8 11.6 %collective-permute-start.6 = (bf16[2,2,25,2048]{3,1,2,0:T(2,128)(2,1)S(1)}, bf16[2,2,25,2048]{3,1,2,0:T(2,128)(2,1)S(1)}, u32[]{:S(2)}, u32[]{:S(2)}) collective-permute-start(bf16[2,2,25,2048]{3,1,2,0:T(2,128)(2,1)S(1)} %pad_maximum_fusion.1), channel_id=1, source_target_pairs={{0,2},{1,3},{2,0},{3,1},{4,6},{5,7},{6,4},{7,5},{8,10},{9,11},{10,... | collective-permute-start | bytes 1228808 | tf_op jit(solution)/shard_map/ppermute | solution.py:142
  46.3 13.4 %copy-start.4 = (bf16[1,25,200]{2,1,0:T(8,128)(2,1)S(1)}, bf16[1,25,200]{2,1,0:T(8,128)(2,1)}, u32[]{:S(2)}) copy-start(bf16[1,25,200]{2,1,0:T(8,128)(2,1)} %param.11) | copy-start | bytes 30004
  57.0 70.4 %collective-permute-start.7 = (bf16[4,2,25,2048]{3,0,2,1:T(4,128)(2,1)}, bf16[4,2,25,2048]{3,0,2,1:T(4,128)(2,1)S(1)}, u32[]{:S(2)}, u32[]{:S(2)}) collective-permute-start(bf16[4,2,25,2048]{3,0,2,1:T(4,128)(2,1)} %pad_maximum_fusion), channel_id=1, source_target_pairs={{0,4},{1,5},{2,6},{3,7},{4,0},{5,1},{6,2},{7,3},{8,12},{9,13},{10,... | collective-permute-start | bytes 2457608 | tf_op jit(solution)/shard_map/ppermute | solution.py:142
  59.7 4.0 %collective-permute-start.8 = (bf16[1,2,25,200]{3,2,1,0:T(8,128)(2,1)S(1)}, bf16[1,2,25,200]{3,2,1,0:T(8,128)(2,1)S(1)}, u32[]{:S(2)}, u32[]{:S(2)}) collective-permute-start(bf16[1,2,25,200]{3,2,1,0:T(8,128)(2,1)S(1)} %maximum_bitcast_fusion.1), channel_id=1, source_target_pairs={{0,1},{1,0},{2,3},{3,2},{4,5},{5,4},{6,7},{7,6},{8,9},{9,8},{10,11... | collective-permute-start | bytes 60008 | tf_op jit(solution)/shard_map/ppermute | solution.py:142
  64.4 6.1 %collective-permute-start.9 = (bf16[2,2,25,200]{3,2,1,0:T(8,128)(2,1)}, bf16[2,2,25,200]{3,2,1,0:T(8,128)(2,1)}, u32[]{:S(2)}, u32[]{:S(2)}) collective-permute-start(bf16[2,2,25,200]{3,2,1,0:T(8,128)(2,1)} %pad_maximum_fusion.6), channel_id=1, source_target_pairs={{0,2},{1,3},{2,0},{3,1},{4,6},{5,7},{6,4},{7,5},{8,10},{9,11},{10,... | collective-permute-start | bytes 120008 | tf_op jit(solution)/shard_map/ppermute | solution.py:142
  72.0 59.6 %collective-permute-start.10 = (bf16[4,2,25,200]{3,2,1,0:T(8,128)(2,1)}, bf16[4,2,25,200]{3,2,1,0:T(8,128)(2,1)}, u32[]{:S(2)}, u32[]{:S(2)}) collective-permute-start(bf16[4,2,25,200]{3,2,1,0:T(8,128)(2,1)} %pad_maximum_fusion.4), channel_id=1, source_target_pairs={{0,4},{1,5},{2,6},{3,7},{4,0},{5,1},{6,2},{7,3},{8,12},{9,13},{10,... | collective-permute-start | bytes 240008 | tf_op jit(solution)/shard_map/ppermute | solution.py:142
  133.1 10.5 %copy-start.6 = (f32[1,64]{1,0:T(1,128)S(1)}, f32[1,64]{1,0:T(1,128)}, u32[]{:S(2)}) copy-start(f32[1,64]{1,0:T(1,128)} %param.15) | copy-start | bytes 772
  133.1 10.6 %copy-start.2 = (bf16[1,25,2048]{1,2,0:T(8,128)(2,1)S(1)}, bf16[1,25,2048]{1,2,0:T(8,128)(2,1)}, u32[]{:S(2)}) copy-start(bf16[1,25,2048]{1,2,0:T(8,128)(2,1)} %copy-done.1) | copy-start | bytes 307204
Sparse Core Ops, SparseCore 0:
  34.6 90.2 all-gather.1

commit v10 on v7

--- a/solution.py
+++ b/solution.py
@@ -17,6 +17,21 @@
 def shift_from(value, axis, steps):
     count = lax.axis_size(axis)
     return lax.ppermute(value, axis, [(i, i + steps) for i in range(count - steps)])
+
+
+def exchange_sum(value, axis):
+    count = lax.axis_size(axis)
+    me = lax.axis_index(axis)
+    received = [value] + [
+        lax.ppermute(value, axis, [(i, (i + step) % count) for i in range(count)])
+        for step in range(1, count)
+    ]
+    stacked = jnp.stack(received)
+    by_source = jnp.take(stacked, (me - jnp.arange(count)) % count, axis=0)
+    total = by_source[0]
+    for source in range(1, count):
+        total = total + by_source[source]
+    return total
 
 
 def butterfly_sum(value, axis):
@@ -196,7 +211,7 @@
     values = partials[0].sum(axis=1)
     hot = (source // KT)[:, None] == jnp.arange(vectors, dtype=source.dtype)[None, :]
     per_vector = jnp.sum(jnp.where(hot, values[:, None], 0.0), axis=0)
-    raw = butterfly_sum(per_vector, "vec")
+    raw = exchange_sum(per_vector, "vec")
     bias = jnp.clip(TIME_STEP_ROOT * raw, -1.0, 1.0)
     scales = TIME_STEP_ROOT * (aux_fields[0] - bias)
     ss = [pick(scales, source // KT)]

time: 166 us -> 172 us (1.036)
  starting transfers between devices: 19.6 us -> 25.3 us
    ppermute x3 -> x7, starting transfers between devices: 6.75 us -> 12.5 us  [exchange_sum(): lax.ppermute(value, axis, [(i, (i + step) % count) for i in range(count)])]
    ppermute x3 -> x7, waiting for transfers between devices: 7.05 us -> 7.45 us  [exchange_sum(): lax.ppermute(value, axis, [(i, (i + step) % count) for i in range(count)])]
  transfers between devices with their start and end apart: 9 -> 13, of which waited for: 7 -> 7; matrix products, arithmetic and copies ran while one was open for 3% -> 3% of each run, Pallas kernels for 0% -> 0%
where the time goes in v10:
time: 172 us
  waiting for transfers between devices  83.2 us (48%)
  Pallas kernels  37.1 us (22%)
  starting transfers between devices  25.3 us (15%)
  between operations  14.9 us (9%)
  other arithmetic  6.38 us (4%)
  local copies, waits for them, and re-layouts  3.7 us (2%)
    all_gather x1, waiting for transfers between devices, shards(): lax.all_gather(xor_gather(payload, order), 'walker', axis=0, tiled=True)  66.1 us
    pallas_call x1, Pallas kernels, propagate(): pl.pallas_call(prop_kernel, out_shape=jax.ShapeDtypeStruct((orbitals, row...  27.1 us
    ppermute x7, starting transfers between devices, exchange_sum(): lax.ppermute(value, axis, [(i, (i + step) % count) for i in range(count)])  12.5 us
    pallas_call x1, Pallas kernels, tile_bias(): pl.pallas_call(bias_kernel, out_shape=[jax.ShapeDtypeStruct((tiles_total,...  10.1 us
    ppermute x3, waiting for transfers between devices, xor_gather(): other = lax.ppermute(x, axis, [(i, i ^ step) for i in range(count)])  9.57 us
    ppermute x7, waiting for transfers between devices, exchange_sum(): lax.ppermute(value, axis, [(i, (i + step) % count) for i in range(count)])  7.45 us
    ppermute x3, starting transfers between devices, xor_gather(): other = lax.ppermute(x, axis, [(i, i ^ step) for i in range(count)])  6.98 us
    ppermute x2, starting transfers between devices, shift_from(): lax.ppermute(value, axis, [(i, i + steps) for i in range(count - steps)])  5.82 us
  transfers between devices with their start and end apart: 13, of which 7 were waited for; matrix products, arithmetic and copies ran while one was open for 3% of the time, Pallas kernels for 0%

profile of v10, /device:TPU:2, one launch (start us, length us, event | category | flops | bytes accessed | tf_op | source)
XLA Modules:
  0.0 171.9 jit_solution(8307742677963601478)
XLA Ops:
  8.1 2.1 %collective-permute-start = (bf16[1,144,128]{2,1,0:T(8,128)(2,1)S(1)}, bf16[1,144,128]{2,1,0:T(8,128)(2,1)S(1)}, u32[]{:S(2)}, u32[]{:S(2)}) collective-permute-start(bf16[1,144,128]{2,1,0:T(8,128)(2,1)S(1)} %pad_maximum_fusion.3), channel_id=1, source_target_pairs={{0,4},{1,5},{2,6},{3,7},{4,0},{5,1},{6,2},{7,3},{8,12},{9,13},{10,... | collective-permute-start | bytes 110600 | tf_op jit(solution)/shard_map/ppermute | solution.py:157
  10.2 3.3 %collective-permute-done = bf16[1,144,128]{2,1,0:T(8,128)(2,1)S(1)} collective-permute-done((bf16[1,144,128]{2,1,0:T(8,128)(2,1)S(1)}, bf16[1,144,128]{2,1,0:T(8,128)(2,1)S(1)}, u32[]{:S(2)}, u32[]{:S(2)}) %collective-permute-start) | collective-permute-done | bytes 36896 | tf_op jit(solution)/shard_map/ppermute | solution.py:157
  14.3 3.2 %collective-permute-start.1 = (bf16[2,144,128]{2,1,0:T(8,128)(2,1)S(1)}, bf16[2,144,128]{2,1,0:T(8,128)(2,1)S(1)}, u32[]{:S(2)}, u32[]{:S(2)}) collective-permute-start(bf16[2,144,128]{2,1,0:T(8,128)(2,1)S(1)} %pad_maximum_fusion.2), channel_id=1, source_target_pairs={{0,2},{1,3},{2,0},{3,1},{4,6},{5,7},{6,4},{7,5},{8,10},{9,11},{10,... | collective-permute-start | bytes 221192 | tf_op jit(solution)/shard_map/ppermute | solution.py:157
  17.5 2.7 %collective-permute-done.1 = bf16[2,144,128]{2,1,0:T(8,128)(2,1)S(1)} collective-permute-done((bf16[2,144,128]{2,1,0:T(8,128)(2,1)S(1)}, bf16[2,144,128]{2,1,0:T(8,128)(2,1)S(1)}, u32[]{:S(2)}, u32[]{:S(2)}) %collective-permute-start.1) | collective-permute-done | bytes 73760 | tf_op jit(solution)/shard_map/ppermute | solution.py:157
  20.9 1.7 collective-permute-start.2
  22.6 3.6 %collective-permute-done.2 = bf16[4,144,128]{2,1,0:T(8,128)(2,1)S(1)} collective-permute-done((bf16[4,144,128]{2,1,0:T(8,128)(2,1)S(1)}, bf16[4,144,128]{2,1,0:T(8,128)(2,1)S(1)}, u32[]{:S(2)}, u32[]{:S(2)}) %collective-permute-start.2) | collective-permute-done | bytes 147488 | tf_op jit(solution)/shard_map/ppermute | solution.py:157
  26.1 1.5 pad_maximum_fusion
  27.7 1.2 copy.17
  28.9 1.9 %collective-permute-start.3 = (bf16[1,25,2048]{1,2,0:T(8,128)(2,1)S(1)}, bf16[1,25,2048]{1,2,0:T(8,128)(2,1)S(1)}, u32[]{:S(2)}, u32[]{:S(2)}) collective-permute-start(bf16[1,25,2048]{1,2,0:T(8,128)(2,1)S(1)} %copy.17), channel_id=1, source_target_pairs={{0,8},{8,16},{16,24},{24,32},{32,40},{40,48},{48,56},{56,64},{64,7... | collective-permute-start | bytes 307208 | tf_op jit(solution)/shard_map/ppermute | solution.py:19
  30.8 3.9 %collective-permute-start.4 = (bf16[1,25,200]{2,1,0:T(8,128)(2,1)}, bf16[1,25,200]{2,1,0:T(8,128)(2,1)S(1)}, u32[]{:S(2)}, u32[]{:S(2)}) collective-permute-start(bf16[1,25,200]{2,1,0:T(8,128)(2,1)} %param.11), channel_id=1, source_target_pairs={{0,8},{8,16},{16,24},{24,32},{32,40},{40,48},{48,56},{56,64},{64,7... | collective-permute-start | bytes 30008 | tf_op jit(solution)/shard_map/ppermute | solution.py:19
  35.9 1.0 convolution_convert_fusion
  36.9 66.1 %all-gather.2.cloned.1.call-done.refs_4_ = bf16[256,144,128]{2,1,0:T(8,128)(2,1)} async-done(((bf16[8,144,128]{2,1,0:T(8,128)(2,1)}), bf16[256,144,128]{2,1,0:T(8,128)(2,1)}) %all-gather.2.cloned.1.call-update) | async-done | bytes 9437200 | tf_op jit(solution)/shard_map/all_gather | solution.py:193
  103.0 1.2 convert_reduce_fusion
  106.0 10.1 %shard_map.73 = f32[256,128]{1,0:T(8,128)S(1)} custom-call(s32[256]{0:T(256)S(1)} %get-tuple-element.18.refs_0_, s32[256]{0:T(256)S(1)} %get-tuple-element.17.refs_1_, bf16[2048,32]{1,0:T(8,128)(2,1)S(1)} %pad_bitcast_fusion.refs_2_.refs_3_, bf16[32,2048]{1,0:T(8,128)(2,1)S(1)} %pad.14.refs_3_, bf16[256,144,128]{2,1,0:T(8,128)(2,1)} %all-gather.2.cloned.1.call-done.refs_4_), custom_call_target="tpu_custom_call" | custom-call | tf_op jit(solution)/shard_map/pallas_call | solution.py:77
  116.2 2.9 %collective-permute-start.7 = (f32[64]{0:T(128)S(1)}, f32[64]{0:T(128)S(1)}, u32[]{:S(2)}, u32[]{:S(2)}) collective-permute-start(f32[64]{0:T(128)S(1)} %select_reduce_fusion.3), channel_id=1, source_target_pairs={{0,3},{1,4},{2,5},{3,6},{4,7},{5,0},{6,1},{7,2},{8,11},{9,12},{10,... | collective-permute-start | bytes 776 | tf_op jit(solution)/shard_map/ppermute | solution.py:26
  119.1 2.0 %collective-permute-start.8 = (f32[64]{0:T(128)S(1)}, f32[64]{0:T(128)S(1)}, u32[]{:S(2)}, u32[]{:S(2)}) collective-permute-start(f32[64]{0:T(128)S(1)} %select_reduce_fusion.3), channel_id=1, source_target_pairs={{0,4},{1,5},{2,6},{3,7},{4,0},{5,1},{6,2},{7,3},{8,12},{9,13},{10,... | collective-permute-start | bytes 776 | tf_op jit(solution)/shard_map/ppermute | solution.py:26
  121.1 1.7 %collective-permute-start.9 = (f32[64]{0:T(128)S(1)}, f32[64]{0:T(128)S(1)}, u32[]{:S(2)}, u32[]{:S(2)}) collective-permute-start(f32[64]{0:T(128)S(1)} %select_reduce_fusion.3), channel_id=1, source_target_pairs={{0,5},{1,6},{2,7},{3,0},{4,1},{5,2},{6,3},{7,4},{8,13},{9,14},{10,... | collective-permute-start | bytes 776 | tf_op jit(solution)/shard_map/ppermute | solution.py:26
  122.9 3.9 %collective-permute-start.10 = (f32[64]{0:T(128)S(1)}, f32[64]{0:T(128)S(1)}, u32[]{:S(2)}, u32[]{:S(2)}) collective-permute-start(f32[64]{0:T(128)S(1)} %select_reduce_fusion.3), channel_id=1, source_target_pairs={{0,6},{1,7},{2,0},{3,1},{4,2},{5,3},{6,4},{7,5},{8,14},{9,15},{10,... | collective-permute-start | bytes 776 | tf_op jit(solution)/shard_map/ppermute | solution.py:26
  126.8 1.2 collective-permute-start.11
  128.8 1.5 collective-permute-done.11
  130.3 4.8 %collective-permute-done.5 = f32[64]{0:T(128)S(1)} collective-permute-done((f32[64]{0:T(128)S(1)}, f32[64]{0:T(128)S(1)}, u32[]{:S(2)}, u32[]{:S(2)}) %collective-permute-start.5) | collective-permute-done | bytes 288 | tf_op jit(solution)/shard_map/ppermute | solution.py:26
  135.1 1.2 collective-permute-done.6
  137.0 27.1 %shard_map.74 = bf16[2048,32]{1,0:T(8,128)(2,1)S(1)} custom-call(s32[256]{0:T(256)S(1)} %get-tuple-element.18.refs_0_, s32[256]{0:T(256)S(1)} %get-tuple-element.17.refs_1_, f32[256]{0:T(256)S(1)} %select_reduce_fusion.2.refs_2_, bf16[2048,32]{1,0:T(8,128)(2,1)S(1)} %pad_bitcast_fusion.refs_2_.refs_3_, ...), custom_call_target="tpu_custom_call" | custom-call | tf_op jit(solution)/shard_map/pallas_call | solution.py:136
  164.2 0.9 copy.19
  (41 shorter events, 6.5 us)
Async XLA Ops:
  6.5 29.4 %copy-start = (bf16[200,2048]{1,0:T(8,128)(2,1)S(1)}, bf16[200,2048]{1,0:T(8,128)(2,1)}, u32[]{:S(2)}) copy-start(bf16[200,2048]{1,0:T(8,128)(2,1)} %param.12) | copy-start | bytes 2457604
  6.5 130.4 %copy-start.1 = (f32[1,64]{1,0:T(1,128)S(1)}, f32[1,64]{1,0:T(1,128)}, u32[]{:S(2)}) copy-start(f32[1,64]{1,0:T(1,128)} %param.15) | copy-start | bytes 772
  6.5 96.5 %all-gather.2.cloned.1.call-start = ((), (), s32[]{:S(2)}) async-start(), calls=%async_computation | async-start | bytes 9732096 | tf_op jit(solution)/shard_map/all_gather | solution.py:193
  8.1 5.5 %collective-permute-start = (bf16[1,144,128]{2,1,0:T(8,128)(2,1)S(1)}, bf16[1,144,128]{2,1,0:T(8,128)(2,1)S(1)}, u32[]{:S(2)}, u32[]{:S(2)}) collective-permute-start(bf16[1,144,128]{2,1,0:T(8,128)(2,1)S(1)} %pad_maximum_fusion.3), channel_id=1, source_target_pairs={{0,4},{1,5},{2,6},{3,7},{4,0},{5,1},{6,2},{7,3},{8,12},{9,13},{10,... | collective-permute-start | bytes 110600 | tf_op jit(solution)/shard_map/ppermute | solution.py:157
  14.3 5.9 %collective-permute-start.1 = (bf16[2,144,128]{2,1,0:T(8,128)(2,1)S(1)}, bf16[2,144,128]{2,1,0:T(8,128)(2,1)S(1)}, u32[]{:S(2)}, u32[]{:S(2)}) collective-permute-start(bf16[2,144,128]{2,1,0:T(8,128)(2,1)S(1)} %pad_maximum_fusion.2), channel_id=1, source_target_pairs={{0,2},{1,3},{2,0},{3,1},{4,6},{5,7},{6,4},{7,5},{8,10},{9,11},{10,... | collective-permute-start | bytes 221192 | tf_op jit(solution)/shard_map/ppermute | solution.py:157
  20.9 5.2 %collective-permute-start.2 = (bf16[4,144,128]{2,1,0:T(8,128)(2,1)S(1)}, bf16[4,144,128]{2,1,0:T(8,128)(2,1)S(1)}, u32[]{:S(2)}, u32[]{:S(2)}) collective-permute-start(bf16[4,144,128]{2,1,0:T(8,128)(2,1)S(1)} %pad_maximum_fusion.1), channel_id=1, source_target_pairs={{0,1},{1,0},{2,3},{3,2},{4,5},{5,4},{6,7},{7,6},{8,9},{9,8},{10,11... | collective-permute-start | bytes 442376 | tf_op jit(solution)/shard_map/ppermute | solution.py:157
  28.9 76.6 %collective-permute-start.3 = (bf16[1,25,2048]{1,2,0:T(8,128)(2,1)S(1)}, bf16[1,25,2048]{1,2,0:T(8,128)(2,1)S(1)}, u32[]{:S(2)}, u32[]{:S(2)}) collective-permute-start(bf16[1,25,2048]{1,2,0:T(8,128)(2,1)S(1)} %copy.17), channel_id=1, source_target_pairs={{0,8},{8,16},{16,24},{24,32},{32,40},{40,48},{48,56},{56,64},{64,7... | collective-permute-start | bytes 307208 | tf_op jit(solution)/shard_map/ppermute | solution.py:19
  30.8 74.9 %collective-permute-start.4 = (bf16[1,25,200]{2,1,0:T(8,128)(2,1)}, bf16[1,25,200]{2,1,0:T(8,128)(2,1)S(1)}, u32[]{:S(2)}, u32[]{:S(2)}) collective-permute-start(bf16[1,25,200]{2,1,0:T(8,128)(2,1)} %param.11), channel_id=1, source_target_pairs={{0,8},{8,16},{16,24},{24,32},{32,40},{40,48},{48,56},{56,64},{64,7... | collective-permute-start | bytes 30008 | tf_op jit(solution)/shard_map/ppermute | solution.py:19
  116.2 11.7 %collective-permute-start.7 = (f32[64]{0:T(128)S(1)}, f32[64]{0:T(128)S(1)}, u32[]{:S(2)}, u32[]{:S(2)}) collective-permute-start(f32[64]{0:T(128)S(1)} %select_reduce_fusion.3), channel_id=1, source_target_pairs={{0,3},{1,4},{2,5},{3,6},{4,7},{5,0},{6,1},{7,2},{8,11},{9,12},{10,... | collective-permute-start | bytes 776 | tf_op jit(solution)/shard_map/ppermute | solution.py:26
  119.1 9.7 %collective-permute-start.8 = (f32[64]{0:T(128)S(1)}, f32[64]{0:T(128)S(1)}, u32[]{:S(2)}, u32[]{:S(2)}) collective-permute-start(f32[64]{0:T(128)S(1)} %select_reduce_fusion.3), channel_id=1, source_target_pairs={{0,4},{1,5},{2,6},{3,7},{4,0},{5,1},{6,2},{7,3},{8,12},{9,13},{10,... | collective-permute-start | bytes 776 | tf_op jit(solution)/shard_map/ppermute | solution.py:26
  121.1 7.7 %collective-permute-start.9 = (f32[64]{0:T(128)S(1)}, f32[64]{0:T(128)S(1)}, u32[]{:S(2)}, u32[]{:S(2)}) collective-permute-start(f32[64]{0:T(128)S(1)} %select_reduce_fusion.3), channel_id=1, source_target_pairs={{0,5},{1,6},{2,7},{3,0},{4,1},{5,2},{6,3},{7,4},{8,13},{9,14},{10,... | collective-permute-start | bytes 776 | tf_op jit(solution)/shard_map/ppermute | solution.py:26
  122.9 5.9 %collective-permute-start.10 = (f32[64]{0:T(128)S(1)}, f32[64]{0:T(128)S(1)}, u32[]{:S(2)}, u32[]{:S(2)}) collective-permute-start(f32[64]{0:T(128)S(1)} %select_reduce_fusion.3), channel_id=1, source_target_pairs={{0,6},{1,7},{2,0},{3,1},{4,2},{5,3},{6,4},{7,5},{8,14},{9,15},{10,... | collective-permute-start | bytes 776 | tf_op jit(solution)/shard_map/ppermute | solution.py:26
  126.8 3.6 %collective-permute-start.11 = (f32[64]{0:T(128)S(1)}, f32[64]{0:T(128)S(1)}, u32[]{:S(2)}, u32[]{:S(2)}) collective-permute-start(f32[64]{0:T(128)S(1)} %select_reduce_fusion.3), channel_id=1, source_target_pairs={{0,7},{1,0},{2,1},{3,2},{4,3},{5,4},{6,5},{7,6},{8,15},{9,8},{10,9... | collective-permute-start | bytes 776 | tf_op jit(solution)/shard_map/ppermute | solution.py:26
  127.9 7.2 %collective-permute-start.5 = (f32[64]{0:T(128)S(1)}, f32[64]{0:T(128)S(1)}, u32[]{:S(2)}, u32[]{:S(2)}) collective-permute-start(f32[64]{0:T(128)S(1)} %select_reduce_fusion.3), channel_id=1, source_target_pairs={{0,1},{1,2},{2,3},{3,4},{4,5},{5,6},{6,7},{7,0},{8,9},{9,10},{10,1... | collective-permute-start | bytes 776 | tf_op jit(solution)/shard_map/ppermute | solution.py:26
  128.8 7.5 %collective-permute-start.6 = (f32[64]{0:T(128)S(1)}, f32[64]{0:T(128)S(1)}, u32[]{:S(2)}, u32[]{:S(2)}) collective-permute-start(f32[64]{0:T(128)S(1)} %select_reduce_fusion.3), channel_id=1, source_target_pairs={{0,2},{1,3},{2,4},{3,5},{4,6},{5,7},{6,0},{7,1},{8,10},{9,11},{10,... | collective-permute-start | bytes 776 | tf_op jit(solution)/shard_map/ppermute | solution.py:26
Sparse Core Ops, SparseCore 0:
  27.8 75.2 all-gather.1

commit v11 on v7

--- a/solution.py
+++ b/solution.py
@@ -28,109 +28,128 @@
     return value
 
 
-def bias_kernel(*refs):
-    count = len(STREAMS)
-    rbs, cbs = refs[:count], refs[count:2 * count]
-    pt_ref, g_ref = refs[2 * count], refs[2 * count + 1]
-    parts = refs[2 * count + 2:3 * count + 2]
-    outs = refs[3 * count + 2:4 * count + 2]
-    m_ref = refs[-1]
+CHUNK = 32
+
+
+def bias_kernel(rb_ref, cb_ref, pt_ref, g_ref, part_ref, out_ref, m_ref):
+    step = pl.program_id(0)
     blocks, size, _ = m_ref.shape
-    for a in range(blocks):
-        m_ref[a] = jnp.dot(
-            pt_ref[a * size:(a + 1) * size, :], g_ref[...], preferred_element_type=jnp.float32
-        )
-
-    def one(t, carry):
-        for (_, low, high), rb_ref, cb_ref, part_ref, out_ref in zip(STREAMS, rbs, cbs, parts, outs):
-            col = pl.multiple_of(cb_ref[t] * size, size)
-            blk = m_ref[rb_ref[t], low:high, pl.ds(col, size)]
-            prod = blk * part_ref[t, 0:high - low, :].astype(jnp.float32)
-            out_ref[pl.ds(t, 1), :] = jnp.sum(prod, axis=0, keepdims=True)
+    chunk = part_ref.shape[0]
+
+    @pl.when(step == 0)
+    def _():
+        for a in range(blocks):
+            m_ref[a] = jnp.dot(
+                pt_ref[a * size:(a + 1) * size, :], g_ref[...], preferred_element_type=jnp.float32
+            )
+
+    def one(j, carry):
+        t = step * chunk + j
+        col = pl.multiple_of(cb_ref[t] * size, size)
+        blk = m_ref[rb_ref[t], :, pl.ds(col, size)]
+        prod = blk * part_ref[j, 0:size, :].astype(jnp.float32)
+        out_ref[pl.ds(j, 1), :] = jnp.sum(prod, axis=0, keepdims=True)
         return carry
 
-    lax.fori_loop(0, parts[0].shape[0], one, 0, unroll=2)
+    lax.fori_loop(0, chunk, one, 0, unroll=2)
 
 
 def tile_bias(panel_t, green, parts, rbs, cbs):
-    tiles_total, _, size = parts[0].shape
+    part = parts[0]
+    tiles_total, rows, size = part.shape
     orbitals = green.shape[1]
     blocks = orbitals // size
-    count = len(parts)
     smem = pl.BlockSpec(memory_space=pltpu.SMEM)
-    vmem = pl.BlockSpec(memory_space=pltpu.VMEM)
-    return pl.pallas_call(
+    return [pl.pallas_call(
         bias_kernel,
-        out_shape=[jax.ShapeDtypeStruct((tiles_total, size), jnp.float32)] * count,
-        in_specs=[smem] * (2 * count) + [vmem] * (2 + count),
-        out_specs=[vmem] * count,
+        out_shape=jax.ShapeDtypeStruct((tiles_total, size), jnp.float32),
+        grid=(tiles_total // CHUNK,),
+        in_specs=[
+            smem,
+            smem,
+            pl.BlockSpec(panel_t.shape, lambda i: (0, 0)),
+            pl.BlockSpec(green.shape, lambda i: (0, 0)),
+            pl.BlockSpec((CHUNK, rows, size), lambda i: (i, 0, 0)),
+        ],
+        out_specs=pl.BlockSpec((CHUNK, size), lambda i: (i, 0)),
         scratch_shapes=[pltpu.VMEM((blocks, size, orbitals), jnp.float32)],
-        compiler_params=pltpu.CompilerParams(vmem_limit_bytes=48 * 1024 * 1024),
+        compiler_params=pltpu.CompilerParams(
+            dimension_semantics=("arbitrary",), vmem_limit_bytes=48 * 1024 * 1024
+        ),
         interpret=INTERPRET,
-    )(*rbs, *cbs, panel_t, green, *parts)
-
-
-def prop_kernel(*refs):
-    count = len(STREAMS)
-    rbs, cbs, ss = refs[:count], refs[count:2 * count], refs[2 * count:3 * count]
-    x_ref = refs[3 * count]
-    parts = refs[3 * count + 1:4 * count + 1]
-    out_ref, hi_ref, lo_ref, y_ref = refs[4 * count + 1:]
+    )(rbs[0], cbs[0], panel_t, green, part)]
+
+
+def prop_kernel(rb_ref, cb_ref, s_ref, x_ref, part_ref, out_ref, hi_ref, lo_ref, y_ref):
+    step = pl.program_id(0)
     orbitals = hi_ref.shape[0]
-    size = parts[0].shape[2]
-    hi_ref[...] = jnp.zeros(hi_ref.shape, hi_ref.dtype)
-    lo_ref[...] = jnp.zeros(lo_ref.shape, lo_ref.dtype)
-
-    def build(t, carry):
-        for (_, low, high), rb_ref, cb_ref, s_ref, part_ref in zip(STREAMS, rbs, cbs, ss, parts):
-            rows = pl.ds(pl.multiple_of(rb_ref[t] * size + low, 16), high - low)
-            cols = pl.ds(pl.multiple_of(cb_ref[t] * size, size), size)
-            whole = (
-                hi_ref[rows, cols].astype(jnp.float32)
-                + lo_ref[rows, cols].astype(jnp.float32)
-                + s_ref[t] * part_ref[t, 0:high - low, :].astype(jnp.float32)
-            )
-            upper = whole.astype(jnp.bfloat16)
-            hi_ref[rows, cols] = upper
-            lo_ref[rows, cols] = (whole - upper.astype(jnp.float32)).astype(jnp.bfloat16)
+    size = part_ref.shape[2]
+    chunk = part_ref.shape[0]
+
+    @pl.when(step == 0)
+    def _():
+        hi_ref[...] = jnp.zeros(hi_ref.shape, hi_ref.dtype)
+        lo_ref[...] = jnp.zeros(lo_ref.shape, lo_ref.dtype)
+
+    def build(j, carry):
+        t = step * chunk + j
+        rows = pl.ds(pl.multiple_of(rb_ref[t] * size, size), size)
+        cols = pl.ds(pl.multiple_of(cb_ref[t] * size, size), size)
+        whole = (
+            hi_ref[rows, cols].astype(jnp.float32)
+            + lo_ref[rows, cols].astype(jnp.float32)
+            + s_ref[t] * part_ref[j, 0:size, :].astype(jnp.float32)
+        )
+        upper = whole.astype(jnp.bfloat16)
+        hi_ref[rows, cols] = upper
+        lo_ref[rows, cols] = (whole - upper.astype(jnp.float32)).astype(jnp.bfloat16)
         return carry
 
-    lax.fori_loop(0, parts[0].shape[0], build, 0)
-
-    chunk = 512
-    series = x_ref[...]
-    running = series.astype(jnp.float32)
-    for degree in range(1, TERMS + 1):
-        for c in range(orbitals // chunk):
-            span = slice(c * chunk, (c + 1) * chunk)
-            y_ref[span, :] = jnp.dot(
-                hi_ref[span, :], series, preferred_element_type=jnp.float32
-            ) + jnp.dot(lo_ref[span, :], series, preferred_element_type=jnp.float32)
-        series = (y_ref[...] / degree).astype(jnp.bfloat16)
-        running = running + series.astype(jnp.float32)
-    out_ref[...] = running.astype(out_ref.dtype)
+    lax.fori_loop(0, chunk, build, 0)
+
+    @pl.when(step == pl.num_programs(0) - 1)
+    def _():
+        span_rows = 512
+        series = x_ref[...]
+        running = series.astype(jnp.float32)
+        for degree in range(1, TERMS + 1):
+            for c in range(orbitals // span_rows):
+                span = slice(c * span_rows, (c + 1) * span_rows)
+                y_ref[span, :] = jnp.dot(
+                    hi_ref[span, :], series, preferred_element_type=jnp.float32
+                ) + jnp.dot(lo_ref[span, :], series, preferred_element_type=jnp.float32)
+            series = (y_ref[...] / degree).astype(jnp.bfloat16)
+            running = running + series.astype(jnp.float32)
+        out_ref[...] = running.astype(out_ref.dtype)
 
 
 def propagate(x0, parts, rbs, cbs, ss):
-    size = parts[0].shape[2]
-    orbitals, rows = x0.shape
-    blocks = orbitals // size
-    count = len(parts)
+    part = parts[0]
+    tiles_total, rows, size = part.shape
+    orbitals, width = x0.shape
     smem = pl.BlockSpec(memory_space=pltpu.SMEM)
-    vmem = pl.BlockSpec(memory_space=pltpu.VMEM)
     return pl.pallas_call(
         prop_kernel,
-        out_shape=jax.ShapeDtypeStruct((orbitals, rows), jnp.bfloat16),
-        in_specs=[smem] * (3 * count) + [vmem] * (1 + count),
-        out_specs=vmem,
+        out_shape=jax.ShapeDtypeStruct((orbitals, width), jnp.bfloat16),
+        grid=(tiles_total // CHUNK,),
+        in_specs=[
+            smem,
+            smem,
+            smem,
+            pl.BlockSpec(x0.shape, lambda i: (0, 0)),
+            pl.BlockSpec((CHUNK, rows, size), lambda i: (i, 0, 0)),
+        ],
+        out_specs=pl.BlockSpec((orbitals, width), lambda i: (0, 0)),
         scratch_shapes=[
             pltpu.VMEM((orbitals, orbitals), jnp.bfloat16),
             pltpu.VMEM((orbitals, orbitals), jnp.bfloat16),
-            pltpu.VMEM((orbitals, rows), jnp.float32),
+            pltpu.VMEM((orbitals, width), jnp.float32),
         ],
-        compiler_params=pltpu.CompilerParams(vmem_limit_bytes=48 * 1024 * 1024),
+        compiler_params=pltpu.CompilerParams(
+            dimension_semantics=("arbitrary",), vmem_limit_bytes=48 * 1024 * 1024
+        ),
         interpret=INTERPRET,
-    )(*rbs, *cbs, *ss, x0, *parts)
+    )(rbs[0], cbs[0], ss[0], x0, part)
 
 
 STREAMS = ((None, 0, 128),)

time: 166 us -> 164 us (0.988)
  no operation moved by 1% of the time
where the time goes in v11:
time: 164 us
  waiting for transfers between devices  82.8 us (50%)
  Pallas kernels  35.6 us (22%)
  starting transfers between devices  19.6 us (12%)
  between operations  14.9 us (9%)
  other arithmetic  6.27 us (4%)
  local copies, waits for them, and re-layouts  3.12 us (2%)
    all_gather x1, waiting for transfers between devices, shards(): lax.all_gather(xor_gather(payload, order), 'walker', axis=0, tiled=True)  66.1 us
    pallas_call x1, Pallas kernels, propagate(): pl.pallas_call(prop_kernel, out_shape=jax.ShapeDtypeStruct((orbitals, wid...  25.3 us
    pallas_call x1, Pallas kernels, tile_bias(): pl.pallas_call(bias_kernel, out_shape=jax.ShapeDtypeStruct((tiles_total,...  10.3 us
    ppermute x3, waiting for transfers between devices, xor_gather(): other = lax.ppermute(x, axis, [(i, i ^ step) for i in range(count)])  9.57 us
    ppermute x3, waiting for transfers between devices, butterfly_sum(): lax.ppermute(value, axis, [(i, i ^ step) for i in range(count)])  7.05 us
    ppermute x3, starting transfers between devices, xor_gather(): other = lax.ppermute(x, axis, [(i, i ^ step) for i in range(count)])  6.98 us
    ppermute x3, starting transfers between devices, butterfly_sum(): lax.ppermute(value, axis, [(i, i ^ step) for i in range(count)])  6.75 us
    ppermute x2, starting transfers between devices, shift_from(): lax.ppermute(value, axis, [(i, i + steps) for i in range(count - steps)])  5.82 us
  transfers between devices with their start and end apart: 9, of which 7 were waited for; matrix products, arithmetic and copies ran while one was open for 3% of the time, Pallas kernels for 0%

profile of v11, /device:TPU:2, one launch (start us, length us, event | category | flops | bytes accessed | tf_op | source)
XLA Modules:
  0.0 163.5 jit_solution(12340180834103599115)
XLA Ops:
  8.1 2.1 %collective-permute-start = (bf16[1,144,128]{2,1,0:T(8,128)(2,1)S(1)}, bf16[1,144,128]{2,1,0:T(8,128)(2,1)S(1)}, u32[]{:S(2)}, u32[]{:S(2)}) collective-permute-start(bf16[1,144,128]{2,1,0:T(8,128)(2,1)S(1)} %pad_maximum_fusion.3), channel_id=1, source_target_pairs={{0,4},{1,5},{2,6},{3,7},{4,0},{5,1},{6,2},{7,3},{8,12},{9,13},{10,... | collective-permute-start | bytes 110600 | tf_op jit(solution)/shard_map/ppermute | solution.py:161
  10.2 3.3 %collective-permute-done = bf16[1,144,128]{2,1,0:T(8,128)(2,1)S(1)} collective-permute-done((bf16[1,144,128]{2,1,0:T(8,128)(2,1)S(1)}, bf16[1,144,128]{2,1,0:T(8,128)(2,1)S(1)}, u32[]{:S(2)}, u32[]{:S(2)}) %collective-permute-start) | collective-permute-done | bytes 36896 | tf_op jit(solution)/shard_map/ppermute | solution.py:161
  14.3 3.2 %collective-permute-start.1 = (bf16[2,144,128]{2,1,0:T(8,128)(2,1)S(1)}, bf16[2,144,128]{2,1,0:T(8,128)(2,1)S(1)}, u32[]{:S(2)}, u32[]{:S(2)}) collective-permute-start(bf16[2,144,128]{2,1,0:T(8,128)(2,1)S(1)} %pad_maximum_fusion.2), channel_id=1, source_target_pairs={{0,2},{1,3},{2,0},{3,1},{4,6},{5,7},{6,4},{7,5},{8,10},{9,11},{10,... | collective-permute-start | bytes 221192 | tf_op jit(solution)/shard_map/ppermute | solution.py:161
  17.5 2.7 %collective-permute-done.1 = bf16[2,144,128]{2,1,0:T(8,128)(2,1)S(1)} collective-permute-done((bf16[2,144,128]{2,1,0:T(8,128)(2,1)S(1)}, bf16[2,144,128]{2,1,0:T(8,128)(2,1)S(1)}, u32[]{:S(2)}, u32[]{:S(2)}) %collective-permute-start.1) | collective-permute-done | bytes 73760 | tf_op jit(solution)/shard_map/ppermute | solution.py:161
  20.1 0.8 pad_maximum_fusion.1
  20.9 1.7 %collective-permute-start.2 = (bf16[4,144,128]{2,1,0:T(8,128)(2,1)S(1)}, bf16[4,144,128]{2,1,0:T(8,128)(2,1)S(1)}, u32[]{:S(2)}, u32[]{:S(2)}) collective-permute-start(bf16[4,144,128]{2,1,0:T(8,128)(2,1)S(1)} %pad_maximum_fusion.1), channel_id=1, source_target_pairs={{0,1},{1,0},{2,3},{3,2},{4,5},{5,4},{6,7},{7,6},{8,9},{9,8},{10,11... | collective-permute-start | bytes 442376 | tf_op jit(solution)/shard_map/ppermute | solution.py:161
  22.6 3.6 %collective-permute-done.2 = bf16[4,144,128]{2,1,0:T(8,128)(2,1)S(1)} collective-permute-done((bf16[4,144,128]{2,1,0:T(8,128)(2,1)S(1)}, bf16[4,144,128]{2,1,0:T(8,128)(2,1)S(1)}, u32[]{:S(2)}, u32[]{:S(2)}) %collective-permute-start.2) | collective-permute-done | bytes 147488 | tf_op jit(solution)/shard_map/ppermute | solution.py:161
  26.1 1.5 pad_maximum_fusion
  27.7 1.2 copy.17
  28.9 1.9 %collective-permute-start.3 = (bf16[1,25,2048]{1,2,0:T(8,128)(2,1)S(1)}, bf16[1,25,2048]{1,2,0:T(8,128)(2,1)S(1)}, u32[]{:S(2)}, u32[]{:S(2)}) collective-permute-start(bf16[1,25,2048]{1,2,0:T(8,128)(2,1)S(1)} %copy.17), channel_id=1, source_target_pairs={{0,8},{8,16},{16,24},{24,32},{32,40},{40,48},{48,56},{56,64},{64,7... | collective-permute-start | bytes 307208 | tf_op jit(solution)/shard_map/ppermute | solution.py:19
  30.8 3.9 %collective-permute-start.4 = (bf16[1,25,200]{2,1,0:T(8,128)(2,1)}, bf16[1,25,200]{2,1,0:T(8,128)(2,1)S(1)}, u32[]{:S(2)}, u32[]{:S(2)}) collective-permute-start(bf16[1,25,200]{2,1,0:T(8,128)(2,1)} %param.11), channel_id=1, source_target_pairs={{0,8},{8,16},{16,24},{24,32},{32,40},{40,48},{48,56},{56,64},{64,7... | collective-permute-start | bytes 30008 | tf_op jit(solution)/shard_map/ppermute | solution.py:19
  34.9 0.8 fusion.15
  35.9 1.0 convolution_convert_fusion
  36.9 66.1 %all-gather.2.cloned.1.call-done.part_ref = bf16[256,144,128]{2,1,0:T(8,128)(2,1)} async-done(((bf16[8,144,128]{2,1,0:T(8,128)(2,1)}), bf16[256,144,128]{2,1,0:T(8,128)(2,1)}) %all-gather.2.cloned.1.call-update) | async-done | bytes 9437200 | tf_op jit(solution)/shard_map/all_gather | solution.py:197
  103.0 1.2 convert_reduce_fusion
  106.0 10.3 %shard_map.73 = f32[256,128]{1,0:T(8,128)S(1)} custom-call(s32[256]{0:T(256)S(1)} %get-tuple-element.18.rb_ref, s32[256]{0:T(256)S(1)} %get-tuple-element.17.cb_ref, bf16[2048,32]{1,0:T(8,128)(2,1)S(1)} %pad_bitcast_fusion.pt_ref.x_ref, bf16[32,2048]{1,0:T(8,128)(2,1)S(1)} %pad.14.g_ref, bf16[256,144,128]{2,1,0:T(8,128)(2,1)} %all-gather.2.cloned.1.call-done.part_ref), custom_call_target="tpu_custom_call" | custom-call | tf_op jit(solution)/shard_map/pallas_call | solution.py:63
  116.5 1.6 collective-permute-start.5
  118.1 2.1 %collective-permute-done.5 = f32[64]{0:T(128)S(1)} collective-permute-done((f32[64]{0:T(128)S(1)}, f32[64]{0:T(128)S(1)}, u32[]{:S(2)}, u32[]{:S(2)}) %collective-permute-start.5) | collective-permute-done | bytes 288 | tf_op jit(solution)/shard_map/ppermute | solution.py:26
  120.2 3.0 %collective-permute-start.6 = (f32[64]{0:T(128)S(1)}, f32[64]{0:T(128)S(1)}, u32[]{:S(2)}, u32[]{:S(2)}) collective-permute-start(f32[64]{0:T(128)S(1)} %add.85), channel_id=1, source_target_pairs={{0,2},{1,3},{2,0},{3,1},{4,6},{5,7},{6,4},{7,5},{8,10},{9,11},{10,... | collective-permute-start | bytes 776 | tf_op jit(solution)/shard_map/ppermute | solution.py:26
  123.2 2.0 %collective-permute-done.6 = f32[64]{0:T(128)S(1)} collective-permute-done((f32[64]{0:T(128)S(1)}, f32[64]{0:T(128)S(1)}, u32[]{:S(2)}, u32[]{:S(2)}) %collective-permute-start.6) | collective-permute-done | bytes 288 | tf_op jit(solution)/shard_map/ppermute | solution.py:26
  125.3 2.1 %collective-permute-start.7 = (f32[64]{0:T(128)S(1)}, f32[64]{0:T(128)S(1)}, u32[]{:S(2)}, u32[]{:S(2)}) collective-permute-start(f32[64]{0:T(128)S(1)} %add.86), channel_id=1, source_target_pairs={{0,4},{1,5},{2,6},{3,7},{4,0},{5,1},{6,2},{7,3},{8,12},{9,13},{10,... | collective-permute-start | bytes 776 | tf_op jit(solution)/shard_map/ppermute | solution.py:26
  127.4 3.0 %collective-permute-done.7 = f32[64]{0:T(128)S(1)} collective-permute-done((f32[64]{0:T(128)S(1)}, f32[64]{0:T(128)S(1)}, u32[]{:S(2)}, u32[]{:S(2)}) %collective-permute-start.7) | collective-permute-done | bytes 288 | tf_op jit(solution)/shard_map/ppermute | solution.py:26
  130.5 25.3 %shard_map.74 = bf16[2048,32]{1,0:T(8,128)(2,1)S(1)} custom-call(s32[256]{0:T(256)S(1)} %get-tuple-element.18.rb_ref, s32[256]{0:T(256)S(1)} %get-tuple-element.17.cb_ref, f32[256]{0:T(256)S(1)} %select_reduce_fusion.2.s_ref, bf16[2048,32]{1,0:T(8,128)(2,1)S(1)} %pad_bitcast_fusion.pt_ref.x_ref, bf16[256,144,128]{2,1,0:T(8,128)(2,1)} %all-gather.2.cloned.1.call-done.part_ref), custom_call_target="tpu_custom_call" | custom-call | tf_op jit(solution)/shard_map/pallas_call | solution.py:131
  155.8 0.9 copy.19
  (29 shorter events, 3.4 us)
Async XLA Ops:
  6.5 29.4 %copy-start = (bf16[200,2048]{1,0:T(8,128)(2,1)S(1)}, bf16[200,2048]{1,0:T(8,128)(2,1)}, u32[]{:S(2)}) copy-start(bf16[200,2048]{1,0:T(8,128)(2,1)} %param.12) | copy-start | bytes 2457604
  6.5 123.8 %copy-start.1 = (f32[1,64]{1,0:T(1,128)S(1)}, f32[1,64]{1,0:T(1,128)}, u32[]{:S(2)}) copy-start(f32[1,64]{1,0:T(1,128)} %param.15) | copy-start | bytes 772
  6.5 96.5 %all-gather.2.cloned.1.call-start = ((), (), s32[]{:S(2)}) async-start(), calls=%async_computation | async-start | bytes 9732096 | tf_op jit(solution)/shard_map/all_gather | solution.py:197
  8.1 5.5 %collective-permute-start = (bf16[1,144,128]{2,1,0:T(8,128)(2,1)S(1)}, bf16[1,144,128]{2,1,0:T(8,128)(2,1)S(1)}, u32[]{:S(2)}, u32[]{:S(2)}) collective-permute-start(bf16[1,144,128]{2,1,0:T(8,128)(2,1)S(1)} %pad_maximum_fusion.3), channel_id=1, source_target_pairs={{0,4},{1,5},{2,6},{3,7},{4,0},{5,1},{6,2},{7,3},{8,12},{9,13},{10,... | collective-permute-start | bytes 110600 | tf_op jit(solution)/shard_map/ppermute | solution.py:161
  14.3 5.9 %collective-permute-start.1 = (bf16[2,144,128]{2,1,0:T(8,128)(2,1)S(1)}, bf16[2,144,128]{2,1,0:T(8,128)(2,1)S(1)}, u32[]{:S(2)}, u32[]{:S(2)}) collective-permute-start(bf16[2,144,128]{2,1,0:T(8,128)(2,1)S(1)} %pad_maximum_fusion.2), channel_id=1, source_target_pairs={{0,2},{1,3},{2,0},{3,1},{4,6},{5,7},{6,4},{7,5},{8,10},{9,11},{10,... | collective-permute-start | bytes 221192 | tf_op jit(solution)/shard_map/ppermute | solution.py:161
  20.9 5.2 %collective-permute-start.2 = (bf16[4,144,128]{2,1,0:T(8,128)(2,1)S(1)}, bf16[4,144,128]{2,1,0:T(8,128)(2,1)S(1)}, u32[]{:S(2)}, u32[]{:S(2)}) collective-permute-start(bf16[4,144,128]{2,1,0:T(8,128)(2,1)S(1)} %pad_maximum_fusion.1), channel_id=1, source_target_pairs={{0,1},{1,0},{2,3},{3,2},{4,5},{5,4},{6,7},{7,6},{8,9},{9,8},{10,11... | collective-permute-start | bytes 442376 | tf_op jit(solution)/shard_map/ppermute | solution.py:161
  28.9 76.6 %collective-permute-start.3 = (bf16[1,25,2048]{1,2,0:T(8,128)(2,1)S(1)}, bf16[1,25,2048]{1,2,0:T(8,128)(2,1)S(1)}, u32[]{:S(2)}, u32[]{:S(2)}) collective-permute-start(bf16[1,25,2048]{1,2,0:T(8,128)(2,1)S(1)} %copy.17), channel_id=1, source_target_pairs={{0,8},{8,16},{16,24},{24,32},{32,40},{40,48},{48,56},{56,64},{64,7... | collective-permute-start | bytes 307208 | tf_op jit(solution)/shard_map/ppermute | solution.py:19
  30.8 74.9 %collective-permute-start.4 = (bf16[1,25,200]{2,1,0:T(8,128)(2,1)}, bf16[1,25,200]{2,1,0:T(8,128)(2,1)S(1)}, u32[]{:S(2)}, u32[]{:S(2)}) collective-permute-start(bf16[1,25,200]{2,1,0:T(8,128)(2,1)} %param.11), channel_id=1, source_target_pairs={{0,8},{8,16},{16,24},{24,32},{32,40},{40,48},{48,56},{56,64},{64,7... | collective-permute-start | bytes 30008 | tf_op jit(solution)/shard_map/ppermute | solution.py:19
  116.5 3.7 %collective-permute-start.5 = (f32[64]{0:T(128)S(1)}, f32[64]{0:T(128)S(1)}, u32[]{:S(2)}, u32[]{:S(2)}) collective-permute-start(f32[64]{0:T(128)S(1)} %select_reduce_fusion.3), channel_id=1, source_target_pairs={{0,1},{1,0},{2,3},{3,2},{4,5},{5,4},{6,7},{7,6},{8,9},{9,8},{10,11... | collective-permute-start | bytes 776 | tf_op jit(solution)/shard_map/ppermute | solution.py:26
  120.2 5.1 %collective-permute-start.6 = (f32[64]{0:T(128)S(1)}, f32[64]{0:T(128)S(1)}, u32[]{:S(2)}, u32[]{:S(2)}) collective-permute-start(f32[64]{0:T(128)S(1)} %add.85), channel_id=1, source_target_pairs={{0,2},{1,3},{2,0},{3,1},{4,6},{5,7},{6,4},{7,5},{8,10},{9,11},{10,... | collective-permute-start | bytes 776 | tf_op jit(solution)/shard_map/ppermute | solution.py:26
  125.3 5.1 %collective-permute-start.7 = (f32[64]{0:T(128)S(1)}, f32[64]{0:T(128)S(1)}, u32[]{:S(2)}, u32[]{:S(2)}) collective-permute-start(f32[64]{0:T(128)S(1)} %add.86), channel_id=1, source_target_pairs={{0,4},{1,5},{2,6},{3,7},{4,0},{5,1},{6,2},{7,3},{8,12},{9,13},{10,... | collective-permute-start | bytes 776 | tf_op jit(solution)/shard_map/ppermute | solution.py:26
Sparse Core Ops, SparseCore 0:
  27.8 75.2 all-gather.1

commit v12 on v11

--- a/solution.py
+++ b/solution.py
@@ -193,14 +193,18 @@
     size = chol_tiles.shape[2]
     meta = jnp.zeros((1, 16, size), chol_tiles.dtype).at[0, 0, 0].set(copy_counts[0].astype(chol_tiles.dtype))
     payload = jnp.concatenate([chol_tiles, meta], axis=1)
-    order = (("vec", 4), ("vec", 2), ("vec", 1))
-    gathered = lax.all_gather(xor_gather(payload, order), "walker", axis=0, tiled=True)
+    vec_id = lax.axis_index("vec")
+    pieces = [payload] + [
+        lax.ppermute(payload, "vec", [(i, (i + step) % vecs) for i in range(vecs)])
+        for step in range(1, vecs)
+    ]
+    gathered = lax.all_gather(jnp.concatenate(pieces, axis=0), "walker", axis=0, tiled=True)
     tiles_rows = chol_tiles.shape[1]
     counts = gathered[::vecs, tiles_rows, 0].astype(jnp.float32)
     walkers = jnp.arange(counts.shape[0])
     surplus = jnp.sum(jnp.where(walkers < walker_id, counts, 0.0)) - walker_id.astype(jnp.float32)
     from_prev = surplus > 0.5
-    local = source_tiles(order) % vecs
+    local = (vec_id - jnp.arange(vecs, dtype=jnp.int32)) % vecs
     source = (walkers[:, None] * vecs + local[None, :]).reshape(-1)
     rbs = [pick(tile_blocks[:, 0], source)]
     cbs = [pick(tile_blocks[:, 1], source)]

time: 164 us -> 164 us (level)
  starting transfers between devices: 19.6 us -> 29.4 us
  waiting for transfers between devices: 82.8 us -> 75 us
  other arithmetic: 6.27 us -> 3.24 us
    ppermute x3 -> x7, starting transfers between devices: 6.98 us -> 15.9 us  [shards(): lax.ppermute(payload, 'vec', [(i, (i + step) % vecs) for i in range(vecs)])]
    ppermute x3 -> x7, waiting for transfers between devices: 9.57 us -> 2.22 us  [shards(): lax.ppermute(payload, 'vec', [(i, (i + step) % vecs) for i in range(vecs)])]
    concatenate x3 -> x0, other arithmetic: 3.03 us -> none  [xor_gather(): x = jnp.concatenate([x, other], axis=0)]
  transfers between devices with their start and end apart: 9 -> 13, of which waited for: 7 -> 6; matrix products, arithmetic and copies ran while one was open for 3% -> 3% of each run, Pallas kernels for 0% -> 0%
where the time goes in v12:
time: 164 us; the launch traced here: 163 us
  waiting for transfers between devices  75 us (46%)
  Pallas kernels  35.6 us (22%)
  starting transfers between devices  29.4 us (18%)
  between operations  15 us (9%)
  local copies, waits for them, and re-layouts  3.9 us (2%)
  other arithmetic  3.24 us (2%)
    all_gather x1, waiting for transfers between devices, shards(): lax.all_gather(jnp.concatenate(pieces, axis=0), 'walker', axis=0, tiled=T...  65.8 us
    pallas_call x1, Pallas kernels, propagate(): pl.pallas_call(prop_kernel, out_shape=jax.ShapeDtypeStruct((orbitals, wid...  25.3 us
    ppermute x7, starting transfers between devices, shards(): lax.ppermute(payload, 'vec', [(i, (i + step) % vecs) for i in range(vecs)])  15.9 us
    pallas_call x1, Pallas kernels, tile_bias(): pl.pallas_call(bias_kernel, out_shape=jax.ShapeDtypeStruct((tiles_total,...  10.3 us
    ppermute x3, waiting for transfers between devices, butterfly_sum(): lax.ppermute(value, axis, [(i, i ^ step) for i in range(count)])  7.03 us
    ppermute x3, starting transfers between devices, butterfly_sum(): lax.ppermute(value, axis, [(i, i ^ step) for i in range(count)])  6.77 us
    ppermute x2, starting transfers between devices, shift_from(): lax.ppermute(value, axis, [(i, i + steps) for i in range(count - steps)])  6.72 us
  transfers between devices with their start and end apart: 13, of which 6 were waited for; matrix products, arithmetic and copies ran while one was open for 3% of the time, Pallas kernels for 0%

profile of v12, /device:TPU:2, one launch (start us, length us, event | category | flops | bytes accessed | tf_op | source)
XLA Modules:
  0.0 163.4 jit_solution(10250741012582979555)
XLA Ops:
  7.3 0.8 fusion.2
  8.0 1.7 %collective-permute-start = (bf16[1,144,128]{2,1,0:T(8,128)(2,1)S(1)}, bf16[1,144,128]{2,1,0:T(8,128)(2,1)S(1)}, u32[]{:S(2)}, u32[]{:S(2)}) collective-permute-start(bf16[1,144,128]{2,1,0:T(8,128)(2,1)S(1)} %get-tuple-element.19), channel_id=1, source_target_pairs={{0,1},{1,2},{2,3},{3,4},{4,5},{5,6},{6,7},{7,0},{8,9},{9,10},{10,1... | collective-permute-start | bytes 110600 | tf_op jit(solution)/shard_map/ppermute | solution.py:198
  9.7 2.9 %collective-permute-start.1 = (bf16[1,144,128]{2,1,0:T(8,128)(2,1)S(1)}, bf16[1,144,128]{2,1,0:T(8,128)(2,1)S(1)}, u32[]{:S(2)}, u32[]{:S(2)}) collective-permute-start(bf16[1,144,128]{2,1,0:T(8,128)(2,1)S(1)} %get-tuple-element.19), channel_id=1, source_target_pairs={{0,2},{1,3},{2,4},{3,5},{4,6},{5,7},{6,0},{7,1},{8,10},{9,11},{10,... | collective-permute-start | bytes 110600 | tf_op jit(solution)/shard_map/ppermute | solution.py:198
  12.6 2.9 %collective-permute-start.2 = (bf16[1,144,128]{2,1,0:T(8,128)(2,1)S(1)}, bf16[1,144,128]{2,1,0:T(8,128)(2,1)S(1)}, u32[]{:S(2)}, u32[]{:S(2)}) collective-permute-start(bf16[1,144,128]{2,1,0:T(8,128)(2,1)S(1)} %get-tuple-element.19), channel_id=1, source_target_pairs={{0,3},{1,4},{2,5},{3,6},{4,7},{5,0},{6,1},{7,2},{8,11},{9,12},{10,... | collective-permute-start | bytes 110600 | tf_op jit(solution)/shard_map/ppermute | solution.py:198
  15.5 1.4 collective-permute-start.3
  16.9 2.2 %collective-permute-start.4 = (bf16[1,144,128]{2,1,0:T(8,128)(2,1)S(1)}, bf16[1,144,128]{2,1,0:T(8,128)(2,1)S(1)}, u32[]{:S(2)}, u32[]{:S(2)}) collective-permute-start(bf16[1,144,128]{2,1,0:T(8,128)(2,1)S(1)} %get-tuple-element.19), channel_id=1, source_target_pairs={{0,5},{1,6},{2,7},{3,0},{4,1},{5,2},{6,3},{7,4},{8,13},{9,14},{10,... | collective-permute-start | bytes 110600 | tf_op jit(solution)/shard_map/ppermute | solution.py:198
  19.2 3.0 %collective-permute-start.5 = (bf16[1,144,128]{2,1,0:T(8,128)(2,1)S(1)}, bf16[1,144,128]{2,1,0:T(8,128)(2,1)S(1)}, u32[]{:S(2)}, u32[]{:S(2)}) collective-permute-start(bf16[1,144,128]{2,1,0:T(8,128)(2,1)S(1)} %get-tuple-element.19), channel_id=1, source_target_pairs={{0,6},{1,7},{2,0},{3,1},{4,2},{5,3},{6,4},{7,5},{8,14},{9,15},{10,... | collective-permute-start | bytes 110600 | tf_op jit(solution)/shard_map/ppermute | solution.py:198
  22.2 1.7 %collective-permute-start.6 = (bf16[1,144,128]{2,1,0:T(8,128)(2,1)S(1)}, bf16[1,144,128]{2,1,0:T(8,128)(2,1)S(1)}, u32[]{:S(2)}, u32[]{:S(2)}) collective-permute-start(bf16[1,144,128]{2,1,0:T(8,128)(2,1)S(1)} %get-tuple-element.19), channel_id=1, source_target_pairs={{0,7},{1,0},{2,1},{3,2},{4,3},{5,4},{6,5},{7,6},{8,15},{9,8},{10,9... | collective-permute-start | bytes 110600 | tf_op jit(solution)/shard_map/ppermute | solution.py:198
  24.6 1.6 collective-permute-done.6
  27.0 1.2 copy.17
  28.2 1.9 %collective-permute-start.7 = (bf16[1,25,2048]{1,2,0:T(8,128)(2,1)S(1)}, bf16[1,25,2048]{1,2,0:T(8,128)(2,1)S(1)}, u32[]{:S(2)}, u32[]{:S(2)}) collective-permute-start(bf16[1,25,2048]{1,2,0:T(8,128)(2,1)S(1)} %copy.17), channel_id=1, source_target_pairs={{0,8},{8,16},{16,24},{24,32},{32,40},{40,48},{48,56},{56,64},{64,7... | collective-permute-start | bytes 307208 | tf_op jit(solution)/shard_map/ppermute | solution.py:19
  30.1 4.8 %collective-permute-start.8 = (bf16[1,25,200]{2,1,0:T(8,128)(2,1)}, bf16[1,25,200]{2,1,0:T(8,128)(2,1)S(1)}, u32[]{:S(2)}, u32[]{:S(2)}) collective-permute-start(bf16[1,25,200]{2,1,0:T(8,128)(2,1)} %param.11), channel_id=1, source_target_pairs={{0,8},{8,16},{16,24},{24,32},{32,40},{40,48},{48,56},{56,64},{64,7... | collective-permute-start | bytes 30008 | tf_op jit(solution)/shard_map/ppermute | solution.py:19
  36.1 1.0 convolution_convert_fusion
  37.1 65.8 %all-gather.2.cloned.1.call-done.part_ref = bf16[256,144,128]{2,1,0:T(8,128)(2,1)} async-done(((bf16[8,144,128]{2,1,0:T(8,128)(2,1)}), bf16[256,144,128]{2,1,0:T(8,128)(2,1)}) %all-gather.2.cloned.1.call-update) | async-done | bytes 9437200 | tf_op jit(solution)/shard_map/all_gather | solution.py:201
  102.9 1.2 convert_reduce_fusion
  105.8 10.3 %shard_map.73 = f32[256,128]{1,0:T(8,128)S(1)} custom-call(s32[256]{0:T(256)S(1)} %get-tuple-element.18.rb_ref, s32[256]{0:T(256)S(1)} %get-tuple-element.17.cb_ref, bf16[2048,32]{1,0:T(8,128)(2,1)S(1)} %pad_bitcast_fusion.pt_ref.x_ref, bf16[32,2048]{1,0:T(8,128)(2,1)S(1)} %pad.14.g_ref, bf16[256,144,128]{2,1,0:T(8,128)(2,1)} %all-gather.2.cloned.1.call-done.part_ref), custom_call_target="tpu_custom_call" | custom-call | tf_op jit(solution)/shard_map/pallas_call | solution.py:63
  116.4 1.6 collective-permute-start.9
  118.0 2.0 %collective-permute-done.9 = f32[64]{0:T(128)S(1)} collective-permute-done((f32[64]{0:T(128)S(1)}, f32[64]{0:T(128)S(1)}, u32[]{:S(2)}, u32[]{:S(2)}) %collective-permute-start.9) | collective-permute-done | bytes 288 | tf_op jit(solution)/shard_map/ppermute | solution.py:26
  120.1 3.0 %collective-permute-start.10 = (f32[64]{0:T(128)S(1)}, f32[64]{0:T(128)S(1)}, u32[]{:S(2)}, u32[]{:S(2)}) collective-permute-start(f32[64]{0:T(128)S(1)} %add.61), channel_id=1, source_target_pairs={{0,2},{1,3},{2,0},{3,1},{4,6},{5,7},{6,4},{7,5},{8,10},{9,11},{10,... | collective-permute-start | bytes 776 | tf_op jit(solution)/shard_map/ppermute | solution.py:26
  123.1 2.0 %collective-permute-done.10 = f32[64]{0:T(128)S(1)} collective-permute-done((f32[64]{0:T(128)S(1)}, f32[64]{0:T(128)S(1)}, u32[]{:S(2)}, u32[]{:S(2)}) %collective-permute-start.10) | collective-permute-done | bytes 288 | tf_op jit(solution)/shard_map/ppermute | solution.py:26
  125.1 2.1 %collective-permute-start.11 = (f32[64]{0:T(128)S(1)}, f32[64]{0:T(128)S(1)}, u32[]{:S(2)}, u32[]{:S(2)}) collective-permute-start(f32[64]{0:T(128)S(1)} %add.62), channel_id=1, source_target_pairs={{0,4},{1,5},{2,6},{3,7},{4,0},{5,1},{6,2},{7,3},{8,12},{9,13},{10,... | collective-permute-start | bytes 776 | tf_op jit(solution)/shard_map/ppermute | solution.py:26
  127.2 3.0 %collective-permute-done.11 = f32[64]{0:T(128)S(1)} collective-permute-done((f32[64]{0:T(128)S(1)}, f32[64]{0:T(128)S(1)}, u32[]{:S(2)}, u32[]{:S(2)}) %collective-permute-start.11) | collective-permute-done | bytes 288 | tf_op jit(solution)/shard_map/ppermute | solution.py:26
  130.3 25.3 %shard_map.74 = bf16[2048,32]{1,0:T(8,128)(2,1)S(1)} custom-call(s32[256]{0:T(256)S(1)} %get-tuple-element.18.rb_ref, s32[256]{0:T(256)S(1)} %get-tuple-element.17.cb_ref, f32[256]{0:T(256)S(1)} %select_reduce_fusion.2.s_ref, bf16[2048,32]{1,0:T(8,128)(2,1)S(1)} %pad_bitcast_fusion.pt_ref.x_ref, bf16[256,144,128]{2,1,0:T(8,128)(2,1)} %all-gather.2.cloned.1.call-done.part_ref), custom_call_target="tpu_custom_call" | custom-call | tf_op jit(solution)/shard_map/pallas_call | solution.py:131
  155.6 0.9 copy.19
  (42 shorter events, 4.0 us)
Async XLA Ops:
  6.5 29.6 %copy-start = (bf16[200,2048]{1,0:T(8,128)(2,1)S(1)}, bf16[200,2048]{1,0:T(8,128)(2,1)}, u32[]{:S(2)}) copy-start(bf16[200,2048]{1,0:T(8,128)(2,1)} %param.12) | copy-start | bytes 2457604
  6.5 123.7 %copy-start.2 = (f32[1,64]{1,0:T(1,128)S(1)}, f32[1,64]{1,0:T(1,128)}, u32[]{:S(2)}) copy-start(f32[1,64]{1,0:T(1,128)} %param.15) | copy-start | bytes 772
  6.5 96.4 %all-gather.2.cloned.1.call-start = ((), (), s32[]{:S(2)}) async-start(), calls=%async_computation | async-start | bytes 9732096 | tf_op jit(solution)/shard_map/all_gather | solution.py:201
  8.0 11.1 %collective-permute-start = (bf16[1,144,128]{2,1,0:T(8,128)(2,1)S(1)}, bf16[1,144,128]{2,1,0:T(8,128)(2,1)S(1)}, u32[]{:S(2)}, u32[]{:S(2)}) collective-permute-start(bf16[1,144,128]{2,1,0:T(8,128)(2,1)S(1)} %get-tuple-element.19), channel_id=1, source_target_pairs={{0,1},{1,2},{2,3},{3,4},{4,5},{5,6},{6,7},{7,0},{8,9},{9,10},{10,1... | collective-permute-start | bytes 110600 | tf_op jit(solution)/shard_map/ppermute | solution.py:198
  9.7 12.5 %collective-permute-start.1 = (bf16[1,144,128]{2,1,0:T(8,128)(2,1)S(1)}, bf16[1,144,128]{2,1,0:T(8,128)(2,1)S(1)}, u32[]{:S(2)}, u32[]{:S(2)}) collective-permute-start(bf16[1,144,128]{2,1,0:T(8,128)(2,1)S(1)} %get-tuple-element.19), channel_id=1, source_target_pairs={{0,2},{1,3},{2,4},{3,5},{4,6},{5,7},{6,0},{7,1},{8,10},{9,11},{10,... | collective-permute-start | bytes 110600 | tf_op jit(solution)/shard_map/ppermute | solution.py:198
  12.6 11.4 %collective-permute-start.2 = (bf16[1,144,128]{2,1,0:T(8,128)(2,1)S(1)}, bf16[1,144,128]{2,1,0:T(8,128)(2,1)S(1)}, u32[]{:S(2)}, u32[]{:S(2)}) collective-permute-start(bf16[1,144,128]{2,1,0:T(8,128)(2,1)S(1)} %get-tuple-element.19), channel_id=1, source_target_pairs={{0,3},{1,4},{2,5},{3,6},{4,7},{5,0},{6,1},{7,2},{8,11},{9,12},{10,... | collective-permute-start | bytes 110600 | tf_op jit(solution)/shard_map/ppermute | solution.py:198
  15.5 8.5 %collective-permute-start.3 = (bf16[1,144,128]{2,1,0:T(8,128)(2,1)S(1)}, bf16[1,144,128]{2,1,0:T(8,128)(2,1)S(1)}, u32[]{:S(2)}, u32[]{:S(2)}) collective-permute-start(bf16[1,144,128]{2,1,0:T(8,128)(2,1)S(1)} %get-tuple-element.19), channel_id=1, source_target_pairs={{0,4},{1,5},{2,6},{3,7},{4,0},{5,1},{6,2},{7,3},{8,12},{9,13},{10,... | collective-permute-start | bytes 110600 | tf_op jit(solution)/shard_map/ppermute | solution.py:198
  16.9 7.1 %collective-permute-start.4 = (bf16[1,144,128]{2,1,0:T(8,128)(2,1)S(1)}, bf16[1,144,128]{2,1,0:T(8,128)(2,1)S(1)}, u32[]{:S(2)}, u32[]{:S(2)}) collective-permute-start(bf16[1,144,128]{2,1,0:T(8,128)(2,1)S(1)} %get-tuple-element.19), channel_id=1, source_target_pairs={{0,5},{1,6},{2,7},{3,0},{4,1},{5,2},{6,3},{7,4},{8,13},{9,14},{10,... | collective-permute-start | bytes 110600 | tf_op jit(solution)/shard_map/ppermute | solution.py:198
  19.2 5.5 %collective-permute-start.5 = (bf16[1,144,128]{2,1,0:T(8,128)(2,1)S(1)}, bf16[1,144,128]{2,1,0:T(8,128)(2,1)S(1)}, u32[]{:S(2)}, u32[]{:S(2)}) collective-permute-start(bf16[1,144,128]{2,1,0:T(8,128)(2,1)S(1)} %get-tuple-element.19), channel_id=1, source_target_pairs={{0,6},{1,7},{2,0},{3,1},{4,2},{5,3},{6,4},{7,5},{8,14},{9,15},{10,... | collective-permute-start | bytes 110600 | tf_op jit(solution)/shard_map/ppermute | solution.py:198
  22.2 4.0 %collective-permute-start.6 = (bf16[1,144,128]{2,1,0:T(8,128)(2,1)S(1)}, bf16[1,144,128]{2,1,0:T(8,128)(2,1)S(1)}, u32[]{:S(2)}, u32[]{:S(2)}) collective-permute-start(bf16[1,144,128]{2,1,0:T(8,128)(2,1)S(1)} %get-tuple-element.19), channel_id=1, source_target_pairs={{0,7},{1,0},{2,1},{3,2},{4,3},{5,4},{6,5},{7,6},{8,15},{9,8},{10,9... | collective-permute-start | bytes 110600 | tf_op jit(solution)/shard_map/ppermute | solution.py:198
  26.3 0.7 copy-start.1
  28.2 77.1 %collective-permute-start.7 = (bf16[1,25,2048]{1,2,0:T(8,128)(2,1)S(1)}, bf16[1,25,2048]{1,2,0:T(8,128)(2,1)S(1)}, u32[]{:S(2)}, u32[]{:S(2)}) collective-permute-start(bf16[1,25,2048]{1,2,0:T(8,128)(2,1)S(1)} %copy.17), channel_id=1, source_target_pairs={{0,8},{8,16},{16,24},{24,32},{32,40},{40,48},{48,56},{56,64},{64,7... | collective-permute-start | bytes 307208 | tf_op jit(solution)/shard_map/ppermute | solution.py:19
  30.1 75.4 %collective-permute-start.8 = (bf16[1,25,200]{2,1,0:T(8,128)(2,1)}, bf16[1,25,200]{2,1,0:T(8,128)(2,1)S(1)}, u32[]{:S(2)}, u32[]{:S(2)}) collective-permute-start(bf16[1,25,200]{2,1,0:T(8,128)(2,1)} %param.11), channel_id=1, source_target_pairs={{0,8},{8,16},{16,24},{24,32},{32,40},{40,48},{48,56},{56,64},{64,7... | collective-permute-start | bytes 30008 | tf_op jit(solution)/shard_map/ppermute | solution.py:19
  116.4 3.7 %collective-permute-start.9 = (f32[64]{0:T(128)S(1)}, f32[64]{0:T(128)S(1)}, u32[]{:S(2)}, u32[]{:S(2)}) collective-permute-start(f32[64]{0:T(128)S(1)} %select_reduce_fusion.3), channel_id=1, source_target_pairs={{0,1},{1,0},{2,3},{3,2},{4,5},{5,4},{6,7},{7,6},{8,9},{9,8},{10,11... | collective-permute-start | bytes 776 | tf_op jit(solution)/shard_map/ppermute | solution.py:26
  120.1 5.1 %collective-permute-start.10 = (f32[64]{0:T(128)S(1)}, f32[64]{0:T(128)S(1)}, u32[]{:S(2)}, u32[]{:S(2)}) collective-permute-start(f32[64]{0:T(128)S(1)} %add.61), channel_id=1, source_target_pairs={{0,2},{1,3},{2,0},{3,1},{4,6},{5,7},{6,4},{7,5},{8,10},{9,11},{10,... | collective-permute-start | bytes 776 | tf_op jit(solution)/shard_map/ppermute | solution.py:26
  125.1 5.1 %collective-permute-start.11 = (f32[64]{0:T(128)S(1)}, f32[64]{0:T(128)S(1)}, u32[]{:S(2)}, u32[]{:S(2)}) collective-permute-start(f32[64]{0:T(128)S(1)} %add.62), channel_id=1, source_target_pairs={{0,4},{1,5},{2,6},{3,7},{4,0},{5,1},{6,2},{7,3},{8,12},{9,13},{10,... | collective-permute-start | bytes 776 | tf_op jit(solution)/shard_map/ppermute | solution.py:26
Sparse Core Ops, SparseCore 0:
  27.1 75.7 all-gather.1

commit v13 on v11

--- a/solution.py
+++ b/solution.py
@@ -28,7 +28,7 @@
     return value
 
 
-CHUNK = 32
+CHUNK = 64
 
 
 def bias_kernel(rb_ref, cb_ref, pt_ref, g_ref, part_ref, out_ref, m_ref):

time: 164 us -> 163 us (level)
  no operation moved by 1% of the time
where the time goes in v13:
time: 163 us; the launch traced here: 162 us
  waiting for transfers between devices  82.8 us (51%)
  Pallas kernels  34.1 us (21%)
  starting transfers between devices  19.6 us (12%)
  between operations  14.9 us (9%)
  other arithmetic  6.27 us (4%)
  local copies, waits for them, and re-layouts  3.12 us (2%)
    all_gather x1, waiting for transfers between devices, shards(): lax.all_gather(xor_gather(payload, order), 'walker', axis=0, tiled=True)  66.1 us
    pallas_call x1, Pallas kernels, propagate(): pl.pallas_call(prop_kernel, out_shape=jax.ShapeDtypeStruct((orbitals, wid...  25.2 us
    ppermute x3, waiting for transfers between devices, xor_gather(): other = lax.ppermute(x, axis, [(i, i ^ step) for i in range(count)])  9.57 us
    pallas_call x1, Pallas kernels, tile_bias(): pl.pallas_call(bias_kernel, out_shape=jax.ShapeDtypeStruct((tiles_total,...  8.93 us
    ppermute x3, waiting for transfers between devices, butterfly_sum(): lax.ppermute(value, axis, [(i, i ^ step) for i in range(count)])  7.02 us
    ppermute x3, starting transfers between devices, xor_gather(): other = lax.ppermute(x, axis, [(i, i ^ step) for i in range(count)])  6.98 us
    ppermute x3, starting transfers between devices, butterfly_sum(): lax.ppermute(value, axis, [(i, i ^ step) for i in range(count)])  6.78 us
    ppermute x2, starting transfers between devices, shift_from(): lax.ppermute(value, axis, [(i, i + steps) for i in range(count - steps)])  5.82 us
  transfers between devices with their start and end apart: 9, of which 7 were waited for; matrix products, arithmetic and copies ran while one was open for 3% of the time, Pallas kernels for 0%

profile of v13, /device:TPU:2, one launch (start us, length us, event | category | flops | bytes accessed | tf_op | source)
XLA Modules:
  0.0 162.0 jit_solution(5684969184035042483)
XLA Ops:
  8.1 2.1 %collective-permute-start = (bf16[1,144,128]{2,1,0:T(8,128)(2,1)S(1)}, bf16[1,144,128]{2,1,0:T(8,128)(2,1)S(1)}, u32[]{:S(2)}, u32[]{:S(2)}) collective-permute-start(bf16[1,144,128]{2,1,0:T(8,128)(2,1)S(1)} %pad_maximum_fusion.3), channel_id=1, source_target_pairs={{0,4},{1,5},{2,6},{3,7},{4,0},{5,1},{6,2},{7,3},{8,12},{9,13},{10,... | collective-permute-start | bytes 110600 | tf_op jit(solution)/shard_map/ppermute | solution.py:161
  10.2 3.3 %collective-permute-done = bf16[1,144,128]{2,1,0:T(8,128)(2,1)S(1)} collective-permute-done((bf16[1,144,128]{2,1,0:T(8,128)(2,1)S(1)}, bf16[1,144,128]{2,1,0:T(8,128)(2,1)S(1)}, u32[]{:S(2)}, u32[]{:S(2)}) %collective-permute-start) | collective-permute-done | bytes 36896 | tf_op jit(solution)/shard_map/ppermute | solution.py:161
  14.3 3.2 %collective-permute-start.1 = (bf16[2,144,128]{2,1,0:T(8,128)(2,1)S(1)}, bf16[2,144,128]{2,1,0:T(8,128)(2,1)S(1)}, u32[]{:S(2)}, u32[]{:S(2)}) collective-permute-start(bf16[2,144,128]{2,1,0:T(8,128)(2,1)S(1)} %pad_maximum_fusion.2), channel_id=1, source_target_pairs={{0,2},{1,3},{2,0},{3,1},{4,6},{5,7},{6,4},{7,5},{8,10},{9,11},{10,... | collective-permute-start | bytes 221192 | tf_op jit(solution)/shard_map/ppermute | solution.py:161
  17.5 2.7 %collective-permute-done.1 = bf16[2,144,128]{2,1,0:T(8,128)(2,1)S(1)} collective-permute-done((bf16[2,144,128]{2,1,0:T(8,128)(2,1)S(1)}, bf16[2,144,128]{2,1,0:T(8,128)(2,1)S(1)}, u32[]{:S(2)}, u32[]{:S(2)}) %collective-permute-start.1) | collective-permute-done | bytes 73760 | tf_op jit(solution)/shard_map/ppermute | solution.py:161
  20.1 0.8 pad_maximum_fusion.1
  20.9 1.7 %collective-permute-start.2 = (bf16[4,144,128]{2,1,0:T(8,128)(2,1)S(1)}, bf16[4,144,128]{2,1,0:T(8,128)(2,1)S(1)}, u32[]{:S(2)}, u32[]{:S(2)}) collective-permute-start(bf16[4,144,128]{2,1,0:T(8,128)(2,1)S(1)} %pad_maximum_fusion.1), channel_id=1, source_target_pairs={{0,1},{1,0},{2,3},{3,2},{4,5},{5,4},{6,7},{7,6},{8,9},{9,8},{10,11... | collective-permute-start | bytes 442376 | tf_op jit(solution)/shard_map/ppermute | solution.py:161
  22.6 3.6 %collective-permute-done.2 = bf16[4,144,128]{2,1,0:T(8,128)(2,1)S(1)} collective-permute-done((bf16[4,144,128]{2,1,0:T(8,128)(2,1)S(1)}, bf16[4,144,128]{2,1,0:T(8,128)(2,1)S(1)}, u32[]{:S(2)}, u32[]{:S(2)}) %collective-permute-start.2) | collective-permute-done | bytes 147488 | tf_op jit(solution)/shard_map/ppermute | solution.py:161
  26.1 1.5 pad_maximum_fusion
  27.7 1.2 copy.17
  28.9 1.9 %collective-permute-start.3 = (bf16[1,25,2048]{1,2,0:T(8,128)(2,1)S(1)}, bf16[1,25,2048]{1,2,0:T(8,128)(2,1)S(1)}, u32[]{:S(2)}, u32[]{:S(2)}) collective-permute-start(bf16[1,25,2048]{1,2,0:T(8,128)(2,1)S(1)} %copy.17), channel_id=1, source_target_pairs={{0,8},{8,16},{16,24},{24,32},{32,40},{40,48},{48,56},{56,64},{64,7... | collective-permute-start | bytes 307208 | tf_op jit(solution)/shard_map/ppermute | solution.py:19
  30.8 3.9 %collective-permute-start.4 = (bf16[1,25,200]{2,1,0:T(8,128)(2,1)}, bf16[1,25,200]{2,1,0:T(8,128)(2,1)S(1)}, u32[]{:S(2)}, u32[]{:S(2)}) collective-permute-start(bf16[1,25,200]{2,1,0:T(8,128)(2,1)} %param.11), channel_id=1, source_target_pairs={{0,8},{8,16},{16,24},{24,32},{32,40},{40,48},{48,56},{56,64},{64,7... | collective-permute-start | bytes 30008 | tf_op jit(solution)/shard_map/ppermute | solution.py:19
  34.9 0.8 fusion.15
  35.9 1.0 convolution_convert_fusion
  36.9 66.1 %all-gather.2.cloned.1.call-done.part_ref = bf16[256,144,128]{2,1,0:T(8,128)(2,1)} async-done(((bf16[8,144,128]{2,1,0:T(8,128)(2,1)}), bf16[256,144,128]{2,1,0:T(8,128)(2,1)}) %all-gather.2.cloned.1.call-update) | async-done | bytes 9437200 | tf_op jit(solution)/shard_map/all_gather | solution.py:197
  103.0 1.2 convert_reduce_fusion
  106.0 8.9 %shard_map.73 = f32[256,128]{1,0:T(8,128)S(1)} custom-call(s32[256]{0:T(256)S(1)} %get-tuple-element.18.rb_ref, s32[256]{0:T(256)S(1)} %get-tuple-element.17.cb_ref, bf16[2048,32]{1,0:T(8,128)(2,1)S(1)} %pad_bitcast_fusion.pt_ref.x_ref, bf16[32,2048]{1,0:T(8,128)(2,1)S(1)} %pad.14.g_ref, bf16[256,144,128]{2,1,0:T(8,128)(2,1)} %all-gather.2.cloned.1.call-done.part_ref), custom_call_target="tpu_custom_call" | custom-call | tf_op jit(solution)/shard_map/pallas_call | solution.py:63
  115.1 1.6 collective-permute-start.5
  116.7 2.0 %collective-permute-done.5 = f32[64]{0:T(128)S(1)} collective-permute-done((f32[64]{0:T(128)S(1)}, f32[64]{0:T(128)S(1)}, u32[]{:S(2)}, u32[]{:S(2)}) %collective-permute-start.5) | collective-permute-done | bytes 288 | tf_op jit(solution)/shard_map/ppermute | solution.py:26
  118.8 3.0 %collective-permute-start.6 = (f32[64]{0:T(128)S(1)}, f32[64]{0:T(128)S(1)}, u32[]{:S(2)}, u32[]{:S(2)}) collective-permute-start(f32[64]{0:T(128)S(1)} %add.85), channel_id=1, source_target_pairs={{0,2},{1,3},{2,0},{3,1},{4,6},{5,7},{6,4},{7,5},{8,10},{9,11},{10,... | collective-permute-start | bytes 776 | tf_op jit(solution)/shard_map/ppermute | solution.py:26
  121.8 2.0 %collective-permute-done.6 = f32[64]{0:T(128)S(1)} collective-permute-done((f32[64]{0:T(128)S(1)}, f32[64]{0:T(128)S(1)}, u32[]{:S(2)}, u32[]{:S(2)}) %collective-permute-start.6) | collective-permute-done | bytes 288 | tf_op jit(solution)/shard_map/ppermute | solution.py:26
  123.9 2.1 %collective-permute-start.7 = (f32[64]{0:T(128)S(1)}, f32[64]{0:T(128)S(1)}, u32[]{:S(2)}, u32[]{:S(2)}) collective-permute-start(f32[64]{0:T(128)S(1)} %add.86), channel_id=1, source_target_pairs={{0,4},{1,5},{2,6},{3,7},{4,0},{5,1},{6,2},{7,3},{8,12},{9,13},{10,... | collective-permute-start | bytes 776 | tf_op jit(solution)/shard_map/ppermute | solution.py:26
  126.0 2.9 %collective-permute-done.7 = f32[64]{0:T(128)S(1)} collective-permute-done((f32[64]{0:T(128)S(1)}, f32[64]{0:T(128)S(1)}, u32[]{:S(2)}, u32[]{:S(2)}) %collective-permute-start.7) | collective-permute-done | bytes 288 | tf_op jit(solution)/shard_map/ppermute | solution.py:26
  129.0 25.2 %shard_map.74 = bf16[2048,32]{1,0:T(8,128)(2,1)S(1)} custom-call(s32[256]{0:T(256)S(1)} %get-tuple-element.18.rb_ref, s32[256]{0:T(256)S(1)} %get-tuple-element.17.cb_ref, f32[256]{0:T(256)S(1)} %select_reduce_fusion.2.s_ref, bf16[2048,32]{1,0:T(8,128)(2,1)S(1)} %pad_bitcast_fusion.pt_ref.x_ref, bf16[256,144,128]{2,1,0:T(8,128)(2,1)} %all-gather.2.cloned.1.call-done.part_ref), custom_call_target="tpu_custom_call" | custom-call | tf_op jit(solution)/shard_map/pallas_call | solution.py:131
  154.3 0.9 copy.19
  (29 shorter events, 3.4 us)
Async XLA Ops:
  6.5 29.4 %copy-start = (bf16[200,2048]{1,0:T(8,128)(2,1)S(1)}, bf16[200,2048]{1,0:T(8,128)(2,1)}, u32[]{:S(2)}) copy-start(bf16[200,2048]{1,0:T(8,128)(2,1)} %param.12) | copy-start | bytes 2457604
  6.5 122.4 %copy-start.1 = (f32[1,64]{1,0:T(1,128)S(1)}, f32[1,64]{1,0:T(1,128)}, u32[]{:S(2)}) copy-start(f32[1,64]{1,0:T(1,128)} %param.15) | copy-start | bytes 772
  6.5 96.5 %all-gather.2.cloned.1.call-start = ((), (), s32[]{:S(2)}) async-start(), calls=%async_computation | async-start | bytes 9732096 | tf_op jit(solution)/shard_map/all_gather | solution.py:197
  8.1 5.5 %collective-permute-start = (bf16[1,144,128]{2,1,0:T(8,128)(2,1)S(1)}, bf16[1,144,128]{2,1,0:T(8,128)(2,1)S(1)}, u32[]{:S(2)}, u32[]{:S(2)}) collective-permute-start(bf16[1,144,128]{2,1,0:T(8,128)(2,1)S(1)} %pad_maximum_fusion.3), channel_id=1, source_target_pairs={{0,4},{1,5},{2,6},{3,7},{4,0},{5,1},{6,2},{7,3},{8,12},{9,13},{10,... | collective-permute-start | bytes 110600 | tf_op jit(solution)/shard_map/ppermute | solution.py:161
  14.3 5.9 %collective-permute-start.1 = (bf16[2,144,128]{2,1,0:T(8,128)(2,1)S(1)}, bf16[2,144,128]{2,1,0:T(8,128)(2,1)S(1)}, u32[]{:S(2)}, u32[]{:S(2)}) collective-permute-start(bf16[2,144,128]{2,1,0:T(8,128)(2,1)S(1)} %pad_maximum_fusion.2), channel_id=1, source_target_pairs={{0,2},{1,3},{2,0},{3,1},{4,6},{5,7},{6,4},{7,5},{8,10},{9,11},{10,... | collective-permute-start | bytes 221192 | tf_op jit(solution)/shard_map/ppermute | solution.py:161
  20.9 5.2 %collective-permute-start.2 = (bf16[4,144,128]{2,1,0:T(8,128)(2,1)S(1)}, bf16[4,144,128]{2,1,0:T(8,128)(2,1)S(1)}, u32[]{:S(2)}, u32[]{:S(2)}) collective-permute-start(bf16[4,144,128]{2,1,0:T(8,128)(2,1)S(1)} %pad_maximum_fusion.1), channel_id=1, source_target_pairs={{0,1},{1,0},{2,3},{3,2},{4,5},{5,4},{6,7},{7,6},{8,9},{9,8},{10,11... | collective-permute-start | bytes 442376 | tf_op jit(solution)/shard_map/ppermute | solution.py:161
  28.9 76.6 %collective-permute-start.3 = (bf16[1,25,2048]{1,2,0:T(8,128)(2,1)S(1)}, bf16[1,25,2048]{1,2,0:T(8,128)(2,1)S(1)}, u32[]{:S(2)}, u32[]{:S(2)}) collective-permute-start(bf16[1,25,2048]{1,2,0:T(8,128)(2,1)S(1)} %copy.17), channel_id=1, source_target_pairs={{0,8},{8,16},{16,24},{24,32},{32,40},{40,48},{48,56},{56,64},{64,7... | collective-permute-start | bytes 307208 | tf_op jit(solution)/shard_map/ppermute | solution.py:19
  30.8 74.9 %collective-permute-start.4 = (bf16[1,25,200]{2,1,0:T(8,128)(2,1)}, bf16[1,25,200]{2,1,0:T(8,128)(2,1)S(1)}, u32[]{:S(2)}, u32[]{:S(2)}) collective-permute-start(bf16[1,25,200]{2,1,0:T(8,128)(2,1)} %param.11), channel_id=1, source_target_pairs={{0,8},{8,16},{16,24},{24,32},{32,40},{40,48},{48,56},{56,64},{64,7... | collective-permute-start | bytes 30008 | tf_op jit(solution)/shard_map/ppermute | solution.py:19
  115.1 3.7 %collective-permute-start.5 = (f32[64]{0:T(128)S(1)}, f32[64]{0:T(128)S(1)}, u32[]{:S(2)}, u32[]{:S(2)}) collective-permute-start(f32[64]{0:T(128)S(1)} %select_reduce_fusion.3), channel_id=1, source_target_pairs={{0,1},{1,0},{2,3},{3,2},{4,5},{5,4},{6,7},{7,6},{8,9},{9,8},{10,11... | collective-permute-start | bytes 776 | tf_op jit(solution)/shard_map/ppermute | solution.py:26
  118.8 5.1 %collective-permute-start.6 = (f32[64]{0:T(128)S(1)}, f32[64]{0:T(128)S(1)}, u32[]{:S(2)}, u32[]{:S(2)}) collective-permute-start(f32[64]{0:T(128)S(1)} %add.85), channel_id=1, source_target_pairs={{0,2},{1,3},{2,0},{3,1},{4,6},{5,7},{6,4},{7,5},{8,10},{9,11},{10,... | collective-permute-start | bytes 776 | tf_op jit(solution)/shard_map/ppermute | solution.py:26
  123.9 5.1 %collective-permute-start.7 = (f32[64]{0:T(128)S(1)}, f32[64]{0:T(128)S(1)}, u32[]{:S(2)}, u32[]{:S(2)}) collective-permute-start(f32[64]{0:T(128)S(1)} %add.86), channel_id=1, source_target_pairs={{0,4},{1,5},{2,6},{3,7},{4,0},{5,1},{6,2},{7,3},{8,12},{9,13},{10,... | collective-permute-start | bytes 776 | tf_op jit(solution)/shard_map/ppermute | solution.py:26
Sparse Core Ops, SparseCore 0:
  27.8 75.2 all-gather.1

commit v14 on v13

--- a/solution.py
+++ b/solution.py
@@ -28,7 +28,7 @@
     return value
 
 
-CHUNK = 64
+CHUNK = 128
 
 
 def bias_kernel(rb_ref, cb_ref, pt_ref, g_ref, part_ref, out_ref, m_ref):

time: 163 us -> 163 us (level)
  no operation moved by 1% of the time
where the time goes in v14:
time: 163 us; the launch traced here: 162 us
  waiting for transfers between devices  82.8 us (51%)
  Pallas kernels  34.6 us (21%)
  starting transfers between devices  19.6 us (12%)
  between operations  14.9 us (9%)
  other arithmetic  6.27 us (4%)
  local copies, waits for them, and re-layouts  3.12 us (2%)
    all_gather x1, waiting for transfers between devices, shards(): lax.all_gather(xor_gather(payload, order), 'walker', axis=0, tiled=True)  66.1 us
    pallas_call x1, Pallas kernels, propagate(): pl.pallas_call(prop_kernel, out_shape=jax.ShapeDtypeStruct((orbitals, wid...  25.8 us
    ppermute x3, waiting for transfers between devices, xor_gather(): other = lax.ppermute(x, axis, [(i, i ^ step) for i in range(count)])  9.57 us
    pallas_call x1, Pallas kernels, tile_bias(): pl.pallas_call(bias_kernel, out_shape=jax.ShapeDtypeStruct((tiles_total,...  8.77 us
    ppermute x3, waiting for transfers between devices, butterfly_sum(): lax.ppermute(value, axis, [(i, i ^ step) for i in range(count)])  7.02 us
    ppermute x3, starting transfers between devices, xor_gather(): other = lax.ppermute(x, axis, [(i, i ^ step) for i in range(count)])  6.98 us
    ppermute x3, starting transfers between devices, butterfly_sum(): lax.ppermute(value, axis, [(i, i ^ step) for i in range(count)])  6.78 us
    ppermute x2, starting transfers between devices, shift_from(): lax.ppermute(value, axis, [(i, i + steps) for i in range(count - steps)])  5.82 us
  transfers between devices with their start and end apart: 9, of which 7 were waited for; matrix products, arithmetic and copies ran while one was open for 3% of the time, Pallas kernels for 0%

profile of v14, /device:TPU:2, one launch (start us, length us, event | category | flops | bytes accessed | tf_op | source)
XLA Modules:
  0.0 162.5 jit_solution(7034345001917961925)
XLA Ops:
  8.1 2.1 %collective-permute-start = (bf16[1,144,128]{2,1,0:T(8,128)(2,1)S(1)}, bf16[1,144,128]{2,1,0:T(8,128)(2,1)S(1)}, u32[]{:S(2)}, u32[]{:S(2)}) collective-permute-start(bf16[1,144,128]{2,1,0:T(8,128)(2,1)S(1)} %pad_maximum_fusion.3), channel_id=1, source_target_pairs={{0,4},{1,5},{2,6},{3,7},{4,0},{5,1},{6,2},{7,3},{8,12},{9,13},{10,... | collective-permute-start | bytes 110600 | tf_op jit(solution)/shard_map/ppermute | solution.py:161
  10.2 3.3 %collective-permute-done = bf16[1,144,128]{2,1,0:T(8,128)(2,1)S(1)} collective-permute-done((bf16[1,144,128]{2,1,0:T(8,128)(2,1)S(1)}, bf16[1,144,128]{2,1,0:T(8,128)(2,1)S(1)}, u32[]{:S(2)}, u32[]{:S(2)}) %collective-permute-start) | collective-permute-done | bytes 36896 | tf_op jit(solution)/shard_map/ppermute | solution.py:161
  14.3 3.2 %collective-permute-start.1 = (bf16[2,144,128]{2,1,0:T(8,128)(2,1)S(1)}, bf16[2,144,128]{2,1,0:T(8,128)(2,1)S(1)}, u32[]{:S(2)}, u32[]{:S(2)}) collective-permute-start(bf16[2,144,128]{2,1,0:T(8,128)(2,1)S(1)} %pad_maximum_fusion.2), channel_id=1, source_target_pairs={{0,2},{1,3},{2,0},{3,1},{4,6},{5,7},{6,4},{7,5},{8,10},{9,11},{10,... | collective-permute-start | bytes 221192 | tf_op jit(solution)/shard_map/ppermute | solution.py:161
  17.5 2.7 %collective-permute-done.1 = bf16[2,144,128]{2,1,0:T(8,128)(2,1)S(1)} collective-permute-done((bf16[2,144,128]{2,1,0:T(8,128)(2,1)S(1)}, bf16[2,144,128]{2,1,0:T(8,128)(2,1)S(1)}, u32[]{:S(2)}, u32[]{:S(2)}) %collective-permute-start.1) | collective-permute-done | bytes 73760 | tf_op jit(solution)/shard_map/ppermute | solution.py:161
  20.1 0.8 pad_maximum_fusion.1
  20.9 1.7 %collective-permute-start.2 = (bf16[4,144,128]{2,1,0:T(8,128)(2,1)S(1)}, bf16[4,144,128]{2,1,0:T(8,128)(2,1)S(1)}, u32[]{:S(2)}, u32[]{:S(2)}) collective-permute-start(bf16[4,144,128]{2,1,0:T(8,128)(2,1)S(1)} %pad_maximum_fusion.1), channel_id=1, source_target_pairs={{0,1},{1,0},{2,3},{3,2},{4,5},{5,4},{6,7},{7,6},{8,9},{9,8},{10,11... | collective-permute-start | bytes 442376 | tf_op jit(solution)/shard_map/ppermute | solution.py:161
  22.6 3.6 %collective-permute-done.2 = bf16[4,144,128]{2,1,0:T(8,128)(2,1)S(1)} collective-permute-done((bf16[4,144,128]{2,1,0:T(8,128)(2,1)S(1)}, bf16[4,144,128]{2,1,0:T(8,128)(2,1)S(1)}, u32[]{:S(2)}, u32[]{:S(2)}) %collective-permute-start.2) | collective-permute-done | bytes 147488 | tf_op jit(solution)/shard_map/ppermute | solution.py:161
  26.1 1.5 pad_maximum_fusion
  27.7 1.2 copy.17
  28.9 1.9 %collective-permute-start.3 = (bf16[1,25,2048]{1,2,0:T(8,128)(2,1)S(1)}, bf16[1,25,2048]{1,2,0:T(8,128)(2,1)S(1)}, u32[]{:S(2)}, u32[]{:S(2)}) collective-permute-start(bf16[1,25,2048]{1,2,0:T(8,128)(2,1)S(1)} %copy.17), channel_id=1, source_target_pairs={{0,8},{8,16},{16,24},{24,32},{32,40},{40,48},{48,56},{56,64},{64,7... | collective-permute-start | bytes 307208 | tf_op jit(solution)/shard_map/ppermute | solution.py:19
  30.8 3.9 %collective-permute-start.4 = (bf16[1,25,200]{2,1,0:T(8,128)(2,1)}, bf16[1,25,200]{2,1,0:T(8,128)(2,1)S(1)}, u32[]{:S(2)}, u32[]{:S(2)}) collective-permute-start(bf16[1,25,200]{2,1,0:T(8,128)(2,1)} %param.11), channel_id=1, source_target_pairs={{0,8},{8,16},{16,24},{24,32},{32,40},{40,48},{48,56},{56,64},{64,7... | collective-permute-start | bytes 30008 | tf_op jit(solution)/shard_map/ppermute | solution.py:19
  34.9 0.8 fusion.15
  35.9 1.0 convolution_convert_fusion
  36.9 66.1 %all-gather.2.cloned.1.call-done.part_ref = bf16[256,144,128]{2,1,0:T(8,128)(2,1)} async-done(((bf16[8,144,128]{2,1,0:T(8,128)(2,1)}), bf16[256,144,128]{2,1,0:T(8,128)(2,1)}) %all-gather.2.cloned.1.call-update) | async-done | bytes 9437200 | tf_op jit(solution)/shard_map/all_gather | solution.py:197
  103.0 1.2 convert_reduce_fusion
  106.0 8.8 %shard_map.73 = f32[256,128]{1,0:T(8,128)S(1)} custom-call(s32[256]{0:T(256)S(1)} %get-tuple-element.18.rb_ref, s32[256]{0:T(256)S(1)} %get-tuple-element.17.cb_ref, bf16[2048,32]{1,0:T(8,128)(2,1)S(1)} %pad_bitcast_fusion.pt_ref.x_ref, bf16[32,2048]{1,0:T(8,128)(2,1)S(1)} %pad.14.g_ref, bf16[256,144,128]{2,1,0:T(8,128)(2,1)} %all-gather.2.cloned.1.call-done.part_ref), custom_call_target="tpu_custom_call" | custom-call | tf_op jit(solution)/shard_map/pallas_call | solution.py:63
  115.0 1.6 collective-permute-start.5
  116.6 2.0 %collective-permute-done.5 = f32[64]{0:T(128)S(1)} collective-permute-done((f32[64]{0:T(128)S(1)}, f32[64]{0:T(128)S(1)}, u32[]{:S(2)}, u32[]{:S(2)}) %collective-permute-start.5) | collective-permute-done | bytes 288 | tf_op jit(solution)/shard_map/ppermute | solution.py:26
  118.6 3.0 %collective-permute-start.6 = (f32[64]{0:T(128)S(1)}, f32[64]{0:T(128)S(1)}, u32[]{:S(2)}, u32[]{:S(2)}) collective-permute-start(f32[64]{0:T(128)S(1)} %add.85), channel_id=1, source_target_pairs={{0,2},{1,3},{2,0},{3,1},{4,6},{5,7},{6,4},{7,5},{8,10},{9,11},{10,... | collective-permute-start | bytes 776 | tf_op jit(solution)/shard_map/ppermute | solution.py:26
  121.7 2.0 %collective-permute-done.6 = f32[64]{0:T(128)S(1)} collective-permute-done((f32[64]{0:T(128)S(1)}, f32[64]{0:T(128)S(1)}, u32[]{:S(2)}, u32[]{:S(2)}) %collective-permute-start.6) | collective-permute-done | bytes 288 | tf_op jit(solution)/shard_map/ppermute | solution.py:26
  123.7 2.1 %collective-permute-start.7 = (f32[64]{0:T(128)S(1)}, f32[64]{0:T(128)S(1)}, u32[]{:S(2)}, u32[]{:S(2)}) collective-permute-start(f32[64]{0:T(128)S(1)} %add.86), channel_id=1, source_target_pairs={{0,4},{1,5},{2,6},{3,7},{4,0},{5,1},{6,2},{7,3},{8,12},{9,13},{10,... | collective-permute-start | bytes 776 | tf_op jit(solution)/shard_map/ppermute | solution.py:26
  125.8 3.0 %collective-permute-done.7 = f32[64]{0:T(128)S(1)} collective-permute-done((f32[64]{0:T(128)S(1)}, f32[64]{0:T(128)S(1)}, u32[]{:S(2)}, u32[]{:S(2)}) %collective-permute-start.7) | collective-permute-done | bytes 288 | tf_op jit(solution)/shard_map/ppermute | solution.py:26
  128.9 25.8 %shard_map.74 = bf16[2048,32]{1,0:T(8,128)(2,1)S(1)} custom-call(s32[256]{0:T(256)S(1)} %get-tuple-element.18.rb_ref, s32[256]{0:T(256)S(1)} %get-tuple-element.17.cb_ref, f32[256]{0:T(256)S(1)} %select_reduce_fusion.2.s_ref, bf16[2048,32]{1,0:T(8,128)(2,1)S(1)} %pad_bitcast_fusion.pt_ref.x_ref, bf16[256,144,128]{2,1,0:T(8,128)(2,1)} %all-gather.2.cloned.1.call-done.part_ref), custom_call_target="tpu_custom_call" | custom-call | tf_op jit(solution)/shard_map/pallas_call | solution.py:131
  154.7 0.9 copy.19
  (29 shorter events, 3.4 us)
Async XLA Ops:
  6.5 29.4 %copy-start = (bf16[200,2048]{1,0:T(8,128)(2,1)S(1)}, bf16[200,2048]{1,0:T(8,128)(2,1)}, u32[]{:S(2)}) copy-start(bf16[200,2048]{1,0:T(8,128)(2,1)} %param.12) | copy-start | bytes 2457604
  6.5 122.2 %copy-start.1 = (f32[1,64]{1,0:T(1,128)S(1)}, f32[1,64]{1,0:T(1,128)}, u32[]{:S(2)}) copy-start(f32[1,64]{1,0:T(1,128)} %param.15) | copy-start | bytes 772
  6.5 96.5 %all-gather.2.cloned.1.call-start = ((), (), s32[]{:S(2)}) async-start(), calls=%async_computation | async-start | bytes 9732096 | tf_op jit(solution)/shard_map/all_gather | solution.py:197
  8.1 5.5 %collective-permute-start = (bf16[1,144,128]{2,1,0:T(8,128)(2,1)S(1)}, bf16[1,144,128]{2,1,0:T(8,128)(2,1)S(1)}, u32[]{:S(2)}, u32[]{:S(2)}) collective-permute-start(bf16[1,144,128]{2,1,0:T(8,128)(2,1)S(1)} %pad_maximum_fusion.3), channel_id=1, source_target_pairs={{0,4},{1,5},{2,6},{3,7},{4,0},{5,1},{6,2},{7,3},{8,12},{9,13},{10,... | collective-permute-start | bytes 110600 | tf_op jit(solution)/shard_map/ppermute | solution.py:161
  14.3 5.9 %collective-permute-start.1 = (bf16[2,144,128]{2,1,0:T(8,128)(2,1)S(1)}, bf16[2,144,128]{2,1,0:T(8,128)(2,1)S(1)}, u32[]{:S(2)}, u32[]{:S(2)}) collective-permute-start(bf16[2,144,128]{2,1,0:T(8,128)(2,1)S(1)} %pad_maximum_fusion.2), channel_id=1, source_target_pairs={{0,2},{1,3},{2,0},{3,1},{4,6},{5,7},{6,4},{7,5},{8,10},{9,11},{10,... | collective-permute-start | bytes 221192 | tf_op jit(solution)/shard_map/ppermute | solution.py:161
  20.9 5.2 %collective-permute-start.2 = (bf16[4,144,128]{2,1,0:T(8,128)(2,1)S(1)}, bf16[4,144,128]{2,1,0:T(8,128)(2,1)S(1)}, u32[]{:S(2)}, u32[]{:S(2)}) collective-permute-start(bf16[4,144,128]{2,1,0:T(8,128)(2,1)S(1)} %pad_maximum_fusion.1), channel_id=1, source_target_pairs={{0,1},{1,0},{2,3},{3,2},{4,5},{5,4},{6,7},{7,6},{8,9},{9,8},{10,11... | collective-permute-start | bytes 442376 | tf_op jit(solution)/shard_map/ppermute | solution.py:161
  28.9 76.6 %collective-permute-start.3 = (bf16[1,25,2048]{1,2,0:T(8,128)(2,1)S(1)}, bf16[1,25,2048]{1,2,0:T(8,128)(2,1)S(1)}, u32[]{:S(2)}, u32[]{:S(2)}) collective-permute-start(bf16[1,25,2048]{1,2,0:T(8,128)(2,1)S(1)} %copy.17), channel_id=1, source_target_pairs={{0,8},{8,16},{16,24},{24,32},{32,40},{40,48},{48,56},{56,64},{64,7... | collective-permute-start | bytes 307208 | tf_op jit(solution)/shard_map/ppermute | solution.py:19
  30.8 74.9 %collective-permute-start.4 = (bf16[1,25,200]{2,1,0:T(8,128)(2,1)}, bf16[1,25,200]{2,1,0:T(8,128)(2,1)S(1)}, u32[]{:S(2)}, u32[]{:S(2)}) collective-permute-start(bf16[1,25,200]{2,1,0:T(8,128)(2,1)} %param.11), channel_id=1, source_target_pairs={{0,8},{8,16},{16,24},{24,32},{32,40},{40,48},{48,56},{56,64},{64,7... | collective-permute-start | bytes 30008 | tf_op jit(solution)/shard_map/ppermute | solution.py:19
  115.0 3.7 %collective-permute-start.5 = (f32[64]{0:T(128)S(1)}, f32[64]{0:T(128)S(1)}, u32[]{:S(2)}, u32[]{:S(2)}) collective-permute-start(f32[64]{0:T(128)S(1)} %select_reduce_fusion.3), channel_id=1, source_target_pairs={{0,1},{1,0},{2,3},{3,2},{4,5},{5,4},{6,7},{7,6},{8,9},{9,8},{10,11... | collective-permute-start | bytes 776 | tf_op jit(solution)/shard_map/ppermute | solution.py:26
  118.6 5.1 %collective-permute-start.6 = (f32[64]{0:T(128)S(1)}, f32[64]{0:T(128)S(1)}, u32[]{:S(2)}, u32[]{:S(2)}) collective-permute-start(f32[64]{0:T(128)S(1)} %add.85), channel_id=1, source_target_pairs={{0,2},{1,3},{2,0},{3,1},{4,6},{5,7},{6,4},{7,5},{8,10},{9,11},{10,... | collective-permute-start | bytes 776 | tf_op jit(solution)/shard_map/ppermute | solution.py:26
  123.7 5.1 %collective-permute-start.7 = (f32[64]{0:T(128)S(1)}, f32[64]{0:T(128)S(1)}, u32[]{:S(2)}, u32[]{:S(2)}) collective-permute-start(f32[64]{0:T(128)S(1)} %add.86), channel_id=1, source_target_pairs={{0,4},{1,5},{2,6},{3,7},{4,0},{5,1},{6,2},{7,3},{8,12},{9,13},{10,... | collective-permute-start | bytes 776 | tf_op jit(solution)/shard_map/ppermute | solution.py:26
Sparse Core Ops, SparseCore 0:
  27.8 75.2 all-gather.1

commit v15 on v13

--- a/solution.py
+++ b/solution.py
@@ -51,7 +51,7 @@
         out_ref[pl.ds(j, 1), :] = jnp.sum(prod, axis=0, keepdims=True)
         return carry
 
-    lax.fori_loop(0, chunk, one, 0, unroll=2)
+    lax.fori_loop(0, chunk, one, 0, unroll=4)
 
 
 def tile_bias(panel_t, green, parts, rbs, cbs):

time: 163 us -> 162 us (level)
  no operation moved by 1% of the time
where the time goes in v15:
time: 162 us
  waiting for transfers between devices  82.8 us (51%)
  Pallas kernels  33.7 us (21%)
  starting transfers between devices  19.6 us (12%)
  between operations  14.9 us (9%)
  other arithmetic  6.27 us (4%)
  local copies, waits for them, and re-layouts  3.12 us (2%)
    all_gather x1, waiting for transfers between devices, shards(): lax.all_gather(xor_gather(payload, order), 'walker', axis=0, tiled=True)  66.1 us
    pallas_call x1, Pallas kernels, propagate(): pl.pallas_call(prop_kernel, out_shape=jax.ShapeDtypeStruct((orbitals, wid...  25.2 us
    ppermute x3, waiting for transfers between devices, xor_gather(): other = lax.ppermute(x, axis, [(i, i ^ step) for i in range(count)])  9.57 us
    pallas_call x1, Pallas kernels, tile_bias(): pl.pallas_call(bias_kernel, out_shape=jax.ShapeDtypeStruct((tiles_total,...  8.47 us
    ppermute x3, waiting for transfers between devices, butterfly_sum(): lax.ppermute(value, axis, [(i, i ^ step) for i in range(count)])  7.03 us
    ppermute x3, starting transfers between devices, xor_gather(): other = lax.ppermute(x, axis, [(i, i ^ step) for i in range(count)])  6.98 us
    ppermute x3, starting transfers between devices, butterfly_sum(): lax.ppermute(value, axis, [(i, i ^ step) for i in range(count)])  6.77 us
    ppermute x2, starting transfers between devices, shift_from(): lax.ppermute(value, axis, [(i, i + steps) for i in range(count - steps)])  5.82 us
  transfers between devices with their start and end apart: 9, of which 7 were waited for; matrix products, arithmetic and copies ran while one was open for 3% of the time, Pallas kernels for 0%

profile of v15, /device:TPU:2, one launch (start us, length us, event | category | flops | bytes accessed | tf_op | source)
XLA Modules:
  0.0 161.6 jit_solution(1487294505390376781)
XLA Ops:
  8.1 2.1 %collective-permute-start = (bf16[1,144,128]{2,1,0:T(8,128)(2,1)S(1)}, bf16[1,144,128]{2,1,0:T(8,128)(2,1)S(1)}, u32[]{:S(2)}, u32[]{:S(2)}) collective-permute-start(bf16[1,144,128]{2,1,0:T(8,128)(2,1)S(1)} %pad_maximum_fusion.3), channel_id=1, source_target_pairs={{0,4},{1,5},{2,6},{3,7},{4,0},{5,1},{6,2},{7,3},{8,12},{9,13},{10,... | collective-permute-start | bytes 110600 | tf_op jit(solution)/shard_map/ppermute | solution.py:161
  10.2 3.3 %collective-permute-done = bf16[1,144,128]{2,1,0:T(8,128)(2,1)S(1)} collective-permute-done((bf16[1,144,128]{2,1,0:T(8,128)(2,1)S(1)}, bf16[1,144,128]{2,1,0:T(8,128)(2,1)S(1)}, u32[]{:S(2)}, u32[]{:S(2)}) %collective-permute-start) | collective-permute-done | bytes 36896 | tf_op jit(solution)/shard_map/ppermute | solution.py:161
  14.3 3.2 %collective-permute-start.1 = (bf16[2,144,128]{2,1,0:T(8,128)(2,1)S(1)}, bf16[2,144,128]{2,1,0:T(8,128)(2,1)S(1)}, u32[]{:S(2)}, u32[]{:S(2)}) collective-permute-start(bf16[2,144,128]{2,1,0:T(8,128)(2,1)S(1)} %pad_maximum_fusion.2), channel_id=1, source_target_pairs={{0,2},{1,3},{2,0},{3,1},{4,6},{5,7},{6,4},{7,5},{8,10},{9,11},{10,... | collective-permute-start | bytes 221192 | tf_op jit(solution)/shard_map/ppermute | solution.py:161
  17.5 2.7 %collective-permute-done.1 = bf16[2,144,128]{2,1,0:T(8,128)(2,1)S(1)} collective-permute-done((bf16[2,144,128]{2,1,0:T(8,128)(2,1)S(1)}, bf16[2,144,128]{2,1,0:T(8,128)(2,1)S(1)}, u32[]{:S(2)}, u32[]{:S(2)}) %collective-permute-start.1) | collective-permute-done | bytes 73760 | tf_op jit(solution)/shard_map/ppermute | solution.py:161
  20.1 0.8 pad_maximum_fusion.1
  20.9 1.7 %collective-permute-start.2 = (bf16[4,144,128]{2,1,0:T(8,128)(2,1)S(1)}, bf16[4,144,128]{2,1,0:T(8,128)(2,1)S(1)}, u32[]{:S(2)}, u32[]{:S(2)}) collective-permute-start(bf16[4,144,128]{2,1,0:T(8,128)(2,1)S(1)} %pad_maximum_fusion.1), channel_id=1, source_target_pairs={{0,1},{1,0},{2,3},{3,2},{4,5},{5,4},{6,7},{7,6},{8,9},{9,8},{10,11... | collective-permute-start | bytes 442376 | tf_op jit(solution)/shard_map/ppermute | solution.py:161
  22.6 3.6 %collective-permute-done.2 = bf16[4,144,128]{2,1,0:T(8,128)(2,1)S(1)} collective-permute-done((bf16[4,144,128]{2,1,0:T(8,128)(2,1)S(1)}, bf16[4,144,128]{2,1,0:T(8,128)(2,1)S(1)}, u32[]{:S(2)}, u32[]{:S(2)}) %collective-permute-start.2) | collective-permute-done | bytes 147488 | tf_op jit(solution)/shard_map/ppermute | solution.py:161
  26.1 1.5 pad_maximum_fusion
  27.7 1.2 copy.17
  28.9 1.9 %collective-permute-start.3 = (bf16[1,25,2048]{1,2,0:T(8,128)(2,1)S(1)}, bf16[1,25,2048]{1,2,0:T(8,128)(2,1)S(1)}, u32[]{:S(2)}, u32[]{:S(2)}) collective-permute-start(bf16[1,25,2048]{1,2,0:T(8,128)(2,1)S(1)} %copy.17), channel_id=1, source_target_pairs={{0,8},{8,16},{16,24},{24,32},{32,40},{40,48},{48,56},{56,64},{64,7... | collective-permute-start | bytes 307208 | tf_op jit(solution)/shard_map/ppermute | solution.py:19
  30.8 3.9 %collective-permute-start.4 = (bf16[1,25,200]{2,1,0:T(8,128)(2,1)}, bf16[1,25,200]{2,1,0:T(8,128)(2,1)S(1)}, u32[]{:S(2)}, u32[]{:S(2)}) collective-permute-start(bf16[1,25,200]{2,1,0:T(8,128)(2,1)} %param.11), channel_id=1, source_target_pairs={{0,8},{8,16},{16,24},{24,32},{32,40},{40,48},{48,56},{56,64},{64,7... | collective-permute-start | bytes 30008 | tf_op jit(solution)/shard_map/ppermute | solution.py:19
  34.9 0.8 fusion.15
  35.9 1.0 convolution_convert_fusion
  36.9 66.1 %all-gather.2.cloned.1.call-done.part_ref = bf16[256,144,128]{2,1,0:T(8,128)(2,1)} async-done(((bf16[8,144,128]{2,1,0:T(8,128)(2,1)}), bf16[256,144,128]{2,1,0:T(8,128)(2,1)}) %all-gather.2.cloned.1.call-update) | async-done | bytes 9437200 | tf_op jit(solution)/shard_map/all_gather | solution.py:197
  103.0 1.2 convert_reduce_fusion
  106.0 8.5 %shard_map.73 = f32[256,128]{1,0:T(8,128)S(1)} custom-call(s32[256]{0:T(256)S(1)} %get-tuple-element.18.rb_ref, s32[256]{0:T(256)S(1)} %get-tuple-element.17.cb_ref, bf16[2048,32]{1,0:T(8,128)(2,1)S(1)} %pad_bitcast_fusion.pt_ref.x_ref, bf16[32,2048]{1,0:T(8,128)(2,1)S(1)} %pad.14.g_ref, bf16[256,144,128]{2,1,0:T(8,128)(2,1)} %all-gather.2.cloned.1.call-done.part_ref), custom_call_target="tpu_custom_call" | custom-call | tf_op jit(solution)/shard_map/pallas_call | solution.py:63
  114.7 1.6 collective-permute-start.5
  116.3 2.0 %collective-permute-done.5 = f32[64]{0:T(128)S(1)} collective-permute-done((f32[64]{0:T(128)S(1)}, f32[64]{0:T(128)S(1)}, u32[]{:S(2)}, u32[]{:S(2)}) %collective-permute-start.5) | collective-permute-done | bytes 288 | tf_op jit(solution)/shard_map/ppermute | solution.py:26
  118.3 3.0 %collective-permute-start.6 = (f32[64]{0:T(128)S(1)}, f32[64]{0:T(128)S(1)}, u32[]{:S(2)}, u32[]{:S(2)}) collective-permute-start(f32[64]{0:T(128)S(1)} %add.85), channel_id=1, source_target_pairs={{0,2},{1,3},{2,0},{3,1},{4,6},{5,7},{6,4},{7,5},{8,10},{9,11},{10,... | collective-permute-start | bytes 776 | tf_op jit(solution)/shard_map/ppermute | solution.py:26
  121.4 2.0 %collective-permute-done.6 = f32[64]{0:T(128)S(1)} collective-permute-done((f32[64]{0:T(128)S(1)}, f32[64]{0:T(128)S(1)}, u32[]{:S(2)}, u32[]{:S(2)}) %collective-permute-start.6) | collective-permute-done | bytes 288 | tf_op jit(solution)/shard_map/ppermute | solution.py:26
  123.4 2.1 %collective-permute-start.7 = (f32[64]{0:T(128)S(1)}, f32[64]{0:T(128)S(1)}, u32[]{:S(2)}, u32[]{:S(2)}) collective-permute-start(f32[64]{0:T(128)S(1)} %add.86), channel_id=1, source_target_pairs={{0,4},{1,5},{2,6},{3,7},{4,0},{5,1},{6,2},{7,3},{8,12},{9,13},{10,... | collective-permute-start | bytes 776 | tf_op jit(solution)/shard_map/ppermute | solution.py:26
  125.5 2.9 %collective-permute-done.7 = f32[64]{0:T(128)S(1)} collective-permute-done((f32[64]{0:T(128)S(1)}, f32[64]{0:T(128)S(1)}, u32[]{:S(2)}, u32[]{:S(2)}) %collective-permute-start.7) | collective-permute-done | bytes 288 | tf_op jit(solution)/shard_map/ppermute | solution.py:26
  128.6 25.2 %shard_map.74 = bf16[2048,32]{1,0:T(8,128)(2,1)S(1)} custom-call(s32[256]{0:T(256)S(1)} %get-tuple-element.18.rb_ref, s32[256]{0:T(256)S(1)} %get-tuple-element.17.cb_ref, f32[256]{0:T(256)S(1)} %select_reduce_fusion.2.s_ref, bf16[2048,32]{1,0:T(8,128)(2,1)S(1)} %pad_bitcast_fusion.pt_ref.x_ref, bf16[256,144,128]{2,1,0:T(8,128)(2,1)} %all-gather.2.cloned.1.call-done.part_ref), custom_call_target="tpu_custom_call" | custom-call | tf_op jit(solution)/shard_map/pallas_call | solution.py:131
  153.8 0.9 copy.19
  (29 shorter events, 3.4 us)
Async XLA Ops:
  6.5 29.4 %copy-start = (bf16[200,2048]{1,0:T(8,128)(2,1)S(1)}, bf16[200,2048]{1,0:T(8,128)(2,1)}, u32[]{:S(2)}) copy-start(bf16[200,2048]{1,0:T(8,128)(2,1)} %param.12) | copy-start | bytes 2457604
  6.5 121.9 %copy-start.1 = (f32[1,64]{1,0:T(1,128)S(1)}, f32[1,64]{1,0:T(1,128)}, u32[]{:S(2)}) copy-start(f32[1,64]{1,0:T(1,128)} %param.15) | copy-start | bytes 772
  6.5 96.5 %all-gather.2.cloned.1.call-start = ((), (), s32[]{:S(2)}) async-start(), calls=%async_computation | async-start | bytes 9732096 | tf_op jit(solution)/shard_map/all_gather | solution.py:197
  8.1 5.5 %collective-permute-start = (bf16[1,144,128]{2,1,0:T(8,128)(2,1)S(1)}, bf16[1,144,128]{2,1,0:T(8,128)(2,1)S(1)}, u32[]{:S(2)}, u32[]{:S(2)}) collective-permute-start(bf16[1,144,128]{2,1,0:T(8,128)(2,1)S(1)} %pad_maximum_fusion.3), channel_id=1, source_target_pairs={{0,4},{1,5},{2,6},{3,7},{4,0},{5,1},{6,2},{7,3},{8,12},{9,13},{10,... | collective-permute-start | bytes 110600 | tf_op jit(solution)/shard_map/ppermute | solution.py:161
  14.3 5.9 %collective-permute-start.1 = (bf16[2,144,128]{2,1,0:T(8,128)(2,1)S(1)}, bf16[2,144,128]{2,1,0:T(8,128)(2,1)S(1)}, u32[]{:S(2)}, u32[]{:S(2)}) collective-permute-start(bf16[2,144,128]{2,1,0:T(8,128)(2,1)S(1)} %pad_maximum_fusion.2), channel_id=1, source_target_pairs={{0,2},{1,3},{2,0},{3,1},{4,6},{5,7},{6,4},{7,5},{8,10},{9,11},{10,... | collective-permute-start | bytes 221192 | tf_op jit(solution)/shard_map/ppermute | solution.py:161
  20.9 5.2 %collective-permute-start.2 = (bf16[4,144,128]{2,1,0:T(8,128)(2,1)S(1)}, bf16[4,144,128]{2,1,0:T(8,128)(2,1)S(1)}, u32[]{:S(2)}, u32[]{:S(2)}) collective-permute-start(bf16[4,144,128]{2,1,0:T(8,128)(2,1)S(1)} %pad_maximum_fusion.1), channel_id=1, source_target_pairs={{0,1},{1,0},{2,3},{3,2},{4,5},{5,4},{6,7},{7,6},{8,9},{9,8},{10,11... | collective-permute-start | bytes 442376 | tf_op jit(solution)/shard_map/ppermute | solution.py:161
  28.9 76.6 %collective-permute-start.3 = (bf16[1,25,2048]{1,2,0:T(8,128)(2,1)S(1)}, bf16[1,25,2048]{1,2,0:T(8,128)(2,1)S(1)}, u32[]{:S(2)}, u32[]{:S(2)}) collective-permute-start(bf16[1,25,2048]{1,2,0:T(8,128)(2,1)S(1)} %copy.17), channel_id=1, source_target_pairs={{0,8},{8,16},{16,24},{24,32},{32,40},{40,48},{48,56},{56,64},{64,7... | collective-permute-start | bytes 307208 | tf_op jit(solution)/shard_map/ppermute | solution.py:19
  30.8 74.9 %collective-permute-start.4 = (bf16[1,25,200]{2,1,0:T(8,128)(2,1)}, bf16[1,25,200]{2,1,0:T(8,128)(2,1)S(1)}, u32[]{:S(2)}, u32[]{:S(2)}) collective-permute-start(bf16[1,25,200]{2,1,0:T(8,128)(2,1)} %param.11), channel_id=1, source_target_pairs={{0,8},{8,16},{16,24},{24,32},{32,40},{40,48},{48,56},{56,64},{64,7... | collective-permute-start | bytes 30008 | tf_op jit(solution)/shard_map/ppermute | solution.py:19
  114.7 3.7 %collective-permute-start.5 = (f32[64]{0:T(128)S(1)}, f32[64]{0:T(128)S(1)}, u32[]{:S(2)}, u32[]{:S(2)}) collective-permute-start(f32[64]{0:T(128)S(1)} %select_reduce_fusion.3), channel_id=1, source_target_pairs={{0,1},{1,0},{2,3},{3,2},{4,5},{5,4},{6,7},{7,6},{8,9},{9,8},{10,11... | collective-permute-start | bytes 776 | tf_op jit(solution)/shard_map/ppermute | solution.py:26
  118.3 5.1 %collective-permute-start.6 = (f32[64]{0:T(128)S(1)}, f32[64]{0:T(128)S(1)}, u32[]{:S(2)}, u32[]{:S(2)}) collective-permute-start(f32[64]{0:T(128)S(1)} %add.85), channel_id=1, source_target_pairs={{0,2},{1,3},{2,0},{3,1},{4,6},{5,7},{6,4},{7,5},{8,10},{9,11},{10,... | collective-permute-start | bytes 776 | tf_op jit(solution)/shard_map/ppermute | solution.py:26
  123.4 5.1 %collective-permute-start.7 = (f32[64]{0:T(128)S(1)}, f32[64]{0:T(128)S(1)}, u32[]{:S(2)}, u32[]{:S(2)}) collective-permute-start(f32[64]{0:T(128)S(1)} %add.86), channel_id=1, source_target_pairs={{0,4},{1,5},{2,6},{3,7},{4,0},{5,1},{6,2},{7,3},{8,12},{9,13},{10,... | collective-permute-start | bytes 776 | tf_op jit(solution)/shard_map/ppermute | solution.py:26
Sparse Core Ops, SparseCore 0:
  27.8 75.2 all-gather.1
